TPU v7x, 256 devices: a whole 4x4x8 slice. The times are simulated.
256 devices in a mesh: seq: 32 (over x, z), exp: 8 (over y, core).
Axes of the slice: x: 4, y: 4, z: 8, core: 2. Of those that a mesh axis runs over, the one named last changes fastest.
Arguments:
- queries: bfloat16 [32768, 4096], P(('seq', 'exp')), may hold values from -1.75 to 1.75
- keys: bfloat16 [32768, 4096], P(('seq', 'exp')), may hold values from -1.75 to 1.75
- values: bfloat16 [32768, 4096], P(('seq', 'exp')), may hold values from -6 to 6
- out_grad: bfloat16 [32768, 4096], P(('seq', 'exp')), may hold values from -0.0625 to 0.0625
- log_decay: bfloat16 [32768, 32], P(('seq', 'exp')), may hold values from -0.7 to 0
Outputs:
- query_grad: bfloat16 [32768, 4096], P(('seq', 'exp'))
- key_grad: bfloat16 [32768, 4096], P(('seq', 'exp'))
- value_grad: bfloat16 [32768, 4096], P(('seq', 'exp'))
All inputs are finite; a program needn't handle non-finite values.
Results may differ from a plain program's by a relative error of at most 0.0095.
Values may be sent and summed in bfloat16 or wider, within the bound.
No kernel may reach another device: no remote copies, remote signals or barrier semaphores. Data moves between devices by JAX's collectives and lax.ppermute only.
A program may use at most 64 MiB of HBM per device.

v0:
```python
import jax
import jax.numpy as jnp
from jax import lax
from jax.sharding import Mesh
from jax.sharding import PartitionSpec as P

BLOCK = 128
SEQ = ("seq_0", "seq_1")
SEQ_EXP = ("seq_0", "seq_1", "exp")


def filled_with(x, identity):
    return jax.tree.map(
        lambda part, zero: jnp.zeros_like(part) + jnp.asarray(zero, part.dtype), x, identity
    )


def carried_in(x, axes, combine, identity, reverse):
    before = start = filled_with(x, identity)
    total = x
    for axis in reversed(axes):
        peers, here = (lax.axis_size(axis), lax.axis_index(axis))
        pieces = jax.tree.map(lambda part: lax.all_gather(part, axis), total)
        inside, total = (start, start)
        for k in reversed(range(peers)) if reverse else range(peers):
            passed = k > here if reverse else k < here
            total = combine(total, jax.tree.map(lambda part: part[k], pieces))
            inside = jax.tree.map(lambda new, old: jnp.where(passed, new, old), total, inside)
        before = combine(inside, before)
    return before


def widen(array):
    return array.astype(jnp.float32)


def halves(array):
    high = array.astype(jnp.bfloat16)
    low = (array - widen(high)).astype(jnp.bfloat16)
    return (high, low)


def product(form, first_op, second_op):
    return jnp.einsum(form, first_op, second_op, preferred_element_type=jnp.float32)


def split_left(form, wide_op, narrow_op):
    high, low = halves(wide_op)
    return product(form, high, narrow_op) + product(form, low, narrow_op)


def split_right(form, narrow_op, wide_op):
    high, low = halves(wide_op)
    return product(form, narrow_op, high) + product(form, narrow_op, low)


def link(earlier, later):
    return (earlier[0] + later[0], jnp.exp(later[0])[:, None, None] * earlier[1] + later[1])


def key_side(key_loc, value_loc, decay_loc):
    rows = key_loc.shape[0]
    heads = decay_loc.shape[1]
    width = key_loc.shape[1] // heads
    blocks = rows // BLOCK
    key_blk = key_loc.reshape(blocks, BLOCK, heads, width)
    value_blk = value_loc.reshape(blocks, BLOCK, heads, width)
    cumul = jnp.cumsum(widen(decay_loc).reshape(blocks, BLOCK, heads), axis=1)
    totals = cumul[:, -1, :]
    after = jnp.exp(totals[:, None, :] - cumul)
    contrib = split_left("nsha,nshb->nhab", after[..., None] * widen(key_blk), value_blk)

    def key_step(carry, item):
        state, logsum = carry
        total, piece = item
        return ((jnp.exp(total)[:, None, None] * state + piece, logsum + total), (state, logsum))

    zero_state = jnp.zeros((heads, width, width), jnp.float32)
    zero_log = jnp.zeros((heads,), jnp.float32)
    (dev_state, dev_log), (prefix, prefix_log) = lax.scan(
        key_step, (zero_state, zero_log), (totals, contrib)
    )
    return (key_blk, value_blk, cumul, totals, after, prefix, prefix_log, dev_state, dev_log)


def query_side(query_loc, grad_loc, cumul, totals):
    blocks, length, heads = cumul.shape
    width = query_loc.shape[1] // heads
    query_blk = query_loc.reshape(blocks, length, heads, width)
    grad_blk = grad_loc.reshape(blocks, length, heads, width)
    before = jnp.exp(cumul)
    updates = split_left("ntha,nthb->nhab", before[..., None] * widen(query_blk), grad_blk)

    def query_step(carry, item):
        adjoint, logsum = carry
        total, piece = item
        return (
            (jnp.exp(total)[:, None, None] * adjoint + piece, logsum + total),
            (adjoint, logsum),
        )

    zero_state = jnp.zeros((heads, width, width), jnp.float32)
    zero_log = jnp.zeros((heads,), jnp.float32)
    (dev_adjoint, unused), (suffix, suffix_log) = lax.scan(
        query_step, (zero_state, zero_log), (totals, updates), reverse=True
    )
    return (query_blk, grad_blk, before, suffix, suffix_log, dev_adjoint)


def finish(
    query_blk,
    key_blk,
    value_blk,
    grad_blk,
    cumul,
    after,
    before,
    prefix,
    prefix_log,
    suffix,
    suffix_log,
    start_state,
    start_adjoint,
):
    state_prev = jnp.exp(prefix_log)[:, :, None, None] * start_state[None] + prefix
    adjoint = jnp.exp(suffix_log)[:, :, None, None] * start_adjoint[None] + suffix
    blocks, length, heads = cumul.shape
    width = key_blk.shape[3]
    heads_first = jnp.transpose(cumul, (0, 2, 1))
    spread = heads_first[:, :, :, None] - heads_first[:, :, None, :]
    causal = lax.broadcasted_iota(jnp.int32, (length, length), 1) <= lax.broadcasted_iota(
        jnp.int32, (length, length), 0
    )
    weights = jnp.where(
        causal[None, None], jnp.exp(jnp.where(causal[None, None], spread, 0.0)), 0.0
    )
    grad_scores = product("nthd,nshd->nhts", grad_blk, value_blk)
    key_scores = product("nthd,nshd->nhts", query_blk, key_blk)
    first = (weights * grad_scores).astype(jnp.bfloat16)
    second = (weights * key_scores).astype(jnp.bfloat16)
    query_part = product("nhts,nshd->nthd", first, key_blk)
    key_part = product("nhts,nthd->nshd", first, query_blk)
    value_part = product("nhts,nthd->nshd", second, grad_blk)
    grad_query = query_part + before[..., None] * split_right(
        "nthb,nhab->ntha", grad_blk, state_prev
    )
    adj_high, adj_low = halves(adjoint)
    grad_key = key_part + after[..., None] * (
        product("nshb,nhab->nsha", value_blk, adj_high)
        + product("nshb,nhab->nsha", value_blk, adj_low)
    )
    grad_value = value_part + after[..., None] * (
        product("nsha,nhab->nshb", key_blk, adj_high) + product("nsha,nhab->nshb", key_blk, adj_low)
    )
    rows = blocks * length
    flat_query = grad_query.astype(jnp.bfloat16).reshape(rows, heads * width)
    flat_key = grad_key.astype(jnp.bfloat16).reshape(rows, heads * width)
    flat_value = grad_value.astype(jnp.bfloat16).reshape(rows, heads * width)
    return (flat_query, flat_key, flat_value)


def body(queries, keys, values, out_grad, log_decay):
    query_loc, key_loc, value_loc, grad_loc, decay_loc = (
        lax.all_to_all(queries, "exp", split_axis=1, concat_axis=0, tiled=True),
        lax.all_to_all(keys, "exp", split_axis=1, concat_axis=0, tiled=True),
        lax.all_to_all(values, "exp", split_axis=1, concat_axis=0, tiled=True),
        lax.all_to_all(out_grad, "exp", split_axis=1, concat_axis=0, tiled=True),
        lax.all_to_all(log_decay, "exp", split_axis=1, concat_axis=0, tiled=True),
    )
    key_blk, value_blk, cumul, totals, after, prefix, prefix_log, dev_state, dev_log = key_side(
        key_loc, value_loc, decay_loc
    )
    heads = cumul.shape[2]
    width = key_blk.shape[3]
    zero_state = jnp.zeros((heads, width, width), jnp.float32)
    zero_log = jnp.zeros((heads,), jnp.float32)
    start_state = carried_in((dev_log, dev_state), SEQ, link, (zero_log, zero_state), False)[1]
    query_blk, grad_blk, before, suffix, suffix_log, dev_adjoint = query_side(
        query_loc, grad_loc, cumul, totals
    )
    start_adjoint = carried_in((dev_log, dev_adjoint), SEQ, link, (zero_log, zero_state), True)[1]
    flat_query, flat_key, flat_value = finish(
        query_blk,
        key_blk,
        value_blk,
        grad_blk,
        cumul,
        after,
        before,
        prefix,
        prefix_log,
        suffix,
        suffix_log,
        start_state,
        start_adjoint,
    )
    result = (
        lax.all_to_all(flat_query, "exp", split_axis=0, concat_axis=1, tiled=True),
        lax.all_to_all(flat_key, "exp", split_axis=0, concat_axis=1, tiled=True),
        lax.all_to_all(flat_value, "exp", split_axis=0, concat_axis=1, tiled=True),
    )
    return result


def solution(mesh):
    torus = Mesh(mesh.devices.reshape(4, 8, mesh.shape["exp"]), ("seq_0", "seq_1", "exp"))
    placed = (
        P(SEQ_EXP, None),
        P(SEQ_EXP, None),
        P(SEQ_EXP, None),
        P(SEQ_EXP, None),
        P(SEQ_EXP, None),
    )
    return jax.shard_map(
        body,
        mesh=torus,
        in_specs=placed,
        out_specs=(P(SEQ_EXP, None), P(SEQ_EXP, None), P(SEQ_EXP, None)),
        check_vma=False,
    )
```

profile of v0, /device:TPU:32, one launch (start us, length us, event | category | flops | bytes accessed | tf_op | source)
XLA Modules:
  0.0 306.2 jit_solution(12512901773788062015)
XLA Ops:
  7.2 4.5 %all-to-all-start = ((bf16[128,8,4]{0,2,1:T(4,128)(2,1)}), bf16[128,8,4]{0,2,1:T(4,128)(2,1)S(1)}, u32[]{:S(2)}, u32[]{:S(2)}) async-start(bf16[128,8,4]{0,2,1:T(4,128)(2,1)} %bitcast.362), calls=%async_computation | async-start | bytes 16384 | tf_op jit(solution)/shard_map/all_to_all | solution.py:168
  17.0 3.6 %all-to-all-start.2 = ((bf16[128,8,512]{0,2,1:T(8,128)(2,1)}), bf16[128,8,512]{0,2,1:T(8,128)(2,1)S(1)}, u32[]{:S(2)}, u32[]{:S(2)}) async-start(bf16[128,8,512]{0,2,1:T(8,128)(2,1)} %bitcast.6), calls=%async_computation.2 | async-start | bytes 2097152 | tf_op jit(solution)/shard_map/all_to_all | solution.py:166
  21.9 14.6 %all-to-all-done.2 = bf16[128,8,512]{0,2,1:T(8,128)(2,1)S(1)} async-done(((bf16[128,8,512]{0,2,1:T(8,128)(2,1)}), bf16[128,8,512]{0,2,1:T(8,128)(2,1)S(1)}, u32[]{:S(2)}, u32[]{:S(2)}) %all-to-all-start.2) | async-done | bytes 1048608 | tf_op jit(solution)/shard_map/all_to_all | solution.py:166
  37.4 3.6 %all-to-all-start.3 = ((bf16[128,8,512]{0,2,1:T(8,128)(2,1)}), bf16[128,8,512]{0,2,1:T(8,128)(2,1)S(1)}, u32[]{:S(2)}, u32[]{:S(2)}) async-start(bf16[128,8,512]{0,2,1:T(8,128)(2,1)} %bitcast.9), calls=%async_computation.3 | async-start | bytes 2097152 | tf_op jit(solution)/shard_map/all_to_all | solution.py:165
  44.8 23.3 %fusion.89 = f32[8,128,4]{2,0,1:T(8,128)S(1)} fusion(f32[8,128,4]{2,0,1:T(8,128)S(1)} %copy.57), kind=kOutput, calls=%fused_computation.176 | output fusion | flops 520192 | bytes 32768 | tf_op jit(solution)/shard_map/jit(cumsum)/reduce_window_sum | solution.py:68
  68.3 4.7 %all-to-all-start.1 = ((bf16[128,8,512]{0,2,1:T(8,128)(2,1)}), bf16[128,8,512]{0,2,1:T(8,128)(2,1)S(1)}, u32[]{:S(2)}, u32[]{:S(2)}) async-start(bf16[128,8,512]{0,2,1:T(8,128)(2,1)} %bitcast.358), calls=%async_computation.1 | async-start | bytes 2097152 | tf_op jit(solution)/shard_map/all_to_all | solution.py:167
  81.0 8.0 %all-to-all-done.1 = bf16[128,8,512]{0,2,1:T(8,128)(2,1)S(1)} async-done(((bf16[128,8,512]{0,2,1:T(8,128)(2,1)}), bf16[128,8,512]{0,2,1:T(8,128)(2,1)S(1)}, u32[]{:S(2)}, u32[]{:S(2)}) %all-to-all-start.1) | async-done | bytes 1048608 | tf_op jit(solution)/shard_map/all_to_all | solution.py:167
  89.0 4.2 %all-to-all-start.5 = ((bf16[128,8,512]{0,2,1:T(8,128)(2,1)}), bf16[128,8,512]{0,2,1:T(8,128)(2,1)}, u32[]{:S(2)}, u32[]{:S(2)}) async-start(bf16[128,8,512]{0,2,1:T(8,128)(2,1)} %bitcast.357), calls=%async_computation.5 | async-start | bytes 2097152 | tf_op jit(solution)/shard_map/all_to_all | solution.py:164
  94.9 14.8 %while.38 = (s32[]{:T(128)}, f32[4,128,128]{2,1,0:T(8,128)S(1)}, f32[4]{0:T(128)S(1)}, f32[8,4,128,128]{3,2,1,0:T(8,128)}, f32[8,4]{1,0:T(8,128)S(1)}, /*index=5...) while((s32[]{:T(128)}, f32[4,128,128]{2,1,0:T(8,128)S(1)}, ...), condition=%wide.region_2.3_spmd.clone, body=%wide.region_1.2_spmd.clone.sunk | while | flops 262155 | bytes 1310977 | solution.py:80
  116.3 9.3 %while.39 = (s32[]{:T(128)}, f32[4,128,128]{2,1,0:T(8,128)S(1)}, f32[4]{0:T(128)S(1)}, f32[8,4,128,128]{3,2,1,0:T(8,128)S(1)}, f32[8,4]{1,0:T(8,128)S(1)}, /*ind...) while((s32[]{:T(128)}, f32[4,128,128]{2,1,0:T(8,128)S(1)}, ...), condition=%wide.region_4.5_spmd.clone, body=%wide.region_3.4_spmd.clone.sunk | while | flops 262156 | bytes 1310997 | solution.py:104
  127.7 17.9 %all-reduce = f32[32]{0:T(128)S(1)} all-reduce(f32[32]{0:T(128)S(1)} %dynamic-update-slice), channel_id=2, replica_groups=mesh['seq_0'=4,'seq_1'=8,'exp'=8] {'seq_1'}, use_global_device_ids=true, to_apply=%add | all-reduce | flops 32 | bytes 256
  145.9 8.3 %all-gather.14.cloned.1.call-done = f32[32,128,128]{2,1,0:T(8,128)} async-done(((f32[4,128,128]{2,1,0:T(8,128)}), f32[32,128,128]{2,1,0:T(8,128)}) %all-gather.14.cloned.1.call-update) | async-done | bytes 2097168 | tf_op jit(solution)/shard_map/all_gather | solution.py:23
  158.1 9.6 %all-gather.3 = f32[4,1,4]{2,1,0:T(1,128)S(1)} all-gather(f32[1,1,4]{2,1,0:T(1,128)S(1)} %get-tuple-element.336), channel_id=1, replica_groups=mesh['seq_0'=4,'seq_1'=8,'exp'=8] {'seq_0'}, dimensions={0}, use_global_device_ids=true | all-gather | bytes 80 | tf_op jit(solution)/shard_map/all_gather | solution.py:23
  167.7 6.9 %all-gather.4 = f32[4,1,4]{2,1,0:T(1,128)S(1)} all-gather(f32[1,1,4]{2,1,0:T(1,128)S(1)} %get-tuple-element.335), channel_id=1, replica_groups=mesh['seq_0'=4,'seq_1'=8,'exp'=8] {'seq_0'}, dimensions={0}, use_global_device_ids=true | all-gather | bytes 80 | tf_op jit(solution)/shard_map/all_gather | solution.py:23
  174.7 3.5 %multiply_convert_fusion.1 = bf16[8,4,128,128]{3,2,1,0:T(8,128)(2,1)} fusion(bf16[8,128,4,128]{1,3,2,0:T(8,128)(2,1)} %bitcast.346, bf16[8,128,4,128]{1,3,2,0:T(8,128)(2,1)} %bitcast.351, f32[8,4,128]{2,1,0:T(4,128)S(1)} %copy.58, pred[128,128]{1,0:T(8,128)(4,1)S(1)} %iota_compare_fusion), kind=kOutput, calls=%fused_computation.36 | convolution fusion | flops 136839168 | bytes 3178496 | tf_op jit(solution)/shard_map/nthd,nshd->nhts/dot_general | solution.py:44
  178.2 17.7 %all-gather.16.cloned.1.call-done = f32[32,128,128]{2,1,0:T(8,128)} async-done(((f32[4,128,128]{2,1,0:T(8,128)}), f32[32,128,128]{2,1,0:T(8,128)}) %all-gather.16.cloned.1.call-update) | async-done | bytes 2097168 | tf_op jit(solution)/shard_map/all_gather | solution.py:23
  201.8 21.3 %all-gather.10.cloned.1.call-done = f32[4,4,128,128]{3,2,1,0:T(8,128)} async-done(((f32[1,4,128,128]{3,2,1,0:T(8,128)}), f32[4,4,128,128]{3,2,1,0:T(8,128)}) %all-gather.10.cloned.1.call-update) | async-done | bytes 1048592 | tf_op jit(solution)/shard_map/all_gather | solution.py:23
  229.2 4.4 %all-to-all-start.4 = ((bf16[8,128,512]{1,2,0:T(8,128)(2,1)}), bf16[8,128,512]{1,2,0:T(8,128)(2,1)}, u32[]{:S(2)}, u32[]{:S(2)}) async-start(bf16[8,128,512]{1,2,0:T(8,128)(2,1)} %bitcast.360), calls=%async_computation.4 | async-start | bytes 2097152 | tf_op jit(solution)/shard_map/all_to_all | solution.py:198
  233.6 18.0 %all-gather.12.cloned.1.call-done = f32[4,4,128,128]{3,2,1,0:T(8,128)} async-done(((f32[1,4,128,128]{3,2,1,0:T(8,128)}), f32[4,4,128,128]{3,2,1,0:T(8,128)}) %all-gather.12.cloned.1.call-update) | async-done | bytes 1048592 | tf_op jit(solution)/shard_map/all_gather | solution.py:23
  258.5 4.3 %all-to-all-start.6 = ((bf16[8,128,512]{1,2,0:T(8,128)(2,1)}), bf16[8,128,512]{1,2,0:T(8,128)(2,1)}, u32[]{:S(2)}, u32[]{:S(2)}) async-start(bf16[8,128,512]{1,2,0:T(8,128)(2,1)} %bitcast.356), calls=%async_computation.6 | async-start | bytes 2097152 | tf_op jit(solution)/shard_map/all_to_all | solution.py:199
  267.0 5.1 %fusion.9 = bf16[8,128,4,128]{1,3,2,0:T(8,128)(2,1)} fusion(f32[8,4,128,128]{3,2,1,0:T(8,128)} %fusion.36, f32[8,4,128,128]{3,2,1,0:T(8,128)} %fusion.84, bf16[8,128,4,128]{1,3,2,0:T(8,128)(2,1)} %bitcast.347, bf16[8,128,4,128]{1,3,2,0:T(8,128)(2,1)} %bitcast.46, bf16[8,128,4,128]{1,3,2,0:T(8,128)(2,1)S(1)} %bitcast.343, f32[8,128,4]{1,2,0:T(4,128)S(1)} %copy.68, ...), kind=kOutput, calls=%fused_computation.18 | convolution fusion | flops 273154048 | bytes 8437760 | tf_op jit(solution)/shard_map/nhts,nthd->nshd/dot_general | solution.py:44
  272.1 6.7 %all-to-all-done.6 = bf16[8,128,512]{1,2,0:T(8,128)(2,1)} async-done(((bf16[8,128,512]{1,2,0:T(8,128)(2,1)}), bf16[8,128,512]{1,2,0:T(8,128)(2,1)}, u32[]{:S(2)}, u32[]{:S(2)}) %all-to-all-start.6) | async-done | bytes 1048608 | tf_op jit(solution)/shard_map/all_to_all | solution.py:199
  278.9 3.6 %all-to-all-start.7 = ((bf16[8,128,512]{1,2,0:T(8,128)(2,1)}), bf16[8,128,512]{1,2,0:T(8,128)(2,1)S(1)}, u32[]{:S(2)}, u32[]{:S(2)}) async-start(bf16[8,128,512]{1,2,0:T(8,128)(2,1)} %bitcast.69), calls=%async_computation.7 | async-start | bytes 2097152 | tf_op jit(solution)/shard_map/all_to_all | solution.py:200
  287.0 11.4 %all-to-all-done.7 = bf16[8,128,512]{1,2,0:T(8,128)(2,1)S(1)} async-done(((bf16[8,128,512]{1,2,0:T(8,128)(2,1)}), bf16[8,128,512]{1,2,0:T(8,128)(2,1)S(1)}, u32[]{:S(2)}, u32[]{:S(2)}) %all-to-all-start.7) | async-done | bytes 1048608 | tf_op jit(solution)/shard_map/all_to_all | solution.py:200
  (158 shorter events, 85.9 us)
Async XLA Ops:
  7.2 9.8 %all-to-all-start = ((bf16[128,8,4]{0,2,1:T(4,128)(2,1)}), bf16[128,8,4]{0,2,1:T(4,128)(2,1)S(1)}, u32[]{:S(2)}, u32[]{:S(2)}) async-start(bf16[128,8,4]{0,2,1:T(4,128)(2,1)} %bitcast.362), calls=%async_computation | async-start | bytes 16384 | tf_op jit(solution)/shard_map/all_to_all | solution.py:168
  11.6 8.9 %copy-start.12 = (bf16[128,4096]{1,0:T(8,128)(2,1)S(1)}, bf16[128,4096]{1,0:T(8,128)(2,1)}, u32[]{:S(2)}) copy-start(bf16[128,4096]{1,0:T(8,128)(2,1)} %param.10) | copy-start | bytes 3145732
  17.0 19.5 %all-to-all-start.2 = ((bf16[128,8,512]{0,2,1:T(8,128)(2,1)}), bf16[128,8,512]{0,2,1:T(8,128)(2,1)S(1)}, u32[]{:S(2)}, u32[]{:S(2)}) async-start(bf16[128,8,512]{0,2,1:T(8,128)(2,1)} %bitcast.6), calls=%async_computation.2 | async-start | bytes 2097152 | tf_op jit(solution)/shard_map/all_to_all | solution.py:166
  20.5 20.5 %copy-start.13 = (bf16[128,4096]{1,0:T(8,128)(2,1)S(1)}, bf16[128,4096]{1,0:T(8,128)(2,1)}, u32[]{:S(2)}) copy-start(bf16[128,4096]{1,0:T(8,128)(2,1)} %param.12) | copy-start | bytes 3145732
  37.4 31.0 %all-to-all-start.3 = ((bf16[128,8,512]{0,2,1:T(8,128)(2,1)}), bf16[128,8,512]{0,2,1:T(8,128)(2,1)S(1)}, u32[]{:S(2)}, u32[]{:S(2)}) async-start(bf16[128,8,512]{0,2,1:T(8,128)(2,1)} %bitcast.9), calls=%async_computation.3 | async-start | bytes 2097152 | tf_op jit(solution)/shard_map/all_to_all | solution.py:165
  68.2 7.2 %copy-start.9 = (f32[8,128,4]{2,0,1:T(8,128)}, f32[8,128,4]{2,0,1:T(8,128)S(1)}, u32[]{:S(2)}) copy-start(f32[8,128,4]{2,0,1:T(8,128)S(1)} %fusion.89) | copy-start | bytes 49156
  68.3 20.7 %all-to-all-start.1 = ((bf16[128,8,512]{0,2,1:T(8,128)(2,1)}), bf16[128,8,512]{0,2,1:T(8,128)(2,1)S(1)}, u32[]{:S(2)}, u32[]{:S(2)}) async-start(bf16[128,8,512]{0,2,1:T(8,128)(2,1)} %bitcast.358), calls=%async_computation.1 | async-start | bytes 2097152 | tf_op jit(solution)/shard_map/all_to_all | solution.py:167
  76.6 2.2 copy-start.5
  89.0 23.6 %copy-start = (bf16[128,8,512]{0,2,1:T(8,128)(2,1)}, bf16[128,8,512]{0,2,1:T(8,128)(2,1)S(1)}, u32[]{:S(2)}) copy-start(bf16[128,8,512]{0,2,1:T(8,128)(2,1)S(1)} %all-to-all-done.1) | copy-start | bytes 3145732
  89.0 21.5 %all-to-all-start.5 = ((bf16[128,8,512]{0,2,1:T(8,128)(2,1)}), bf16[128,8,512]{0,2,1:T(8,128)(2,1)}, u32[]{:S(2)}, u32[]{:S(2)}) async-start(bf16[128,8,512]{0,2,1:T(8,128)(2,1)} %bitcast.357), calls=%async_computation.5 | async-start | bytes 2097152 | tf_op jit(solution)/shard_map/all_to_all | solution.py:164
  93.2 61.0 %all-gather.14.cloned.1.call-start = ((), (), s32[]{:S(2)}) async-start(), calls=%async_computation.10 | async-start | bytes 2359296 | tf_op jit(solution)/shard_map/all_gather | solution.py:23
  110.5 85.4 %all-gather.16.cloned.1.call-start = ((), (), s32[]{:S(2)}) async-start(), calls=%async_computation.11 | async-start | bytes 2359296 | tf_op jit(solution)/shard_map/all_gather | solution.py:23
  116.2 10.1 %copy-start.14 = (u32[256]{0:T(256)S(1)}, u32[256]{0:T(256)}, u32[]{:S(2)}) copy-start(u32[256]{0:T(256)} %constant.92) | copy-start | bytes 3076
  126.3 96.8 %all-gather.10.cloned.1.call-start = ((), (), s32[]{:S(2)}) async-start(), calls=%async_computation.8 | async-start | bytes 1310720 | tf_op jit(solution)/shard_map/all_gather | solution.py:23
  156.7 94.9 %all-gather.12.cloned.1.call-start = ((), (), s32[]{:S(2)}) async-start(), calls=%async_computation.9 | async-start | bytes 1310720 | tf_op jit(solution)/shard_map/all_gather | solution.py:23
  198.4 24.7 %copy-start.11 = (f32[1,4,128,128]{3,2,1,0:T(8,128)S(1)}, f32[1,4,128,128]{3,2,1,0:T(8,128)}, u32[]{:S(2)}) copy-start(f32[1,4,128,128]{3,2,1,0:T(8,128)} %get-tuple-element.313) | copy-start | bytes 786436
  223.1 2.4 copy-start.1
  223.1 2.8 copy-start.7
  225.9 1.6 copy-start.8
  229.2 29.3 %all-to-all-start.4 = ((bf16[8,128,512]{1,2,0:T(8,128)(2,1)}), bf16[8,128,512]{1,2,0:T(8,128)(2,1)}, u32[]{:S(2)}, u32[]{:S(2)}) async-start(bf16[8,128,512]{1,2,0:T(8,128)(2,1)} %bitcast.360), calls=%async_computation.4 | async-start | bytes 2097152 | tf_op jit(solution)/shard_map/all_to_all | solution.py:198
  251.7 2.3 copy-start.6
  254.5 1.2 copy-start.10
  258.5 20.4 %all-to-all-start.6 = ((bf16[8,128,512]{1,2,0:T(8,128)(2,1)}), bf16[8,128,512]{1,2,0:T(8,128)(2,1)}, u32[]{:S(2)}, u32[]{:S(2)}) async-start(bf16[8,128,512]{1,2,0:T(8,128)(2,1)} %bitcast.356), calls=%async_computation.6 | async-start | bytes 2097152 | tf_op jit(solution)/shard_map/all_to_all | solution.py:199
  278.9 19.4 %all-to-all-start.7 = ((bf16[8,128,512]{1,2,0:T(8,128)(2,1)}), bf16[8,128,512]{1,2,0:T(8,128)(2,1)S(1)}, u32[]{:S(2)}, u32[]{:S(2)}) async-start(bf16[8,128,512]{1,2,0:T(8,128)(2,1)} %bitcast.69), calls=%async_computation.7 | async-start | bytes 2097152 | tf_op jit(solution)/shard_map/all_to_all | solution.py:200
  (3 other events, 2.4 us)
Sparse Core Ops, SparseCore 0:
  110.6 43.5 all-gather.13
  156.0 39.8 all-gather.15
  197.7 25.3 all-gather.9
  224.8 26.8 all-gather.11
where the time goes:
time: 309 us; the launch traced here: 306 us
  waiting for transfers between devices  109 us (35%)
  other arithmetic  57.4 us (19%)
  blocking collectives  34.4 us (11%)
  starting transfers between devices  33 us (11%)
  matrix products  32.2 us (10%)
  local copies, waits for them, and re-layouts  25.1 us (8%)
  between operations  14.7 us (5%)
    all_gather x4, waiting for transfers between devices, carried_in(): pieces = jax.tree.map(lambda part: lax.all_gather(part, axis), total)  65.3 us
    dot_general x14, matrix products, product(): jnp.einsum(form, first_op, second_op, preferred_element_type=jnp.float32)  32.2 us
    another operation x1, other arithmetic, key_side(): cumul = jnp.cumsum(widen(decay_loc).reshape(blocks, BLOCK, heads), axis=1)  23.3 us
    unnamed x1, blocking collectives  17.9 us
    all_gather x2, blocking collectives, carried_in(): pieces = jax.tree.map(lambda part: lax.all_gather(part, axis), total)  16.5 us
    all_to_all x1, waiting for transfers between devices, body(): lax.all_to_all(values, 'exp', split_axis=1, concat_axis=0, tiled=True)  14.6 us
    all_to_all x1, waiting for transfers between devices, body(): lax.all_to_all(flat_value, 'exp', split_axis=0, concat_axis=1, tiled=True)  11.4 us
    unnamed x36, local copies, waits for them, and re-layouts  9.11 us
  transfers between devices with their start and end apart: 12, of which 9 were waited for; matrix products, arithmetic and copies ran while one was open for 36% of the time, Pallas kernels for 0%

commit v1 on v0

v1 whole, which is shorter than its diff:
```python
import jax
import jax.numpy as jnp
from jax import lax
from jax.sharding import PartitionSpec as P

BLOCK = 128
SEQ_EXP = ("seq", "exp")


def widen(array):
    return array.astype(jnp.float32)


def halves(array):
    high = array.astype(jnp.bfloat16)
    low = (array - widen(high)).astype(jnp.bfloat16)
    return (high, low)


def product(form, first_op, second_op):
    return jnp.einsum(form, first_op, second_op, preferred_element_type=jnp.float32)


def split_left(form, wide_op, narrow_op):
    high, low = halves(wide_op)
    return product(form, high, narrow_op) + product(form, low, narrow_op)


def split_right(form, narrow_op, wide_op):
    high, low = halves(wide_op)
    return product(form, narrow_op, high) + product(form, narrow_op, low)


def link(earlier, later):
    return (earlier[0] + later[0], jnp.exp(later[0])[:, None, None] * earlier[1] + later[1])


def carried_in(elem, axis, reverse):
    peers = lax.axis_size(axis)
    inclusive = elem
    exclusive = jax.tree.map(jnp.zeros_like, elem)
    shift = 1
    while shift < peers:
        if reverse:
            pairs = [(i, i - shift) for i in range(shift, peers)]
        else:
            pairs = [(i, i + shift) for i in range(peers - shift)]
        got = jax.tree.map(lambda part: lax.ppermute(part, axis, pairs), inclusive)
        exclusive = link(got, exclusive)
        shift *= 2
        if shift < peers:
            inclusive = link(got, inclusive)
    return exclusive


def running_sum(decay_blk):
    length = decay_blk.shape[1]
    lower = (
        lax.broadcasted_iota(jnp.int32, (length, length), 1)
        <= lax.broadcasted_iota(jnp.int32, (length, length), 0)
    ).astype(decay_blk.dtype)
    return jnp.einsum("ts,nsh->nth", lower, decay_blk, preferred_element_type=jnp.float32)


def unrolled(totals, pieces, reverse):
    blocks = totals.shape[0]
    heads, width = pieces.shape[1], pieces.shape[2]
    carry = jnp.zeros((heads, width, width), jnp.float32)
    logsum = jnp.zeros((heads,), jnp.float32)
    seen = [None] * blocks
    seen_log = [None] * blocks
    order = reversed(range(blocks)) if reverse else range(blocks)
    for i in order:
        seen[i] = carry
        seen_log[i] = logsum
        carry = jnp.exp(totals[i])[:, None, None] * carry + pieces[i]
        logsum = logsum + totals[i]
    return jnp.stack(seen), jnp.stack(seen_log), carry, logsum


def key_side(key_loc, value_loc, decay_loc):
    rows = key_loc.shape[0]
    heads = decay_loc.shape[1]
    width = key_loc.shape[1] // heads
    blocks = rows // BLOCK
    key_blk = key_loc.reshape(blocks, BLOCK, heads, width)
    value_blk = value_loc.reshape(blocks, BLOCK, heads, width)
    cumul = running_sum(decay_loc.reshape(blocks, BLOCK, heads))
    totals = cumul[:, -1, :]
    after = jnp.exp(totals[:, None, :] - cumul)
    contrib = split_left("nsha,nshb->nhab", after[..., None] * widen(key_blk), value_blk)
    prefix, prefix_log, dev_state, dev_log = unrolled(totals, contrib, False)
    return (key_blk, value_blk, cumul, totals, after, prefix, prefix_log, dev_state, dev_log)


def query_side(query_loc, grad_loc, cumul, totals):
    blocks, length, heads = cumul.shape
    width = query_loc.shape[1] // heads
    query_blk = query_loc.reshape(blocks, length, heads, width)
    grad_blk = grad_loc.reshape(blocks, length, heads, width)
    before = jnp.exp(cumul)
    updates = split_left("ntha,nthb->nhab", before[..., None] * widen(query_blk), grad_blk)
    suffix, suffix_log, dev_adjoint, unused = unrolled(totals, updates, True)
    return (query_blk, grad_blk, before, suffix, suffix_log, dev_adjoint)


def finish(
    query_blk,
    key_blk,
    value_blk,
    grad_blk,
    cumul,
    after,
    before,
    prefix,
    prefix_log,
    suffix,
    suffix_log,
    start_state,
    start_adjoint,
):
    state_prev = jnp.exp(prefix_log)[:, :, None, None] * start_state[None] + prefix
    adjoint = jnp.exp(suffix_log)[:, :, None, None] * start_adjoint[None] + suffix
    blocks, length, heads = cumul.shape
    width = key_blk.shape[3]
    heads_first = jnp.transpose(cumul, (0, 2, 1))
    spread = heads_first[:, :, :, None] - heads_first[:, :, None, :]
    causal = lax.broadcasted_iota(jnp.int32, (length, length), 1) <= lax.broadcasted_iota(
        jnp.int32, (length, length), 0
    )
    weights = jnp.where(
        causal[None, None], jnp.exp(jnp.where(causal[None, None], spread, 0.0)), 0.0
    )
    grad_scores = product("nthd,nshd->nhts", grad_blk, value_blk)
    key_scores = product("nthd,nshd->nhts", query_blk, key_blk)
    first = (weights * grad_scores).astype(jnp.bfloat16)
    second = (weights * key_scores).astype(jnp.bfloat16)
    query_part = product("nhts,nshd->nthd", first, key_blk)
    key_part = product("nhts,nthd->nshd", first, query_blk)
    value_part = product("nhts,nthd->nshd", second, grad_blk)
    grad_query = query_part + before[..., None] * split_right(
        "nthb,nhab->ntha", grad_blk, state_prev
    )
    adj_high, adj_low = halves(adjoint)
    grad_key = key_part + after[..., None] * (
        product("nshb,nhab->nsha", value_blk, adj_high)
        + product("nshb,nhab->nsha", value_blk, adj_low)
    )
    grad_value = value_part + after[..., None] * (
        product("nsha,nhab->nshb", key_blk, adj_high) + product("nsha,nhab->nshb", key_blk, adj_low)
    )
    rows = blocks * length
    flat_query = grad_query.astype(jnp.bfloat16).reshape(rows, heads * width)
    flat_key = grad_key.astype(jnp.bfloat16).reshape(rows, heads * width)
    flat_value = grad_value.astype(jnp.bfloat16).reshape(rows, heads * width)
    return (flat_query, flat_key, flat_value)


def by_target(array, peers):
    rows = array.shape[0]
    return jnp.transpose(array.reshape(rows, peers, -1), (1, 0, 2))


def body(queries, keys, values, out_grad, log_decay):
    peers = lax.axis_size("exp")
    rows = queries.shape[0]
    width = queries.shape[1] // peers
    lanes = 128
    decay_part = by_target(log_decay, peers)
    narrow = decay_part.shape[2]
    decay_part = jnp.pad(decay_part, ((0, 0), (0, 0), (0, lanes - narrow)))
    packed = jnp.concatenate(
        [by_target(x, peers) for x in (queries, keys, values, out_grad)] + [decay_part], axis=2
    )
    arrived = lax.all_to_all(packed, "exp", 0, 0, tiled=True)
    group_rows = peers * rows

    def column(i, size):
        return arrived[:, :, i * width : i * width + size].reshape(group_rows, size)

    query_loc, key_loc, value_loc, grad_loc = (column(i, width) for i in range(4))
    decay_loc = column(4, narrow)
    key_blk, value_blk, cumul, totals, after, prefix, prefix_log, dev_state, dev_log = key_side(
        key_loc, value_loc, decay_loc
    )
    start_state = carried_in((dev_log, dev_state), "seq", False)[1]
    query_blk, grad_blk, before, suffix, suffix_log, dev_adjoint = query_side(
        query_loc, grad_loc, cumul, totals
    )
    start_adjoint = carried_in((dev_log, dev_adjoint), "seq", True)[1]
    flat_query, flat_key, flat_value = finish(
        query_blk,
        key_blk,
        value_blk,
        grad_blk,
        cumul,
        after,
        before,
        prefix,
        prefix_log,
        suffix,
        suffix_log,
        start_state,
        start_adjoint,
    )
    out_packed = jnp.concatenate([flat_query, flat_key, flat_value], axis=1).reshape(
        peers, rows, 3 * width
    )
    back = lax.all_to_all(out_packed, "exp", 0, 0, tiled=True)

    def gathered(i):
        return jnp.transpose(back[:, :, i * width : (i + 1) * width], (1, 0, 2)).reshape(
            rows, peers * width
        )

    return tuple(gathered(i) for i in range(3))


def solution(mesh):
    placed = tuple(P(SEQ_EXP, None) for _ in range(5))
    return jax.shard_map(
        body,
        mesh=mesh,
        in_specs=placed,
        out_specs=(P(SEQ_EXP, None), P(SEQ_EXP, None), P(SEQ_EXP, None)),
        check_vma=False,
    )
```

time: 309 us -> 271 us (0.88)
  starting transfers between devices: 33 us -> 97.6 us
  waiting for transfers between devices: 109 us -> 60.3 us
  other arithmetic: 57.4 us -> 17.7 us
  between operations: 14.7 us -> 1.27 us
  blocking collectives: 34.4 us -> 41.4 us
  matrix products: 32.2 us -> 26.9 us
    ppermute x0 -> x18, starting transfers between devices: none -> 93 us  [carried_in(): got = jax.tree.map(lambda part: lax.ppermute(part, axis, pairs), inclusive)]
    all_gather x4 -> x0, waiting for transfers between devices: 65.3 us -> none  [carried_in(): pieces = jax.tree.map(lambda part: lax.all_gather(part, axis), total)]
    all_to_all x0 -> x1, blocking collectives: none -> 41.4 us  [body(): back = lax.all_to_all(out_packed, 'exp', 0, 0, tiled=True)]
    all_to_all x8 -> x1, starting transfers between devices: 32.8 us -> 4.56 us  [body(): arrived = lax.all_to_all(packed, 'exp', 0, 0, tiled=True)]
    another operation x1, other arithmetic: 23.3 us -> 0.81 us  [unrolled(): return (jnp.stack(seen), jnp.stack(seen_log), carry, logsum)]
    unnamed x1 -> x0, blocking collectives: 17.9 us -> none
    all_gather x2 -> x0, blocking collectives: 16.5 us -> none  [carried_in(): pieces = jax.tree.map(lambda part: lax.all_gather(part, axis), total)]
    add x32 -> x3, other arithmetic: 17 us -> 2.43 us  [the longest x2 1.84 us: unrolled(): carry = jnp.exp(totals[i])[:, None, None] * carry + pieces[i]]
  transfers between devices with their start and end apart: 12 -> 19, of which waited for: 9 -> 5; matrix products, arithmetic and copies ran while one was open for 36% -> 18% of each run, Pallas kernels for 0% -> 0%
where the time goes in v1:
time: 271 us; the launch traced here: 270 us
  starting transfers between devices  97.6 us (36%)
  waiting for transfers between devices  60.3 us (22%)
  blocking collectives  41.4 us (15%)
  matrix products  26.9 us (10%)
  local copies, waits for them, and re-layouts  24.7 us (9%)
  other arithmetic  17.7 us (7%)
    ppermute x18, starting transfers between devices, carried_in(): got = jax.tree.map(lambda part: lax.ppermute(part, axis, pairs), inclusive)  93 us
    all_to_all x1, waiting for transfers between devices, body(): arrived = lax.all_to_all(packed, 'exp', 0, 0, tiled=True)  51.7 us
    all_to_all x1, blocking collectives, body(): back = lax.all_to_all(out_packed, 'exp', 0, 0, tiled=True)  41.4 us
    dot_general x14, matrix products, product(): jnp.einsum(form, first_op, second_op, preferred_element_type=jnp.float32)  26.8 us
    unnamed x42, local copies, waits for them, and re-layouts  13.9 us
    ppermute x18, waiting for transfers between devices, carried_in(): got = jax.tree.map(lambda part: lax.ppermute(part, axis, pairs), inclusive)  8.55 us
    unnamed x9, other arithmetic  7.57 us
  transfers between devices with their start and end apart: 19, of which 5 were waited for; matrix products, arithmetic and copies ran while one was open for 18% of the time, Pallas kernels for 0%

profile of v1, /device:TPU:32, one launch (start us, length us, event | category | flops | bytes accessed | tf_op | source)
XLA Modules:
  0.0 269.9 jit_solution(10898722376862073764)
XLA Ops:
  11.3 4.6 %all-to-all-start = ((bf16[8,128,2176]{1,2,0:T(8,128)(2,1)}), bf16[8,128,2176]{1,2,0:T(8,128)(2,1)}, u32[]{:S(2)}, u32[]{:S(2)}) async-start(bf16[8,128,2176]{1,2,0:T(8,128)(2,1)} %pad_dynamic-update-slice_fusion), calls=%async_computation | async-start | bytes 8912896 | tf_op jit(solution)/shard_map/all_to_all | solution.py:175
  16.6 51.7 %all-to-all-done = bf16[8,128,2176]{1,2,0:T(8,128)(2,1)} async-done(((bf16[8,128,2176]{1,2,0:T(8,128)(2,1)}), bf16[8,128,2176]{1,2,0:T(8,128)(2,1)}, u32[]{:S(2)}, u32[]{:S(2)}) %all-to-all-start) | async-done | bytes 4456480 | tf_op jit(solution)/shard_map/all_to_all | solution.py:175
  69.7 3.8 %collective-permute-start = (f32[4]{0:T(128)S(1)}, f32[4]{0:T(128)}, u32[]{:S(2)}, u32[]{:S(2)}) collective-permute-start(f32[4]{0:T(128)S(1)} %get-tuple-element.10), channel_id=1, source_target_pairs={{0,8},{8,16},{16,24},{24,32},{32,40},{40,48},{48,56},{56,64},{64,7... | collective-permute-start | bytes 56 | tf_op jit(solution)/shard_map/ppermute | solution.py:48
  73.5 2.6 collective-permute-start.9
  76.1 3.5 %fusion.61 = (bf16[8,128,512]{1,2,0:T(8,128)(2,1)S(1)}, bf16[8,128,512]{1,2,0:T(8,128)(2,1)}, bf16[8,128,512]{1,2,0:T(8,128)(2,1)S(1)}, bf16[8,128,512]{1,2,0:T(8,128)(2,1)S(1)}) fusion(bf16[8,128,2176]{1,2,0:T(8,128)(2,1)} %all-to-all-done), kind=kLoop, calls=%fused_computation.171 | loop fusion | bytes 8388608 | tf_op jit(solution)/shard_map/slice | solution.py:179
  81.6 3.6 %fusion.14 = f32[8,4,128,128]{3,2,1,0:T(8,128)} fusion(bf16[8,128,4,128]{1,3,2,0:T(8,128)(2,1)S(1)} %bitcast.245, bf16[8,128,4,128]{1,3,2,0:T(8,128)(2,1)} %bitcast.255, bf16[8,128,4,128]{1,3,2,0:T(8,128)(2,1)S(1)} %bitcast.238, f32[8,4,128]{2,1,0:T(4,128)S(1)} %copy.93, pred[128,128]{1,0:T(8,128)(4,1)S(1)} %iota_compare_fusion), kind=kOutput, calls=%fused_computation.29 | convolution fusion | flops 271056896 | bytes 5275648 | tf_op jit(solution)/shard_map/nhts,nthd->nshd/dot_general | solution.py:21
  85.2 3.4 %fusion.64 = f32[8,4,128,128]{3,2,1,0:T(8,128)} fusion(bf16[8,128,4,128]{1,3,2,0:T(8,128)(2,1)} %bitcast.256, bf16[8,4,128,128]{3,2,1,0:T(8,128)(2,1)} %multiply_convert_fusion.1), kind=kOutput, calls=%fused_computation.174 | convolution fusion | flops 134217728 | bytes 4194304 | tf_op jit(solution)/shard_map/nhts,nthd->nshd/dot_general | solution.py:21
  88.6 2.2 fusion.63
  91.8 2.2 convolution_add_fusion.1
  110.0 3.9 %collective-permute-start.4 = (f32[4,128,128]{2,1,0:T(8,128)}, f32[4,128,128]{2,1,0:T(8,128)}, u32[]{:S(2)}, u32[]{:S(2)}) collective-permute-start(f32[4,128,128]{2,1,0:T(8,128)} %fusion.32), channel_id=1, source_target_pairs={{0,8},{8,16},{16,24},{24,32},{32,40},{40,48},{48,56},{56,64},{64,7... | collective-permute-start | bytes 786440 | tf_op jit(solution)/shard_map/ppermute | solution.py:48
  118.0 7.6 %collective-permute-start.1 = (f32[4]{0:T(128)S(1)}, f32[4]{0:T(128)S(1)}, u32[]{:S(2)}, u32[]{:S(2)}) collective-permute-start(f32[4]{0:T(128)S(1)} %get-tuple-element.31), channel_id=1, source_target_pairs={{0,16},{8,24},{16,32},{24,40},{32,48},{40,56},{48,64},{56,72},{64,... | collective-permute-start | bytes 56 | tf_op jit(solution)/shard_map/ppermute | solution.py:48
  130.4 10.2 %collective-permute-start.2 = (f32[4]{0:T(128)S(1)}, f32[4]{0:T(128)S(1)}, u32[]{:S(2)}, u32[]{:S(2)}) collective-permute-start(f32[4]{0:T(128)S(1)} %get-tuple-element.29), channel_id=1, source_target_pairs={{0,32},{8,40},{16,48},{24,56},{32,64},{40,72},{48,80},{56,88},{64,... | collective-permute-start | bytes 56 | tf_op jit(solution)/shard_map/ppermute | solution.py:48
  141.9 4.9 %collective-permute-start.5 = (f32[4,128,128]{2,1,0:T(8,128)S(1)}, f32[4,128,128]{2,1,0:T(8,128)S(1)}, u32[]{:S(2)}, u32[]{:S(2)}) collective-permute-start(f32[4,128,128]{2,1,0:T(8,128)S(1)} %get-tuple-element.89), channel_id=1, source_target_pairs={{0,16},{8,24},{16,32},{24,40},{32,48},{40,56},{48,64},{56,72},{64,... | collective-permute-start | bytes 786440 | tf_op jit(solution)/shard_map/ppermute | solution.py:48
  148.3 10.0 %collective-permute-start.3 = (f32[4]{0:T(128)S(1)}, f32[4]{0:T(128)S(1)}, u32[]{:S(2)}, u32[]{:S(2)}) collective-permute-start(f32[4]{0:T(128)S(1)} %get-tuple-element.27), channel_id=1, source_target_pairs={{0,64},{8,72},{16,80},{24,88},{32,96},{40,104},{48,112},{56,120},{... | collective-permute-start | bytes 56 | tf_op jit(solution)/shard_map/ppermute | solution.py:48
  158.4 5.2 %collective-permute-start.6 = (f32[4,128,128]{2,1,0:T(8,128)S(1)}, f32[4,128,128]{2,1,0:T(8,128)S(1)}, u32[]{:S(2)}, u32[]{:S(2)}) collective-permute-start(f32[4,128,128]{2,1,0:T(8,128)S(1)} %multiply_add_fusion.18), channel_id=1, source_target_pairs={{0,32},{8,40},{16,48},{24,56},{32,64},{40,72},{48,80},{56,88},{64,... | collective-permute-start | bytes 786440 | tf_op jit(solution)/shard_map/ppermute | solution.py:48
  167.0 4.6 %collective-permute-done.6 = f32[4,128,128]{2,1,0:T(8,128)S(1)} collective-permute-done((f32[4,128,128]{2,1,0:T(8,128)S(1)}, f32[4,128,128]{2,1,0:T(8,128)S(1)}, u32[]{:S(2)}, u32[]{:S(2)}) %collective-permute-start.6) | collective-permute-done | bytes 262176 | tf_op jit(solution)/shard_map/ppermute | solution.py:48
  171.7 27.7 %collective-permute-start.7 = (f32[4,128,128]{2,1,0:T(8,128)S(1)}, f32[4,128,128]{2,1,0:T(8,128)S(1)}, u32[]{:S(2)}, u32[]{:S(2)}) collective-permute-start(f32[4,128,128]{2,1,0:T(8,128)S(1)} %multiply_add_fusion.17), channel_id=1, source_target_pairs={{0,64},{8,72},{16,80},{24,88},{32,96},{40,104},{48,112},{56,120},{... | collective-permute-start | bytes 786440 | tf_op jit(solution)/shard_map/ppermute | solution.py:48
  200.8 2.4 collective-permute-done.7
  203.3 6.0 %collective-permute-start.8 = (f32[4,128,128]{2,1,0:T(8,128)S(1)}, f32[4,128,128]{2,1,0:T(8,128)S(1)}, u32[]{:S(2)}, u32[]{:S(2)}) collective-permute-start(f32[4,128,128]{2,1,0:T(8,128)S(1)} %multiply_add_fusion.16), channel_id=1, source_target_pairs={{0,128},{8,136},{16,144},{24,152},{32,160},{40,168},{48,176},{56,1... | collective-permute-start | bytes 786440 | tf_op jit(solution)/shard_map/ppermute | solution.py:48
  210.8 2.4 fusion.53
  213.2 2.2 fusion.54
  215.5 2.5 fusion.1
  218.0 2.4 fusion.3
  224.3 41.4 %all_to_all.10 = bf16[8,128,1536]{1,2,0:T(8,128)(2,1)S(1)} all-to-all(bf16[8,128,1536]{1,2,0:T(8,128)(2,1)S(1)} %pad_maximum_fusion), channel_id=1, replica_groups=mesh['seq'=32,'exp'=8] {'exp'}, dimensions={0} | all-to-all | bytes 6291456 | tf_op jit(solution)/shard_map/all_to_all | solution.py:209
  (124 shorter events, 57.4 us)
Async XLA Ops:
  0.6 2.9 %copy-start.12 = (bf16[128,4096]{1,0:T(8,128)(2,1)S(1)}, bf16[128,4096]{1,0:T(8,128)(2,1)}, u32[]{:S(2)}) copy-start(bf16[128,4096]{1,0:T(8,128)(2,1)} %param.6) | copy-start | bytes 3145732
  11.3 57.1 %all-to-all-start = ((bf16[8,128,2176]{1,2,0:T(8,128)(2,1)}), bf16[8,128,2176]{1,2,0:T(8,128)(2,1)}, u32[]{:S(2)}, u32[]{:S(2)}) async-start(bf16[8,128,2176]{1,2,0:T(8,128)(2,1)} %pad_dynamic-update-slice_fusion), calls=%async_computation | async-start | bytes 8912896 | tf_op jit(solution)/shard_map/all_to_all | solution.py:175
  69.7 46.3 %collective-permute-start = (f32[4]{0:T(128)S(1)}, f32[4]{0:T(128)}, u32[]{:S(2)}, u32[]{:S(2)}) collective-permute-start(f32[4]{0:T(128)S(1)} %get-tuple-element.10), channel_id=1, source_target_pairs={{0,8},{8,16},{16,24},{24,32},{32,40},{40,48},{48,56},{56,64},{64,7... | collective-permute-start | bytes 56 | tf_op jit(solution)/shard_map/ppermute | solution.py:48
  73.5 42.5 %collective-permute-start.9 = (f32[4]{0:T(128)S(1)}, f32[4]{0:T(128)S(1)}, u32[]{:S(2)}, u32[]{:S(2)}) collective-permute-start(f32[4]{0:T(128)S(1)} %get-tuple-element.10), channel_id=1, source_target_pairs={{8,0},{16,8},{24,16},{32,24},{40,32},{48,40},{56,48},{64,56},{72,6... | collective-permute-start | bytes 56 | tf_op jit(solution)/shard_map/ppermute | solution.py:48
  79.6 11.2 %copy-start.4 = (bf16[8,128,512]{1,2,0:T(8,128)(2,1)}, bf16[8,128,512]{1,2,0:T(8,128)(2,1)S(1)}, u32[]{:S(2)}) copy-start(bf16[8,128,512]{1,2,0:T(8,128)(2,1)S(1)} %get-tuple-element.54) | copy-start | bytes 3145732
  85.2 3.4 %copy-start.10 = (bf16[8,4,128,128]{3,2,1,0:T(8,128)(2,1)S(1)}, bf16[8,4,128,128]{3,2,1,0:T(8,128)(2,1)}, u32[]{:S(2)}) copy-start(bf16[8,4,128,128]{3,2,1,0:T(8,128)(2,1)} %multiply_convert_fusion.1) | copy-start | bytes 3145732
  95.7 10.8 %copy-start = (f32[8,4,128,128]{3,2,1,0:T(8,128)}, f32[8,4,128,128]{3,2,1,0:T(8,128)S(1)}, u32[]{:S(2)}) copy-start(f32[8,4,128,128]{3,2,1,0:T(8,128)S(1)} %convolution_add_fusion) | copy-start | bytes 6291460
  108.1 18.9 %collective-permute-start.13 = (f32[4,128,128]{2,1,0:T(8,128)}, f32[4,128,128]{2,1,0:T(8,128)}, u32[]{:S(2)}, u32[]{:S(2)}) collective-permute-start(f32[4,128,128]{2,1,0:T(8,128)} %fusion.31), channel_id=1, source_target_pairs={{8,0},{16,8},{24,16},{32,24},{40,32},{48,40},{56,48},{64,56},{72,6... | collective-permute-start | bytes 786440 | tf_op jit(solution)/shard_map/ppermute | solution.py:48
  110.0 17.0 %collective-permute-start.4 = (f32[4,128,128]{2,1,0:T(8,128)}, f32[4,128,128]{2,1,0:T(8,128)}, u32[]{:S(2)}, u32[]{:S(2)}) collective-permute-start(f32[4,128,128]{2,1,0:T(8,128)} %fusion.32), channel_id=1, source_target_pairs={{0,8},{8,16},{16,24},{24,32},{32,40},{40,48},{48,56},{56,64},{64,7... | collective-permute-start | bytes 786440 | tf_op jit(solution)/shard_map/ppermute | solution.py:48
  116.7 8.9 %collective-permute-start.10 = (f32[4]{0:T(128)S(1)}, f32[4]{0:T(128)S(1)}, u32[]{:S(2)}, u32[]{:S(2)}) collective-permute-start(f32[4]{0:T(128)S(1)} %get-tuple-element.86), channel_id=1, source_target_pairs={{16,0},{24,8},{32,16},{40,24},{48,32},{56,40},{64,48},{72,56},{80,... | collective-permute-start | bytes 56 | tf_op jit(solution)/shard_map/ppermute | solution.py:48
  118.0 12.3 %collective-permute-start.1 = (f32[4]{0:T(128)S(1)}, f32[4]{0:T(128)S(1)}, u32[]{:S(2)}, u32[]{:S(2)}) collective-permute-start(f32[4]{0:T(128)S(1)} %get-tuple-element.31), channel_id=1, source_target_pairs={{0,16},{8,24},{16,32},{24,40},{32,48},{40,56},{48,64},{56,72},{64,... | collective-permute-start | bytes 56 | tf_op jit(solution)/shard_map/ppermute | solution.py:48
  125.6 15.0 %collective-permute-start.11 = (f32[4]{0:T(128)S(1)}, f32[4]{0:T(128)S(1)}, u32[]{:S(2)}, u32[]{:S(2)}) collective-permute-start(f32[4]{0:T(128)S(1)} %get-tuple-element.47), channel_id=1, source_target_pairs={{32,0},{40,8},{48,16},{56,24},{64,32},{72,40},{80,48},{88,56},{96,... | collective-permute-start | bytes 56 | tf_op jit(solution)/shard_map/ppermute | solution.py:48
  129.1 17.8 %collective-permute-start.14 = (f32[4,128,128]{2,1,0:T(8,128)S(1)}, f32[4,128,128]{2,1,0:T(8,128)S(1)}, u32[]{:S(2)}, u32[]{:S(2)}) collective-permute-start(f32[4,128,128]{2,1,0:T(8,128)S(1)} %get-tuple-element.90), channel_id=1, source_target_pairs={{16,0},{24,8},{32,16},{40,24},{48,32},{56,40},{64,48},{72,56},{80,... | collective-permute-start | bytes 786440 | tf_op jit(solution)/shard_map/ppermute | solution.py:48
  130.4 17.9 %collective-permute-start.2 = (f32[4]{0:T(128)S(1)}, f32[4]{0:T(128)S(1)}, u32[]{:S(2)}, u32[]{:S(2)}) collective-permute-start(f32[4]{0:T(128)S(1)} %get-tuple-element.29), channel_id=1, source_target_pairs={{0,32},{8,40},{16,48},{24,56},{32,64},{40,72},{48,80},{56,88},{64,... | collective-permute-start | bytes 56 | tf_op jit(solution)/shard_map/ppermute | solution.py:48
  140.6 60.1 %collective-permute-start.12 = (f32[4]{0:T(128)S(1)}, f32[4]{0:T(128)S(1)}, u32[]{:S(2)}, u32[]{:S(2)}) collective-permute-start(f32[4]{0:T(128)S(1)} %get-tuple-element.45), channel_id=1, source_target_pairs={{64,0},{72,8},{80,16},{88,24},{96,32},{104,40},{112,48},{120,56},{... | collective-permute-start | bytes 56 | tf_op jit(solution)/shard_map/ppermute | solution.py:48
  141.9 16.4 %collective-permute-start.5 = (f32[4,128,128]{2,1,0:T(8,128)S(1)}, f32[4,128,128]{2,1,0:T(8,128)S(1)}, u32[]{:S(2)}, u32[]{:S(2)}) collective-permute-start(f32[4,128,128]{2,1,0:T(8,128)S(1)} %get-tuple-element.89), channel_id=1, source_target_pairs={{0,16},{8,24},{16,32},{24,40},{32,48},{40,56},{48,64},{56,72},{64,... | collective-permute-start | bytes 786440 | tf_op jit(solution)/shard_map/ppermute | solution.py:48
  147.0 17.9 %collective-permute-start.15 = (f32[4,128,128]{2,1,0:T(8,128)S(1)}, f32[4,128,128]{2,1,0:T(8,128)S(1)}, u32[]{:S(2)}, u32[]{:S(2)}) collective-permute-start(f32[4,128,128]{2,1,0:T(8,128)S(1)} %multiply_add_fusion.9), channel_id=1, source_target_pairs={{32,0},{40,8},{48,16},{56,24},{64,32},{72,40},{80,48},{88,56},{96,... | collective-permute-start | bytes 786440 | tf_op jit(solution)/shard_map/ppermute | solution.py:48
  148.3 18.0 %collective-permute-start.3 = (f32[4]{0:T(128)S(1)}, f32[4]{0:T(128)S(1)}, u32[]{:S(2)}, u32[]{:S(2)}) collective-permute-start(f32[4]{0:T(128)S(1)} %get-tuple-element.27), channel_id=1, source_target_pairs={{0,64},{8,72},{16,80},{24,88},{32,96},{40,104},{48,112},{56,120},{... | collective-permute-start | bytes 56 | tf_op jit(solution)/shard_map/ppermute | solution.py:48
  158.4 13.1 %collective-permute-start.6 = (f32[4,128,128]{2,1,0:T(8,128)S(1)}, f32[4,128,128]{2,1,0:T(8,128)S(1)}, u32[]{:S(2)}, u32[]{:S(2)}) collective-permute-start(f32[4,128,128]{2,1,0:T(8,128)S(1)} %multiply_add_fusion.18), channel_id=1, source_target_pairs={{0,32},{8,40},{16,48},{24,56},{32,64},{40,72},{48,80},{56,88},{64,... | collective-permute-start | bytes 786440 | tf_op jit(solution)/shard_map/ppermute | solution.py:48
  165.0 34.4 %collective-permute-start.16 = (f32[4,128,128]{2,1,0:T(8,128)S(1)}, f32[4,128,128]{2,1,0:T(8,128)S(1)}, u32[]{:S(2)}, u32[]{:S(2)}) collective-permute-start(f32[4,128,128]{2,1,0:T(8,128)S(1)} %multiply_add_fusion.8), channel_id=1, source_target_pairs={{64,0},{72,8},{80,16},{88,24},{96,32},{104,40},{112,48},{120,56},{... | collective-permute-start | bytes 786440 | tf_op jit(solution)/shard_map/ppermute | solution.py:48
  171.7 31.6 %collective-permute-start.7 = (f32[4,128,128]{2,1,0:T(8,128)S(1)}, f32[4,128,128]{2,1,0:T(8,128)S(1)}, u32[]{:S(2)}, u32[]{:S(2)}) collective-permute-start(f32[4,128,128]{2,1,0:T(8,128)S(1)} %multiply_add_fusion.17), channel_id=1, source_target_pairs={{0,64},{8,72},{16,80},{24,88},{32,96},{40,104},{48,112},{56,120},{... | collective-permute-start | bytes 786440 | tf_op jit(solution)/shard_map/ppermute | solution.py:48
  199.5 10.2 %collective-permute-start.17 = (f32[4,128,128]{2,1,0:T(8,128)S(1)}, f32[4,128,128]{2,1,0:T(8,128)S(1)}, u32[]{:S(2)}, u32[]{:S(2)}) collective-permute-start(f32[4,128,128]{2,1,0:T(8,128)S(1)} %multiply_add_fusion.7), channel_id=1, source_target_pairs={{128,0},{136,8},{144,16},{152,24},{160,32},{168,40},{176,48},{184,... | collective-permute-start | bytes 786440 | tf_op jit(solution)/shard_map/ppermute | solution.py:48
  203.3 17.1 %collective-permute-start.8 = (f32[4,128,128]{2,1,0:T(8,128)S(1)}, f32[4,128,128]{2,1,0:T(8,128)S(1)}, u32[]{:S(2)}, u32[]{:S(2)}) collective-permute-start(f32[4,128,128]{2,1,0:T(8,128)S(1)} %multiply_add_fusion.16), channel_id=1, source_target_pairs={{0,128},{8,136},{16,144},{24,152},{32,160},{40,168},{48,176},{56,1... | collective-permute-start | bytes 786440 | tf_op jit(solution)/shard_map/ppermute | solution.py:48
  218.0 3.6 %copy-start.7 = (f32[8,4,128,128]{3,2,1,0:T(8,128)S(1)}, f32[8,4,128,128]{3,2,1,0:T(8,128)}, u32[]{:S(2)}) copy-start(f32[8,4,128,128]{3,2,1,0:T(8,128)} %add_dynamic-update-slice_fusion.1) | copy-start | bytes 6291460
  (10 other events, 20.2 us)

commit v2 on v1

--- a/solution.py
+++ b/solution.py
@@ -35,22 +35,47 @@
     return (earlier[0] + later[0], jnp.exp(later[0])[:, None, None] * earlier[1] + later[1])
 
 
-def carried_in(elem, axis, reverse):
+def carried_both(dev_log, dev_state, dev_adjoint, axis):
     peers = lax.axis_size(axis)
-    inclusive = elem
-    exclusive = jax.tree.map(jnp.zeros_like, elem)
-    shift = 1
-    while shift < peers:
-        if reverse:
-            pairs = [(i, i - shift) for i in range(shift, peers)]
-        else:
-            pairs = [(i, i + shift) for i in range(peers - shift)]
-        got = jax.tree.map(lambda part: lax.ppermute(part, axis, pairs), inclusive)
-        exclusive = link(got, exclusive)
-        shift *= 2
-        if shift < peers:
-            inclusive = link(got, inclusive)
-    return exclusive
+    here = lax.axis_index(axis)
+    heads, width = dev_state.shape[0], dev_state.shape[2]
+    share = heads * width // peers
+    spare = 8
+    logs = jnp.zeros((spare, width), jnp.float32).at[:heads, :].set(
+        jnp.broadcast_to(dev_log[:, None], (heads, width))
+    )
+    payload = jnp.concatenate(
+        [
+            dev_state.reshape(peers, share, width),
+            dev_adjoint.reshape(peers, share, width),
+            jnp.broadcast_to(logs[None], (peers, spare, width)),
+        ],
+        axis=1,
+    )
+    got = lax.all_to_all(payload, axis, 0, 0, tiled=True)
+    head = (here * share) // width
+    pick = (lax.broadcasted_iota(jnp.int32, (heads,), 0) == head).astype(jnp.float32)
+    totals = jnp.sum(got[:, 2 * share : 2 * share + heads, 0] * pick[None, :], axis=1)
+    dst = lax.broadcasted_iota(jnp.int32, (peers, peers, peers), 0)
+    src = lax.broadcasted_iota(jnp.int32, (peers, peers, peers), 1)
+    mid = lax.broadcasted_iota(jnp.int32, (peers, peers, peers), 2)
+    between_fwd = (src < mid) & (mid < dst)
+    between_bwd = (dst < mid) & (mid < src)
+    log_fwd = jnp.sum(jnp.where(between_fwd, totals[None, None, :], 0.0), axis=2)
+    log_bwd = jnp.sum(jnp.where(between_bwd, totals[None, None, :], 0.0), axis=2)
+    dst2 = lax.broadcasted_iota(jnp.int32, (peers, peers), 0)
+    src2 = lax.broadcasted_iota(jnp.int32, (peers, peers), 1)
+    w_fwd = jnp.where(src2 < dst2, jnp.exp(jnp.where(src2 < dst2, log_fwd, 0.0)), 0.0)
+    w_bwd = jnp.where(src2 > dst2, jnp.exp(jnp.where(src2 > dst2, log_bwd, 0.0)), 0.0)
+    highest = lax.Precision.HIGHEST
+    state_rows = jnp.einsum("di,irc->drc", w_fwd, got[:, :share], precision=highest)
+    adjoint_rows = jnp.einsum("di,irc->drc", w_bwd, got[:, share : 2 * share], precision=highest)
+    back = lax.all_to_all(
+        jnp.concatenate([state_rows, adjoint_rows], axis=1), axis, 0, 0, tiled=True
+    )
+    start_state = back[:, :share].reshape(heads, width, width)
+    start_adjoint = back[:, share:].reshape(heads, width, width)
+    return start_state, start_adjoint
 
 
 def running_sum(decay_blk):
@@ -183,11 +208,10 @@
     key_blk, value_blk, cumul, totals, after, prefix, prefix_log, dev_state, dev_log = key_side(
         key_loc, value_loc, decay_loc
     )
-    start_state = carried_in((dev_log, dev_state), "seq", False)[1]
     query_blk, grad_blk, before, suffix, suffix_log, dev_adjoint = query_side(
         query_loc, grad_loc, cumul, totals
     )
-    start_adjoint = carried_in((dev_log, dev_adjoint), "seq", True)[1]
+    start_state, start_adjoint = carried_both(dev_log, dev_state, dev_adjoint, "seq")
     flat_query, flat_key, flat_value = finish(
         query_blk,
         key_blk,

time: 271 us -> 206 us (0.76)
  starting transfers between devices: 97.6 us -> 20.9 us
  waiting for transfers between devices: 60.3 us -> 72.2 us
  local copies, waits for them, and re-layouts: 24.7 us -> 31.6 us
  matrix products: 26.9 us -> 22.4 us
    ppermute x18 -> x0, starting transfers between devices: 93 us -> none  [carried_in(): got = jax.tree.map(lambda part: lax.ppermute(part, axis, pairs), inclusive)]
    all_to_all x0 -> x2, waiting for transfers between devices: none -> 21 us  [the longest x1 13.5 us: carried_both(): got = lax.all_to_all(payload, axis, 0, 0, tiled=True)]
    all_to_all x0 -> x2, starting transfers between devices: none -> 16.3 us  [the longest x1 11.2 us: carried_both(): got = lax.all_to_all(payload, axis, 0, 0, tiled=True)]
    ppermute x18 -> x0, waiting for transfers between devices: 8.55 us -> none  [carried_in(): got = jax.tree.map(lambda part: lax.ppermute(part, axis, pairs), inclusive)]
    dot_general x14, matrix products: 26.8 us -> 21.4 us  [product(): jnp.einsum(form, first_op, second_op, preferred_element_type=jnp.float32)]
    add x9 -> x0, other arithmetic: 4.91 us -> none  [link(): jnp.exp(later[0])[:, None, None] * earlier[1] + later[1]]
    slice x0 -> x4, local copies, waits for them, and re-layouts: none -> 3.16 us  [the longest x1 1.08 us: carried_both(): got[:, :share]]
    unnamed x42 -> x66, local copies, waits for them, and re-layouts: 13.9 us -> 16.7 us
  transfers between devices with their start and end apart: 19 -> 3, of which waited for: 5 -> 3; matrix products, arithmetic and copies ran while one was open for 18% -> 8% of each run, Pallas kernels for 0% -> 0%
where the time goes in v2:
time: 206 us; the launch traced here: 205 us
  waiting for transfers between devices  72.2 us (35%)
  blocking collectives  41.4 us (20%)
  local copies, waits for them, and re-layouts  31.6 us (15%)
  matrix products  22.4 us (11%)
  starting transfers between devices  20.9 us (10%)
  other arithmetic  15.4 us (7%)
    all_to_all x1, waiting for transfers between devices, body(): arrived = lax.all_to_all(packed, 'exp', 0, 0, tiled=True)  51.2 us
    all_to_all x1, blocking collectives, body(): back = lax.all_to_all(out_packed, 'exp', 0, 0, tiled=True)  41.4 us
    dot_general x14, matrix products, product(): jnp.einsum(form, first_op, second_op, preferred_element_type=jnp.float32)  21.4 us
    unnamed x66, local copies, waits for them, and re-layouts  16.7 us
    all_to_all x1, waiting for transfers between devices, carried_both(): got = lax.all_to_all(payload, axis, 0, 0, tiled=True)  13.5 us
    all_to_all x1, starting transfers between devices, carried_both(): got = lax.all_to_all(payload, axis, 0, 0, tiled=True)  11.2 us
    unnamed x8, other arithmetic  9.1 us
    all_to_all x1, waiting for transfers between devices, carried_both(): lax.all_to_all(jnp.concatenate([state_rows, adjoint_rows], axis=1), axis,...  7.51 us
  transfers between devices with their start and end apart: 3, of which 3 were waited for; matrix products, arithmetic and copies ran while one was open for 8% of the time, Pallas kernels for 0%

profile of v2, /device:TPU:32, one launch (start us, length us, event | category | flops | bytes accessed | tf_op | source)
XLA Modules:
  0.0 205.0 jit_solution(6072547173308986500)
XLA Ops:
  0.6 1.7 copy.158
  2.4 1.2 constant_dynamic-update-slice_fusion.3
  5.4 1.6 copy.161
  7.0 1.2 constant_dynamic-update-slice_fusion.2
  9.4 1.2 constant_dynamic-update-slice_fusion
  11.3 4.6 %all-to-all-start = ((bf16[8,128,2176]{1,2,0:T(8,128)(2,1)}), bf16[8,128,2176]{1,2,0:T(8,128)(2,1)}, u32[]{:S(2)}, u32[]{:S(2)}) async-start(bf16[8,128,2176]{1,2,0:T(8,128)(2,1)} %pad_dynamic-update-slice_fusion), calls=%async_computation | async-start | bytes 8912896 | tf_op jit(solution)/shard_map/all_to_all | solution.py:200
  17.1 51.2 %all-to-all-done = bf16[8,128,2176]{1,2,0:T(8,128)(2,1)} async-done(((bf16[8,128,2176]{1,2,0:T(8,128)(2,1)}), bf16[8,128,2176]{1,2,0:T(8,128)(2,1)}, u32[]{:S(2)}, u32[]{:S(2)}) %all-to-all-start) | async-done | bytes 4456480 | tf_op jit(solution)/shard_map/all_to_all | solution.py:200
  70.3 2.6 %fusion.56 = (bf16[8,128,512]{1,2,0:T(8,128)(2,1)S(1)}, bf16[8,128,512]{1,2,0:T(8,128)(2,1)S(1)}, bf16[8,128,512]{1,2,0:T(8,128)(2,1)S(1)}, bf16[8,128,512]{1,2,0:T(8,128)(2,1)S(1)}) fusion(bf16[8,128,2176]{1,2,0:T(8,128)(2,1)} %all-to-all-done), kind=kLoop, calls=%fused_computation.149 | loop fusion | bytes 8388608 | tf_op jit(solution)/shard_map/slice | solution.py:204
  75.7 2.2 %convolution_add_fusion = f32[8,4,128,128]{3,2,1,0:T(8,128)} fusion(f32[8,4,128,128]{3,2,1,0:T(8,128)S(1)} %fusion.12, bf16[8,128,4,128]{1,3,2,0:T(8,128)(2,1)S(1)} %bitcast.154, bf16[8,128,4,128]{1,3,2,0:T(8,128)(2,1)S(1)} %bitcast.160, f32[8,128,4]{1,2,0:T(4,128)S(1)} %copy.167), kind=kOutput, calls=%fused_computation.25 | convolution fusion | flops 137887744 | bytes 6307840 | tf_op jit(solution)/shard_map/ntha,nthb->nhab/dot_general | solution.py:21
  84.2 2.7 %constant_dynamic-update-slice_fusion.4 = (f32[8,4,128,128]{3,2,1,0:T(8,128)}, f32[1,4,128,128]{3,2,1,0:T(8,128)S(1)}, f32[8,4,128,128]{3,2,1,0:T(8,128)S(1)}, f...) fusion(f32[8,4,128,128]{3,2,1,0:T(8,128)} %constant_dynamic-update-slice_fusion.5, ...), kind=kLoop, calls=%fused_computation.85 | loop fusion | flops 1114111 | bytes 4194416
  90.6 11.2 %all-to-all-start.1 = ((f32[32,40,128]{2,1,0:T(8,128)}), f32[32,40,128]{2,1,0:T(8,128)}, u32[]{:S(2)}, u32[]{:S(2)}) async-start(f32[32,40,128]{2,1,0:T(8,128)} %maximum_maximum_fusion), calls=%async_computation.1 | async-start | bytes 1310720 | tf_op jit(solution)/shard_map/all_to_all | solution.py:55
  103.2 1.3 constant_dynamic-update-slice_fusion.10
  106.6 1.9 multiply_convert_fusion.1
  108.5 13.5 %all-to-all-done.1 = f32[32,40,128]{2,1,0:T(8,128)} async-done(((f32[32,40,128]{2,1,0:T(8,128)}), f32[32,40,128]{2,1,0:T(8,128)}, u32[]{:S(2)}, u32[]{:S(2)}) %all-to-all-start.1) | async-done | bytes 655392 | tf_op jit(solution)/shard_map/all_to_all | solution.py:55
  126.5 5.1 %all-to-all-start.2 = ((f32[32,32,128]{2,1,0:T(8,128)}), f32[32,32,128]{2,1,0:T(8,128)}, u32[]{:S(2)}, u32[]{:S(2)}) async-start(f32[32,32,128]{2,1,0:T(8,128)} %copy.176), calls=%async_computation.2 | async-start | bytes 1048576 | tf_op jit(solution)/shard_map/all_to_all | solution.py:73
  131.7 3.6 %fusion.61 = f32[8,4,128,128]{3,2,1,0:T(8,128)} fusion(bf16[8,128,4,128]{1,3,2,0:T(8,128)(2,1)S(1)} %bitcast.144, bf16[8,4,128,128]{3,2,1,0:T(8,128)(2,1)} %multiply_convert_fusion.1), kind=kOutput, calls=%fused_computation.154 | convolution fusion | flops 134217728 | bytes 4194304 | tf_op jit(solution)/shard_map/nhts,nshd->nthd/dot_general | solution.py:21
  135.2 1.8 fusion.62
  137.0 4.0 %fusion.14 = f32[8,4,128,128]{3,2,1,0:T(8,128)} fusion(bf16[8,128,4,128]{1,3,2,0:T(8,128)(2,1)} %bitcast.155, bf16[8,128,4,128]{1,3,2,0:T(8,128)(2,1)} %bitcast.161, bf16[8,128,4,128]{1,3,2,0:T(8,128)(2,1)S(1)} %bitcast.145, f32[8,4,128]{2,1,0:T(4,128)S(1)} %copy.163, pred[128,128]{1,0:T(8,128)(4,1)S(1)} %iota_compare_fusion.4), kind=kOutput, calls=%fused_computation.29 | convolution fusion | flops 271056896 | bytes 5275648 | tf_op jit(solution)/shard_map/nhts,nthd->nshd/dot_general | solution.py:21
  141.0 7.5 %all-to-all-done.2 = f32[32,32,128]{2,1,0:T(8,128)} async-done(((f32[32,32,128]{2,1,0:T(8,128)}), f32[32,32,128]{2,1,0:T(8,128)}, u32[]{:S(2)}, u32[]{:S(2)}) %all-to-all-start.2) | async-done | bytes 524320 | tf_op jit(solution)/shard_map/all_to_all | solution.py:73
  149.5 1.7 fusion.33
  159.5 41.4 %all_to_all.20 = bf16[8,128,1536]{1,2,0:T(8,128)(2,1)S(1)} all-to-all(bf16[8,128,1536]{1,2,0:T(8,128)(2,1)S(1)} %pad_maximum_fusion), channel_id=1, replica_groups=mesh['seq'=32,'exp'=8] {'exp'}, dimensions={0} | all-to-all | bytes 6291456 | tf_op jit(solution)/shard_map/all_to_all | solution.py:233
  201.1 1.3 copy.206
  202.4 1.3 copy.207
  203.7 1.3 copy.208
  (132 shorter events, 36.8 us)
Async XLA Ops:
  0.6 2.9 %copy-start.17 = (bf16[128,4096]{1,0:T(8,128)(2,1)S(1)}, bf16[128,4096]{1,0:T(8,128)(2,1)}, u32[]{:S(2)}) copy-start(bf16[128,4096]{1,0:T(8,128)(2,1)} %param.8) | copy-start | bytes 3145732
  8.2 2.3 %copy-start.19 = (bf16[128,32]{0,1:T(8,128)(2,1)S(1)}, bf16[128,32]{0,1:T(8,128)(2,1)}, u32[]{:S(2)}) copy-start(bf16[128,32]{0,1:T(8,128)(2,1)} %param.11) | copy-start | bytes 24580
  11.3 57.1 %all-to-all-start = ((bf16[8,128,2176]{1,2,0:T(8,128)(2,1)}), bf16[8,128,2176]{1,2,0:T(8,128)(2,1)}, u32[]{:S(2)}, u32[]{:S(2)}) async-start(bf16[8,128,2176]{1,2,0:T(8,128)(2,1)} %pad_dynamic-update-slice_fusion), calls=%async_computation | async-start | bytes 8912896 | tf_op jit(solution)/shard_map/all_to_all | solution.py:200
  72.9 2.7 %copy-start.3 = (bf16[8,128,512]{1,2,0:T(8,128)(2,1)}, bf16[8,128,512]{1,2,0:T(8,128)(2,1)S(1)}, u32[]{:S(2)}) copy-start(bf16[8,128,512]{1,2,0:T(8,128)(2,1)S(1)} %get-tuple-element.58) | copy-start | bytes 3145732
  73.0 2.7 %copy-start.9 = (bf16[8,128,512]{1,2,0:T(8,128)(2,1)}, bf16[8,128,512]{1,2,0:T(8,128)(2,1)S(1)}, u32[]{:S(2)}) copy-start(bf16[8,128,512]{1,2,0:T(8,128)(2,1)S(1)} %get-tuple-element.57) | copy-start | bytes 3145732
  74.8 8.6 %copy-start.6 = (f32[8,4,128,128]{3,2,1,0:T(8,128)}, f32[8,4,128,128]{3,2,1,0:T(8,128)S(1)}, u32[]{:S(2)}) copy-start(f32[8,4,128,128]{3,2,1,0:T(8,128)S(1)} %convolution_add_fusion.1) | copy-start | bytes 6291460
  81.3 2.1 %copy-start.15 = (f32[1,4,128,128]{3,2,1,0:T(8,128)}, f32[1,4,128,128]{3,2,1,0:T(8,128)S(1)}, u32[]{:S(2)}) copy-start(f32[1,4,128,128]{3,2,1,0:T(8,128)S(1)} %get-tuple-element.43) | copy-start | bytes 786436
  84.2 2.7 %copy-start.7 = (f32[8,4,128,128]{3,2,1,0:T(8,128)S(1)}, f32[8,4,128,128]{3,2,1,0:T(8,128)}, u32[]{:S(2)}) copy-start(f32[8,4,128,128]{3,2,1,0:T(8,128)} %copy-done.6) | copy-start | bytes 6291460
  86.9 1.7 copy-start.8
  89.2 12.6 %copy-start.20 = (f32[4]{0:T(128)S(1)}, f32[4]{0:T(128)}, u32[]{:S(2)}) copy-start(f32[4]{0:T(128)} %get-tuple-element.25) | copy-start | bytes 52
  89.3 12.6 %copy-start.21 = (f32[4]{0:T(128)S(1)}, f32[4]{0:T(128)}, u32[]{:S(2)}) copy-start(f32[4]{0:T(128)} %get-tuple-element.26) | copy-start | bytes 52
  89.3 12.6 %copy-start.22 = (f32[4]{0:T(128)S(1)}, f32[4]{0:T(128)}, u32[]{:S(2)}) copy-start(f32[4]{0:T(128)} %get-tuple-element.88) | copy-start | bytes 52
  89.3 12.6 %copy-start.23 = (f32[4]{0:T(128)S(1)}, f32[4]{0:T(128)}, u32[]{:S(2)}) copy-start(f32[4]{0:T(128)} %get-tuple-element.89) | copy-start | bytes 52
  89.3 12.6 %copy-start.24 = (f32[4]{0:T(128)S(1)}, f32[4]{0:T(128)}, u32[]{:S(2)}) copy-start(f32[4]{0:T(128)} %get-tuple-element.90) | copy-start | bytes 52
  89.3 12.6 %copy-start.25 = (f32[4]{0:T(128)S(1)}, f32[4]{0:T(128)}, u32[]{:S(2)}) copy-start(f32[4]{0:T(128)} %get-tuple-element.91) | copy-start | bytes 52
  90.6 31.4 %all-to-all-start.1 = ((f32[32,40,128]{2,1,0:T(8,128)}), f32[32,40,128]{2,1,0:T(8,128)}, u32[]{:S(2)}, u32[]{:S(2)}) async-start(f32[32,40,128]{2,1,0:T(8,128)} %maximum_maximum_fusion), calls=%async_computation.1 | async-start | bytes 1310720 | tf_op jit(solution)/shard_map/all_to_all | solution.py:55
  103.2 3.4 %copy-start.1 = (bf16[8,128,512]{1,2,0:T(8,128)(2,1)S(1)}, bf16[8,128,512]{1,2,0:T(8,128)(2,1)}, u32[]{:S(2)}) copy-start(bf16[8,128,512]{1,2,0:T(8,128)(2,1)} %copy-done) | copy-start | bytes 3145732
  103.2 3.4 %copy-start.4 = (bf16[8,128,512]{1,2,0:T(8,128)(2,1)S(1)}, bf16[8,128,512]{1,2,0:T(8,128)(2,1)}, u32[]{:S(2)}) copy-start(bf16[8,128,512]{1,2,0:T(8,128)(2,1)} %copy-done.3) | copy-start | bytes 3145732
  106.5 16.4 %copy-start.26 = (f32[4]{0:T(128)S(1)}, f32[4]{0:T(128)}, u32[]{:S(2)}) copy-start(f32[4]{0:T(128)} %compare_convert_fusion) | copy-start | bytes 52
  126.5 21.9 %all-to-all-start.2 = ((f32[32,32,128]{2,1,0:T(8,128)}), f32[32,32,128]{2,1,0:T(8,128)}, u32[]{:S(2)}, u32[]{:S(2)}) async-start(f32[32,32,128]{2,1,0:T(8,128)} %copy.176), calls=%async_computation.2 | async-start | bytes 1048576 | tf_op jit(solution)/shard_map/all_to_all | solution.py:73
  131.6 3.6 %copy-start.10 = (bf16[8,128,512]{1,2,0:T(8,128)(2,1)S(1)}, bf16[8,128,512]{1,2,0:T(8,128)(2,1)}, u32[]{:S(2)}) copy-start(bf16[8,128,512]{1,2,0:T(8,128)(2,1)} %copy-done.9) | copy-start | bytes 3145732
  131.6 3.6 %copy-start.14 = (bf16[8,4,128,128]{3,2,1,0:T(8,128)(2,1)S(1)}, bf16[8,4,128,128]{3,2,1,0:T(8,128)(2,1)}, u32[]{:S(2)}) copy-start(bf16[8,4,128,128]{3,2,1,0:T(8,128)(2,1)} %multiply_convert_fusion.1) | copy-start | bytes 3145732
  151.3 1.9 copy-start.11
  154.8 1.9 copy-start.12
  (6 other events, 7.8 us)

commit v3 on v2

v3 whole, which is shorter than its diff:
```python
import jax
import jax.numpy as jnp
from jax import lax
from jax.sharding import PartitionSpec as P

BLOCK = 128
SEQ_EXP = ("seq", "exp")


def widen(array):
    return array.astype(jnp.float32)


def halves(array):
    high = array.astype(jnp.bfloat16)
    low = (array - widen(high)).astype(jnp.bfloat16)
    return (high, low)


def product(form, first_op, second_op):
    return jnp.einsum(form, first_op, second_op, preferred_element_type=jnp.float32)


def split_left(form, wide_op, narrow_op):
    high, low = halves(wide_op)
    return product(form, high, narrow_op) + product(form, low, narrow_op)


def split_right(form, narrow_op, wide_op):
    high, low = halves(wide_op)
    return product(form, narrow_op, high) + product(form, narrow_op, low)


def link(earlier, later):
    return (earlier[0] + later[0], jnp.exp(later[0])[:, None, None] * earlier[1] + later[1])


def carried_both(dev_log, dev_state, dev_adjoint, axis):
    peers = lax.axis_size(axis)
    here = lax.axis_index(axis)
    heads, width = dev_state.shape[0], dev_state.shape[2]
    share = heads * width // peers
    spare = 8
    logs = jnp.zeros((spare, width), jnp.float32).at[:heads, :].set(
        jnp.broadcast_to(dev_log[:, None], (heads, width))
    )
    payload = jnp.concatenate(
        [
            dev_state.reshape(peers, share, width),
            dev_adjoint.reshape(peers, share, width),
            jnp.broadcast_to(logs[None], (peers, spare, width)),
        ],
        axis=1,
    )
    got = lax.all_to_all(payload, axis, 0, 0, tiled=True)
    head = (here * share) // width
    pick = (lax.broadcasted_iota(jnp.int32, (heads,), 0) == head).astype(jnp.float32)
    totals = jnp.sum(got[:, 2 * share : 2 * share + heads, 0] * pick[None, :], axis=1)
    dst = lax.broadcasted_iota(jnp.int32, (peers, peers, peers), 0)
    src = lax.broadcasted_iota(jnp.int32, (peers, peers, peers), 1)
    mid = lax.broadcasted_iota(jnp.int32, (peers, peers, peers), 2)
    between_fwd = (src < mid) & (mid < dst)
    between_bwd = (dst < mid) & (mid < src)
    log_fwd = jnp.sum(jnp.where(between_fwd, totals[None, None, :], 0.0), axis=2)
    log_bwd = jnp.sum(jnp.where(between_bwd, totals[None, None, :], 0.0), axis=2)
    dst2 = lax.broadcasted_iota(jnp.int32, (peers, peers), 0)
    src2 = lax.broadcasted_iota(jnp.int32, (peers, peers), 1)
    w_fwd = jnp.where(src2 < dst2, jnp.exp(jnp.where(src2 < dst2, log_fwd, 0.0)), 0.0)
    w_bwd = jnp.where(src2 > dst2, jnp.exp(jnp.where(src2 > dst2, log_bwd, 0.0)), 0.0)
    highest = lax.Precision.HIGHEST
    state_rows = jnp.einsum("di,irc->drc", w_fwd, got[:, :share], precision=highest)
    adjoint_rows = jnp.einsum("di,irc->drc", w_bwd, got[:, share : 2 * share], precision=highest)
    back = lax.all_to_all(
        jnp.concatenate([state_rows, adjoint_rows], axis=1), axis, 0, 0, tiled=True
    )
    start_state = back[:, :share].reshape(heads, width, width)
    start_adjoint = back[:, share:].reshape(heads, width, width)
    return start_state, start_adjoint


def running_sum(decay_blk):
    length = decay_blk.shape[1]
    lower = (
        lax.broadcasted_iota(jnp.int32, (length, length), 1)
        <= lax.broadcasted_iota(jnp.int32, (length, length), 0)
    ).astype(decay_blk.dtype)
    return jnp.einsum("ts,nsh->nth", lower, decay_blk, preferred_element_type=jnp.float32)


def unrolled(totals, pieces, reverse):
    blocks = totals.shape[0]
    heads, width = pieces.shape[1], pieces.shape[2]
    carry = jnp.zeros((heads, width, width), jnp.float32)
    logsum = jnp.zeros((heads,), jnp.float32)
    seen = [None] * blocks
    seen_log = [None] * blocks
    order = reversed(range(blocks)) if reverse else range(blocks)
    for i in order:
        seen[i] = carry
        seen_log[i] = logsum
        carry = jnp.exp(totals[i])[:, None, None] * carry + pieces[i]
        logsum = logsum + totals[i]
    return jnp.stack(seen), jnp.stack(seen_log), carry, logsum


def local_block(queries, keys, values, out_grad, log_decay):
    length = queries.shape[0]
    heads = log_decay.shape[1]
    width = queries.shape[1] // heads
    query_blk = queries.reshape(length, heads, width)
    key_blk = keys.reshape(length, heads, width)
    value_blk = values.reshape(length, heads, width)
    grad_blk = out_grad.reshape(length, heads, width)
    cumul = running_sum(log_decay[None])[0]
    total = cumul[-1]
    after = jnp.exp(total[None, :] - cumul)
    before = jnp.exp(cumul)
    contrib = split_left("sha,shb->hab", after[..., None] * widen(key_blk), value_blk)
    update = split_left("tha,thb->hab", before[..., None] * widen(query_blk), grad_blk)
    return (query_blk, key_blk, value_blk, grad_blk, cumul, after, before, contrib, update)


def intra(query_blk, key_blk, value_blk, grad_blk, cumul):
    length = cumul.shape[0]
    heads_first = cumul.T
    spread = heads_first[:, :, None] - heads_first[:, None, :]
    causal = lax.broadcasted_iota(jnp.int32, (length, length), 1) <= lax.broadcasted_iota(
        jnp.int32, (length, length), 0
    )
    weights = jnp.where(causal[None], jnp.exp(jnp.where(causal[None], spread, 0.0)), 0.0)
    grad_scores = product("thd,shd->hts", grad_blk, value_blk)
    key_scores = product("thd,shd->hts", query_blk, key_blk)
    first = (weights * grad_scores).astype(jnp.bfloat16)
    second = (weights * key_scores).astype(jnp.bfloat16)
    query_part = product("hts,shd->thd", first, key_blk)
    key_part = product("hts,thd->shd", first, query_blk)
    value_part = product("hts,thd->shd", second, grad_blk)
    return query_part, key_part, value_part


def body(queries, keys, values, out_grad, log_decay):
    peers = lax.axis_size("exp")
    length = queries.shape[0]
    heads = log_decay.shape[1]
    width = queries.shape[1] // heads
    group = heads // peers
    (query_blk, key_blk, value_blk, grad_blk, cumul, after, before, contrib, update) = local_block(
        queries, keys, values, out_grad, log_decay
    )
    share = group * width
    decay_rows = jnp.transpose(log_decay.reshape(length, peers, group), (1, 2, 0))
    pad_rows = 16
    decay_rows = jnp.pad(decay_rows, ((0, 0), (0, pad_rows - group), (0, 0)))
    packed = jnp.concatenate(
        [
            contrib.astype(jnp.bfloat16).reshape(peers, share, width),
            update.astype(jnp.bfloat16).reshape(peers, share, width),
            decay_rows.astype(jnp.bfloat16),
        ],
        axis=1,
    )
    got = lax.all_to_all(packed, "exp", 0, 0, tiled=True)
    contrib_g = widen(got[:, :share]).reshape(peers, group, width, width)
    update_g = widen(got[:, share : 2 * share]).reshape(peers, group, width, width)
    totals = jnp.sum(widen(got[:, 2 * share : 2 * share + group]), axis=2)
    prefix, prefix_log, dev_state, dev_log = unrolled(totals, contrib_g, False)
    suffix, suffix_log, dev_adjoint, unused = unrolled(totals, update_g, True)
    start_state, start_adjoint = carried_both(dev_log, dev_state, dev_adjoint, "seq")
    state_prev = jnp.exp(prefix_log)[:, :, None, None] * start_state[None] + prefix
    adjoint = jnp.exp(suffix_log)[:, :, None, None] * start_adjoint[None] + suffix
    returned = jnp.concatenate(
        [
            state_prev.astype(jnp.bfloat16).reshape(peers, share, width),
            adjoint.astype(jnp.bfloat16).reshape(peers, share, width),
        ],
        axis=1,
    )
    back = lax.all_to_all(returned, "exp", 0, 0, tiled=True)
    state_in = back[:, :share].reshape(heads, width, width)
    adjoint_in = back[:, share:].reshape(heads, width, width)
    query_part, key_part, value_part = intra(query_blk, key_blk, value_blk, grad_blk, cumul)
    grad_query = query_part + before[..., None] * product("thb,hab->tha", grad_blk, state_in)
    grad_key = key_part + after[..., None] * product("shb,hab->sha", value_blk, adjoint_in)
    grad_value = value_part + after[..., None] * product("sha,hab->shb", key_blk, adjoint_in)
    flat = lambda x: x.astype(jnp.bfloat16).reshape(length, heads * width)
    return (flat(grad_query), flat(grad_key), flat(grad_value))


def solution(mesh):
    placed = tuple(P(SEQ_EXP, None) for _ in range(5))
    return jax.shard_map(
        body,
        mesh=mesh,
        in_specs=placed,
        out_specs=(P(SEQ_EXP, None), P(SEQ_EXP, None), P(SEQ_EXP, None)),
        check_vma=False,
    )
```

time: 206 us -> 187 us (0.908)
  blocking collectives: 41.4 us -> 0 us
  other arithmetic: 15.4 us -> 27 us
  waiting for transfers between devices: 72.2 us -> 82.2 us
  local copies, waits for them, and re-layouts: 31.6 us -> 26.9 us
  starting transfers between devices: 20.9 us -> 25.3 us
    all_to_all x1 -> x0, blocking collectives: 41.4 us -> none  [body(): back = lax.all_to_all(out_packed, 'exp', 0, 0, tiled=True)]
    all_to_all x1, waiting for transfers between devices: 13.5 us -> 19.6 us  [carried_both(): got = lax.all_to_all(payload, axis, 0, 0, tiled=True)]
    convert_element_type x0 -> x3, other arithmetic: none -> 5.87 us  [the longest x1 1.96 us: body(): state_prev.astype(jnp.bfloat16).reshape(peers, share, width)]
    all_to_all x1, waiting for transfers between devices: 7.51 us -> 13.1 us  [carried_both(): lax.all_to_all(jnp.concatenate([state_rows, adjoint_rows], axis=1), axis,...]
    all_to_all x1 -> x2, starting transfers between devices: 4.56 us -> 9.01 us  [the longest x1 4.53 us: body(): back = lax.all_to_all(returned, 'exp', 0, 0, tiled=True)]
    concatenate x1 -> x2, other arithmetic: 0.25 us -> 2.99 us  [the longest x1 1.51 us: body(): jnp.concatenate([state_prev.astype(jnp.bfloat16).reshape(peers, share, wi...]
    reshape x3 -> x1, local copies, waits for them, and re-layouts: 3.92 us -> 1.63 us  [local_block(): grad_blk = out_grad.reshape(length, heads, width)]
    all_to_all x1 -> x2, waiting for transfers between devices: 51.2 us -> 49.5 us  [the longest x1 26.9 us: body(): got = lax.all_to_all(packed, 'exp', 0, 0, tiled=True)]
  transfers between devices with their start and end apart: 3 -> 4, of which waited for: 3 -> 4; matrix products, arithmetic and copies ran while one was open for 8% -> 5% of each run, Pallas kernels for 0% -> 0%
where the time goes in v3:
time: 187 us; the launch traced here: 186 us
  waiting for transfers between devices  82.2 us (44%)
  other arithmetic  27 us (14%)
  local copies, waits for them, and re-layouts  26.9 us (14%)
  starting transfers between devices  25.3 us (14%)
  matrix products  22.9 us (12%)
    all_to_all x1, waiting for transfers between devices, body(): got = lax.all_to_all(packed, 'exp', 0, 0, tiled=True)  26.9 us
    all_to_all x1, waiting for transfers between devices, body(): back = lax.all_to_all(returned, 'exp', 0, 0, tiled=True)  22.6 us
    dot_general x11, matrix products, product(): jnp.einsum(form, first_op, second_op, preferred_element_type=jnp.float32)  21.2 us
    all_to_all x1, waiting for transfers between devices, carried_both(): got = lax.all_to_all(payload, axis, 0, 0, tiled=True)  19.6 us
    unnamed x57, local copies, waits for them, and re-layouts  15 us
    all_to_all x1, waiting for transfers between devices, carried_both(): lax.all_to_all(jnp.concatenate([state_rows, adjoint_rows], axis=1), axis,...  13.1 us
    all_to_all x1, starting transfers between devices, carried_both(): got = lax.all_to_all(payload, axis, 0, 0, tiled=True)  11.2 us
    unnamed x7, other arithmetic  7.95 us
  transfers between devices with their start and end apart: 4, of which 4 were waited for; matrix products, arithmetic and copies ran while one was open for 5% of the time, Pallas kernels for 0%

profile of v3, /device:TPU:32, one launch (start us, length us, event | category | flops | bytes accessed | tf_op | source)
XLA Modules:
  0.0 185.5 jit_solution(17155390728342158023)
XLA Ops:
  1.8 1.6 copy.116
  6.1 1.8 add_convert_fusion.2
  12.7 4.5 %all-to-all-start = ((bf16[8,1040,128]{2,1,0:T(8,128)(2,1)}), bf16[8,1040,128]{2,1,0:T(8,128)(2,1)}, u32[]{:S(2)}, u32[]{:S(2)}) async-start(bf16[8,1040,128]{2,1,0:T(8,128)(2,1)} %fusion.1), calls=%async_computation | async-start | bytes 4259840 | tf_op jit(solution)/shard_map/all_to_all | solution.py:162
  17.9 26.9 %all-to-all-done = bf16[8,1040,128]{2,1,0:T(8,128)(2,1)} async-done(((bf16[8,1040,128]{2,1,0:T(8,128)(2,1)}), bf16[8,1040,128]{2,1,0:T(8,128)(2,1)}, u32[]{:S(2)}, u32[]{:S(2)}) %all-to-all-start) | async-done | bytes 2129952 | tf_op jit(solution)/shard_map/all_to_all | solution.py:162
  47.4 2.0 %slice_convert_fusion.1 = (f32[8,512,128]{2,1,0:T(8,128)S(1)}, f32[8,512,128]{2,1,0:T(8,128)S(1)}) fusion(bf16[8,1040,128]{2,1,0:T(8,128)(2,1)} %all-to-all-done), kind=kLoop, calls=%fused_computation.34 | loop fusion | flops 1048576 | bytes 6291456 | tf_op jit(solution)/shard_map/convert_element_type | solution.py:11
  60.6 2.7 %add_dynamic-update-slice_fusion.1 = (f32[8,512,128]{2,1,0:T(8,128)}, f32[1,512,128]{2,1,0:T(8,128)S(1)}, f32[1,512,128]{2,1,0:T(8,128)S(1)}, f32[1,512,128]{2,1...) fusion(f32[8,512,128]{2,1,0:T(8,128)} %get-tuple-element.29, ...), kind=kLoop, calls=%fused_computation.67 | loop fusion | flops 262144 | bytes 5509120 | tf_op jit(solution)/shard_map/stack | solution.py:103
  66.2 11.2 %all-to-all-start.1 = ((f32[32,40,128]{2,1,0:T(8,128)}), f32[32,40,128]{2,1,0:T(8,128)}, u32[]{:S(2)}, u32[]{:S(2)}) async-start(f32[32,40,128]{2,1,0:T(8,128)} %maximum_maximum_fusion), calls=%async_computation.1 | async-start | bytes 1310720 | tf_op jit(solution)/shard_map/all_to_all | solution.py:55
  77.9 19.6 %all-to-all-done.1 = f32[32,40,128]{2,1,0:T(8,128)} async-done(((f32[32,40,128]{2,1,0:T(8,128)}), f32[32,40,128]{2,1,0:T(8,128)}, u32[]{:S(2)}, u32[]{:S(2)}) %all-to-all-start.1) | async-done | bytes 655392 | tf_op jit(solution)/shard_map/all_to_all | solution.py:55
  102.8 5.1 %all-to-all-start.2 = ((f32[32,32,128]{2,1,0:T(8,128)}), f32[32,32,128]{2,1,0:T(8,128)}, u32[]{:S(2)}, u32[]{:S(2)}) async-start(f32[32,32,128]{2,1,0:T(8,128)} %copy.98), calls=%async_computation.2 | async-start | bytes 1048576 | tf_op jit(solution)/shard_map/all_to_all | solution.py:73
  109.0 1.8 add_dynamic-update-slice_fusion.2
  111.7 13.1 %all-to-all-done.2 = f32[32,32,128]{2,1,0:T(8,128)} async-done(((f32[32,32,128]{2,1,0:T(8,128)}), f32[32,32,128]{2,1,0:T(8,128)}, u32[]{:S(2)}, u32[]{:S(2)}) %all-to-all-start.2) | async-done | bytes 524320 | tf_op jit(solution)/shard_map/all_to_all | solution.py:73
  125.8 2.0 %add_convert_fusion.1 = bf16[8,512,128]{2,1,0:T(8,128)(2,1)S(1)} fusion(f32[8,512,128]{2,1,0:T(8,128)} %get-tuple-element.56, f32[512,128]{1,0:T(8,128)S(1)} %bitcast.189, f32[8,512]{1,0:T(8,128)S(1)} %broadcast_bitcast_fusion.1), kind=kLoop, calls=%fused_computation.15 | loop fusion | flops 1572864 | bytes 3424256 | tf_op jit(solution)/shard_map/convert_element_type | solution.py:173
  127.8 2.0 %add_convert_fusion = bf16[8,512,128]{2,1,0:T(8,128)(2,1)S(1)} fusion(f32[8,512,128]{2,1,0:T(8,128)} %broadcast_dynamic-update-slice_fusion, f32[512,128]{1,0:T(8,128)S(1)} %bitcast.188, f32[8,512]{1,0:T(8,128)S(1)} %broadcast_bitcast_fusion), kind=kLoop, calls=%fused_computation.14 | loop fusion | flops 1572864 | bytes 3424256 | tf_op jit(solution)/shard_map/convert_element_type | solution.py:174
  131.3 4.5 %all-to-all-start.3 = ((bf16[8,1024,128]{2,1,0:T(8,128)(2,1)}), bf16[8,1024,128]{2,1,0:T(8,128)(2,1)}, u32[]{:S(2)}, u32[]{:S(2)}) async-start(bf16[8,1024,128]{2,1,0:T(8,128)(2,1)} %pad_maximum_fusion), calls=%async_computation.3 | async-start | bytes 4194304 | tf_op jit(solution)/shard_map/all_to_all | solution.py:178
  138.0 2.2 %fusion.61 = f32[32,128,128]{1,2,0:T(8,128)} fusion(bf16[32,128,128]{2,1,0:T(8,128)(2,1)S(1)} %multiply_convert_fusion.1, bf16[128,32,128]{0,2,1:T(8,128)(2,1)S(1)} %bitcast.152), kind=kOutput, calls=%fused_computation.151 | convolution fusion | flops 134217728 | bytes 4194304 | tf_op jit(solution)/shard_map/hts,shd->thd/dot_general | solution.py:21
  140.2 22.6 %all-to-all-done.3 = bf16[8,1024,128]{2,1,0:T(8,128)(2,1)} async-done(((bf16[8,1024,128]{2,1,0:T(8,128)(2,1)}), bf16[8,1024,128]{2,1,0:T(8,128)(2,1)}, u32[]{:S(2)}, u32[]{:S(2)}) %all-to-all-start.3) | async-done | bytes 2097184 | tf_op jit(solution)/shard_map/all_to_all | solution.py:178
  162.8 2.6 %fusion.56 = (bf16[8,512,128]{2,1,0:T(8,128)(2,1)S(1)}, bf16[8,512,128]{2,1,0:T(8,128)(2,1)}) fusion(bf16[8,1024,128]{2,1,0:T(8,128)(2,1)} %all-to-all-done.3), kind=kLoop, calls=%fused_computation.146 | loop fusion | bytes 4194304 | tf_op jit(solution)/shard_map/slice | solution.py:180
  165.5 1.9 %fusion.62 = f32[32,128,128]{2,1,0:T(8,128)} fusion(bf16[32,128,128]{2,1,0:T(8,128)(2,1)S(1)} %bitcast.164, bf16[128,32,128]{0,2,1:T(8,128)(2,1)S(1)} %bitcast.153), kind=kOutput, calls=%fused_computation.152 | convolution fusion | flops 134217728 | bytes 4194304 | tf_op jit(solution)/shard_map/sha,hab->shb/dot_general | solution.py:21
  167.4 2.2 %fusion.14 = f32[32,128,128]{2,1,0:T(8,128)} fusion(bf16[32,128,128]{2,1,0:T(8,128)(2,1)S(1)} %bitcast.165, bf16[128,4096]{1,0:T(8,128)(2,1)S(1)} %copy-done), kind=kOutput, calls=%fused_computation.28 | convolution fusion | flops 134217728 | bytes 4194304 | tf_op jit(solution)/shard_map/shb,hab->sha/dot_general | solution.py:21
  169.5 4.2 %fusion.3 = bf16[128,32,128]{0,2,1:T(8,128)(2,1)} fusion(f32[32,128,128]{2,1,0:T(8,128)} %fusion.62, bf16[128,32,128]{0,2,1:T(8,128)(2,1)S(1)} %bitcast.158, bf16[128,32,128]{0,2,1:T(8,128)(2,1)} %bitcast.162, bf16[128,32,128]{0,2,1:T(8,128)(2,1)S(1)} %bitcast.154, f32[128,32]{0,1:T(8,128)S(1)} %get-tuple-element.78, f32[32,128]{1,0:T(8,128)S(1)} %bitcast.192, ...), kind=kOutput, calls=%fused_computation.6 | convolution fusion | flops 272629760 | bytes 6340608 | tf_op jit(solution)/shard_map/hts,thd->shd/dot_general | solution.py:21
  173.8 2.4 %copy.109 = bf16[128,4096]{1,0:T(8,128)(2,1)} copy(bf16[128,4096]{0,1:T(8,128)(2,1)} %bitcast.187) | data formatting | bytes 2097152
  176.1 3.4 %fusion.5 = bf16[128,32,128]{0,2,1:T(8,128)(2,1)} fusion(f32[32,128,128]{2,1,0:T(8,128)} %fusion.14, bf16[128,32,128]{0,2,1:T(8,128)(2,1)S(1)} %bitcast.163, bf16[32,128,128]{2,1,0:T(8,128)(2,1)} %copy-done.5, f32[128,32]{0,1:T(8,128)S(1)} %get-tuple-element.78), kind=kOutput, calls=%fused_computation.9 | convolution fusion | flops 135790592 | bytes 5259264 | tf_op jit(solution)/shard_map/hts,thd->shd/dot_general | solution.py:21
  179.5 2.3 %copy.108 = bf16[128,4096]{1,0:T(8,128)(2,1)} copy(bf16[128,4096]{0,1:T(8,128)(2,1)} %bitcast.166) | data formatting | bytes 2097152
  181.8 2.4 %fusion.7 = bf16[128,32,128]{0,2,1:T(8,128)(2,1)S(1)} fusion(f32[32,128,128]{1,2,0:T(8,128)} %fusion.61, bf16[32,128,128]{2,1,0:T(8,128)(2,1)} %bitcast.168, bf16[128,32,128]{0,2,1:T(8,128)(2,1)S(1)} %bitcast.159, f32[128,32]{0,1:T(8,128)S(1)} %get-tuple-element.79), kind=kOutput, calls=%fused_computation.12 | convolution fusion | flops 135790592 | bytes 5259264 | tf_op jit(solution)/shard_map/thb,hab->tha/dot_general | solution.py:21
  (129 shorter events, 39.5 us)
Async XLA Ops:
  0.6 8.9 %copy-start = (bf16[128,4096]{1,0:T(8,128)(2,1)S(1)}, bf16[128,4096]{1,0:T(8,128)(2,1)}, u32[]{:S(2)}) copy-start(bf16[128,4096]{1,0:T(8,128)(2,1)} %param.9) | copy-start | bytes 3145732
  10.0 1.2 copy-start.6
  10.0 1.2 copy-start.15
  12.7 32.1 %all-to-all-start = ((bf16[8,1040,128]{2,1,0:T(8,128)(2,1)}), bf16[8,1040,128]{2,1,0:T(8,128)(2,1)}, u32[]{:S(2)}, u32[]{:S(2)}) async-start(bf16[8,1040,128]{2,1,0:T(8,128)(2,1)} %fusion.1), calls=%async_computation | async-start | bytes 4259840 | tf_op jit(solution)/shard_map/all_to_all | solution.py:162
  49.3 4.8 %copy-start.1 = (f32[8,512,128]{2,1,0:T(8,128)}, f32[8,512,128]{2,1,0:T(8,128)S(1)}, u32[]{:S(2)}) copy-start(f32[8,512,128]{2,1,0:T(8,128)S(1)} %get-tuple-element.52) | copy-start | bytes 6291460
  49.3 6.9 %copy-start.2 = (f32[8,512,128]{2,1,0:T(8,128)}, f32[8,512,128]{2,1,0:T(8,128)S(1)}, u32[]{:S(2)}) copy-start(f32[8,512,128]{2,1,0:T(8,128)S(1)} %get-tuple-element.53) | copy-start | bytes 6291460
  63.4 1.1 copy-start.9
  63.4 1.2 copy-start.10
  63.4 1.2 copy-start.11
  63.4 1.3 copy-start.12
  63.4 1.4 copy-start.13
  63.4 1.5 copy-start.14
  66.2 31.4 %all-to-all-start.1 = ((f32[32,40,128]{2,1,0:T(8,128)}), f32[32,40,128]{2,1,0:T(8,128)}, u32[]{:S(2)}, u32[]{:S(2)}) async-start(f32[32,40,128]{2,1,0:T(8,128)} %maximum_maximum_fusion), calls=%async_computation.1 | async-start | bytes 1310720 | tf_op jit(solution)/shard_map/all_to_all | solution.py:55
  100.7 7.2 %copy-start.17 = (f32[1,4]{1,0:T(1,128)S(1)}, f32[1,4]{1,0:T(1,128)}, u32[]{:S(2)}) copy-start(f32[1,4]{1,0:T(1,128)} %get-tuple-element.80) | copy-start | bytes 52
  100.7 7.2 %copy-start.18 = (f32[1,4]{1,0:T(1,128)S(1)}, f32[1,4]{1,0:T(1,128)}, u32[]{:S(2)}) copy-start(f32[1,4]{1,0:T(1,128)} %get-tuple-element.42) | copy-start | bytes 52
  100.8 7.2 %copy-start.19 = (f32[1,4]{1,0:T(1,128)S(1)}, f32[1,4]{1,0:T(1,128)}, u32[]{:S(2)}) copy-start(f32[1,4]{1,0:T(1,128)} %get-tuple-element.43) | copy-start | bytes 52
  100.8 7.2 %copy-start.20 = (f32[1,4]{1,0:T(1,128)S(1)}, f32[1,4]{1,0:T(1,128)}, u32[]{:S(2)}) copy-start(f32[1,4]{1,0:T(1,128)} %get-tuple-element.44) | copy-start | bytes 52
  100.8 7.2 %copy-start.21 = (f32[1,4]{1,0:T(1,128)S(1)}, f32[1,4]{1,0:T(1,128)}, u32[]{:S(2)}) copy-start(f32[1,4]{1,0:T(1,128)} %get-tuple-element.45) | copy-start | bytes 52
  100.8 7.2 %copy-start.22 = (f32[1,4]{1,0:T(1,128)S(1)}, f32[1,4]{1,0:T(1,128)}, u32[]{:S(2)}) copy-start(f32[1,4]{1,0:T(1,128)} %get-tuple-element.46) | copy-start | bytes 52
  100.8 7.2 %copy-start.23 = (f32[1,4]{1,0:T(1,128)S(1)}, f32[1,4]{1,0:T(1,128)}, u32[]{:S(2)}) copy-start(f32[1,4]{1,0:T(1,128)} %get-tuple-element.47) | copy-start | bytes 52
  100.8 7.3 %copy-start.16 = (f32[1,4]{1,0:T(1,128)S(1)}, f32[1,4]{1,0:T(1,128)}, u32[]{:S(2)}) copy-start(f32[1,4]{1,0:T(1,128)} %get-tuple-element.92) | copy-start | bytes 52
  102.8 21.9 %all-to-all-start.2 = ((f32[32,32,128]{2,1,0:T(8,128)}), f32[32,32,128]{2,1,0:T(8,128)}, u32[]{:S(2)}, u32[]{:S(2)}) async-start(f32[32,32,128]{2,1,0:T(8,128)} %copy.98), calls=%async_computation.2 | async-start | bytes 1048576 | tf_op jit(solution)/shard_map/all_to_all | solution.py:73
  131.3 31.6 %all-to-all-start.3 = ((bf16[8,1024,128]{2,1,0:T(8,128)(2,1)}), bf16[8,1024,128]{2,1,0:T(8,128)(2,1)}, u32[]{:S(2)}, u32[]{:S(2)}) async-start(bf16[8,1024,128]{2,1,0:T(8,128)(2,1)} %pad_maximum_fusion), calls=%async_computation.3 | async-start | bytes 4194304 | tf_op jit(solution)/shard_map/all_to_all | solution.py:178
  173.8 2.4 %copy-start.4 = (bf16[128,4096]{0,1:T(8,128)(2,1)S(1)}, bf16[128,4096]{0,1:T(8,128)(2,1)}, u32[]{:S(2)}) copy-start(bf16[128,4096]{0,1:T(8,128)(2,1)} %copy-done.3) | copy-start | bytes 3145732
  (4 other events, 3.9 us)

commit v4 on v3

--- a/solution.py
+++ b/solution.py
@@ -87,20 +87,24 @@
     return jnp.einsum("ts,nsh->nth", lower, decay_blk, preferred_element_type=jnp.float32)
 
 
-def unrolled(totals, pieces, reverse):
+def within_group(totals, pieces, reverse):
     blocks = totals.shape[0]
-    heads, width = pieces.shape[1], pieces.shape[2]
-    carry = jnp.zeros((heads, width, width), jnp.float32)
-    logsum = jnp.zeros((heads,), jnp.float32)
-    seen = [None] * blocks
-    seen_log = [None] * blocks
-    order = reversed(range(blocks)) if reverse else range(blocks)
-    for i in order:
-        seen[i] = carry
-        seen_log[i] = logsum
-        carry = jnp.exp(totals[i])[:, None, None] * carry + pieces[i]
-        logsum = logsum + totals[i]
-    return jnp.stack(seen), jnp.stack(seen_log), carry, logsum
+    at = lax.broadcasted_iota(jnp.int32, (blocks, blocks, blocks), 0)
+    src = lax.broadcasted_iota(jnp.int32, (blocks, blocks, blocks), 1)
+    mid = lax.broadcasted_iota(jnp.int32, (blocks, blocks, blocks), 2)
+    between = ((at < mid) & (mid < src)) if reverse else ((src < mid) & (mid < at))
+    logs = jnp.sum(jnp.where(between[..., None], totals[None, None], 0.0), axis=2)
+    pos = lax.broadcasted_iota(jnp.int32, (blocks, blocks), 0)
+    other = lax.broadcasted_iota(jnp.int32, (blocks, blocks), 1)
+    earlier = (other > pos) if reverse else (other < pos)
+    later = (other < pos) if reverse else (other > pos)
+    weights = jnp.where(earlier[..., None], jnp.exp(jnp.where(earlier[..., None], logs, 0.0)), 0.0)
+    seen_log = jnp.sum(jnp.where(earlier[..., None], totals[None], 0.0), axis=1)
+    tail_log = jnp.sum(jnp.where(later[..., None], totals[None], 0.0), axis=1)
+    highest = lax.Precision.HIGHEST
+    seen = jnp.einsum("ijh,jhab->ihab", weights, pieces, precision=highest)
+    whole = jnp.einsum("jh,jhab->hab", jnp.exp(tail_log), pieces, precision=highest)
+    return seen, seen_log, whole, jnp.sum(totals, axis=0)
 
 
 def local_block(queries, keys, values, out_grad, log_decay):
@@ -163,8 +167,12 @@
     contrib_g = widen(got[:, :share]).reshape(peers, group, width, width)
     update_g = widen(got[:, share : 2 * share]).reshape(peers, group, width, width)
     totals = jnp.sum(widen(got[:, 2 * share : 2 * share + group]), axis=2)
-    prefix, prefix_log, dev_state, dev_log = unrolled(totals, contrib_g, False)
-    suffix, suffix_log, dev_adjoint, unused = unrolled(totals, update_g, True)
+    query_part, key_part, value_part = intra(query_blk, key_blk, value_blk, grad_blk, cumul)
+    totals, contrib_g, update_g, query_part, key_part, value_part = lax.optimization_barrier(
+        (totals, contrib_g, update_g, query_part, key_part, value_part)
+    )
+    prefix, prefix_log, dev_state, dev_log = within_group(totals, contrib_g, False)
+    suffix, suffix_log, dev_adjoint, unused = within_group(totals, update_g, True)
     start_state, start_adjoint = carried_both(dev_log, dev_state, dev_adjoint, "seq")
     state_prev = jnp.exp(prefix_log)[:, :, None, None] * start_state[None] + prefix
     adjoint = jnp.exp(suffix_log)[:, :, None, None] * start_adjoint[None] + suffix
@@ -178,7 +186,6 @@
     back = lax.all_to_all(returned, "exp", 0, 0, tiled=True)
     state_in = back[:, :share].reshape(heads, width, width)
     adjoint_in = back[:, share:].reshape(heads, width, width)
-    query_part, key_part, value_part = intra(query_blk, key_blk, value_blk, grad_blk, cumul)
     grad_query = query_part + before[..., None] * product("thb,hab->tha", grad_blk, state_in)
     grad_key = key_part + after[..., None] * product("shb,hab->sha", value_blk, adjoint_in)
     grad_value = value_part + after[..., None] * product("sha,hab->shb", key_blk, adjoint_in)

time: 187 us -> 179 us (0.957)
  blocking collectives: 0 us -> 30 us
  waiting for transfers between devices: 82.2 us -> 55.8 us
  other arithmetic: 27 us -> 6.08 us
  matrix products: 22.9 us -> 37.9 us
  starting transfers between devices: 25.3 us -> 20.8 us
    all_to_all x0 -> x1, blocking collectives: none -> 30 us  [body(): back = lax.all_to_all(returned, 'exp', 0, 0, tiled=True)]
    all_to_all x1 -> x0, waiting for transfers between devices: 22.6 us -> none  [body(): back = lax.all_to_all(returned, 'exp', 0, 0, tiled=True)]
    dot_general x0 -> x4, matrix products: none -> 13.8 us  [the longest x2 8.07 us: within_group(): seen = jnp.einsum('ijh,jhab->ihab', weights, pieces, precision=highest)]
    unnamed x7 -> x0, other arithmetic: 7.95 us -> none
    all_to_all x1, waiting for transfers between devices: 26.9 us -> 19.1 us  [body(): got = lax.all_to_all(packed, 'exp', 0, 0, tiled=True)]
    convert_element_type x3 -> x0, other arithmetic: 5.87 us -> none  [the longest x1 1.96 us: body(): state_prev.astype(jnp.bfloat16).reshape(peers, share, width)]
    convert_element_type x0 -> x3, local copies, waits for them, and re-layouts: none -> 4.68 us  [body(): flat = lambda x: x.astype(jnp.bfloat16).reshape(length, heads * width)]
    all_to_all x1 -> x0, starting transfers between devices: 4.53 us -> none  [body(): back = lax.all_to_all(returned, 'exp', 0, 0, tiled=True)]
  transfers between devices with their start and end apart: 4 -> 3, of which waited for: 4 -> 3; matrix products, arithmetic and copies ran while one was open for 5% -> 5% of each run, Pallas kernels for 0% -> 0%
where the time goes in v4:
time: 179 us; the launch traced here: 178 us
  waiting for transfers between devices  55.8 us (31%)
  matrix products  37.9 us (21%)
  blocking collectives  30 us (17%)
  local copies, waits for them, and re-layouts  26 us (15%)
  starting transfers between devices  20.8 us (12%)
  other arithmetic  6.08 us (3%)
    all_to_all x1, blocking collectives, body(): back = lax.all_to_all(returned, 'exp', 0, 0, tiled=True)  30 us
    dot_general x11, matrix products, product(): jnp.einsum(form, first_op, second_op, preferred_element_type=jnp.float32)  22.4 us
    all_to_all x1, waiting for transfers between devices, carried_both(): got = lax.all_to_all(payload, axis, 0, 0, tiled=True)  20.1 us
    all_to_all x1, waiting for transfers between devices, body(): got = lax.all_to_all(packed, 'exp', 0, 0, tiled=True)  19.1 us
    all_to_all x1, waiting for transfers between devices, carried_both(): lax.all_to_all(jnp.concatenate([state_rows, adjoint_rows], axis=1), axis,...  16.7 us
    all_to_all x1, starting transfers between devices, carried_both(): got = lax.all_to_all(payload, axis, 0, 0, tiled=True)  11.2 us
    unnamed x35, local copies, waits for them, and re-layouts  10.8 us
    dot_general x2, matrix products, within_group(): seen = jnp.einsum('ijh,jhab->ihab', weights, pieces, precision=highest)  8.07 us
  transfers between devices with their start and end apart: 3, of which 3 were waited for; matrix products, arithmetic and copies ran while one was open for 5% of the time, Pallas kernels for 0%

profile of v4, /device:TPU:32, one launch (start us, length us, event | category | flops | bytes accessed | tf_op | source)
XLA Modules:
  0.0 177.6 jit_solution(3978770930186207506)
XLA Ops:
  1.8 1.6 copy.168
  5.8 1.7 copy.162
  8.8 2.7 %fusion.24 = f32[32,128,128]{2,1,0:T(8,128)S(1)} fusion(bf16[128,32,128]{2,0,1:T(8,128)(2,1)} %copy.163, f32[128,32]{0,1:T(8,128)S(1)} %get-tuple-element.53, bf16[128,4096]{1,0:T(8,128)(2,1)S(1)} %copy-done.4), kind=kOutput, calls=%fused_computation.39 | convolution fusion | flops 135790592 | bytes 4210688 | tf_op jit(solution)/shard_map/sha,shb->hab/dot_general | solution.py:21
  14.7 1.6 add_convert_fusion
  17.7 4.5 %all-to-all-start = ((bf16[8,1040,128]{2,1,0:T(8,128)(2,1)}), bf16[8,1040,128]{2,1,0:T(8,128)(2,1)}, u32[]{:S(2)}, u32[]{:S(2)}) async-start(bf16[8,1040,128]{2,1,0:T(8,128)(2,1)} %fusion.1), calls=%async_computation | async-start | bytes 4259840 | tf_op jit(solution)/shard_map/all_to_all | solution.py:166
  23.5 2.2 %convolution_bitcast_fusion.1 = f32[128,32,128]{2,0,1:T(8,128)} fusion(bf16[32,128,128]{2,1,0:T(8,128)(2,1)S(1)} %multiply_convert_fusion.1, bf16[128,32,128]{0,2,1:T(8,128)(2,1)S(1)} %bitcast.152), kind=kOutput, calls=%fused_computation.37 | convolution fusion | flops 134217728 | bytes 4194304 | tf_op jit(solution)/shard_map/hts,thd->shd/dot_general | solution.py:21
  25.8 2.2 %convolution_bitcast_fusion.2 = f32[128,32,128]{2,0,1:T(8,128)} fusion(bf16[32,128,128]{2,1,0:T(8,128)(2,1)S(1)} %multiply_convert_fusion.1, bf16[128,32,128]{0,2,1:T(8,128)(2,1)S(1)} %bitcast.146), kind=kOutput, calls=%fused_computation.38 | convolution fusion | flops 134217728 | bytes 4194304 | tf_op jit(solution)/shard_map/hts,shd->thd/dot_general | solution.py:21
  28.0 2.8 %convolution_bitcast_fusion = f32[128,32,128]{2,0,1:T(8,128)} fusion(bf16[128,32,128]{0,2,1:T(8,128)(2,1)S(1)} %bitcast.153, bf16[128,32,128]{0,2,1:T(8,128)(2,1)S(1)} %bitcast.147, f32[32,128]{1,0:T(8,128)S(1)} %bitcast.170, pred[128,128]{1,0:T(8,128)(4,1)S(1)} %iota_compare_fusion.5, bf16[128,4096]{1,0:T(8,128)(2,1)S(1)} %copy-done), kind=kOutput, calls=%fused_computation.36 | convolution fusion | flops 271056896 | bytes 5275648 | tf_op jit(solution)/shard_map/hts,thd->shd/dot_general | solution.py:21
  30.8 19.1 %all-to-all-done = bf16[8,1040,128]{2,1,0:T(8,128)(2,1)} async-done(((bf16[8,1040,128]{2,1,0:T(8,128)(2,1)}), bf16[8,1040,128]{2,1,0:T(8,128)(2,1)}, u32[]{:S(2)}, u32[]{:S(2)}) %all-to-all-start) | async-done | bytes 2129952 | tf_op jit(solution)/shard_map/all_to_all | solution.py:166
  49.9 1.7 fusion.79
  54.8 2.8 %fusion.12 = f32[4,1,128,128]{3,1,2,0:T(1,128)S(1)} fusion(f32[8,4,1,1]{0,2,3,1:T(1,128)S(1)} %copy.222, f32[8,4,128,128]{3,2,1,0:T(8,128)S(1)} %convert.3), kind=kOutput, calls=%fused_computation.28 | convolution fusion | flops 6291456 | bytes 2359424 | tf_op jit(solution)/shard_map/jh,jhab->hab/dot_general | solution.py:106
  57.6 2.8 %fusion.16 = f32[4,1,128,128]{3,1,2,0:T(1,128)S(1)} fusion(f32[8,4,1,1]{0,2,3,1:T(1,128)S(1)} %copy.220, f32[8,4,128,128]{3,2,1,0:T(8,128)S(1)} %copy-done.1), kind=kOutput, calls=%fused_computation.32 | convolution fusion | flops 6291456 | bytes 2359424 | tf_op jit(solution)/shard_map/jh,jhab->hab/dot_general | solution.py:106
  61.4 11.2 %all-to-all-start.1 = ((f32[32,40,128]{2,1,0:T(8,128)}), f32[32,40,128]{2,1,0:T(8,128)}, u32[]{:S(2)}, u32[]{:S(2)}) async-start(f32[32,40,128]{2,1,0:T(8,128)} %maximum_maximum_fusion), calls=%async_computation.1 | async-start | bytes 1310720 | tf_op jit(solution)/shard_map/all_to_all | solution.py:55
  72.7 20.1 %all-to-all-done.1 = f32[32,40,128]{2,1,0:T(8,128)} async-done(((f32[32,40,128]{2,1,0:T(8,128)}), f32[32,40,128]{2,1,0:T(8,128)}, u32[]{:S(2)}, u32[]{:S(2)}) %all-to-all-start.1) | async-done | bytes 655392 | tf_op jit(solution)/shard_map/all_to_all | solution.py:55
  97.3 5.1 %all-to-all-start.2 = ((f32[32,32,128]{2,1,0:T(8,128)}), f32[32,32,128]{2,1,0:T(8,128)}, u32[]{:S(2)}, u32[]{:S(2)}) async-start(f32[32,32,128]{2,1,0:T(8,128)} %copy.188), calls=%async_computation.2 | async-start | bytes 1048576 | tf_op jit(solution)/shard_map/all_to_all | solution.py:73
  102.6 16.7 %all-to-all-done.2 = f32[32,32,128]{2,1,0:T(8,128)} async-done(((f32[32,32,128]{2,1,0:T(8,128)}), f32[32,32,128]{2,1,0:T(8,128)}, u32[]{:S(2)}, u32[]{:S(2)}) %all-to-all-start.2) | async-done | bytes 524320 | tf_op jit(solution)/shard_map/all_to_all | solution.py:73
  120.4 4.8 %fusion.9 = bf16[8,4,128,128]{3,0,2,1:T(8,128)(2,1)S(1)} fusion(f32[8,4,128,128]{3,2,1,0:T(8,128)} %convert.2, f32[4,128,128]{2,1,0:T(8,128)S(1)} %bitcast.165, f32[8,4]{0,1:T(4,128)S(1)} %copy.184, f32[8,8,4,1]{1,2,0,3:T(4,128)S(1)} %get-tuple-element.59), kind=kOutput, calls=%fused_computation.16 | convolution fusion | flops 51904512 | bytes 3409024 | tf_op jit(solution)/shard_map/ijh,jhab->ihab/dot_general | solution.py:105
  125.3 3.3 %fusion.8 = bf16[8,4,128,128]{3,0,2,1:T(8,128)(2,1)S(1)} fusion(f32[8,4,128,128]{3,2,1,0:T(8,128)S(1)} %convert.3, f32[4,128,128]{2,1,0:T(8,128)S(1)} %bitcast.164, f32[8,4]{0,1:T(4,128)S(1)} %copy.192, f32[8,8,4,1]{1,2,0,3:T(4,128)S(1)} %get-tuple-element.60), kind=kOutput, calls=%fused_computation.14 | convolution fusion | flops 51904512 | bytes 3409024 | tf_op jit(solution)/shard_map/ijh,jhab->ihab/dot_general | solution.py:105
  128.9 30.0 %all_to_all.20 = bf16[8,1024,128]{2,1,0:T(8,128)(2,1)S(1)} all-to-all(bf16[8,1024,128]{2,1,0:T(8,128)(2,1)S(1)} %pad_maximum_fusion), channel_id=1, replica_groups=mesh['seq'=32,'exp'=8] {'exp'}, dimensions={0} | all-to-all | bytes 4194304 | tf_op jit(solution)/shard_map/all_to_all | solution.py:186
  161.1 1.9 %fusion.3 = bf16[128,32,128]{2,0,1:T(8,128)(2,1)} fusion(f32[128,32,128]{2,0,1:T(8,128)S(1)} %copy-done.13, bf16[32,128,128]{2,1,0:T(8,128)(2,1)S(1)} %bitcast.149, bf16[128,32,128]{0,2,1:T(8,128)(2,1)S(1)} %bitcast.148, f32[128,32]{0,1:T(8,128)S(1)} %get-tuple-element.53), kind=kOutput, calls=%fused_computation.6 | convolution fusion | flops 135790592 | bytes 5259264 | tf_op jit(solution)/shard_map/sha,hab->shb/dot_general | solution.py:21
  166.3 2.4 %copy.206 = bf16[128,32,128]{0,2,1:T(8,128)(2,1)} copy(bf16[128,32,128]{2,0,1:T(8,128)(2,1)} %fusion.3) | data formatting | bytes 2097152 | tf_op jit(solution)/shard_map/convert_element_type | solution.py:192
  168.7 2.3 %copy.209 = bf16[128,4096]{1,0:T(8,128)(2,1)} copy(bf16[128,4096]{0,1:T(8,128)(2,1)} %bitcast.162) | data formatting | bytes 2097152
  171.0 3.7 %fusion.7 = bf16[128,32,128]{2,0,1:T(8,128)(2,1)} fusion(f32[128,32,128]{2,0,1:T(8,128)S(1)} %copy-done.11, bf16[32,128,128]{2,1,0:T(8,128)(2,1)} %bitcast.156, f32[128,32]{0,1:T(8,128)S(1)} %get-tuple-element.54, bf16[128,4096]{1,0:T(8,128)(2,1)S(1)} %copy-done), kind=kOutput, calls=%fused_computation.12 | convolution fusion | flops 135790592 | bytes 5259264 | tf_op jit(solution)/shard_map/thb,hab->tha/dot_general | solution.py:21
  174.7 1.6 copy.199
  (76 shorter events, 27.8 us)
Async XLA Ops:
  0.6 12.5 %copy-start = (bf16[128,4096]{1,0:T(8,128)(2,1)S(1)}, bf16[128,4096]{1,0:T(8,128)(2,1)}, u32[]{:S(2)}) copy-start(bf16[128,4096]{1,0:T(8,128)(2,1)} %param.10) | copy-start | bytes 3145732
  3.5 1.0 copy-start.8
  5.8 3.0 %copy-start.4 = (bf16[128,4096]{1,0:T(8,128)(2,1)S(1)}, bf16[128,4096]{1,0:T(8,128)(2,1)}, u32[]{:S(2)}) copy-start(bf16[128,4096]{1,0:T(8,128)(2,1)} %param.9) | copy-start | bytes 3145732
  7.5 20.5 %copy-start.2 = (bf16[128,4096]{0,1:T(8,128)(2,1)}, bf16[128,4096]{0,1:T(8,128)(2,1)S(1)}, u32[]{:S(2)}) copy-start(bf16[128,4096]{0,1:T(8,128)(2,1)S(1)} %copy.162) | copy-start | bytes 3145732
  8.8 2.7 %copy-start.7 = (bf16[128,32,128]{2,0,1:T(8,128)(2,1)S(1)}, bf16[128,32,128]{2,0,1:T(8,128)(2,1)}, u32[]{:S(2)}) copy-start(bf16[128,32,128]{2,0,1:T(8,128)(2,1)} %copy.163) | copy-start | bytes 3145732
  11.5 1.6 copy-start.6
  14.7 1.6 copy-start.14
  17.7 32.1 %all-to-all-start = ((bf16[8,1040,128]{2,1,0:T(8,128)(2,1)}), bf16[8,1040,128]{2,1,0:T(8,128)(2,1)}, u32[]{:S(2)}, u32[]{:S(2)}) async-start(bf16[8,1040,128]{2,1,0:T(8,128)(2,1)} %fusion.1), calls=%async_computation | async-start | bytes 4259840 | tf_op jit(solution)/shard_map/all_to_all | solution.py:166
  22.3 1.2 copy-start.9
  25.8 2.2 %copy-start.10 = (bf16[128,4096]{0,1:T(8,128)(2,1)S(1)}, bf16[128,4096]{0,1:T(8,128)(2,1)}, u32[]{:S(2)}) copy-start(bf16[128,4096]{0,1:T(8,128)(2,1)} %copy-done.8) | copy-start | bytes 3145732
  54.8 2.9 %copy-start.1 = (f32[8,4,128,128]{3,2,1,0:T(8,128)S(1)}, f32[8,4,128,128]{3,2,1,0:T(8,128)}, u32[]{:S(2)}) copy-start(f32[8,4,128,128]{3,2,1,0:T(8,128)} %convert.2) | copy-start | bytes 6291460
  61.4 31.4 %all-to-all-start.1 = ((f32[32,40,128]{2,1,0:T(8,128)}), f32[32,40,128]{2,1,0:T(8,128)}, u32[]{:S(2)}, u32[]{:S(2)}) async-start(f32[32,40,128]{2,1,0:T(8,128)} %maximum_maximum_fusion), calls=%async_computation.1 | async-start | bytes 1310720 | tf_op jit(solution)/shard_map/all_to_all | solution.py:55
  97.3 21.9 %all-to-all-start.2 = ((f32[32,32,128]{2,1,0:T(8,128)}), f32[32,32,128]{2,1,0:T(8,128)}, u32[]{:S(2)}, u32[]{:S(2)}) async-start(f32[32,32,128]{2,1,0:T(8,128)} %copy.188), calls=%async_computation.2 | async-start | bytes 1048576 | tf_op jit(solution)/shard_map/all_to_all | solution.py:73
  158.8 1.6 copy-start.3
  158.8 2.3 %copy-start.13 = (f32[128,32,128]{2,0,1:T(8,128)S(1)}, f32[128,32,128]{2,0,1:T(8,128)}, u32[]{:S(2)}) copy-start(f32[128,32,128]{2,0,1:T(8,128)} %convolution_bitcast_fusion) | copy-start | bytes 6291460
  161.1 1.9 %copy-start.5 = (bf16[128,4096]{1,0:T(8,128)(2,1)S(1)}, bf16[128,4096]{1,0:T(8,128)(2,1)}, u32[]{:S(2)}) copy-start(bf16[128,4096]{1,0:T(8,128)(2,1)} %param.9) | copy-start | bytes 3145732
  161.1 2.2 %copy-start.12 = (f32[128,32,128]{2,0,1:T(8,128)S(1)}, f32[128,32,128]{2,0,1:T(8,128)}, u32[]{:S(2)}) copy-start(f32[128,32,128]{2,0,1:T(8,128)} %convolution_bitcast_fusion.1) | copy-start | bytes 6291460
  166.3 4.7 %copy-start.11 = (f32[128,32,128]{2,0,1:T(8,128)S(1)}, f32[128,32,128]{2,0,1:T(8,128)}, u32[]{:S(2)}) copy-start(f32[128,32,128]{2,0,1:T(8,128)} %convolution_bitcast_fusion.2) | copy-start | bytes 6291460

commit v5 on v4

--- a/solution.py
+++ b/solution.py
@@ -33,6 +33,14 @@
 
 def link(earlier, later):
     return (earlier[0] + later[0], jnp.exp(later[0])[:, None, None] * earlier[1] + later[1])
+
+
+def pieces_of(array):
+    high = array.astype(jnp.bfloat16)
+    rest = array - widen(high)
+    mid = rest.astype(jnp.bfloat16)
+    low = (rest - widen(mid)).astype(jnp.bfloat16)
+    return high, mid, low
 
 
 def carried_both(dev_log, dev_state, dev_adjoint, axis):
@@ -40,14 +48,16 @@
     here = lax.axis_index(axis)
     heads, width = dev_state.shape[0], dev_state.shape[2]
     share = heads * width // peers
-    spare = 8
-    logs = jnp.zeros((spare, width), jnp.float32).at[:heads, :].set(
-        jnp.broadcast_to(dev_log[:, None], (heads, width))
-    )
+    spare = 16
+    logs = jnp.zeros((spare, width), jnp.bfloat16)
+    for i, part in enumerate(pieces_of(dev_log)):
+        logs = logs.at[i * heads : (i + 1) * heads, :].set(
+            jnp.broadcast_to(part[:, None], (heads, width))
+        )
     payload = jnp.concatenate(
         [
-            dev_state.reshape(peers, share, width),
-            dev_adjoint.reshape(peers, share, width),
+            dev_state.astype(jnp.bfloat16).reshape(peers, share, width),
+            dev_adjoint.astype(jnp.bfloat16).reshape(peers, share, width),
             jnp.broadcast_to(logs[None], (peers, spare, width)),
         ],
         axis=1,
@@ -55,7 +65,10 @@
     got = lax.all_to_all(payload, axis, 0, 0, tiled=True)
     head = (here * share) // width
     pick = (lax.broadcasted_iota(jnp.int32, (heads,), 0) == head).astype(jnp.float32)
-    totals = jnp.sum(got[:, 2 * share : 2 * share + heads, 0] * pick[None, :], axis=1)
+    log_rows = widen(got[:, 2 * share : 2 * share + 3 * heads, 0]).reshape(peers, 3, heads)
+    totals = jnp.sum(log_rows[:, 0] * pick[None, :], axis=1)
+    totals = totals + jnp.sum(log_rows[:, 1] * pick[None, :], axis=1)
+    totals = totals + jnp.sum(log_rows[:, 2] * pick[None, :], axis=1)
     dst = lax.broadcasted_iota(jnp.int32, (peers, peers, peers), 0)
     src = lax.broadcasted_iota(jnp.int32, (peers, peers, peers), 1)
     mid = lax.broadcasted_iota(jnp.int32, (peers, peers, peers), 2)
@@ -68,13 +81,19 @@
     w_fwd = jnp.where(src2 < dst2, jnp.exp(jnp.where(src2 < dst2, log_fwd, 0.0)), 0.0)
     w_bwd = jnp.where(src2 > dst2, jnp.exp(jnp.where(src2 > dst2, log_bwd, 0.0)), 0.0)
     highest = lax.Precision.HIGHEST
-    state_rows = jnp.einsum("di,irc->drc", w_fwd, got[:, :share], precision=highest)
-    adjoint_rows = jnp.einsum("di,irc->drc", w_bwd, got[:, share : 2 * share], precision=highest)
+    state_rows = jnp.einsum("di,irc->drc", w_fwd, widen(got[:, :share]), precision=highest)
+    adjoint_rows = jnp.einsum(
+        "di,irc->drc", w_bwd, widen(got[:, share : 2 * share]), precision=highest
+    )
     back = lax.all_to_all(
-        jnp.concatenate([state_rows, adjoint_rows], axis=1), axis, 0, 0, tiled=True
-    )
-    start_state = back[:, :share].reshape(heads, width, width)
-    start_adjoint = back[:, share:].reshape(heads, width, width)
+        jnp.concatenate([state_rows, adjoint_rows], axis=1).astype(jnp.bfloat16),
+        axis,
+        0,
+        0,
+        tiled=True,
+    )
+    start_state = widen(back[:, :share]).reshape(heads, width, width)
+    start_adjoint = widen(back[:, share:]).reshape(heads, width, width)
     return start_state, start_adjoint
 
 

time: 179 us -> 172 us (0.961)
  waiting for transfers between devices: 55.8 us -> 44.8 us
  other arithmetic: 6.08 us -> 8.36 us
    all_to_all x1, waiting for transfers between devices: 20.1 us -> 14.3 us  [carried_both(): got = lax.all_to_all(payload, axis, 0, 0, tiled=True)]
    all_to_all x1, waiting for transfers between devices: 16.7 us -> 11.5 us  [carried_both(): lax.all_to_all(jnp.concatenate([state_rows, adjoint_rows], axis=1).astype...]
    unnamed x35 -> x46, local copies, waits for them, and re-layouts: 10.8 us -> 13 us
    slice x3 -> x1, local copies, waits for them, and re-layouts: 2.08 us -> 0.02 us  [carried_both(): start_state = widen(back[:, :share]).reshape(heads, width, width)]
where the time goes in v5:
time: 172 us; the launch traced here: 170 us
  waiting for transfers between devices  44.8 us (26%)
  matrix products  39.2 us (23%)
  blocking collectives  30 us (17%)
  local copies, waits for them, and re-layouts  26.3 us (15%)
  starting transfers between devices  20.4 us (12%)
  other arithmetic  8.36 us (5%)
    all_to_all x1, blocking collectives, body(): back = lax.all_to_all(returned, 'exp', 0, 0, tiled=True)  30 us
    dot_general x11, matrix products, product(): jnp.einsum(form, first_op, second_op, preferred_element_type=jnp.float32)  22.4 us
    all_to_all x1, waiting for transfers between devices, body(): got = lax.all_to_all(packed, 'exp', 0, 0, tiled=True)  19 us
    all_to_all x1, waiting for transfers between devices, carried_both(): got = lax.all_to_all(payload, axis, 0, 0, tiled=True)  14.3 us
    unnamed x46, local copies, waits for them, and re-layouts  13 us
    all_to_all x1, waiting for transfers between devices, carried_both(): lax.all_to_all(jnp.concatenate([state_rows, adjoint_rows], axis=1).astype...  11.5 us
    all_to_all x1, starting transfers between devices, carried_both(): got = lax.all_to_all(payload, axis, 0, 0, tiled=True)  11.2 us
    dot_general x2, matrix products, within_group(): seen = jnp.einsum('ijh,jhab->ihab', weights, pieces, precision=highest)  8.07 us
  transfers between devices with their start and end apart: 3, of which 3 were waited for; matrix products, arithmetic and copies ran while one was open for 5% of the time, Pallas kernels for 0%

profile of v5, /device:TPU:32, one launch (start us, length us, event | category | flops | bytes accessed | tf_op | source)
XLA Modules:
  0.0 170.1 jit_solution(702569848144677186)
XLA Ops:
  1.9 1.6 copy.216
  5.8 1.7 copy.210
  8.8 2.7 %fusion.24 = f32[32,128,128]{2,1,0:T(8,128)S(1)} fusion(bf16[128,32,128]{2,0,1:T(8,128)(2,1)} %copy.211, f32[128,32]{0,1:T(8,128)S(1)} %get-tuple-element.83, bf16[128,4096]{1,0:T(8,128)(2,1)S(1)} %copy-done.3), kind=kOutput, calls=%fused_computation.39 | convolution fusion | flops 135790592 | bytes 4210688 | tf_op jit(solution)/shard_map/sha,shb->hab/dot_general | solution.py:21
  17.7 4.5 %all-to-all-start = ((bf16[8,1040,128]{2,1,0:T(8,128)(2,1)}), bf16[8,1040,128]{2,1,0:T(8,128)(2,1)}, u32[]{:S(2)}, u32[]{:S(2)}) async-start(bf16[8,1040,128]{2,1,0:T(8,128)(2,1)} %fusion.1), calls=%async_computation | async-start | bytes 4259840 | tf_op jit(solution)/shard_map/all_to_all | solution.py:185
  23.6 2.2 %convolution_bitcast_fusion.1 = f32[128,32,128]{2,0,1:T(8,128)} fusion(bf16[32,128,128]{2,1,0:T(8,128)(2,1)S(1)} %multiply_convert_fusion.1, bf16[128,32,128]{0,2,1:T(8,128)(2,1)S(1)} %bitcast.171), kind=kOutput, calls=%fused_computation.37 | convolution fusion | flops 134217728 | bytes 4194304 | tf_op jit(solution)/shard_map/hts,thd->shd/dot_general | solution.py:21
  25.8 2.2 %convolution_bitcast_fusion.2 = f32[128,32,128]{2,0,1:T(8,128)} fusion(bf16[32,128,128]{2,1,0:T(8,128)(2,1)S(1)} %multiply_convert_fusion.1, bf16[128,32,128]{0,2,1:T(8,128)(2,1)S(1)} %bitcast.165), kind=kOutput, calls=%fused_computation.38 | convolution fusion | flops 134217728 | bytes 4194304 | tf_op jit(solution)/shard_map/hts,shd->thd/dot_general | solution.py:21
  28.0 2.8 %convolution_bitcast_fusion = f32[128,32,128]{2,0,1:T(8,128)} fusion(bf16[128,32,128]{0,2,1:T(8,128)(2,1)S(1)} %bitcast.172, bf16[128,32,128]{0,2,1:T(8,128)(2,1)S(1)} %bitcast.166, f32[32,128]{1,0:T(8,128)S(1)} %bitcast.191, pred[128,128]{1,0:T(8,128)(4,1)S(1)} %iota_compare_fusion.5, bf16[128,4096]{1,0:T(8,128)(2,1)S(1)} %copy-done), kind=kOutput, calls=%fused_computation.36 | convolution fusion | flops 271056896 | bytes 5275648 | tf_op jit(solution)/shard_map/hts,thd->shd/dot_general | solution.py:21
  30.8 19.0 %all-to-all-done = bf16[8,1040,128]{2,1,0:T(8,128)(2,1)} async-done(((bf16[8,1040,128]{2,1,0:T(8,128)(2,1)}), bf16[8,1040,128]{2,1,0:T(8,128)(2,1)}, u32[]{:S(2)}, u32[]{:S(2)}) %all-to-all-start) | async-done | bytes 2129952 | tf_op jit(solution)/shard_map/all_to_all | solution.py:185
  49.9 1.7 fusion.83
  56.5 4.4 %fusion.12 = f32[4,1,128,128]{3,1,2,0:T(1,128)S(1)} fusion(f32[8,4,1,1]{0,2,3,1:T(1,128)S(1)} %copy.270, f32[8,4,128,128]{3,2,1,0:T(8,128)} %convert.14), kind=kOutput, calls=%fused_computation.28 | convolution fusion | flops 6291456 | bytes 2359424 | tf_op jit(solution)/shard_map/jh,jhab->hab/dot_general | solution.py:125
  60.9 2.8 %fusion.16 = f32[4,1,128,128]{3,1,2,0:T(1,128)S(1)} fusion(f32[8,4,1,1]{0,2,3,1:T(1,128)S(1)} %copy.268, f32[8,4,128,128]{3,2,1,0:T(8,128)S(1)} %convert.13), kind=kOutput, calls=%fused_computation.32 | convolution fusion | flops 6291456 | bytes 2359424 | tf_op jit(solution)/shard_map/jh,jhab->hab/dot_general | solution.py:125
  64.8 11.2 %all-to-all-start.1 = ((bf16[32,48,128]{2,1,0:T(8,128)(2,1)}), bf16[32,48,128]{2,1,0:T(8,128)(2,1)S(1)}, u32[]{:S(2)}, u32[]{:S(2)}) async-start(bf16[32,48,128]{2,1,0:T(8,128)(2,1)} %pad_maximum_fusion.1), calls=%async_computation.1 | async-start | bytes 786432 | tf_op jit(solution)/shard_map/all_to_all | solution.py:65
  76.5 14.3 %all-to-all-done.1 = bf16[32,48,128]{2,1,0:T(8,128)(2,1)S(1)} async-done(((bf16[32,48,128]{2,1,0:T(8,128)(2,1)}), bf16[32,48,128]{2,1,0:T(8,128)(2,1)S(1)}, u32[]{:S(2)}, u32[]{:S(2)}) %all-to-all-start.1) | async-done | bytes 393248 | tf_op jit(solution)/shard_map/all_to_all | solution.py:65
  91.5 1.7 copy.288
  95.8 4.7 %all-to-all-start.2 = ((bf16[32,32,128]{2,1,0:T(8,128)(2,1)}), bf16[32,32,128]{2,1,0:T(8,128)(2,1)S(1)}, u32[]{:S(2)}, u32[]{:S(2)}) async-start(bf16[32,32,128]{2,1,0:T(8,128)(2,1)} %copy.236), calls=%async_computation.2 | async-start | bytes 524288 | tf_op jit(solution)/shard_map/all_to_all | solution.py:88
  100.7 11.5 %all-to-all-done.2 = bf16[32,32,128]{2,1,0:T(8,128)(2,1)S(1)} async-done(((bf16[32,32,128]{2,1,0:T(8,128)(2,1)}), bf16[32,32,128]{2,1,0:T(8,128)(2,1)S(1)}, u32[]{:S(2)}, u32[]{:S(2)}) %all-to-all-start.2) | async-done | bytes 262176 | tf_op jit(solution)/shard_map/all_to_all | solution.py:88
  112.2 4.8 %fusion.8 = bf16[8,4,128,128]{3,0,2,1:T(8,128)(2,1)S(1)} fusion(f32[8,4,128,128]{3,2,1,0:T(8,128)} %convert.14, f32[4,128,128]{2,1,0:T(8,128)S(1)} %bitcast_convert_fusion, f32[8,4]{0,1:T(4,128)S(1)} %copy.240, f32[8,8,4,1]{1,2,0,3:T(4,128)S(1)} %copy-done.16), kind=kOutput, calls=%fused_computation.14 | convolution fusion | flops 51904512 | bytes 3409024 | tf_op jit(solution)/shard_map/ijh,jhab->ihab/dot_general | solution.py:124
  117.7 3.3 %fusion.9 = bf16[8,4,128,128]{3,0,2,1:T(8,128)(2,1)S(1)} fusion(f32[8,4,128,128]{3,2,1,0:T(8,128)S(1)} %convert.13, f32[4,128,128]{2,1,0:T(8,128)S(1)} %bitcast_convert_fusion.1, f32[8,4]{0,1:T(4,128)S(1)} %copy.232, f32[8,8,4,1]{1,2,0,3:T(4,128)S(1)} %copy-done.15), kind=kOutput, calls=%fused_computation.16 | convolution fusion | flops 51904512 | bytes 3409024 | tf_op jit(solution)/shard_map/ijh,jhab->ihab/dot_general | solution.py:124
  121.3 30.0 %all_to_all.20 = bf16[8,1024,128]{2,1,0:T(8,128)(2,1)S(1)} all-to-all(bf16[8,1024,128]{2,1,0:T(8,128)(2,1)S(1)} %pad_maximum_fusion), channel_id=1, replica_groups=mesh['seq'=32,'exp'=8] {'exp'}, dimensions={0} | all-to-all | bytes 4194304 | tf_op jit(solution)/shard_map/all_to_all | solution.py:205
  153.6 1.9 %fusion.3 = bf16[128,32,128]{2,0,1:T(8,128)(2,1)} fusion(f32[128,32,128]{2,0,1:T(8,128)S(1)} %copy-done.12, bf16[32,128,128]{2,1,0:T(8,128)(2,1)S(1)} %bitcast.168, bf16[128,32,128]{0,2,1:T(8,128)(2,1)S(1)} %bitcast.167, f32[128,32]{0,1:T(8,128)S(1)} %get-tuple-element.83), kind=kOutput, calls=%fused_computation.6 | convolution fusion | flops 135790592 | bytes 5259264 | tf_op jit(solution)/shard_map/sha,hab->shb/dot_general | solution.py:21
  158.7 2.4 %copy.254 = bf16[128,32,128]{0,2,1:T(8,128)(2,1)} copy(bf16[128,32,128]{2,0,1:T(8,128)(2,1)} %fusion.3) | data formatting | bytes 2097152 | tf_op jit(solution)/shard_map/convert_element_type | solution.py:211
  161.2 2.3 %copy.257 = bf16[128,4096]{1,0:T(8,128)(2,1)} copy(bf16[128,4096]{0,1:T(8,128)(2,1)} %bitcast.181) | data formatting | bytes 2097152
  163.4 3.7 %fusion.7 = bf16[128,32,128]{2,0,1:T(8,128)(2,1)} fusion(f32[128,32,128]{2,0,1:T(8,128)S(1)} %copy-done.10, bf16[32,128,128]{2,1,0:T(8,128)(2,1)} %bitcast.175, f32[128,32]{0,1:T(8,128)S(1)} %copy-done.14, bf16[128,4096]{1,0:T(8,128)(2,1)S(1)} %copy-done), kind=kOutput, calls=%fused_computation.12 | convolution fusion | flops 135790592 | bytes 5259264 | tf_op jit(solution)/shard_map/thb,hab->tha/dot_general | solution.py:21
  167.1 1.6 copy.247
  (96 shorter events, 30.0 us)
Async XLA Ops:
  0.6 12.5 %copy-start = (bf16[128,4096]{1,0:T(8,128)(2,1)S(1)}, bf16[128,4096]{1,0:T(8,128)(2,1)}, u32[]{:S(2)}) copy-start(bf16[128,4096]{1,0:T(8,128)(2,1)} %param.14) | copy-start | bytes 3145732
  1.8 12.8 %copy-start.13 = (f32[128,32]{0,1:T(8,128)}, f32[128,32]{0,1:T(8,128)S(1)}, u32[]{:S(2)}) copy-start(f32[128,32]{0,1:T(8,128)S(1)} %get-tuple-element.84) | copy-start | bytes 49156
  3.5 1.0 copy-start.7
  5.8 3.0 %copy-start.3 = (bf16[128,4096]{1,0:T(8,128)(2,1)S(1)}, bf16[128,4096]{1,0:T(8,128)(2,1)}, u32[]{:S(2)}) copy-start(bf16[128,4096]{1,0:T(8,128)(2,1)} %param.13) | copy-start | bytes 3145732
  7.5 20.5 %copy-start.1 = (bf16[128,4096]{0,1:T(8,128)(2,1)}, bf16[128,4096]{0,1:T(8,128)(2,1)S(1)}, u32[]{:S(2)}) copy-start(bf16[128,4096]{0,1:T(8,128)(2,1)S(1)} %copy.210) | copy-start | bytes 3145732
  8.8 2.7 %copy-start.6 = (bf16[128,32,128]{2,0,1:T(8,128)(2,1)S(1)}, bf16[128,32,128]{2,0,1:T(8,128)(2,1)}, u32[]{:S(2)}) copy-start(bf16[128,32,128]{2,0,1:T(8,128)(2,1)} %copy.211) | copy-start | bytes 3145732
  11.5 1.6 copy-start.5
  14.7 1.6 copy-start.17
  17.7 32.1 %all-to-all-start = ((bf16[8,1040,128]{2,1,0:T(8,128)(2,1)}), bf16[8,1040,128]{2,1,0:T(8,128)(2,1)}, u32[]{:S(2)}, u32[]{:S(2)}) async-start(bf16[8,1040,128]{2,1,0:T(8,128)(2,1)} %fusion.1), calls=%async_computation | async-start | bytes 4259840 | tf_op jit(solution)/shard_map/all_to_all | solution.py:185
  22.3 1.2 copy-start.8
  25.8 2.2 %copy-start.9 = (bf16[128,4096]{0,1:T(8,128)(2,1)S(1)}, bf16[128,4096]{0,1:T(8,128)(2,1)}, u32[]{:S(2)}) copy-start(bf16[128,4096]{0,1:T(8,128)(2,1)} %copy-done.7) | copy-start | bytes 3145732
  64.8 26.0 %all-to-all-start.1 = ((bf16[32,48,128]{2,1,0:T(8,128)(2,1)}), bf16[32,48,128]{2,1,0:T(8,128)(2,1)S(1)}, u32[]{:S(2)}, u32[]{:S(2)}) async-start(bf16[32,48,128]{2,1,0:T(8,128)(2,1)} %pad_maximum_fusion.1), calls=%async_computation.1 | async-start | bytes 786432 | tf_op jit(solution)/shard_map/all_to_all | solution.py:65
  94.4 6.1 %copy-start.18 = (f32[8,4]{1,0:T(8,128)S(1)}, f32[8,4]{1,0:T(8,128)}, u32[]{:S(2)}) copy-start(f32[8,4]{1,0:T(8,128)} %get-tuple-element.87) | copy-start | bytes 388
  94.4 6.2 %copy-start.19 = (f32[8,4]{1,0:T(8,128)S(1)}, f32[8,4]{1,0:T(8,128)}, u32[]{:S(2)}) copy-start(f32[8,4]{1,0:T(8,128)} %get-tuple-element.85) | copy-start | bytes 388
  94.4 17.8 %copy-start.16 = (f32[8,8,4,1]{1,2,0,3:T(4,128)S(1)}, f32[8,8,4,1]{1,2,0,3:T(4,128)}, u32[]{:S(2)}) copy-start(f32[8,8,4,1]{1,2,0,3:T(4,128)} %get-tuple-element.90) | copy-start | bytes 3076
  95.8 16.4 %all-to-all-start.2 = ((bf16[32,32,128]{2,1,0:T(8,128)(2,1)}), bf16[32,32,128]{2,1,0:T(8,128)(2,1)S(1)}, u32[]{:S(2)}, u32[]{:S(2)}) async-start(bf16[32,32,128]{2,1,0:T(8,128)(2,1)} %copy.236), calls=%async_computation.2 | async-start | bytes 524288 | tf_op jit(solution)/shard_map/all_to_all | solution.py:88
  117.0 0.7 copy-start.15
  151.3 1.6 copy-start.2
  151.3 2.3 %copy-start.12 = (f32[128,32,128]{2,0,1:T(8,128)S(1)}, f32[128,32,128]{2,0,1:T(8,128)}, u32[]{:S(2)}) copy-start(f32[128,32,128]{2,0,1:T(8,128)} %convolution_bitcast_fusion) | copy-start | bytes 6291460
  153.6 1.9 %copy-start.4 = (bf16[128,4096]{1,0:T(8,128)(2,1)S(1)}, bf16[128,4096]{1,0:T(8,128)(2,1)}, u32[]{:S(2)}) copy-start(bf16[128,4096]{1,0:T(8,128)(2,1)} %param.13) | copy-start | bytes 3145732
  153.6 2.2 %copy-start.11 = (f32[128,32,128]{2,0,1:T(8,128)S(1)}, f32[128,32,128]{2,0,1:T(8,128)}, u32[]{:S(2)}) copy-start(f32[128,32,128]{2,0,1:T(8,128)} %convolution_bitcast_fusion.1) | copy-start | bytes 6291460
  158.7 4.7 %copy-start.10 = (f32[128,32,128]{2,0,1:T(8,128)S(1)}, f32[128,32,128]{2,0,1:T(8,128)}, u32[]{:S(2)}) copy-start(f32[128,32,128]{2,0,1:T(8,128)} %convolution_bitcast_fusion.2) | copy-start | bytes 6291460
  158.7 4.7 %copy-start.14 = (f32[128,32]{0,1:T(8,128)S(1)}, f32[128,32]{0,1:T(8,128)}, u32[]{:S(2)}) copy-start(f32[128,32]{0,1:T(8,128)} %copy-done.13) | copy-start | bytes 49156

commit v6 on v5

--- a/solution.py
+++ b/solution.py
@@ -43,7 +43,7 @@
     return high, mid, low
 
 
-def carried_both(dev_log, dev_state, dev_adjoint, axis):
+def carried_both(dev_log, dev_state, dev_adjoint, axis, riders):
     peers = lax.axis_size(axis)
     here = lax.axis_index(axis)
     heads, width = dev_state.shape[0], dev_state.shape[2]
@@ -63,6 +63,7 @@
         axis=1,
     )
     got = lax.all_to_all(payload, axis, 0, 0, tiled=True)
+    got, riders = lax.optimization_barrier((got, riders))
     head = (here * share) // width
     pick = (lax.broadcasted_iota(jnp.int32, (heads,), 0) == head).astype(jnp.float32)
     log_rows = widen(got[:, 2 * share : 2 * share + 3 * heads, 0]).reshape(peers, 3, heads)
@@ -94,7 +95,7 @@
     )
     start_state = widen(back[:, :share]).reshape(heads, width, width)
     start_adjoint = widen(back[:, share:]).reshape(heads, width, width)
-    return start_state, start_adjoint
+    return start_state, start_adjoint, riders
 
 
 def running_sum(decay_blk):
@@ -192,7 +193,9 @@
     )
     prefix, prefix_log, dev_state, dev_log = within_group(totals, contrib_g, False)
     suffix, suffix_log, dev_adjoint, unused = within_group(totals, update_g, True)
-    start_state, start_adjoint = carried_both(dev_log, dev_state, dev_adjoint, "seq")
+    start_state, start_adjoint, (prefix, suffix) = carried_both(
+        dev_log, dev_state, dev_adjoint, "seq", (prefix, suffix)
+    )
     state_prev = jnp.exp(prefix_log)[:, :, None, None] * start_state[None] + prefix
     adjoint = jnp.exp(suffix_log)[:, :, None, None] * start_adjoint[None] + suffix
     returned = jnp.concatenate(

time: 172 us -> 170 us (0.988)
  waiting for transfers between devices: 44.8 us -> 34.3 us
  matrix products: 39.2 us -> 44.7 us
    all_to_all x1, waiting for transfers between devices: 14.3 us -> 3.85 us  [carried_both(): got = lax.all_to_all(payload, axis, 0, 0, tiled=True)]
    optimization_barrier x0 -> x2, local copies, waits for them, and re-layouts: none -> 2.41 us  [carried_both(): got, riders = lax.optimization_barrier((got, riders))]
    dot_general x2, matrix products: 8.07 us -> 10.4 us  [within_group(): seen = jnp.einsum('ijh,jhab->ihab', weights, pieces, precision=highest)]
    dot_general x11, matrix products: 22.4 us -> 24.5 us  [product(): jnp.einsum(form, first_op, second_op, preferred_element_type=jnp.float32)]
    unnamed x46 -> x41, local copies, waits for them, and re-layouts: 13 us -> 12.2 us
  transfers between devices with their start and end apart: 3 -> 3, of which waited for: 3 -> 3; matrix products, arithmetic and copies ran while one was open for 5% -> 12% of each run, Pallas kernels for 0% -> 0%
where the time goes in v6:
time: 170 us; the launch traced here: 168 us
  matrix products  44.7 us (26%)
  waiting for transfers between devices  34.3 us (20%)
  blocking collectives  30 us (18%)
  local copies, waits for them, and re-layouts  27.9 us (16%)
  starting transfers between devices  21.7 us (13%)
  other arithmetic  8.91 us (5%)
    all_to_all x1, blocking collectives, body(): back = lax.all_to_all(returned, 'exp', 0, 0, tiled=True)  30 us
    dot_general x11, matrix products, product(): jnp.einsum(form, first_op, second_op, preferred_element_type=jnp.float32)  24.5 us
    all_to_all x1, waiting for transfers between devices, body(): got = lax.all_to_all(packed, 'exp', 0, 0, tiled=True)  19.1 us
    unnamed x41, local copies, waits for them, and re-layouts  12.2 us
    all_to_all x1, waiting for transfers between devices, carried_both(): lax.all_to_all(jnp.concatenate([state_rows, adjoint_rows], axis=1).astype...  11.4 us
    all_to_all x1, starting transfers between devices, carried_both(): got = lax.all_to_all(payload, axis, 0, 0, tiled=True)  11.2 us
    dot_general x2, matrix products, within_group(): seen = jnp.einsum('ijh,jhab->ihab', weights, pieces, precision=highest)  10.4 us
    dot_general x2, matrix products, within_group(): jnp.einsum('jh,jhab->hab', jnp.exp(tail_log), pieces, precision=highest)  7.26 us
  transfers between devices with their start and end apart: 3, of which 3 were waited for; matrix products, arithmetic and copies ran while one was open for 12% of the time, Pallas kernels for 0%

profile of v6, /device:TPU:32, one launch (start us, length us, event | category | flops | bytes accessed | tf_op | source)
XLA Modules:
  0.0 168.4 jit_solution(3853674330927180016)
XLA Ops:
  0.7 1.7 %copy.216 = bf16[128,4096]{0,1:T(8,128)(2,1)S(1)} copy(bf16[128,4096]{1,0:T(8,128)(2,1)} %param.11) | data formatting | bytes 2097152 | tf_op args[0]
  5.1 2.4 %add_convert_fusion.2 = bf16[32,128,128]{2,1,0:T(8,128)(2,1)} fusion(f32[32,128,128]{2,1,0:T(8,128)S(1)} %fusion.26, bf16[128,32,128]{2,0,1:T(8,128)(2,1)S(1)} %copy.217, f32[128,32]{0,1:T(8,128)S(1)} %get-tuple-element.88, bf16[128,4096]{1,0:T(8,128)(2,1)S(1)} %copy-done), kind=kOutput, calls=%fused_computation.18 | convolution fusion | flops 138412032 | bytes 5259264 | tf_op jit(solution)/shard_map/tha,thb->hab/dot_general | solution.py:21
  10.5 2.7 %fusion.24 = f32[32,128,128]{2,1,0:T(8,128)S(1)} fusion(bf16[128,32,128]{2,0,1:T(8,128)(2,1)} %copy.211, f32[128,32]{0,1:T(8,128)S(1)} %get-tuple-element.87, bf16[128,4096]{1,0:T(8,128)(2,1)S(1)} %copy-done.3), kind=kOutput, calls=%fused_computation.39 | convolution fusion | flops 135790592 | bytes 4210688 | tf_op jit(solution)/shard_map/sha,shb->hab/dot_general | solution.py:21
  16.3 4.5 %all-to-all-start = ((bf16[8,1040,128]{2,1,0:T(8,128)(2,1)}), bf16[8,1040,128]{2,1,0:T(8,128)(2,1)}, u32[]{:S(2)}, u32[]{:S(2)}) async-start(bf16[8,1040,128]{2,1,0:T(8,128)(2,1)} %fusion.1), calls=%async_computation | async-start | bytes 4259840 | tf_op jit(solution)/shard_map/all_to_all | solution.py:186
  22.0 2.2 %convolution_bitcast_fusion.2 = f32[128,32,128]{2,0,1:T(8,128)} fusion(bf16[32,128,128]{2,1,0:T(8,128)(2,1)S(1)} %multiply_convert_fusion.1, bf16[128,32,128]{0,2,1:T(8,128)(2,1)S(1)} %bitcast.161), kind=kOutput, calls=%fused_computation.38 | convolution fusion | flops 134217728 | bytes 4194304 | tf_op jit(solution)/shard_map/hts,shd->thd/dot_general | solution.py:21
  24.2 2.2 %convolution_bitcast_fusion.1 = f32[128,32,128]{2,0,1:T(8,128)} fusion(bf16[32,128,128]{2,1,0:T(8,128)(2,1)S(1)} %multiply_convert_fusion.1, bf16[128,32,128]{0,2,1:T(8,128)(2,1)S(1)} %bitcast.167), kind=kOutput, calls=%fused_computation.37 | convolution fusion | flops 134217728 | bytes 4194304 | tf_op jit(solution)/shard_map/hts,thd->shd/dot_general | solution.py:21
  26.5 2.8 %convolution_bitcast_fusion = f32[128,32,128]{2,0,1:T(8,128)} fusion(bf16[128,32,128]{0,2,1:T(8,128)(2,1)S(1)} %bitcast.168, bf16[128,32,128]{0,2,1:T(8,128)(2,1)S(1)} %bitcast.162, f32[32,128]{1,0:T(8,128)S(1)} %bitcast.187, pred[128,128]{1,0:T(8,128)(4,1)S(1)} %iota_compare_fusion.5, bf16[128,4096]{1,0:T(8,128)(2,1)S(1)} %copy-done), kind=kOutput, calls=%fused_computation.36 | convolution fusion | flops 271056896 | bytes 5275648 | tf_op jit(solution)/shard_map/hts,thd->shd/dot_general | solution.py:21
  29.3 19.1 %all-to-all-done = bf16[8,1040,128]{2,1,0:T(8,128)(2,1)} async-done(((bf16[8,1040,128]{2,1,0:T(8,128)(2,1)}), bf16[8,1040,128]{2,1,0:T(8,128)(2,1)}, u32[]{:S(2)}, u32[]{:S(2)}) %all-to-all-start) | async-done | bytes 2129952 | tf_op jit(solution)/shard_map/all_to_all | solution.py:186
  54.3 2.8 %fusion.10 = f32[4,1,128,128]{3,1,2,0:T(1,128)S(1)} fusion(f32[8,4,1,1]{0,2,3,1:T(1,128)S(1)} %copy.270, f32[8,4,128,128]{3,2,1,0:T(8,128)S(1)} %convert.14), kind=kOutput, calls=%fused_computation.26 | convolution fusion | flops 6291456 | bytes 2359424 | tf_op jit(solution)/shard_map/jh,jhab->hab/dot_general | solution.py:126
  57.9 4.4 %fusion.14 = f32[4,1,128,128]{3,1,2,0:T(1,128)S(1)} fusion(f32[8,4,1,1]{0,2,3,1:T(1,128)S(1)} %copy.268, f32[8,4,128,128]{3,2,1,0:T(8,128)} %convert.13), kind=kOutput, calls=%fused_computation.30 | convolution fusion | flops 6291456 | bytes 2359424 | tf_op jit(solution)/shard_map/jh,jhab->hab/dot_general | solution.py:126
  63.4 11.2 %all-to-all-start.1 = ((bf16[32,48,128]{2,1,0:T(8,128)(2,1)}), bf16[32,48,128]{2,1,0:T(8,128)(2,1)S(1)}, u32[]{:S(2)}, u32[]{:S(2)}) async-start(bf16[32,48,128]{2,1,0:T(8,128)(2,1)} %pad_maximum_fusion.1), calls=%async_computation.1 | async-start | bytes 786432 | tf_op jit(solution)/shard_map/all_to_all | solution.py:65
  75.0 6.0 %fusion.18 = f32[8,4,128,128]{3,0,2,1:T(8,128)} fusion(f32[8,4,128,128]{3,2,1,0:T(8,128)} %convert.13, f32[8,8,4,1]{1,2,0,3:T(4,128)} %get-tuple-element.94), kind=kOutput, calls=%fused_computation.34 | convolution fusion | flops 50331648 | bytes 4195328 | tf_op jit(solution)/shard_map/ijh,jhab->ihab/dot_general | solution.py:125
  81.1 4.4 %fusion.21 = f32[8,4,128,128]{3,0,2,1:T(8,128)} fusion(f32[8,4,128,128]{3,2,1,0:T(8,128)S(1)} %convert.14, f32[8,8,4,1]{1,2,0,3:T(4,128)S(1)} %copy-done.14), kind=kOutput, calls=%fused_computation.35 | convolution fusion | flops 50331648 | bytes 4195328 | tf_op jit(solution)/shard_map/ijh,jhab->ihab/dot_general | solution.py:125
  85.5 3.8 %all-to-all-done.1 = bf16[32,48,128]{2,1,0:T(8,128)(2,1)S(1)} async-done(((bf16[32,48,128]{2,1,0:T(8,128)(2,1)}), bf16[32,48,128]{2,1,0:T(8,128)(2,1)S(1)}, u32[]{:S(2)}, u32[]{:S(2)}) %all-to-all-start.1) | async-done | bytes 393248 | tf_op jit(solution)/shard_map/all_to_all | solution.py:65
  96.7 5.9 %all-to-all-start.2 = ((bf16[32,32,128]{2,1,0:T(8,128)(2,1)}), bf16[32,32,128]{2,1,0:T(8,128)(2,1)S(1)}, u32[]{:S(2)}, u32[]{:S(2)}) async-start(bf16[32,32,128]{2,1,0:T(8,128)(2,1)} %copy.241), calls=%async_computation.2 | async-start | bytes 524288 | tf_op jit(solution)/shard_map/all_to_all | solution.py:89
  102.8 11.4 %all-to-all-done.2 = bf16[32,32,128]{2,1,0:T(8,128)(2,1)S(1)} async-done(((bf16[32,32,128]{2,1,0:T(8,128)(2,1)}), bf16[32,32,128]{2,1,0:T(8,128)(2,1)S(1)}, u32[]{:S(2)}, u32[]{:S(2)}) %all-to-all-start.2) | async-done | bytes 262176 | tf_op jit(solution)/shard_map/all_to_all | solution.py:89
  116.7 30.0 %all_to_all.20 = bf16[8,1024,128]{2,1,0:T(8,128)(2,1)S(1)} all-to-all(bf16[8,1024,128]{2,1,0:T(8,128)(2,1)S(1)} %pad_maximum_fusion), channel_id=1, replica_groups=mesh['seq'=32,'exp'=8] {'exp'}, dimensions={0} | all-to-all | bytes 4194304 | tf_op jit(solution)/shard_map/all_to_all | solution.py:208
  148.3 1.8 %fusion.7 = bf16[128,32,128]{2,0,1:T(8,128)(2,1)} fusion(f32[128,32,128]{2,0,1:T(8,128)S(1)} %copy-done.8, bf16[32,128,128]{2,1,0:T(8,128)(2,1)S(1)} %bitcast.172, f32[128,32]{0,1:T(8,128)S(1)} %copy-done.13, bf16[128,4096]{1,0:T(8,128)(2,1)S(1)} %copy-done), kind=kOutput, calls=%fused_computation.12 | convolution fusion | flops 135790592 | bytes 5259264 | tf_op jit(solution)/shard_map/thb,hab->tha/dot_general | solution.py:21
  150.1 2.4 %copy.247 = bf16[128,32,128]{0,2,1:T(8,128)(2,1)} copy(bf16[128,32,128]{2,0,1:T(8,128)(2,1)} %fusion.7) | data formatting | bytes 2097152 | tf_op jit(solution)/shard_map/convert_element_type | solution.py:214
  152.5 2.3 %copy.255 = bf16[128,4096]{1,0:T(8,128)(2,1)} copy(bf16[128,4096]{0,1:T(8,128)(2,1)} %bitcast.176) | data formatting | bytes 2097152
  154.7 3.0 %fusion.5 = bf16[128,32,128]{2,0,1:T(8,128)(2,1)} fusion(f32[128,32,128]{2,0,1:T(8,128)} %convolution_bitcast_fusion.1, bf16[32,128,128]{2,1,0:T(8,128)(2,1)S(1)} %bitcast.164, f32[128,32]{0,1:T(8,128)S(1)} %get-tuple-element.87, bf16[128,4096]{1,0:T(8,128)(2,1)S(1)} %copy-done.4), kind=kOutput, calls=%fused_computation.9 | convolution fusion | flops 135790592 | bytes 5259264 | tf_op jit(solution)/shard_map/shb,hab->sha/dot_general | solution.py:21
  157.8 2.4 %copy.250 = bf16[128,32,128]{0,2,1:T(8,128)(2,1)} copy(bf16[128,32,128]{2,0,1:T(8,128)(2,1)} %fusion.5) | data formatting | bytes 2097152 | tf_op jit(solution)/shard_map/convert_element_type | solution.py:214
  160.1 2.3 %copy.256 = bf16[128,4096]{1,0:T(8,128)(2,1)} copy(bf16[128,4096]{0,1:T(8,128)(2,1)} %bitcast.177) | data formatting | bytes 2097152
  162.4 3.1 %fusion.3 = bf16[128,32,128]{2,0,1:T(8,128)(2,1)} fusion(f32[128,32,128]{2,0,1:T(8,128)} %convolution_bitcast_fusion, bf16[32,128,128]{2,1,0:T(8,128)(2,1)S(1)} %bitcast.165, bf16[128,32,128]{0,2,1:T(8,128)(2,1)S(1)} %bitcast.163, f32[128,32]{0,1:T(8,128)S(1)} %get-tuple-element.87), kind=kOutput, calls=%fused_computation.6 | convolution fusion | flops 135790592 | bytes 5259264 | tf_op jit(solution)/shard_map/sha,hab->shb/dot_general | solution.py:21
  (94 shorter events, 32.5 us)
Async XLA Ops:
  0.6 2.9 %copy-start = (bf16[128,4096]{1,0:T(8,128)(2,1)S(1)}, bf16[128,4096]{1,0:T(8,128)(2,1)}, u32[]{:S(2)}) copy-start(bf16[128,4096]{1,0:T(8,128)(2,1)} %param.14) | copy-start | bytes 3145732
  0.6 2.4 %copy-start.15 = (bf16[128,32]{0,1:T(8,128)(2,1)S(1)}, bf16[128,32]{0,1:T(8,128)(2,1)}, u32[]{:S(2)}) copy-start(bf16[128,32]{0,1:T(8,128)(2,1)} %param.15) | copy-start | bytes 24580
  2.4 2.7 %copy-start.6 = (bf16[128,4096]{0,1:T(8,128)(2,1)}, bf16[128,4096]{0,1:T(8,128)(2,1)S(1)}, u32[]{:S(2)}) copy-start(bf16[128,4096]{0,1:T(8,128)(2,1)S(1)} %copy.216) | copy-start | bytes 3145732
  3.5 1.6 copy-start.12
  7.5 3.0 %copy-start.3 = (bf16[128,4096]{1,0:T(8,128)(2,1)S(1)}, bf16[128,4096]{1,0:T(8,128)(2,1)}, u32[]{:S(2)}) copy-start(bf16[128,4096]{1,0:T(8,128)(2,1)} %param.13) | copy-start | bytes 3145732
  9.2 17.3 %copy-start.1 = (bf16[128,4096]{0,1:T(8,128)(2,1)}, bf16[128,4096]{0,1:T(8,128)(2,1)S(1)}, u32[]{:S(2)}) copy-start(bf16[128,4096]{0,1:T(8,128)(2,1)S(1)} %copy.210) | copy-start | bytes 3145732
  10.5 2.7 %copy-start.5 = (bf16[128,32,128]{2,0,1:T(8,128)(2,1)S(1)}, bf16[128,32,128]{2,0,1:T(8,128)(2,1)}, u32[]{:S(2)}) copy-start(bf16[128,32,128]{2,0,1:T(8,128)(2,1)} %copy.211) | copy-start | bytes 3145732
  13.2 1.6 copy-start.11
  16.3 32.1 %all-to-all-start = ((bf16[8,1040,128]{2,1,0:T(8,128)(2,1)}), bf16[8,1040,128]{2,1,0:T(8,128)(2,1)}, u32[]{:S(2)}, u32[]{:S(2)}) async-start(bf16[8,1040,128]{2,1,0:T(8,128)(2,1)} %fusion.1), calls=%async_computation | async-start | bytes 4259840 | tf_op jit(solution)/shard_map/all_to_all | solution.py:186
  22.0 2.2 %copy-start.7 = (bf16[128,4096]{0,1:T(8,128)(2,1)S(1)}, bf16[128,4096]{0,1:T(8,128)(2,1)}, u32[]{:S(2)}) copy-start(bf16[128,4096]{0,1:T(8,128)(2,1)} %copy-done.6) | copy-start | bytes 3145732
  63.4 26.0 %all-to-all-start.1 = ((bf16[32,48,128]{2,1,0:T(8,128)(2,1)}), bf16[32,48,128]{2,1,0:T(8,128)(2,1)S(1)}, u32[]{:S(2)}, u32[]{:S(2)}) async-start(bf16[32,48,128]{2,1,0:T(8,128)(2,1)} %pad_maximum_fusion.1), calls=%async_computation.1 | async-start | bytes 786432 | tf_op jit(solution)/shard_map/all_to_all | solution.py:65
  75.0 6.0 %copy-start.14 = (f32[8,8,4,1]{1,2,0,3:T(4,128)S(1)}, f32[8,8,4,1]{1,2,0,3:T(4,128)}, u32[]{:S(2)}) copy-start(f32[8,8,4,1]{1,2,0,3:T(4,128)} %get-tuple-element.93) | copy-start | bytes 3076
  90.2 24.0 %copy-start.10 = (f32[8,4,128,128]{3,0,2,1:T(8,128)S(1)}, f32[8,4,128,128]{3,0,2,1:T(8,128)}, u32[]{:S(2)}) copy-start(f32[8,4,128,128]{3,0,2,1:T(8,128)} %fusion.21) | copy-start | bytes 6291460
  91.7 10.9 %copy-start.17 = (f32[8,4]{1,0:T(8,128)S(1)}, f32[8,4]{1,0:T(8,128)}, u32[]{:S(2)}) copy-start(f32[8,4]{1,0:T(8,128)} %get-tuple-element.91) | copy-start | bytes 388
  91.7 11.0 %copy-start.16 = (f32[8,4]{1,0:T(8,128)S(1)}, f32[8,4]{1,0:T(8,128)}, u32[]{:S(2)}) copy-start(f32[8,4]{1,0:T(8,128)} %get-tuple-element.89) | copy-start | bytes 388
  96.7 17.5 %all-to-all-start.2 = ((bf16[32,32,128]{2,1,0:T(8,128)(2,1)}), bf16[32,32,128]{2,1,0:T(8,128)(2,1)S(1)}, u32[]{:S(2)}, u32[]{:S(2)}) async-start(bf16[32,32,128]{2,1,0:T(8,128)(2,1)} %copy.241), calls=%async_computation.2 | async-start | bytes 524288 | tf_op jit(solution)/shard_map/all_to_all | solution.py:89
  114.6 1.6 copy-start.9
  146.7 1.6 copy-start.8
  146.7 1.6 copy-start.13
  150.1 4.6 %copy-start.4 = (bf16[128,4096]{1,0:T(8,128)(2,1)S(1)}, bf16[128,4096]{1,0:T(8,128)(2,1)}, u32[]{:S(2)}) copy-start(bf16[128,4096]{1,0:T(8,128)(2,1)} %param.13) | copy-start | bytes 3145732
  157.8 4.6 %copy-start.2 = (bf16[128,4096]{0,1:T(8,128)(2,1)S(1)}, bf16[128,4096]{0,1:T(8,128)(2,1)}, u32[]{:S(2)}) copy-start(bf16[128,4096]{0,1:T(8,128)(2,1)} %copy-done.1) | copy-start | bytes 3145732

commit v7 on v6

--- a/solution.py
+++ b/solution.py
@@ -2,6 +2,7 @@
 import jax.numpy as jnp
 from jax import lax
 from jax.sharding import PartitionSpec as P
+from jax.experimental import pallas as pl
 
 BLOCK = 128
 SEQ_EXP = ("seq", "exp")
@@ -156,10 +157,51 @@
     key_scores = product("thd,shd->hts", query_blk, key_blk)
     first = (weights * grad_scores).astype(jnp.bfloat16)
     second = (weights * key_scores).astype(jnp.bfloat16)
-    query_part = product("hts,shd->thd", first, key_blk)
-    key_part = product("hts,thd->shd", first, query_blk)
-    value_part = product("hts,thd->shd", second, grad_blk)
+    query_part = product("hts,shd->htd", first, key_blk)
+    key_part = product("hts,thd->hsd", first, query_blk)
+    value_part = product("hts,thd->hsd", second, grad_blk)
     return query_part, key_part, value_part
+
+
+def finish_kernel(
+    grad_ref, value_ref, key_ref, state_ref, adjoint_ref, qp_ref, kp_ref, vp_ref, before_ref,
+    after_ref, gq_ref, gk_ref, gv_ref,
+):
+    group, width = state_ref.shape[0], state_ref.shape[2]
+    back = (((1,), (1,)), ((), ()))
+    for i in range(group):
+        cols = slice(i * width, (i + 1) * width)
+        grad = grad_ref[:, cols]
+        value = value_ref[:, cols]
+        key = key_ref[:, cols]
+        state = state_ref[i]
+        adjoint = adjoint_ref[i]
+        with_state = lax.dot_general(grad, state, back, preferred_element_type=jnp.float32)
+        with_adjoint_v = lax.dot_general(value, adjoint, back, preferred_element_type=jnp.float32)
+        with_adjoint_k = jnp.dot(key, adjoint, preferred_element_type=jnp.float32)
+        gq_ref[:, cols] = (qp_ref[i] + before_ref[i] * with_state).astype(gq_ref.dtype)
+        gk_ref[:, cols] = (kp_ref[i] + after_ref[i] * with_adjoint_v).astype(gk_ref.dtype)
+        gv_ref[:, cols] = (vp_ref[i] + after_ref[i] * with_adjoint_k).astype(gv_ref.dtype)
+
+
+def finish_call(out_grad, values, keys, state_in, adjoint_in, qp, kp, vp, before_t, after_t):
+    length, columns = out_grad.shape
+    heads, width = state_in.shape[0], state_in.shape[2]
+    group = 4
+    steps = heads // group
+    flat_spec = pl.BlockSpec((length, group * width), lambda h: (0, h))
+    head_spec = pl.BlockSpec((group, width, width), lambda h: (h, 0, 0))
+    part_spec = pl.BlockSpec((group, length, width), lambda h: (h, 0, 0))
+    scale_spec = pl.BlockSpec((group, length, 1), lambda h: (h, 0, 0))
+    out = jax.ShapeDtypeStruct((length, columns), jnp.bfloat16)
+    return pl.pallas_call(
+        finish_kernel,
+        grid=(steps,),
+        in_specs=[flat_spec, flat_spec, flat_spec, head_spec, head_spec, part_spec, part_spec,
+                  part_spec, scale_spec, scale_spec],
+        out_specs=[flat_spec, flat_spec, flat_spec],
+        out_shape=[out, out, out],
+    )(out_grad, values, keys, state_in, adjoint_in, qp, kp, vp, before_t, after_t)
 
 
 def body(queries, keys, values, out_grad, log_decay):
@@ -208,11 +250,11 @@
     back = lax.all_to_all(returned, "exp", 0, 0, tiled=True)
     state_in = back[:, :share].reshape(heads, width, width)
     adjoint_in = back[:, share:].reshape(heads, width, width)
-    grad_query = query_part + before[..., None] * product("thb,hab->tha", grad_blk, state_in)
-    grad_key = key_part + after[..., None] * product("shb,hab->sha", value_blk, adjoint_in)
-    grad_value = value_part + after[..., None] * product("sha,hab->shb", key_blk, adjoint_in)
-    flat = lambda x: x.astype(jnp.bfloat16).reshape(length, heads * width)
-    return (flat(grad_query), flat(grad_key), flat(grad_value))
+    grad_query, grad_key, grad_value = finish_call(
+        out_grad, values, keys, state_in, adjoint_in, query_part, key_part, value_part,
+        before.T[:, :, None], after.T[:, :, None],
+    )
+    return (grad_query, grad_key, grad_value)
 
 
 def solution(mesh):

time: 170 us -> 151 us (0.89)
  blocking collectives: 30 us -> 0 us
  waiting for transfers between devices: 34.3 us -> 56 us
  matrix products: 44.7 us -> 31.2 us
  local copies, waits for them, and re-layouts: 27.9 us -> 17.1 us
  Pallas kernels: 0 us -> 9.65 us
  starting transfers between devices: 21.7 us -> 24.8 us
    all_to_all x1 -> x0, blocking collectives: 30 us -> none  [body(): back = lax.all_to_all(returned, 'exp', 0, 0, tiled=True)]
    all_to_all x0 -> x1, waiting for transfers between devices: none -> 23 us  [body(): back = lax.all_to_all(returned, 'exp', 0, 0, tiled=True)]
    dot_general x11 -> x8, matrix products: 24.5 us -> 12.1 us  [product(): jnp.einsum(form, first_op, second_op, preferred_element_type=jnp.float32)]
    pallas_call x0 -> x1, Pallas kernels: none -> 9.65 us  [finish_call(): pl.pallas_call(finish_kernel, grid=(steps,), in_specs=[flat_spec, flat_sp...]
    unnamed x41 -> x12, local copies, waits for them, and re-layouts: 12.2 us -> 3.02 us
    convert_element_type x3 -> x0, local copies, waits for them, and re-layouts: 6.32 us -> none  [body(): flat = lambda x: x.astype(jnp.bfloat16).reshape(length, heads * width)]
    broadcast_in_dim x0 -> x2, local copies, waits for them, and re-layouts: none -> 4.05 us  [the longest x1 2.05 us: body(): after.T[:, :, None]]
    all_to_all x0 -> x1, starting transfers between devices: none -> 3.6 us  [body(): back = lax.all_to_all(returned, 'exp', 0, 0, tiled=True)]
  transfers between devices with their start and end apart: 3 -> 4, of which waited for: 3 -> 4; matrix products, arithmetic and copies ran while one was open for 12% -> 17% of each run, Pallas kernels for 0% -> 0%
where the time goes in v7:
time: 151 us; the launch traced here: 149 us
  waiting for transfers between devices  56 us (37%)
  matrix products  31.2 us (21%)
  starting transfers between devices  24.8 us (16%)
  local copies, waits for them, and re-layouts  17.1 us (11%)
  Pallas kernels  9.65 us (6%)
  other arithmetic  8.77 us (6%)
    all_to_all x1, waiting for transfers between devices, body(): back = lax.all_to_all(returned, 'exp', 0, 0, tiled=True)  23 us
    all_to_all x1, waiting for transfers between devices, body(): got = lax.all_to_all(packed, 'exp', 0, 0, tiled=True)  17.4 us
    dot_general x8, matrix products, product(): jnp.einsum(form, first_op, second_op, preferred_element_type=jnp.float32)  12.1 us
    all_to_all x1, waiting for transfers between devices, carried_both(): lax.all_to_all(jnp.concatenate([state_rows, adjoint_rows], axis=1).astype...  11.3 us
    all_to_all x1, starting transfers between devices, carried_both(): got = lax.all_to_all(payload, axis, 0, 0, tiled=True)  11.2 us
    dot_general x2, matrix products, within_group(): seen = jnp.einsum('ijh,jhab->ihab', weights, pieces, precision=highest)  10.5 us
    pallas_call x1, Pallas kernels, finish_call(): pl.pallas_call(finish_kernel, grid=(steps,), in_specs=[flat_spec, flat_sp...  9.65 us
    dot_general x2, matrix products, within_group(): jnp.einsum('jh,jhab->hab', jnp.exp(tail_log), pieces, precision=highest)  7.27 us
  transfers between devices with their start and end apart: 4, of which 4 were waited for; matrix products, arithmetic and copies ran while one was open for 17% of the time, Pallas kernels for 0%

profile of v7, /device:TPU:32, one launch (start us, length us, event | category | flops | bytes accessed | tf_op | source)
XLA Modules:
  0.0 148.7 jit_solution(5856203018743627149)
XLA Ops:
  1.8 1.7 %copy.206 = bf16[128,4096]{0,1:T(8,128)(2,1)S(1)} copy(bf16[128,4096]{1,0:T(8,128)(2,1)} %param.11) | data formatting | bytes 2097152 | tf_op jit(solution)/shard_map/reshape | solution.py:135
  3.5 1.6 %copy.205 = bf16[128,4096]{0,1:T(8,128)(2,1)S(1)} copy(bf16[128,4096]{1,0:T(8,128)(2,1)} %key_ref.1) | data formatting | bytes 2097152 | tf_op jit(solution)/shard_map/reshape | solution.py:136
  10.2 4.5 %all-to-all-start = ((bf16[8,1040,128]{2,1,0:T(8,128)(2,1)}), bf16[8,1040,128]{2,1,0:T(8,128)(2,1)}, u32[]{:S(2)}, u32[]{:S(2)}) async-start(bf16[8,1040,128]{2,1,0:T(8,128)(2,1)} %fusion.1), calls=%async_computation | async-start | bytes 4259840 | tf_op jit(solution)/shard_map/all_to_all | solution.py:228
  14.8 2.9 %multiply_convert_fusion.1 = bf16[32,128,128]{2,1,0:T(8,128)(2,1)S(1)} fusion(f32[32,128]{1,0:T(8,128)S(1)} %bitcast.148, pred[128,128]{1,0:T(8,128)(4,1)S(1)} %iota_compare_fusion.5, bf16[128,4096]{1,0:T(8,128)(2,1)S(1)} %copy-done, bf16[128,4096]{1,0:T(8,128)(2,1)} %value_ref.1), kind=kOutput, calls=%fused_computation.7 | convolution fusion | flops 136839168 | bytes 3178496 | tf_op jit(solution)/shard_map/thd,shd->hts/dot_general | solution.py:22
  17.7 2.2 %fusion.79.qp_ref = f32[32,128,128]{2,1,0:T(8,128)} fusion(bf16[32,128,128]{2,1,0:T(8,128)(2,1)S(1)} %multiply_convert_fusion.1, bf16[128,32,128]{0,2,1:T(8,128)(2,1)S(1)} %bitcast.131), kind=kOutput, calls=%fused_computation.130 | convolution fusion | flops 134217728 | bytes 4194304 | tf_op jit(solution)/shard_map/hts,shd->htd/dot_general | solution.py:22
  20.0 2.2 %fusion.80.kp_ref = f32[32,128,128]{2,1,0:T(8,128)} fusion(bf16[32,128,128]{2,1,0:T(8,128)(2,1)S(1)} %multiply_convert_fusion.1, bf16[128,32,128]{0,2,1:T(8,128)(2,1)S(1)} %bitcast.127), kind=kOutput, calls=%fused_computation.131 | convolution fusion | flops 134217728 | bytes 4194304 | tf_op jit(solution)/shard_map/hts,thd->hsd/dot_general | solution.py:22
  22.1 2.8 %fusion.22.vp_ref = f32[32,128,128]{2,1,0:T(8,128)} fusion(bf16[128,32,128]{0,2,1:T(8,128)(2,1)S(1)} %bitcast.128, bf16[128,32,128]{0,2,1:T(8,128)(2,1)S(1)} %bitcast.132, f32[32,128]{1,0:T(8,128)S(1)} %bitcast.149, pred[128,128]{1,0:T(8,128)(4,1)S(1)} %iota_compare_fusion.5, bf16[128,4096]{1,0:T(8,128)(2,1)S(1)} %copy-done), kind=kOutput, calls=%fused_computation.29 | convolution fusion | flops 271056896 | bytes 5275648 | tf_op jit(solution)/shard_map/hts,thd->hsd/dot_general | solution.py:22
  24.9 17.4 %all-to-all-done = bf16[8,1040,128]{2,1,0:T(8,128)(2,1)} async-done(((bf16[8,1040,128]{2,1,0:T(8,128)(2,1)}), bf16[8,1040,128]{2,1,0:T(8,128)(2,1)}, u32[]{:S(2)}, u32[]{:S(2)}) %all-to-all-start) | async-done | bytes 2129952 | tf_op jit(solution)/shard_map/all_to_all | solution.py:228
  42.3 1.7 %fusion.74 = (bf16[8,512,128]{2,1,0:T(8,128)(2,1)S(1)}, bf16[8,512,128]{2,1,0:T(8,128)(2,1)S(1)}) fusion(bf16[8,1040,128]{2,1,0:T(8,128)(2,1)} %all-to-all-done), kind=kLoop, calls=%fused_computation.125 | loop fusion | bytes 4194304 | tf_op jit(solution)/shard_map/slice | solution.py:230
  44.3 1.6 %convert.14 = f32[8,4,128,128]{3,2,1,0:T(8,128)} convert(bf16[8,4,128,128]{3,2,1,0:T(8,128)(2,1)S(1)} %bitcast.137) | non-fusion elementwise | flops 524288 | bytes 3145728 | tf_op jit(solution)/shard_map/reshape | solution.py:230
  47.3 4.4 %fusion.4 = f32[4,1,128,128]{3,1,2,0:T(1,128)S(1)} fusion(f32[8,4,1,1]{0,2,3,1:T(1,128)S(1)} %copy.197, f32[8,4,128,128]{3,2,1,0:T(8,128)} %convert.14), kind=kOutput, calls=%fused_computation.17 | convolution fusion | flops 6291456 | bytes 2359424 | tf_op jit(solution)/shard_map/jh,jhab->hab/dot_general | solution.py:127
  51.7 2.8 %fusion.8 = f32[4,1,128,128]{3,1,2,0:T(1,128)S(1)} fusion(f32[8,4,1,1]{0,2,3,1:T(1,128)S(1)} %copy.195, f32[8,4,128,128]{3,2,1,0:T(8,128)S(1)} %convert.13), kind=kOutput, calls=%fused_computation.21 | convolution fusion | flops 6291456 | bytes 2359424 | tf_op jit(solution)/shard_map/jh,jhab->hab/dot_general | solution.py:127
  55.6 11.2 %all-to-all-start.1 = ((bf16[32,48,128]{2,1,0:T(8,128)(2,1)}), bf16[32,48,128]{2,1,0:T(8,128)(2,1)S(1)}, u32[]{:S(2)}, u32[]{:S(2)}) async-start(bf16[32,48,128]{2,1,0:T(8,128)(2,1)} %pad_maximum_fusion.1), calls=%async_computation.1 | async-start | bytes 786432 | tf_op jit(solution)/shard_map/all_to_all | solution.py:66
  66.9 6.0 %fusion.15 = f32[8,4,128,128]{3,0,2,1:T(8,128)} fusion(f32[8,4,128,128]{3,2,1,0:T(8,128)} %convert.14, f32[8,8,4,1]{1,2,0,3:T(4,128)S(1)} %get-tuple-element.80), kind=kOutput, calls=%fused_computation.26 | convolution fusion | flops 50331648 | bytes 4195328 | tf_op jit(solution)/shard_map/ijh,jhab->ihab/dot_general | solution.py:126
  72.8 4.5 %fusion.12 = f32[8,4,128,128]{3,0,2,1:T(8,128)} fusion(f32[8,4,128,128]{3,2,1,0:T(8,128)S(1)} %convert.13, f32[8,8,4,1]{1,2,0,3:T(4,128)S(1)} %get-tuple-element.81), kind=kOutput, calls=%fused_computation.25 | convolution fusion | flops 50331648 | bytes 4195328 | tf_op jit(solution)/shard_map/ijh,jhab->ihab/dot_general | solution.py:126
  77.3 4.3 %all-to-all-done.1 = bf16[32,48,128]{2,1,0:T(8,128)(2,1)S(1)} async-done(((bf16[32,48,128]{2,1,0:T(8,128)(2,1)}), bf16[32,48,128]{2,1,0:T(8,128)(2,1)S(1)}, u32[]{:S(2)}, u32[]{:S(2)}) %all-to-all-start.1) | async-done | bytes 393248 | tf_op jit(solution)/shard_map/all_to_all | solution.py:66
  81.7 1.5 %copy.184 = bf16[32,48,128]{0,2,1:T(8,128)(2,1)} copy(bf16[32,48,128]{2,1,0:T(8,128)(2,1)S(1)} %all-to-all-done.1) | data formatting | bytes 786432 | tf_op jit(solution)/shard_map/optimization_barrier | solution.py:67
  85.8 5.5 %all-to-all-start.2 = ((bf16[32,32,128]{2,1,0:T(8,128)(2,1)}), bf16[32,32,128]{2,1,0:T(8,128)(2,1)S(1)}, u32[]{:S(2)}, u32[]{:S(2)}) async-start(bf16[32,32,128]{2,1,0:T(8,128)(2,1)} %copy.187), calls=%async_computation.2 | async-start | bytes 524288 | tf_op jit(solution)/shard_map/all_to_all | solution.py:90
  91.5 11.3 %all-to-all-done.2 = bf16[32,32,128]{2,1,0:T(8,128)(2,1)S(1)} async-done(((bf16[32,32,128]{2,1,0:T(8,128)(2,1)}), bf16[32,32,128]{2,1,0:T(8,128)(2,1)S(1)}, u32[]{:S(2)}, u32[]{:S(2)}) %all-to-all-start.2) | async-done | bytes 262176 | tf_op jit(solution)/shard_map/all_to_all | solution.py:90
  106.7 3.6 %all-to-all-start.3 = ((bf16[8,1024,128]{2,1,0:T(8,128)(2,1)}), bf16[8,1024,128]{2,1,0:T(8,128)(2,1)S(1)}, u32[]{:S(2)}, u32[]{:S(2)}) async-start(bf16[8,1024,128]{2,1,0:T(8,128)(2,1)} %pad_maximum_fusion), calls=%async_computation.3 | async-start | bytes 4194304 | tf_op jit(solution)/shard_map/all_to_all | solution.py:250
  110.4 2.1 %copy.192.after_ref = f32[32,128,1]{2,1,0:T(8,128)} copy(f32[32,128,1]{1,0,2:T(8,128)S(1)} %get-tuple-element.72) | data formatting | bytes 32768 | tf_op jit(solution)/shard_map/broadcast_in_dim | solution.py:255
  112.4 2.0 %copy.191.before_ref = f32[32,128,1]{2,1,0:T(8,128)} copy(f32[32,128,1]{1,0,2:T(8,128)S(1)} %get-tuple-element.73) | data formatting | bytes 32768 | tf_op jit(solution)/shard_map/broadcast_in_dim | solution.py:255
  114.4 23.0 %all-to-all-done.3 = bf16[8,1024,128]{2,1,0:T(8,128)(2,1)S(1)} async-done(((bf16[8,1024,128]{2,1,0:T(8,128)(2,1)}), bf16[8,1024,128]{2,1,0:T(8,128)(2,1)S(1)}, u32[]{:S(2)}, u32[]{:S(2)}) %all-to-all-start.3) | async-done | bytes 2097184 | tf_op jit(solution)/shard_map/all_to_all | solution.py:250
  138.9 9.7 %shard_map.76 = (bf16[128,4096]{1,0:T(8,128)(2,1)}, bf16[128,4096]{1,0:T(8,128)(2,1)}, bf16[128,4096]{1,0:T(8,128)(2,1)}) custom-call(bf16[128,4096]{1,0:T(8,128)(2,1)} %grad_ref.1, bf16[128,4096]{1,0:T(8,128)(2,1)} %value_ref.1, bf16[128,4096]{1,0:T(8,128)(2,1)} %key_ref.1, bf16[32,128,128]{2,1,0:T(8,128)(2,1)} %bitcast.140, ...), custom_call_target="tpu_custom_call" | custom-call | tf_op jit(solution)/shard_map/pallas_call | solution.py:197
  (64 shorter events, 17.0 us)
Async XLA Ops:
  1.7 3.4 %copy-start.1 = (bf16[128,4096]{1,0:T(8,128)(2,1)S(1)}, bf16[128,4096]{1,0:T(8,128)(2,1)}, u32[]{:S(2)}) copy-start(bf16[128,4096]{1,0:T(8,128)(2,1)} %value_ref.1) | copy-start | bytes 3145732
  5.1 1.2 copy-start.2
  6.3 1.2 copy-start
  8.0 0.7 copy-start.5
  10.2 32.1 %all-to-all-start = ((bf16[8,1040,128]{2,1,0:T(8,128)(2,1)}), bf16[8,1040,128]{2,1,0:T(8,128)(2,1)}, u32[]{:S(2)}, u32[]{:S(2)}) async-start(bf16[8,1040,128]{2,1,0:T(8,128)(2,1)} %fusion.1), calls=%async_computation | async-start | bytes 4259840 | tf_op jit(solution)/shard_map/all_to_all | solution.py:228
  55.6 26.0 %all-to-all-start.1 = ((bf16[32,48,128]{2,1,0:T(8,128)(2,1)}), bf16[32,48,128]{2,1,0:T(8,128)(2,1)S(1)}, u32[]{:S(2)}, u32[]{:S(2)}) async-start(bf16[32,48,128]{2,1,0:T(8,128)(2,1)} %pad_maximum_fusion.1), calls=%async_computation.1 | async-start | bytes 786432 | tf_op jit(solution)/shard_map/all_to_all | solution.py:66
  81.7 21.2 %copy-start.4 = (f32[8,4,128,128]{3,0,2,1:T(8,128)S(1)}, f32[8,4,128,128]{3,0,2,1:T(8,128)}, u32[]{:S(2)}) copy-start(f32[8,4,128,128]{3,0,2,1:T(8,128)} %fusion.15) | copy-start | bytes 6291460
  85.8 17.0 %all-to-all-start.2 = ((bf16[32,32,128]{2,1,0:T(8,128)(2,1)}), bf16[32,32,128]{2,1,0:T(8,128)(2,1)S(1)}, u32[]{:S(2)}, u32[]{:S(2)}) async-start(bf16[32,32,128]{2,1,0:T(8,128)(2,1)} %copy.187), calls=%async_computation.2 | async-start | bytes 524288 | tf_op jit(solution)/shard_map/all_to_all | solution.py:90
  103.2 1.6 %copy-start.3 = (f32[8,4,128,128]{3,0,2,1:T(8,128)S(1)}, f32[8,4,128,128]{3,0,2,1:T(8,128)}, u32[]{:S(2)}) copy-start(f32[8,4,128,128]{3,0,2,1:T(8,128)} %fusion.12) | copy-start | bytes 6291460
  106.7 30.7 %all-to-all-start.3 = ((bf16[8,1024,128]{2,1,0:T(8,128)(2,1)}), bf16[8,1024,128]{2,1,0:T(8,128)(2,1)S(1)}, u32[]{:S(2)}, u32[]{:S(2)}) async-start(bf16[8,1024,128]{2,1,0:T(8,128)(2,1)} %pad_maximum_fusion), calls=%async_computation.3 | async-start | bytes 4194304 | tf_op jit(solution)/shard_map/all_to_all | solution.py:250

commit v8 on v7

--- a/solution.py
+++ b/solution.py
@@ -88,14 +88,10 @@
         "di,irc->drc", w_bwd, widen(got[:, share : 2 * share]), precision=highest
     )
     back = lax.all_to_all(
-        jnp.concatenate([state_rows, adjoint_rows], axis=1).astype(jnp.bfloat16),
-        axis,
-        0,
-        0,
-        tiled=True,
-    )
-    start_state = widen(back[:, :share]).reshape(heads, width, width)
-    start_adjoint = widen(back[:, share:]).reshape(heads, width, width)
+        jnp.concatenate([state_rows, adjoint_rows], axis=1), axis, 0, 0, tiled=True
+    )
+    start_state = back[:, :share].reshape(heads, width, width)
+    start_adjoint = back[:, share:].reshape(heads, width, width)
     return start_state, start_adjoint, riders
 
 

time: 151 us -> 154 us (1.020)
  waiting for transfers between devices: 56 us -> 61.4 us
    all_to_all x1, waiting for transfers between devices: 11.3 us -> 16.7 us  [carried_both(): lax.all_to_all(jnp.concatenate([state_rows, adjoint_rows], axis=1), axis,...]
  transfers between devices with their start and end apart: 4 -> 4, of which waited for: 4 -> 4; matrix products, arithmetic and copies ran while one was open for 17% -> 16% of each run, Pallas kernels for 0% -> 0%
where the time goes in v8:
time: 154 us; the launch traced here: 153 us
  waiting for transfers between devices  61.4 us (40%)
  matrix products  31.2 us (20%)
  starting transfers between devices  24.8 us (16%)
  local copies, waits for them, and re-layouts  16.5 us (11%)
  Pallas kernels  9.65 us (6%)
  other arithmetic  8.01 us (5%)
    all_to_all x1, waiting for transfers between devices, body(): back = lax.all_to_all(returned, 'exp', 0, 0, tiled=True)  23 us
    all_to_all x1, waiting for transfers between devices, body(): got = lax.all_to_all(packed, 'exp', 0, 0, tiled=True)  17.4 us
    all_to_all x1, waiting for transfers between devices, carried_both(): lax.all_to_all(jnp.concatenate([state_rows, adjoint_rows], axis=1), axis,...  16.7 us
    dot_general x8, matrix products, product(): jnp.einsum(form, first_op, second_op, preferred_element_type=jnp.float32)  12.1 us
    all_to_all x1, starting transfers between devices, carried_both(): got = lax.all_to_all(payload, axis, 0, 0, tiled=True)  11.2 us
    dot_general x2, matrix products, within_group(): seen = jnp.einsum('ijh,jhab->ihab', weights, pieces, precision=highest)  10.5 us
    pallas_call x1, Pallas kernels, finish_call(): pl.pallas_call(finish_kernel, grid=(steps,), in_specs=[flat_spec, flat_sp...  9.65 us
    dot_general x2, matrix products, within_group(): jnp.einsum('jh,jhab->hab', jnp.exp(tail_log), pieces, precision=highest)  7.27 us
  transfers between devices with their start and end apart: 4, of which 4 were waited for; matrix products, arithmetic and copies ran while one was open for 16% of the time, Pallas kernels for 0%

profile of v8, /device:TPU:32, one launch (start us, length us, event | category | flops | bytes accessed | tf_op | source)
XLA Modules:
  0.0 152.6 jit_solution(6085453432119165303)
XLA Ops:
  1.8 1.7 %copy.206 = bf16[128,4096]{0,1:T(8,128)(2,1)S(1)} copy(bf16[128,4096]{1,0:T(8,128)(2,1)} %param.11) | data formatting | bytes 2097152 | tf_op jit(solution)/shard_map/reshape | solution.py:131
  3.5 1.6 %copy.205 = bf16[128,4096]{0,1:T(8,128)(2,1)S(1)} copy(bf16[128,4096]{1,0:T(8,128)(2,1)} %key_ref.1) | data formatting | bytes 2097152 | tf_op jit(solution)/shard_map/reshape | solution.py:132
  8.7 1.5 fusion.1
  10.2 4.5 %all-to-all-start = ((bf16[8,1040,128]{2,1,0:T(8,128)(2,1)}), bf16[8,1040,128]{2,1,0:T(8,128)(2,1)}, u32[]{:S(2)}, u32[]{:S(2)}) async-start(bf16[8,1040,128]{2,1,0:T(8,128)(2,1)} %fusion.1), calls=%async_computation | async-start | bytes 4259840 | tf_op jit(solution)/shard_map/all_to_all | solution.py:224
  14.8 2.9 %multiply_convert_fusion.1 = bf16[32,128,128]{2,1,0:T(8,128)(2,1)S(1)} fusion(f32[32,128]{1,0:T(8,128)S(1)} %bitcast.142, pred[128,128]{1,0:T(8,128)(4,1)S(1)} %iota_compare_fusion.5, bf16[128,4096]{1,0:T(8,128)(2,1)S(1)} %copy-done, bf16[128,4096]{1,0:T(8,128)(2,1)} %value_ref.1), kind=kOutput, calls=%fused_computation.7 | convolution fusion | flops 136839168 | bytes 3178496 | tf_op jit(solution)/shard_map/thd,shd->hts/dot_general | solution.py:22
  17.7 2.2 %fusion.81.qp_ref = f32[32,128,128]{2,1,0:T(8,128)} fusion(bf16[32,128,128]{2,1,0:T(8,128)(2,1)S(1)} %multiply_convert_fusion.1, bf16[128,32,128]{0,2,1:T(8,128)(2,1)S(1)} %bitcast.125), kind=kOutput, calls=%fused_computation.128 | convolution fusion | flops 134217728 | bytes 4194304 | tf_op jit(solution)/shard_map/hts,shd->htd/dot_general | solution.py:22
  20.0 2.2 %fusion.82.kp_ref = f32[32,128,128]{2,1,0:T(8,128)} fusion(bf16[32,128,128]{2,1,0:T(8,128)(2,1)S(1)} %multiply_convert_fusion.1, bf16[128,32,128]{0,2,1:T(8,128)(2,1)S(1)} %bitcast.121), kind=kOutput, calls=%fused_computation.129 | convolution fusion | flops 134217728 | bytes 4194304 | tf_op jit(solution)/shard_map/hts,thd->hsd/dot_general | solution.py:22
  22.1 2.8 %fusion.22.vp_ref = f32[32,128,128]{2,1,0:T(8,128)} fusion(bf16[128,32,128]{0,2,1:T(8,128)(2,1)S(1)} %bitcast.122, bf16[128,32,128]{0,2,1:T(8,128)(2,1)S(1)} %bitcast.126, f32[32,128]{1,0:T(8,128)S(1)} %bitcast.143, pred[128,128]{1,0:T(8,128)(4,1)S(1)} %iota_compare_fusion.5, bf16[128,4096]{1,0:T(8,128)(2,1)S(1)} %copy-done), kind=kOutput, calls=%fused_computation.29 | convolution fusion | flops 271056896 | bytes 5275648 | tf_op jit(solution)/shard_map/hts,thd->hsd/dot_general | solution.py:22
  24.9 17.4 %all-to-all-done = bf16[8,1040,128]{2,1,0:T(8,128)(2,1)} async-done(((bf16[8,1040,128]{2,1,0:T(8,128)(2,1)}), bf16[8,1040,128]{2,1,0:T(8,128)(2,1)}, u32[]{:S(2)}, u32[]{:S(2)}) %all-to-all-start) | async-done | bytes 2129952 | tf_op jit(solution)/shard_map/all_to_all | solution.py:224
  42.3 1.7 %fusion.76 = (bf16[8,512,128]{2,1,0:T(8,128)(2,1)S(1)}, bf16[8,512,128]{2,1,0:T(8,128)(2,1)S(1)}) fusion(bf16[8,1040,128]{2,1,0:T(8,128)(2,1)} %all-to-all-done), kind=kLoop, calls=%fused_computation.123 | loop fusion | bytes 4194304 | tf_op jit(solution)/shard_map/slice | solution.py:226
  44.3 1.6 %convert.4 = f32[8,4,128,128]{3,2,1,0:T(8,128)} convert(bf16[8,4,128,128]{3,2,1,0:T(8,128)(2,1)S(1)} %bitcast.131) | non-fusion elementwise | flops 524288 | bytes 3145728 | tf_op jit(solution)/shard_map/reshape | solution.py:226
  47.3 4.4 %fusion.4 = f32[4,1,128,128]{3,1,2,0:T(1,128)S(1)} fusion(f32[8,4,1,1]{0,2,3,1:T(1,128)S(1)} %copy.197, f32[8,4,128,128]{3,2,1,0:T(8,128)} %convert.4), kind=kOutput, calls=%fused_computation.17 | convolution fusion | flops 6291456 | bytes 2359424 | tf_op jit(solution)/shard_map/jh,jhab->hab/dot_general | solution.py:123
  51.7 2.8 %fusion.8 = f32[4,1,128,128]{3,1,2,0:T(1,128)S(1)} fusion(f32[8,4,1,1]{0,2,3,1:T(1,128)S(1)} %copy.195, f32[8,4,128,128]{3,2,1,0:T(8,128)S(1)} %convert.3), kind=kOutput, calls=%fused_computation.21 | convolution fusion | flops 6291456 | bytes 2359424 | tf_op jit(solution)/shard_map/jh,jhab->hab/dot_general | solution.py:123
  55.6 11.2 %all-to-all-start.1 = ((bf16[32,48,128]{2,1,0:T(8,128)(2,1)}), bf16[32,48,128]{2,1,0:T(8,128)(2,1)S(1)}, u32[]{:S(2)}, u32[]{:S(2)}) async-start(bf16[32,48,128]{2,1,0:T(8,128)(2,1)} %pad_maximum_fusion.2), calls=%async_computation.1 | async-start | bytes 786432 | tf_op jit(solution)/shard_map/all_to_all | solution.py:66
  66.9 6.0 %fusion.15 = f32[8,4,128,128]{3,0,2,1:T(8,128)} fusion(f32[8,4,128,128]{3,2,1,0:T(8,128)} %convert.4, f32[8,8,4,1]{1,2,0,3:T(4,128)S(1)} %get-tuple-element.80), kind=kOutput, calls=%fused_computation.26 | convolution fusion | flops 50331648 | bytes 4195328 | tf_op jit(solution)/shard_map/ijh,jhab->ihab/dot_general | solution.py:122
  72.8 4.5 %fusion.12 = f32[8,4,128,128]{3,0,2,1:T(8,128)} fusion(f32[8,4,128,128]{3,2,1,0:T(8,128)S(1)} %convert.3, f32[8,8,4,1]{1,2,0,3:T(4,128)S(1)} %get-tuple-element.81), kind=kOutput, calls=%fused_computation.25 | convolution fusion | flops 50331648 | bytes 4195328 | tf_op jit(solution)/shard_map/ijh,jhab->ihab/dot_general | solution.py:122
  77.3 4.3 %all-to-all-done.1 = bf16[32,48,128]{2,1,0:T(8,128)(2,1)S(1)} async-done(((bf16[32,48,128]{2,1,0:T(8,128)(2,1)}), bf16[32,48,128]{2,1,0:T(8,128)(2,1)S(1)}, u32[]{:S(2)}, u32[]{:S(2)}) %all-to-all-start.1) | async-done | bytes 393248 | tf_op jit(solution)/shard_map/all_to_all | solution.py:66
  84.8 5.5 %all-to-all-start.2 = ((f32[32,32,128]{2,1,0:T(8,128)}), f32[32,32,128]{2,1,0:T(8,128)S(1)}, u32[]{:S(2)}, u32[]{:S(2)}) async-start(f32[32,32,128]{2,1,0:T(8,128)} %copy.187), calls=%async_computation.2 | async-start | bytes 1048576 | tf_op jit(solution)/shard_map/all_to_all | solution.py:90
  90.4 16.7 %all-to-all-done.2 = f32[32,32,128]{2,1,0:T(8,128)S(1)} async-done(((f32[32,32,128]{2,1,0:T(8,128)}), f32[32,32,128]{2,1,0:T(8,128)S(1)}, u32[]{:S(2)}, u32[]{:S(2)}) %all-to-all-start.2) | async-done | bytes 524320 | tf_op jit(solution)/shard_map/all_to_all | solution.py:90
  110.7 3.6 %all-to-all-start.3 = ((bf16[8,1024,128]{2,1,0:T(8,128)(2,1)}), bf16[8,1024,128]{2,1,0:T(8,128)(2,1)S(1)}, u32[]{:S(2)}, u32[]{:S(2)}) async-start(bf16[8,1024,128]{2,1,0:T(8,128)(2,1)} %pad_maximum_fusion), calls=%async_computation.3 | async-start | bytes 4194304 | tf_op jit(solution)/shard_map/all_to_all | solution.py:246
  114.3 2.1 %copy.192.after_ref = f32[32,128,1]{2,1,0:T(8,128)} copy(f32[32,128,1]{1,0,2:T(8,128)S(1)} %get-tuple-element.72) | data formatting | bytes 32768 | tf_op jit(solution)/shard_map/broadcast_in_dim | solution.py:251
  116.4 2.0 %copy.191.before_ref = f32[32,128,1]{2,1,0:T(8,128)} copy(f32[32,128,1]{1,0,2:T(8,128)S(1)} %get-tuple-element.73) | data formatting | bytes 32768 | tf_op jit(solution)/shard_map/broadcast_in_dim | solution.py:251
  118.4 23.0 %all-to-all-done.3 = bf16[8,1024,128]{2,1,0:T(8,128)(2,1)S(1)} async-done(((bf16[8,1024,128]{2,1,0:T(8,128)(2,1)}), bf16[8,1024,128]{2,1,0:T(8,128)(2,1)S(1)}, u32[]{:S(2)}, u32[]{:S(2)}) %all-to-all-start.3) | async-done | bytes 2097184 | tf_op jit(solution)/shard_map/all_to_all | solution.py:246
  142.8 9.6 %shard_map.76 = (bf16[128,4096]{1,0:T(8,128)(2,1)}, bf16[128,4096]{1,0:T(8,128)(2,1)}, bf16[128,4096]{1,0:T(8,128)(2,1)}) custom-call(bf16[128,4096]{1,0:T(8,128)(2,1)} %grad_ref.1, bf16[128,4096]{1,0:T(8,128)(2,1)} %value_ref.1, bf16[128,4096]{1,0:T(8,128)(2,1)} %key_ref.1, bf16[32,128,128]{2,1,0:T(8,128)(2,1)} %bitcast.134, ...), custom_call_target="tpu_custom_call" | custom-call | tf_op jit(solution)/shard_map/pallas_call | solution.py:193
  (62 shorter events, 15.6 us)
Async XLA Ops:
  1.7 3.4 %copy-start.1 = (bf16[128,4096]{1,0:T(8,128)(2,1)S(1)}, bf16[128,4096]{1,0:T(8,128)(2,1)}, u32[]{:S(2)}) copy-start(bf16[128,4096]{1,0:T(8,128)(2,1)} %value_ref.1) | copy-start | bytes 3145732
  5.1 1.2 copy-start.2
  6.3 1.2 copy-start
  8.0 0.7 copy-start.5
  10.2 32.1 %all-to-all-start = ((bf16[8,1040,128]{2,1,0:T(8,128)(2,1)}), bf16[8,1040,128]{2,1,0:T(8,128)(2,1)}, u32[]{:S(2)}, u32[]{:S(2)}) async-start(bf16[8,1040,128]{2,1,0:T(8,128)(2,1)} %fusion.1), calls=%async_computation | async-start | bytes 4259840 | tf_op jit(solution)/shard_map/all_to_all | solution.py:224
  55.6 26.0 %all-to-all-start.1 = ((bf16[32,48,128]{2,1,0:T(8,128)(2,1)}), bf16[32,48,128]{2,1,0:T(8,128)(2,1)S(1)}, u32[]{:S(2)}, u32[]{:S(2)}) async-start(bf16[32,48,128]{2,1,0:T(8,128)(2,1)} %pad_maximum_fusion.2), calls=%async_computation.1 | async-start | bytes 786432 | tf_op jit(solution)/shard_map/all_to_all | solution.py:66
  83.6 23.6 %copy-start.4 = (f32[8,4,128,128]{3,0,2,1:T(8,128)S(1)}, f32[8,4,128,128]{3,0,2,1:T(8,128)}, u32[]{:S(2)}) copy-start(f32[8,4,128,128]{3,0,2,1:T(8,128)} %fusion.12) | copy-start | bytes 6291460
  84.8 22.4 %all-to-all-start.2 = ((f32[32,32,128]{2,1,0:T(8,128)}), f32[32,32,128]{2,1,0:T(8,128)S(1)}, u32[]{:S(2)}, u32[]{:S(2)}) async-start(f32[32,32,128]{2,1,0:T(8,128)} %copy.187), calls=%async_computation.2 | async-start | bytes 1048576 | tf_op jit(solution)/shard_map/all_to_all | solution.py:90
  107.2 1.6 %copy-start.3 = (f32[8,4,128,128]{3,0,2,1:T(8,128)S(1)}, f32[8,4,128,128]{3,0,2,1:T(8,128)}, u32[]{:S(2)}) copy-start(f32[8,4,128,128]{3,0,2,1:T(8,128)} %fusion.15) | copy-start | bytes 6291460
  110.7 30.7 %all-to-all-start.3 = ((bf16[8,1024,128]{2,1,0:T(8,128)(2,1)}), bf16[8,1024,128]{2,1,0:T(8,128)(2,1)S(1)}, u32[]{:S(2)}, u32[]{:S(2)}) async-start(bf16[8,1024,128]{2,1,0:T(8,128)(2,1)} %pad_maximum_fusion), calls=%async_computation.3 | async-start | bytes 4194304 | tf_op jit(solution)/shard_map/all_to_all | solution.py:246

commit v9 on v8

--- a/solution.py
+++ b/solution.py
@@ -136,9 +136,7 @@
     total = cumul[-1]
     after = jnp.exp(total[None, :] - cumul)
     before = jnp.exp(cumul)
-    contrib = split_left("sha,shb->hab", after[..., None] * widen(key_blk), value_blk)
-    update = split_left("tha,thb->hab", before[..., None] * widen(query_blk), grad_blk)
-    return (query_blk, key_blk, value_blk, grad_blk, cumul, after, before, contrib, update)
+    return (query_blk, key_blk, value_blk, grad_blk, cumul, after, before)
 
 
 def intra(query_blk, key_blk, value_blk, grad_blk, cumul):
@@ -157,6 +155,48 @@
     key_part = product("hts,thd->hsd", first, query_blk)
     value_part = product("hts,thd->hsd", second, grad_blk)
     return query_part, key_part, value_part
+
+
+def contrib_kernel(key_ref, value_ref, query_ref, grad_ref, after_ref, before_ref, out_ref):
+    width = out_ref.shape[2]
+    group = out_ref.shape[1] // (2 * width)
+    step = pl.program_id(0)
+    lanes = lax.broadcasted_iota(jnp.int32, after_ref.shape, 1)
+    after_all = after_ref[...]
+    before_all = before_ref[...]
+    for i in range(group):
+        head = step * group + i
+        cols = slice(i * width, (i + 1) * width)
+        after = jnp.sum(jnp.where(lanes == head, after_all, 0.0), axis=1, keepdims=True)
+        before = jnp.sum(jnp.where(lanes == head, before_all, 0.0), axis=1, keepdims=True)
+        for slot, scale, left_ref, right_ref in (
+            (i, after, key_ref, value_ref),
+            (group + i, before, query_ref, grad_ref),
+        ):
+            scaled = (scale * left_ref[:, cols].astype(jnp.float32)).T
+            high = scaled.astype(jnp.bfloat16)
+            low = (scaled - high.astype(jnp.float32)).astype(jnp.bfloat16)
+            right = right_ref[:, cols]
+            total = jnp.dot(high, right, preferred_element_type=jnp.float32) + jnp.dot(
+                low, right, preferred_element_type=jnp.float32
+            )
+            out_ref[0, slot * width : (slot + 1) * width, :] = total.astype(out_ref.dtype)
+
+
+def contrib_call(keys, values, queries, out_grad, after, before, peers):
+    length, columns = keys.shape
+    heads = after.shape[1]
+    width = columns // heads
+    group = heads // peers
+    flat_spec = pl.BlockSpec((length, group * width), lambda t: (0, t))
+    scale_spec = pl.BlockSpec((length, heads), lambda t: (0, 0))
+    return pl.pallas_call(
+        contrib_kernel,
+        grid=(peers,),
+        in_specs=[flat_spec, flat_spec, flat_spec, flat_spec, scale_spec, scale_spec],
+        out_specs=pl.BlockSpec((1, 2 * group * width, width), lambda t: (t, 0, 0)),
+        out_shape=jax.ShapeDtypeStruct((peers, 2 * group * width, width), jnp.bfloat16),
+    )(keys, values, queries, out_grad, after, before)
 
 
 def finish_kernel(
@@ -206,21 +246,15 @@
     heads = log_decay.shape[1]
     width = queries.shape[1] // heads
     group = heads // peers
-    (query_blk, key_blk, value_blk, grad_blk, cumul, after, before, contrib, update) = local_block(
+    (query_blk, key_blk, value_blk, grad_blk, cumul, after, before) = local_block(
         queries, keys, values, out_grad, log_decay
     )
     share = group * width
     decay_rows = jnp.transpose(log_decay.reshape(length, peers, group), (1, 2, 0))
     pad_rows = 16
     decay_rows = jnp.pad(decay_rows, ((0, 0), (0, pad_rows - group), (0, 0)))
-    packed = jnp.concatenate(
-        [
-            contrib.astype(jnp.bfloat16).reshape(peers, share, width),
-            update.astype(jnp.bfloat16).reshape(peers, share, width),
-            decay_rows.astype(jnp.bfloat16),
-        ],
-        axis=1,
-    )
+    both = contrib_call(keys, values, queries, out_grad, after, before, peers)
+    packed = jnp.concatenate([both, decay_rows.astype(jnp.bfloat16)], axis=1)
     got = lax.all_to_all(packed, "exp", 0, 0, tiled=True)
     contrib_g = widen(got[:, :share]).reshape(peers, group, width, width)
     update_g = widen(got[:, share : 2 * share]).reshape(peers, group, width, width)

time: 154 us -> 158 us (1.026)
  Pallas kernels: 9.65 us -> 17.8 us
  matrix products: 31.2 us -> 26.5 us
  local copies, waits for them, and re-layouts: 16.5 us -> 12.5 us
  waiting for transfers between devices: 61.4 us -> 64 us
  other arithmetic: 8.01 us -> 10.2 us
    pallas_call x0 -> x1, Pallas kernels: none -> 8.17 us  [contrib_call(): pl.pallas_call(contrib_kernel, grid=(peers,), in_specs=[flat_spec, flat_s...]
    dot_general x8 -> x4, matrix products: 12.1 us -> 7.4 us  [product(): jnp.einsum(form, first_op, second_op, preferred_element_type=jnp.float32)]
    reshape x2 -> x0, local copies, waits for them, and re-layouts: 3.32 us -> none  [the longest x1 1.7 us: local_block(): query_blk = queries.reshape(length, heads, width)]
    all_to_all x1, waiting for transfers between devices: 17.4 us -> 20.1 us  [body(): got = lax.all_to_all(packed, 'exp', 0, 0, tiled=True)]
    concatenate x1, other arithmetic: 1.51 us -> 3.1 us  [body(): packed = jnp.concatenate([both, decay_rows.astype(jnp.bfloat16)], axis=1)]
  transfers between devices with their start and end apart: 4 -> 4, of which waited for: 4 -> 4; matrix products, arithmetic and copies ran while one was open for 16% -> 14% of each run, Pallas kernels for 0% -> 0%
where the time goes in v9:
time: 158 us; the launch traced here: 157 us
  waiting for transfers between devices  64 us (41%)
  matrix products  26.5 us (17%)
  starting transfers between devices  24.9 us (16%)
  Pallas kernels  17.8 us (11%)
  local copies, waits for them, and re-layouts  12.5 us (8%)
  other arithmetic  10.2 us (6%)
    all_to_all x1, waiting for transfers between devices, body(): back = lax.all_to_all(returned, 'exp', 0, 0, tiled=True)  23 us
    all_to_all x1, waiting for transfers between devices, body(): got = lax.all_to_all(packed, 'exp', 0, 0, tiled=True)  20.1 us
    all_to_all x1, waiting for transfers between devices, carried_both(): lax.all_to_all(jnp.concatenate([state_rows, adjoint_rows], axis=1), axis,...  16.7 us
    all_to_all x1, starting transfers between devices, carried_both(): got = lax.all_to_all(payload, axis, 0, 0, tiled=True)  11.2 us
    dot_general x2, matrix products, within_group(): seen = jnp.einsum('ijh,jhab->ihab', weights, pieces, precision=highest)  10.5 us
    pallas_call x1, Pallas kernels, finish_call(): pl.pallas_call(finish_kernel, grid=(steps,), in_specs=[flat_spec, flat_sp...  9.65 us
    pallas_call x1, Pallas kernels, contrib_call(): pl.pallas_call(contrib_kernel, grid=(peers,), in_specs=[flat_spec, flat_s...  8.17 us
    dot_general x4, matrix products, product(): jnp.einsum(form, first_op, second_op, preferred_element_type=jnp.float32)  7.4 us
  transfers between devices with their start and end apart: 4, of which 4 were waited for; matrix products, arithmetic and copies ran while one was open for 14% of the time, Pallas kernels for 0%

profile of v9, /device:TPU:32, one launch (start us, length us, event | category | flops | bytes accessed | tf_op | source)
XLA Modules:
  0.0 156.9 jit_solution(2351355657445671939)
XLA Ops:
  3.2 8.2 %shard_map.76 = bf16[8,1024,128]{2,1,0:T(8,128)(2,1)} custom-call(bf16[128,4096]{1,0:T(8,128)(2,1)} %key_ref.3, bf16[128,4096]{1,0:T(8,128)(2,1)} %value_ref.3, bf16[128,4096]{1,0:T(8,128)(2,1)} %query_ref.1, bf16[128,4096]{1,0:T(8,128)(2,1)} %grad_ref.3, f32[128,32]{1,0:T(8,128)} %subtract_exponential_fusion.after_ref, f32[128,32]{1,0:T(8,128)} %copy.140.before_ref), custom_call_target="tpu_custom_call" | custom-call | tf_op jit(solution)/shard_map/pallas_call | solution.py:193
  11.3 3.1 %fusion.1 = bf16[8,1040,128]{2,1,0:T(8,128)(2,1)} fusion(bf16[8,4,128]{2,1,0:T(4,128)(2,1)S(1)} %bitcast.134, bf16[8,1024,128]{2,1,0:T(8,128)(2,1)} %shard_map.76), kind=kLoop, calls=%fused_computation.2 | loop fusion | flops 6389760 | bytes 4235264 | tf_op jit(solution)/shard_map/concatenate | solution.py:257
  14.4 4.6 %all-to-all-start = ((bf16[8,1040,128]{2,1,0:T(8,128)(2,1)}), bf16[8,1040,128]{2,1,0:T(8,128)(2,1)}, u32[]{:S(2)}, u32[]{:S(2)}) async-start(bf16[8,1040,128]{2,1,0:T(8,128)(2,1)} %fusion.1), calls=%async_computation | async-start | bytes 4259840 | tf_op jit(solution)/shard_map/all_to_all | solution.py:258
  20.3 1.8 %fusion.19.kp_ref = f32[32,128,128]{2,1,0:T(8,128)} fusion(bf16[32,128,128]{2,1,0:T(8,128)(2,1)S(1)} %multiply_convert_fusion.1, bf16[128,4096]{1,0:T(8,128)(2,1)S(1)} %copy-done.3), kind=kOutput, calls=%fused_computation.21 | convolution fusion | flops 134217728 | bytes 4194304 | tf_op jit(solution)/shard_map/hts,thd->hsd/dot_general | solution.py:22
  22.2 1.8 %fusion.23.qp_ref = f32[32,128,128]{2,1,0:T(8,128)} fusion(bf16[32,128,128]{2,1,0:T(8,128)(2,1)S(1)} %multiply_convert_fusion.1, bf16[128,4096]{1,0:T(8,128)(2,1)S(1)} %copy-done), kind=kOutput, calls=%fused_computation.24 | convolution fusion | flops 134217728 | bytes 4194304 | tf_op jit(solution)/shard_map/hts,shd->htd/dot_general | solution.py:22
  24.0 2.7 %fusion.16.vp_ref = f32[32,128,128]{2,1,0:T(8,128)} fusion(f32[32,128]{1,0:T(8,128)S(1)} %bitcast.133, pred[128,128]{1,0:T(8,128)(4,1)S(1)} %iota_compare_fusion.5, bf16[128,4096]{1,0:T(8,128)(2,1)S(1)} %copy-done.3, bf16[128,4096]{1,0:T(8,128)(2,1)S(1)} %copy-done, bf16[128,4096]{1,0:T(8,128)(2,1)S(1)} %copy-done.4), kind=kOutput, calls=%fused_computation.19 | convolution fusion | flops 271056896 | bytes 5275648 | tf_op jit(solution)/shard_map/hts,thd->hsd/dot_general | solution.py:22
  26.6 20.1 %all-to-all-done = bf16[8,1040,128]{2,1,0:T(8,128)(2,1)} async-done(((bf16[8,1040,128]{2,1,0:T(8,128)(2,1)}), bf16[8,1040,128]{2,1,0:T(8,128)(2,1)}, u32[]{:S(2)}, u32[]{:S(2)}) %all-to-all-start) | async-done | bytes 2129952 | tf_op jit(solution)/shard_map/all_to_all | solution.py:258
  46.7 1.7 %fusion.72 = (bf16[8,512,128]{2,1,0:T(8,128)(2,1)S(1)}, bf16[8,512,128]{2,1,0:T(8,128)(2,1)S(1)}) fusion(bf16[8,1040,128]{2,1,0:T(8,128)(2,1)} %all-to-all-done), kind=kLoop, calls=%fused_computation.111 | loop fusion | bytes 4194304 | tf_op jit(solution)/shard_map/slice | solution.py:260
  48.6 1.6 %convert.4 = f32[8,4,128,128]{3,2,1,0:T(8,128)} convert(bf16[8,4,128,128]{3,2,1,0:T(8,128)(2,1)S(1)} %bitcast.121) | non-fusion elementwise | flops 524288 | bytes 3145728 | tf_op jit(solution)/shard_map/reshape | solution.py:260
  51.6 4.4 %fusion.2 = f32[4,1,128,128]{3,1,2,0:T(1,128)S(1)} fusion(f32[8,4,1,1]{0,2,3,1:T(1,128)S(1)} %copy.170, f32[8,4,128,128]{3,2,1,0:T(8,128)} %convert.4), kind=kOutput, calls=%fused_computation.9 | convolution fusion | flops 6291456 | bytes 2359424 | tf_op jit(solution)/shard_map/jh,jhab->hab/dot_general | solution.py:123
  56.1 2.8 %fusion.6 = f32[4,1,128,128]{3,1,2,0:T(1,128)S(1)} fusion(f32[8,4,1,1]{0,2,3,1:T(1,128)S(1)} %copy.168, f32[8,4,128,128]{3,2,1,0:T(8,128)S(1)} %convert.3), kind=kOutput, calls=%fused_computation.13 | convolution fusion | flops 6291456 | bytes 2359424 | tf_op jit(solution)/shard_map/jh,jhab->hab/dot_general | solution.py:123
  60.0 11.2 %all-to-all-start.1 = ((bf16[32,48,128]{2,1,0:T(8,128)(2,1)}), bf16[32,48,128]{2,1,0:T(8,128)(2,1)S(1)}, u32[]{:S(2)}, u32[]{:S(2)}) async-start(bf16[32,48,128]{2,1,0:T(8,128)(2,1)} %pad_maximum_fusion.2), calls=%async_computation.1 | async-start | bytes 786432 | tf_op jit(solution)/shard_map/all_to_all | solution.py:66
  71.2 6.0 %fusion.13 = f32[8,4,128,128]{3,0,2,1:T(8,128)} fusion(f32[8,4,128,128]{3,2,1,0:T(8,128)} %convert.4, f32[8,8,4,1]{1,2,0,3:T(4,128)S(1)} %get-tuple-element.78), kind=kOutput, calls=%fused_computation.18 | convolution fusion | flops 50331648 | bytes 4195328 | tf_op jit(solution)/shard_map/ijh,jhab->ihab/dot_general | solution.py:122
  77.2 4.5 %fusion.10 = f32[8,4,128,128]{3,0,2,1:T(8,128)} fusion(f32[8,4,128,128]{3,2,1,0:T(8,128)S(1)} %convert.3, f32[8,8,4,1]{1,2,0,3:T(4,128)S(1)} %get-tuple-element.79), kind=kOutput, calls=%fused_computation.17 | convolution fusion | flops 50331648 | bytes 4195328 | tf_op jit(solution)/shard_map/ijh,jhab->ihab/dot_general | solution.py:122
  81.7 4.3 %all-to-all-done.1 = bf16[32,48,128]{2,1,0:T(8,128)(2,1)S(1)} async-done(((bf16[32,48,128]{2,1,0:T(8,128)(2,1)}), bf16[32,48,128]{2,1,0:T(8,128)(2,1)S(1)}, u32[]{:S(2)}, u32[]{:S(2)}) %all-to-all-start.1) | async-done | bytes 393248 | tf_op jit(solution)/shard_map/all_to_all | solution.py:66
  89.1 5.5 %all-to-all-start.2 = ((f32[32,32,128]{2,1,0:T(8,128)}), f32[32,32,128]{2,1,0:T(8,128)S(1)}, u32[]{:S(2)}, u32[]{:S(2)}) async-start(f32[32,32,128]{2,1,0:T(8,128)} %copy.160), calls=%async_computation.2 | async-start | bytes 1048576 | tf_op jit(solution)/shard_map/all_to_all | solution.py:90
  94.8 16.7 %all-to-all-done.2 = f32[32,32,128]{2,1,0:T(8,128)S(1)} async-done(((f32[32,32,128]{2,1,0:T(8,128)}), f32[32,32,128]{2,1,0:T(8,128)S(1)}, u32[]{:S(2)}, u32[]{:S(2)}) %all-to-all-start.2) | async-done | bytes 524320 | tf_op jit(solution)/shard_map/all_to_all | solution.py:90
  113.5 1.4 pad_maximum_fusion
  115.0 3.6 %all-to-all-start.3 = ((bf16[8,1024,128]{2,1,0:T(8,128)(2,1)}), bf16[8,1024,128]{2,1,0:T(8,128)(2,1)S(1)}, u32[]{:S(2)}, u32[]{:S(2)}) async-start(bf16[8,1024,128]{2,1,0:T(8,128)(2,1)} %pad_maximum_fusion), calls=%async_computation.3 | async-start | bytes 4194304 | tf_op jit(solution)/shard_map/all_to_all | solution.py:280
  118.7 2.1 %copy.165.after_ref = f32[32,128,1]{2,1,0:T(8,128)} copy(f32[32,128,1]{1,0,2:T(8,128)S(1)} %get-tuple-element.72) | data formatting | bytes 32768 | tf_op jit(solution)/shard_map/broadcast_in_dim | solution.py:285
  120.7 2.0 %copy.164.before_ref = f32[32,128,1]{2,1,0:T(8,128)} copy(f32[32,128,1]{1,0,2:T(8,128)S(1)} %get-tuple-element.73) | data formatting | bytes 32768 | tf_op jit(solution)/shard_map/broadcast_in_dim | solution.py:285
  122.7 23.0 %all-to-all-done.3 = bf16[8,1024,128]{2,1,0:T(8,128)(2,1)S(1)} async-done(((bf16[8,1024,128]{2,1,0:T(8,128)(2,1)}), bf16[8,1024,128]{2,1,0:T(8,128)(2,1)S(1)}, u32[]{:S(2)}, u32[]{:S(2)}) %all-to-all-start.3) | async-done | bytes 2097184 | tf_op jit(solution)/shard_map/all_to_all | solution.py:280
  145.7 1.4 fusion.73
  147.2 9.6 %shard_map.77 = (bf16[128,4096]{1,0:T(8,128)(2,1)}, bf16[128,4096]{1,0:T(8,128)(2,1)}, bf16[128,4096]{1,0:T(8,128)(2,1)}) custom-call(bf16[128,4096]{1,0:T(8,128)(2,1)} %grad_ref.3, bf16[128,4096]{1,0:T(8,128)(2,1)} %value_ref.3, bf16[128,4096]{1,0:T(8,128)(2,1)} %key_ref.3, bf16[32,128,128]{2,1,0:T(8,128)(2,1)} %bitcast.124, ...), custom_call_target="tpu_custom_call" | custom-call | tf_op jit(solution)/shard_map/pallas_call | solution.py:233
  (61 shorter events, 11.8 us)
Async XLA Ops:
  3.2 8.2 %copy-start.6 = (bf16[128,32]{0,1:T(8,128)(2,1)S(1)}, bf16[128,32]{0,1:T(8,128)(2,1)}, u32[]{:S(2)}) copy-start(bf16[128,32]{0,1:T(8,128)(2,1)} %param.15) | copy-start | bytes 24580
  14.4 4.7 %copy-start.4 = (bf16[128,4096]{1,0:T(8,128)(2,1)S(1)}, bf16[128,4096]{1,0:T(8,128)(2,1)}, u32[]{:S(2)}) copy-start(bf16[128,4096]{1,0:T(8,128)(2,1)} %grad_ref.3) | copy-start | bytes 3145732
  14.4 4.7 %copy-start.5 = (bf16[128,4096]{1,0:T(8,128)(2,1)S(1)}, bf16[128,4096]{1,0:T(8,128)(2,1)}, u32[]{:S(2)}) copy-start(bf16[128,4096]{1,0:T(8,128)(2,1)} %value_ref.3) | copy-start | bytes 3145732
  14.4 32.3 %all-to-all-start = ((bf16[8,1040,128]{2,1,0:T(8,128)(2,1)}), bf16[8,1040,128]{2,1,0:T(8,128)(2,1)}, u32[]{:S(2)}, u32[]{:S(2)}) async-start(bf16[8,1040,128]{2,1,0:T(8,128)(2,1)} %fusion.1), calls=%async_computation | async-start | bytes 4259840 | tf_op jit(solution)/shard_map/all_to_all | solution.py:258
  19.1 1.2 copy-start.3
  20.3 1.8 %copy-start = (bf16[128,4096]{1,0:T(8,128)(2,1)S(1)}, bf16[128,4096]{1,0:T(8,128)(2,1)}, u32[]{:S(2)}) copy-start(bf16[128,4096]{1,0:T(8,128)(2,1)} %key_ref.3) | copy-start | bytes 3145732
  60.0 26.0 %all-to-all-start.1 = ((bf16[32,48,128]{2,1,0:T(8,128)(2,1)}), bf16[32,48,128]{2,1,0:T(8,128)(2,1)S(1)}, u32[]{:S(2)}, u32[]{:S(2)}) async-start(bf16[32,48,128]{2,1,0:T(8,128)(2,1)} %pad_maximum_fusion.2), calls=%async_computation.1 | async-start | bytes 786432 | tf_op jit(solution)/shard_map/all_to_all | solution.py:66
  87.9 23.5 %copy-start.2 = (f32[8,4,128,128]{3,0,2,1:T(8,128)S(1)}, f32[8,4,128,128]{3,0,2,1:T(8,128)}, u32[]{:S(2)}) copy-start(f32[8,4,128,128]{3,0,2,1:T(8,128)} %fusion.10) | copy-start | bytes 6291460
  89.1 22.3 %all-to-all-start.2 = ((f32[32,32,128]{2,1,0:T(8,128)}), f32[32,32,128]{2,1,0:T(8,128)S(1)}, u32[]{:S(2)}, u32[]{:S(2)}) async-start(f32[32,32,128]{2,1,0:T(8,128)} %copy.160), calls=%async_computation.2 | async-start | bytes 1048576 | tf_op jit(solution)/shard_map/all_to_all | solution.py:90
  111.5 1.6 %copy-start.1 = (f32[8,4,128,128]{3,0,2,1:T(8,128)S(1)}, f32[8,4,128,128]{3,0,2,1:T(8,128)}, u32[]{:S(2)}) copy-start(f32[8,4,128,128]{3,0,2,1:T(8,128)} %fusion.13) | copy-start | bytes 6291460
  115.0 30.7 %all-to-all-start.3 = ((bf16[8,1024,128]{2,1,0:T(8,128)(2,1)}), bf16[8,1024,128]{2,1,0:T(8,128)(2,1)S(1)}, u32[]{:S(2)}, u32[]{:S(2)}) async-start(bf16[8,1024,128]{2,1,0:T(8,128)(2,1)} %pad_maximum_fusion), calls=%async_computation.3 | async-start | bytes 4194304 | tf_op jit(solution)/shard_map/all_to_all | solution.py:280

commit v10 on v8

--- a/solution.py
+++ b/solution.py
@@ -82,11 +82,8 @@
     src2 = lax.broadcasted_iota(jnp.int32, (peers, peers), 1)
     w_fwd = jnp.where(src2 < dst2, jnp.exp(jnp.where(src2 < dst2, log_fwd, 0.0)), 0.0)
     w_bwd = jnp.where(src2 > dst2, jnp.exp(jnp.where(src2 > dst2, log_bwd, 0.0)), 0.0)
-    highest = lax.Precision.HIGHEST
-    state_rows = jnp.einsum("di,irc->drc", w_fwd, widen(got[:, :share]), precision=highest)
-    adjoint_rows = jnp.einsum(
-        "di,irc->drc", w_bwd, widen(got[:, share : 2 * share]), precision=highest
-    )
+    state_rows = split_left("di,irc->drc", w_fwd, got[:, :share])
+    adjoint_rows = split_left("di,irc->drc", w_bwd, got[:, share : 2 * share])
     back = lax.all_to_all(
         jnp.concatenate([state_rows, adjoint_rows], axis=1), axis, 0, 0, tiled=True
     )
@@ -118,9 +115,8 @@
     weights = jnp.where(earlier[..., None], jnp.exp(jnp.where(earlier[..., None], logs, 0.0)), 0.0)
     seen_log = jnp.sum(jnp.where(earlier[..., None], totals[None], 0.0), axis=1)
     tail_log = jnp.sum(jnp.where(later[..., None], totals[None], 0.0), axis=1)
-    highest = lax.Precision.HIGHEST
-    seen = jnp.einsum("ijh,jhab->ihab", weights, pieces, precision=highest)
-    whole = jnp.einsum("jh,jhab->hab", jnp.exp(tail_log), pieces, precision=highest)
+    seen = split_left("ijh,jhab->ihab", weights, pieces)
+    whole = split_left("jh,jhab->hab", jnp.exp(tail_log), pieces)
     return seen, seen_log, whole, jnp.sum(totals, axis=0)
 
 
@@ -222,8 +218,8 @@
         axis=1,
     )
     got = lax.all_to_all(packed, "exp", 0, 0, tiled=True)
-    contrib_g = widen(got[:, :share]).reshape(peers, group, width, width)
-    update_g = widen(got[:, share : 2 * share]).reshape(peers, group, width, width)
+    contrib_g = got[:, :share].reshape(peers, group, width, width)
+    update_g = got[:, share : 2 * share].reshape(peers, group, width, width)
     totals = jnp.sum(widen(got[:, 2 * share : 2 * share + group]), axis=2)
     query_part, key_part, value_part = intra(query_blk, key_blk, value_blk, grad_blk, cumul)
     totals, contrib_g, update_g, query_part, key_part, value_part = lax.optimization_barrier(

time: 154 us -> 151 us (0.981)
  matrix products: 31.2 us -> 20.8 us
  waiting for transfers between devices: 61.4 us -> 67.2 us
    dot_general x6 -> x0, matrix products: 18.2 us -> none  [the longest x2 10.5 us: within_group(): seen = jnp.einsum('ijh,jhab->ihab', weights, pieces, precision=highest)]
    dot_general x8 -> x20, matrix products: 12.1 us -> 20 us  [product(): jnp.einsum(form, first_op, second_op, preferred_element_type=jnp.float32)]
    all_to_all x1, waiting for transfers between devices: 4.3 us -> 10.5 us  [carried_both(): got = lax.all_to_all(payload, axis, 0, 0, tiled=True)]
    reshape x2 -> x0, other arithmetic: 1.84 us -> none  [the longest x1 1.61 us: body(): widen(got[:, share:2 * share]).reshape(peers, group, width, width)]
  transfers between devices with their start and end apart: 4 -> 4, of which waited for: 4 -> 4; matrix products, arithmetic and copies ran while one was open for 16% -> 13% of each run, Pallas kernels for 0% -> 0%
where the time goes in v10:
time: 151 us; the launch traced here: 150 us
  waiting for transfers between devices  67.2 us (45%)
  starting transfers between devices  24.1 us (16%)
  matrix products  20.8 us (14%)
  local copies, waits for them, and re-layouts  17.4 us (12%)
  Pallas kernels  9.65 us (6%)
  other arithmetic  9.2 us (6%)
    all_to_all x1, waiting for transfers between devices, body(): back = lax.all_to_all(returned, 'exp', 0, 0, tiled=True)  23 us
    dot_general x20, matrix products, product(): jnp.einsum(form, first_op, second_op, preferred_element_type=jnp.float32)  20 us
    all_to_all x1, waiting for transfers between devices, body(): got = lax.all_to_all(packed, 'exp', 0, 0, tiled=True)  16.9 us
    all_to_all x1, waiting for transfers between devices, carried_both(): lax.all_to_all(jnp.concatenate([state_rows, adjoint_rows], axis=1), axis,...  16.8 us
    all_to_all x1, starting transfers between devices, carried_both(): got = lax.all_to_all(payload, axis, 0, 0, tiled=True)  11.2 us
    all_to_all x1, waiting for transfers between devices, carried_both(): got = lax.all_to_all(payload, axis, 0, 0, tiled=True)  10.5 us
    pallas_call x1, Pallas kernels, finish_call(): pl.pallas_call(finish_kernel, grid=(steps,), in_specs=[flat_spec, flat_sp...  9.65 us
    all_to_all x1, starting transfers between devices, carried_both(): lax.all_to_all(jnp.concatenate([state_rows, adjoint_rows], axis=1), axis,...  4.69 us
  transfers between devices with their start and end apart: 4, of which 4 were waited for; matrix products, arithmetic and copies ran while one was open for 13% of the time, Pallas kernels for 0%

profile of v10, /device:TPU:32, one launch (start us, length us, event | category | flops | bytes accessed | tf_op | source)
XLA Modules:
  0.0 149.5 jit_solution(15278790611754386447)
XLA Ops:
  1.8 1.7 %copy.230 = bf16[128,4096]{0,1:T(8,128)(2,1)S(1)} copy(bf16[128,4096]{1,0:T(8,128)(2,1)} %param.11) | data formatting | bytes 2097152 | tf_op jit(solution)/shard_map/reshape | solution.py:127
  3.5 1.6 %copy.229 = bf16[128,4096]{0,1:T(8,128)(2,1)S(1)} copy(bf16[128,4096]{1,0:T(8,128)(2,1)} %key_ref.1) | data formatting | bytes 2097152 | tf_op jit(solution)/shard_map/reshape | solution.py:128
  8.7 1.5 %fusion.1 = bf16[8,1040,128]{2,1,0:T(8,128)(2,1)} fusion(bf16[8,4,128]{2,1,0:T(4,128)(2,1)S(1)} %bitcast.170, bf16[8,512,128]{2,1,0:T(8,128)(2,1)S(1)} %bitcast.156, bf16[8,512,128]{2,1,0:T(8,128)(2,1)S(1)} %bitcast.155), kind=kLoop, calls=%fused_computation.2 | loop fusion | flops 8519680 | bytes 4235264 | tf_op jit(solution)/shard_map/concatenate | solution.py:212
  10.2 4.5 %all-to-all-start = ((bf16[8,1040,128]{2,1,0:T(8,128)(2,1)}), bf16[8,1040,128]{2,1,0:T(8,128)(2,1)}, u32[]{:S(2)}, u32[]{:S(2)}) async-start(bf16[8,1040,128]{2,1,0:T(8,128)(2,1)} %fusion.1), calls=%async_computation | async-start | bytes 4259840 | tf_op jit(solution)/shard_map/all_to_all | solution.py:220
  15.3 2.9 %multiply_convert_fusion.1 = bf16[32,128,128]{2,1,0:T(8,128)(2,1)S(1)} fusion(f32[32,128]{1,0:T(8,128)S(1)} %bitcast.168, pred[128,128]{1,0:T(8,128)(4,1)S(1)} %iota_compare_fusion.5, bf16[128,4096]{1,0:T(8,128)(2,1)S(1)} %copy-done, bf16[128,4096]{1,0:T(8,128)(2,1)} %value_ref.1), kind=kOutput, calls=%fused_computation.9 | convolution fusion | flops 136839168 | bytes 3178496 | tf_op jit(solution)/shard_map/thd,shd->hts/dot_general | solution.py:22
  18.2 2.2 %fusion.95.qp_ref = f32[32,128,128]{2,1,0:T(8,128)} fusion(bf16[32,128,128]{2,1,0:T(8,128)(2,1)S(1)} %multiply_convert_fusion.1, bf16[128,32,128]{0,2,1:T(8,128)(2,1)S(1)} %bitcast.151), kind=kOutput, calls=%fused_computation.158 | convolution fusion | flops 134217728 | bytes 4194304 | tf_op jit(solution)/shard_map/hts,shd->htd/dot_general | solution.py:22
  20.4 2.2 %fusion.96.kp_ref = f32[32,128,128]{2,1,0:T(8,128)} fusion(bf16[32,128,128]{2,1,0:T(8,128)(2,1)S(1)} %multiply_convert_fusion.1, bf16[128,32,128]{0,2,1:T(8,128)(2,1)S(1)} %bitcast.147), kind=kOutput, calls=%fused_computation.159 | convolution fusion | flops 134217728 | bytes 4194304 | tf_op jit(solution)/shard_map/hts,thd->hsd/dot_general | solution.py:22
  22.6 2.8 %fusion.8.vp_ref = f32[32,128,128]{2,1,0:T(8,128)} fusion(bf16[128,32,128]{0,2,1:T(8,128)(2,1)S(1)} %bitcast.148, bf16[128,32,128]{0,2,1:T(8,128)(2,1)S(1)} %bitcast.152, f32[32,128]{1,0:T(8,128)S(1)} %bitcast.169, pred[128,128]{1,0:T(8,128)(4,1)S(1)} %iota_compare_fusion.5, bf16[128,4096]{1,0:T(8,128)(2,1)S(1)} %copy-done), kind=kOutput, calls=%fused_computation.21 | convolution fusion | flops 271056896 | bytes 5275648 | tf_op jit(solution)/shard_map/hts,thd->hsd/dot_general | solution.py:22
  25.4 16.9 %all-to-all-done = bf16[8,1040,128]{2,1,0:T(8,128)(2,1)} async-done(((bf16[8,1040,128]{2,1,0:T(8,128)(2,1)}), bf16[8,1040,128]{2,1,0:T(8,128)(2,1)}, u32[]{:S(2)}, u32[]{:S(2)}) %all-to-all-start) | async-done | bytes 2129952 | tf_op jit(solution)/shard_map/all_to_all | solution.py:220
  43.1 1.7 %fusion.90 = (bf16[8,512,128]{2,1,0:T(8,128)(2,1)S(1)}, bf16[8,512,128]{2,1,0:T(8,128)(2,1)S(1)}) fusion(bf16[8,1040,128]{2,1,0:T(8,128)(2,1)} %all-to-all-done), kind=kLoop, calls=%fused_computation.153 | loop fusion | bytes 4194304 | tf_op jit(solution)/shard_map/slice | solution.py:222
  51.5 11.2 %all-to-all-start.1 = ((bf16[32,48,128]{2,1,0:T(8,128)(2,1)}), bf16[32,48,128]{2,1,0:T(8,128)(2,1)S(1)}, u32[]{:S(2)}, u32[]{:S(2)}) async-start(bf16[32,48,128]{2,1,0:T(8,128)(2,1)} %pad_maximum_fusion.2), calls=%async_computation.1 | async-start | bytes 786432 | tf_op jit(solution)/shard_map/all_to_all | solution.py:66
  64.1 2.1 %add_bitcast_fusion = f32[8,4,128,128]{3,0,2,1:T(8,128)} fusion(f32[4,128,128,8]{2,3,1,0:T(8,128)S(1)} %fusion.36, bf16[8,4,128,128]{3,2,1,0:T(8,128)(2,1)S(1)} %bitcast.144, bf16[8,8,4,1]{1,2,0,3:T(4,128)(2,1)S(1)} %get-tuple-element.72), kind=kOutput, calls=%fused_computation.6 | convolution fusion | flops 8912896 | bytes 5243392 | tf_op jit(solution)/shard_map/ijh,jhab->ihab/dot_general | solution.py:22
  67.0 10.5 %all-to-all-done.1 = bf16[32,48,128]{2,1,0:T(8,128)(2,1)S(1)} async-done(((bf16[32,48,128]{2,1,0:T(8,128)(2,1)}), bf16[32,48,128]{2,1,0:T(8,128)(2,1)S(1)}, u32[]{:S(2)}, u32[]{:S(2)}) %all-to-all-start.1) | async-done | bytes 393248 | tf_op jit(solution)/shard_map/all_to_all | solution.py:66
  77.5 1.6 %copy.198 = bf16[32,48,128]{0,2,1:T(8,128)(2,1)} copy(bf16[32,48,128]{2,1,0:T(8,128)(2,1)S(1)} %all-to-all-done.1) | data formatting | bytes 786432 | tf_op jit(solution)/shard_map/optimization_barrier | solution.py:67
  82.2 4.7 %all-to-all-start.2 = ((f32[32,32,128]{2,1,0:T(8,128)}), f32[32,32,128]{2,1,0:T(8,128)S(1)}, u32[]{:S(2)}, u32[]{:S(2)}) async-start(f32[32,32,128]{2,1,0:T(8,128)} %copy.201), calls=%async_computation.2 | async-start | bytes 1048576 | tf_op jit(solution)/shard_map/all_to_all | solution.py:87
  87.0 16.8 %all-to-all-done.2 = f32[32,32,128]{2,1,0:T(8,128)S(1)} async-done(((f32[32,32,128]{2,1,0:T(8,128)}), f32[32,32,128]{2,1,0:T(8,128)S(1)}, u32[]{:S(2)}, u32[]{:S(2)}) %all-to-all-start.2) | async-done | bytes 524320 | tf_op jit(solution)/shard_map/all_to_all | solution.py:87
  104.4 1.1 copy-done.3
  106.0 1.4 pad_maximum_fusion
  107.4 3.7 %all-to-all-start.3 = ((bf16[8,1024,128]{2,1,0:T(8,128)(2,1)}), bf16[8,1024,128]{2,1,0:T(8,128)(2,1)S(1)}, u32[]{:S(2)}, u32[]{:S(2)}) async-start(bf16[8,1024,128]{2,1,0:T(8,128)(2,1)} %pad_maximum_fusion), calls=%async_computation.3 | async-start | bytes 4194304 | tf_op jit(solution)/shard_map/all_to_all | solution.py:242
  111.2 2.1 %copy.206.after_ref = f32[32,128,1]{2,1,0:T(8,128)} copy(f32[32,128,1]{1,0,2:T(8,128)S(1)} %get-tuple-element.76) | data formatting | bytes 32768 | tf_op jit(solution)/shard_map/broadcast_in_dim | solution.py:247
  113.3 2.0 %copy.205.before_ref = f32[32,128,1]{2,1,0:T(8,128)} copy(f32[32,128,1]{1,0,2:T(8,128)S(1)} %get-tuple-element.77) | data formatting | bytes 32768 | tf_op jit(solution)/shard_map/broadcast_in_dim | solution.py:247
  115.3 23.0 %all-to-all-done.3 = bf16[8,1024,128]{2,1,0:T(8,128)(2,1)S(1)} async-done(((bf16[8,1024,128]{2,1,0:T(8,128)(2,1)}), bf16[8,1024,128]{2,1,0:T(8,128)(2,1)S(1)}, u32[]{:S(2)}, u32[]{:S(2)}) %all-to-all-start.3) | async-done | bytes 2097184 | tf_op jit(solution)/shard_map/all_to_all | solution.py:242
  138.3 1.4 fusion.91
  139.7 9.7 %shard_map.76 = (bf16[128,4096]{1,0:T(8,128)(2,1)}, bf16[128,4096]{1,0:T(8,128)(2,1)}, bf16[128,4096]{1,0:T(8,128)(2,1)}) custom-call(bf16[128,4096]{1,0:T(8,128)(2,1)} %grad_ref.1, bf16[128,4096]{1,0:T(8,128)(2,1)} %value_ref.1, bf16[128,4096]{1,0:T(8,128)(2,1)} %key_ref.1, bf16[32,128,128]{2,1,0:T(8,128)(2,1)} %bitcast.158, ...), custom_call_target="tpu_custom_call" | custom-call | tf_op jit(solution)/shard_map/pallas_call | solution.py:189
  (78 shorter events, 19.1 us)
Async XLA Ops:
  1.7 3.4 %copy-start.8 = (f32[32]{0:T(128)}, f32[32]{0:T(128)S(1)}, u32[]{:S(2)}) copy-start(f32[32]{0:T(128)S(1)} %slice_reduce_fusion) | copy-start | bytes 388
  1.7 3.4 %copy-start.1 = (bf16[128,4096]{1,0:T(8,128)(2,1)S(1)}, bf16[128,4096]{1,0:T(8,128)(2,1)}, u32[]{:S(2)}) copy-start(bf16[128,4096]{1,0:T(8,128)(2,1)} %value_ref.1) | copy-start | bytes 3145732
  5.1 1.2 copy-start.2
  6.3 1.2 copy-start
  8.0 0.7 copy-start.4
  10.2 32.1 %all-to-all-start = ((bf16[8,1040,128]{2,1,0:T(8,128)(2,1)}), bf16[8,1040,128]{2,1,0:T(8,128)(2,1)}, u32[]{:S(2)}, u32[]{:S(2)}) async-start(bf16[8,1040,128]{2,1,0:T(8,128)(2,1)} %fusion.1), calls=%async_computation | async-start | bytes 4259840 | tf_op jit(solution)/shard_map/all_to_all | solution.py:220
  51.5 26.0 %all-to-all-start.1 = ((bf16[32,48,128]{2,1,0:T(8,128)(2,1)}), bf16[32,48,128]{2,1,0:T(8,128)(2,1)S(1)}, u32[]{:S(2)}, u32[]{:S(2)}) async-start(bf16[32,48,128]{2,1,0:T(8,128)(2,1)} %pad_maximum_fusion.2), calls=%async_computation.1 | async-start | bytes 786432 | tf_op jit(solution)/shard_map/all_to_all | solution.py:66
  64.1 2.1 %copy-start.5 = (bf16[8,8,4,1]{1,2,0,3:T(4,128)(2,1)S(1)}, bf16[8,8,4,1]{1,2,0,3:T(4,128)(2,1)}, u32[]{:S(2)}) copy-start(bf16[8,8,4,1]{1,2,0,3:T(4,128)(2,1)} %get-tuple-element.89) | copy-start | bytes 1540
  67.0 12.9 %copy-start.10 = (f32[4]{0:T(128)S(1)}, f32[4]{0:T(128)}, u32[]{:S(2)}) copy-start(f32[4]{0:T(128)} %compare_convert_fusion) | copy-start | bytes 52
  80.7 6.2 %copy-start.6 = (f32[8,4]{1,0:T(8,128)S(1)}, f32[8,4]{1,0:T(8,128)}, u32[]{:S(2)}) copy-start(f32[8,4]{1,0:T(8,128)} %get-tuple-element.80) | copy-start | bytes 388
  80.7 6.3 %copy-start.7 = (f32[8,4]{1,0:T(8,128)S(1)}, f32[8,4]{1,0:T(8,128)}, u32[]{:S(2)}) copy-start(f32[8,4]{1,0:T(8,128)} %get-tuple-element.83) | copy-start | bytes 388
  82.2 21.7 %all-to-all-start.2 = ((f32[32,32,128]{2,1,0:T(8,128)}), f32[32,32,128]{2,1,0:T(8,128)S(1)}, u32[]{:S(2)}, u32[]{:S(2)}) async-start(f32[32,32,128]{2,1,0:T(8,128)} %copy.201), calls=%async_computation.2 | async-start | bytes 1048576 | tf_op jit(solution)/shard_map/all_to_all | solution.py:87
  103.9 1.6 %copy-start.3 = (f32[8,4,128,128]{3,0,2,1:T(8,128)S(1)}, f32[8,4,128,128]{3,0,2,1:T(8,128)}, u32[]{:S(2)}) copy-start(f32[8,4,128,128]{3,0,2,1:T(8,128)} %add_bitcast_fusion) | copy-start | bytes 6291460
  107.4 3.7 %copy-start.9 = (f32[32]{0:T(128)S(1)}, f32[32]{0:T(128)}, u32[]{:S(2)}) copy-start(f32[32]{0:T(128)} %copy-done.8) | copy-start | bytes 388
  107.4 30.9 %all-to-all-start.3 = ((bf16[8,1024,128]{2,1,0:T(8,128)(2,1)}), bf16[8,1024,128]{2,1,0:T(8,128)(2,1)S(1)}, u32[]{:S(2)}, u32[]{:S(2)}) async-start(bf16[8,1024,128]{2,1,0:T(8,128)(2,1)} %pad_maximum_fusion), calls=%async_computation.3 | async-start | bytes 4194304 | tf_op jit(solution)/shard_map/all_to_all | solution.py:242

commit v11 on v10

--- a/solution.py
+++ b/solution.py
@@ -13,9 +13,9 @@
 
 
 def halves(array):
-    high = array.astype(jnp.bfloat16)
-    low = (array - widen(high)).astype(jnp.bfloat16)
-    return (high, low)
+    rounded = lax.reduce_precision(array, exponent_bits=8, mantissa_bits=7)
+    low = (array - rounded).astype(jnp.bfloat16)
+    return (rounded.astype(jnp.bfloat16), low)
 
 
 def product(form, first_op, second_op):

time: 151 us -> 150 us (level)
  no operation moved by 1% of the time
where the time goes in v11:
time: 150 us; the launch traced here: 149 us
  waiting for transfers between devices  66.4 us (44%)
  starting transfers between devices  24.2 us (16%)
  matrix products  21 us (14%)
  local copies, waits for them, and re-layouts  17.5 us (12%)
  Pallas kernels  9.64 us (6%)
  other arithmetic  9.29 us (6%)
    all_to_all x1, waiting for transfers between devices, body(): back = lax.all_to_all(returned, 'exp', 0, 0, tiled=True)  23 us
    dot_general x20, matrix products, product(): jnp.einsum(form, first_op, second_op, preferred_element_type=jnp.float32)  20.1 us
    all_to_all x1, waiting for transfers between devices, carried_both(): lax.all_to_all(jnp.concatenate([state_rows, adjoint_rows], axis=1), axis,...  16.8 us
    all_to_all x1, waiting for transfers between devices, body(): got = lax.all_to_all(packed, 'exp', 0, 0, tiled=True)  16.3 us
    all_to_all x1, starting transfers between devices, carried_both(): got = lax.all_to_all(payload, axis, 0, 0, tiled=True)  11.3 us
    all_to_all x1, waiting for transfers between devices, carried_both(): got = lax.all_to_all(payload, axis, 0, 0, tiled=True)  10.2 us
    pallas_call x1, Pallas kernels, finish_call(): pl.pallas_call(finish_kernel, grid=(steps,), in_specs=[flat_spec, flat_sp...  9.64 us
    all_to_all x1, starting transfers between devices, carried_both(): lax.all_to_all(jnp.concatenate([state_rows, adjoint_rows], axis=1), axis,...  4.69 us
  transfers between devices with their start and end apart: 4, of which 4 were waited for; matrix products, arithmetic and copies ran while one was open for 13% of the time, Pallas kernels for 0%

profile of v11, /device:TPU:32, one launch (start us, length us, event | category | flops | bytes accessed | tf_op | source)
XLA Modules:
  0.0 149.1 jit_solution(14034308966984985041)
XLA Ops:
  1.8 1.7 %copy.224 = bf16[128,4096]{0,1:T(8,128)(2,1)S(1)} copy(bf16[128,4096]{1,0:T(8,128)(2,1)} %param.11) | data formatting | bytes 2097152 | tf_op jit(solution)/shard_map/reshape | solution.py:127
  3.5 1.6 %copy.223 = bf16[128,4096]{0,1:T(8,128)(2,1)S(1)} copy(bf16[128,4096]{1,0:T(8,128)(2,1)} %key_ref.1) | data formatting | bytes 2097152 | tf_op jit(solution)/shard_map/reshape | solution.py:128
  8.7 1.5 %fusion.1 = bf16[8,1040,128]{2,1,0:T(8,128)(2,1)} fusion(bf16[8,4,128]{2,1,0:T(4,128)(2,1)S(1)} %bitcast.182, bf16[8,512,128]{2,1,0:T(8,128)(2,1)S(1)} %bitcast.168, bf16[8,512,128]{2,1,0:T(8,128)(2,1)S(1)} %bitcast.167), kind=kLoop, calls=%fused_computation.6 | loop fusion | flops 8519680 | bytes 4235264 | tf_op jit(solution)/shard_map/concatenate | solution.py:212
  10.2 4.5 %all-to-all-start = ((bf16[8,1040,128]{2,1,0:T(8,128)(2,1)}), bf16[8,1040,128]{2,1,0:T(8,128)(2,1)}, u32[]{:S(2)}, u32[]{:S(2)}) async-start(bf16[8,1040,128]{2,1,0:T(8,128)(2,1)} %fusion.1), calls=%async_computation | async-start | bytes 4259840 | tf_op jit(solution)/shard_map/all_to_all | solution.py:220
  15.9 2.9 %multiply_convert_fusion.1 = bf16[32,128,128]{2,1,0:T(8,128)(2,1)S(1)} fusion(f32[32,128]{1,0:T(8,128)S(1)} %bitcast.180, pred[128,128]{1,0:T(8,128)(4,1)S(1)} %iota_compare_fusion.5, bf16[128,4096]{1,0:T(8,128)(2,1)S(1)} %copy-done, bf16[128,4096]{1,0:T(8,128)(2,1)} %value_ref.1), kind=kOutput, calls=%fused_computation.15 | convolution fusion | flops 136839168 | bytes 3178496 | tf_op jit(solution)/shard_map/thd,shd->hts/dot_general | solution.py:22
  18.8 2.2 %fusion.119.qp_ref = f32[32,128,128]{2,1,0:T(8,128)} fusion(bf16[32,128,128]{2,1,0:T(8,128)(2,1)S(1)} %multiply_convert_fusion.1, bf16[128,32,128]{0,2,1:T(8,128)(2,1)S(1)} %bitcast.163), kind=kOutput, calls=%fused_computation.182 | convolution fusion | flops 134217728 | bytes 4194304 | tf_op jit(solution)/shard_map/hts,shd->htd/dot_general | solution.py:22
  21.0 2.2 %fusion.120.kp_ref = f32[32,128,128]{2,1,0:T(8,128)} fusion(bf16[32,128,128]{2,1,0:T(8,128)(2,1)S(1)} %multiply_convert_fusion.1, bf16[128,32,128]{0,2,1:T(8,128)(2,1)S(1)} %bitcast.159), kind=kOutput, calls=%fused_computation.183 | convolution fusion | flops 134217728 | bytes 4194304 | tf_op jit(solution)/shard_map/hts,thd->hsd/dot_general | solution.py:22
  23.2 2.8 %fusion.4.vp_ref = f32[32,128,128]{2,1,0:T(8,128)} fusion(bf16[128,32,128]{0,2,1:T(8,128)(2,1)S(1)} %bitcast.160, bf16[128,32,128]{0,2,1:T(8,128)(2,1)S(1)} %bitcast.164, f32[32,128]{1,0:T(8,128)S(1)} %bitcast.181, pred[128,128]{1,0:T(8,128)(4,1)S(1)} %iota_compare_fusion.5, bf16[128,4096]{1,0:T(8,128)(2,1)S(1)} %copy-done), kind=kOutput, calls=%fused_computation.21 | convolution fusion | flops 271056896 | bytes 5275648 | tf_op jit(solution)/shard_map/hts,thd->hsd/dot_general | solution.py:22
  26.0 16.3 %all-to-all-done = bf16[8,1040,128]{2,1,0:T(8,128)(2,1)} async-done(((bf16[8,1040,128]{2,1,0:T(8,128)(2,1)}), bf16[8,1040,128]{2,1,0:T(8,128)(2,1)}, u32[]{:S(2)}, u32[]{:S(2)}) %all-to-all-start) | async-done | bytes 2129952 | tf_op jit(solution)/shard_map/all_to_all | solution.py:220
  43.1 1.7 %fusion.114 = (bf16[8,512,128]{2,1,0:T(8,128)(2,1)S(1)}, bf16[8,512,128]{2,1,0:T(8,128)(2,1)S(1)}) fusion(bf16[8,1040,128]{2,1,0:T(8,128)(2,1)} %all-to-all-done), kind=kLoop, calls=%fused_computation.177 | loop fusion | bytes 4194304 | tf_op jit(solution)/shard_map/slice | solution.py:222
  50.9 11.3 %all-to-all-start.1 = ((bf16[32,48,128]{2,1,0:T(8,128)(2,1)}), bf16[32,48,128]{2,1,0:T(8,128)(2,1)S(1)}, u32[]{:S(2)}, u32[]{:S(2)}) async-start(bf16[32,48,128]{2,1,0:T(8,128)(2,1)} %pad_maximum_fusion.2), calls=%async_computation.1 | async-start | bytes 786432 | tf_op jit(solution)/shard_map/all_to_all | solution.py:66
  63.9 2.1 %add_bitcast_fusion = f32[8,4,128,128]{3,0,2,1:T(8,128)} fusion(f32[4,128,128,8]{2,3,1,0:T(8,128)S(1)} %fusion.36, bf16[8,4,128,128]{3,2,1,0:T(8,128)(2,1)S(1)} %bitcast.156, f32[8,8,4]{1,2,0:T(4,128)S(1)} %get-tuple-element.60, pred[8,8]{1,0:T(8,128)(4,1)S(1)} %copy-done.13), kind=kOutput, calls=%fused_computation.12 | convolution fusion | flops 8914176 | bytes 5243968 | tf_op jit(solution)/shard_map/ijh,jhab->ihab/dot_general | solution.py:22
  66.9 10.2 %all-to-all-done.1 = bf16[32,48,128]{2,1,0:T(8,128)(2,1)S(1)} async-done(((bf16[32,48,128]{2,1,0:T(8,128)(2,1)}), bf16[32,48,128]{2,1,0:T(8,128)(2,1)S(1)}, u32[]{:S(2)}, u32[]{:S(2)}) %all-to-all-start.1) | async-done | bytes 393248 | tf_op jit(solution)/shard_map/all_to_all | solution.py:66
  77.1 1.6 %copy.198 = bf16[32,48,128]{0,2,1:T(8,128)(2,1)} copy(bf16[32,48,128]{2,1,0:T(8,128)(2,1)S(1)} %all-to-all-done.1) | data formatting | bytes 786432 | tf_op jit(solution)/shard_map/optimization_barrier | solution.py:67
  81.7 4.7 %all-to-all-start.2 = ((f32[32,32,128]{2,1,0:T(8,128)}), f32[32,32,128]{2,1,0:T(8,128)S(1)}, u32[]{:S(2)}, u32[]{:S(2)}) async-start(f32[32,32,128]{2,1,0:T(8,128)} %copy.201), calls=%async_computation.2 | async-start | bytes 1048576 | tf_op jit(solution)/shard_map/all_to_all | solution.py:87
  86.6 16.8 %all-to-all-done.2 = f32[32,32,128]{2,1,0:T(8,128)S(1)} async-done(((f32[32,32,128]{2,1,0:T(8,128)}), f32[32,32,128]{2,1,0:T(8,128)S(1)}, u32[]{:S(2)}, u32[]{:S(2)}) %all-to-all-start.2) | async-done | bytes 524320 | tf_op jit(solution)/shard_map/all_to_all | solution.py:87
  103.9 1.1 copy-done.3
  105.6 1.4 pad_maximum_fusion
  107.0 3.7 %all-to-all-start.3 = ((bf16[8,1024,128]{2,1,0:T(8,128)(2,1)}), bf16[8,1024,128]{2,1,0:T(8,128)(2,1)S(1)}, u32[]{:S(2)}, u32[]{:S(2)}) async-start(bf16[8,1024,128]{2,1,0:T(8,128)(2,1)} %pad_maximum_fusion), calls=%async_computation.3 | async-start | bytes 4194304 | tf_op jit(solution)/shard_map/all_to_all | solution.py:242
  110.8 2.0 %copy.206.after_ref = f32[32,128,1]{2,1,0:T(8,128)} copy(f32[32,128,1]{1,0,2:T(8,128)S(1)} %get-tuple-element.72) | data formatting | bytes 32768 | tf_op jit(solution)/shard_map/broadcast_in_dim | solution.py:247
  112.9 2.0 %copy.205.before_ref = f32[32,128,1]{2,1,0:T(8,128)} copy(f32[32,128,1]{1,0,2:T(8,128)S(1)} %get-tuple-element.73) | data formatting | bytes 32768 | tf_op jit(solution)/shard_map/broadcast_in_dim | solution.py:247
  114.8 23.0 %all-to-all-done.3 = bf16[8,1024,128]{2,1,0:T(8,128)(2,1)S(1)} async-done(((bf16[8,1024,128]{2,1,0:T(8,128)(2,1)}), bf16[8,1024,128]{2,1,0:T(8,128)(2,1)S(1)}, u32[]{:S(2)}, u32[]{:S(2)}) %all-to-all-start.3) | async-done | bytes 2097184 | tf_op jit(solution)/shard_map/all_to_all | solution.py:242
  137.9 1.5 fusion.115
  139.3 9.6 %shard_map.76 = (bf16[128,4096]{1,0:T(8,128)(2,1)}, bf16[128,4096]{1,0:T(8,128)(2,1)}, bf16[128,4096]{1,0:T(8,128)(2,1)}) custom-call(bf16[128,4096]{1,0:T(8,128)(2,1)} %grad_ref.1, bf16[128,4096]{1,0:T(8,128)(2,1)} %value_ref.1, bf16[128,4096]{1,0:T(8,128)(2,1)} %key_ref.1, bf16[32,128,128]{2,1,0:T(8,128)(2,1)} %bitcast.170, ...), custom_call_target="tpu_custom_call" | custom-call | tf_op jit(solution)/shard_map/pallas_call | solution.py:189
  (92 shorter events, 19.4 us)
Async XLA Ops:
  1.7 3.4 %copy-start.14 = (f32[32]{0:T(128)}, f32[32]{0:T(128)S(1)}, u32[]{:S(2)}) copy-start(f32[32]{0:T(128)S(1)} %slice_reduce_fusion) | copy-start | bytes 388
  1.7 3.4 %copy-start.1 = (bf16[128,4096]{1,0:T(8,128)(2,1)S(1)}, bf16[128,4096]{1,0:T(8,128)(2,1)}, u32[]{:S(2)}) copy-start(bf16[128,4096]{1,0:T(8,128)(2,1)} %value_ref.1) | copy-start | bytes 3145732
  5.1 1.2 copy-start.2
  6.3 1.2 copy-start
  8.0 0.7 copy-start.4
  10.2 32.1 %all-to-all-start = ((bf16[8,1040,128]{2,1,0:T(8,128)(2,1)}), bf16[8,1040,128]{2,1,0:T(8,128)(2,1)}, u32[]{:S(2)}, u32[]{:S(2)}) async-start(bf16[8,1040,128]{2,1,0:T(8,128)(2,1)} %fusion.1), calls=%async_computation | async-start | bytes 4259840 | tf_op jit(solution)/shard_map/all_to_all | solution.py:220
  15.3 29.7 %copy-start.9 = (pred[8,8]{1,0:T(8,128)(4,1)}, pred[8,8]{1,0:T(8,128)(4,1)S(1)}, u32[]{:S(2)}) copy-start(pred[8,8]{1,0:T(8,128)(4,1)S(1)} %get-tuple-element.86) | copy-start | bytes 196
  15.3 29.7 %copy-start.12 = (pred[8,8]{1,0:T(8,128)(4,1)}, pred[8,8]{1,0:T(8,128)(4,1)S(1)}, u32[]{:S(2)}) copy-start(pred[8,8]{1,0:T(8,128)(4,1)S(1)} %get-tuple-element.85) | copy-start | bytes 196
  49.0 13.2 %copy-start.5 = (pred[8,8,8]{2,1,0:T(8,128)(4,1)S(1)}, pred[8,8,8]{2,1,0:T(8,128)(4,1)}, u32[]{:S(2)}) copy-start(pred[8,8,8]{2,1,0:T(8,128)(4,1)} %get-tuple-element.87) | copy-start | bytes 1540
  49.0 13.2 %copy-start.6 = (pred[8,8,8]{2,1,0:T(8,128)(4,1)S(1)}, pred[8,8,8]{2,1,0:T(8,128)(4,1)}, u32[]{:S(2)}) copy-start(pred[8,8,8]{2,1,0:T(8,128)(4,1)} %get-tuple-element.88) | copy-start | bytes 1540
  49.1 13.4 %copy-start.13 = (pred[8,8]{1,0:T(8,128)(4,1)S(1)}, pred[8,8]{1,0:T(8,128)(4,1)}, u32[]{:S(2)}) copy-start(pred[8,8]{1,0:T(8,128)(4,1)} %copy-done.12) | copy-start | bytes 196
  50.9 12.3 %copy-start.10 = (pred[8,8]{1,0:T(8,128)(4,1)S(1)}, pred[8,8]{1,0:T(8,128)(4,1)}, u32[]{:S(2)}) copy-start(pred[8,8]{1,0:T(8,128)(4,1)} %copy-done.9) | copy-start | bytes 196
  50.9 26.1 %all-to-all-start.1 = ((bf16[32,48,128]{2,1,0:T(8,128)(2,1)}), bf16[32,48,128]{2,1,0:T(8,128)(2,1)S(1)}, u32[]{:S(2)}, u32[]{:S(2)}) async-start(bf16[32,48,128]{2,1,0:T(8,128)(2,1)} %pad_maximum_fusion.2), calls=%async_computation.1 | async-start | bytes 786432 | tf_op jit(solution)/shard_map/all_to_all | solution.py:66
  63.9 2.2 %copy-start.11 = (pred[8,8]{1,0:T(8,128)(4,1)S(1)}, pred[8,8]{1,0:T(8,128)(4,1)}, u32[]{:S(2)}) copy-start(pred[8,8]{1,0:T(8,128)(4,1)} %copy-done.9) | copy-start | bytes 196
  66.8 12.6 %copy-start.16 = (f32[4]{0:T(128)S(1)}, f32[4]{0:T(128)}, u32[]{:S(2)}) copy-start(f32[4]{0:T(128)} %compare_convert_fusion) | copy-start | bytes 52
  80.2 6.2 %copy-start.7 = (f32[8,4]{1,0:T(8,128)S(1)}, f32[8,4]{1,0:T(8,128)}, u32[]{:S(2)}) copy-start(f32[8,4]{1,0:T(8,128)} %get-tuple-element.76) | copy-start | bytes 388
  80.2 6.3 %copy-start.8 = (f32[8,4]{1,0:T(8,128)S(1)}, f32[8,4]{1,0:T(8,128)}, u32[]{:S(2)}) copy-start(f32[8,4]{1,0:T(8,128)} %get-tuple-element.79) | copy-start | bytes 388
  81.7 21.7 %all-to-all-start.2 = ((f32[32,32,128]{2,1,0:T(8,128)}), f32[32,32,128]{2,1,0:T(8,128)S(1)}, u32[]{:S(2)}, u32[]{:S(2)}) async-start(f32[32,32,128]{2,1,0:T(8,128)} %copy.201), calls=%async_computation.2 | async-start | bytes 1048576 | tf_op jit(solution)/shard_map/all_to_all | solution.py:87
  103.5 1.6 %copy-start.3 = (f32[8,4,128,128]{3,0,2,1:T(8,128)S(1)}, f32[8,4,128,128]{3,0,2,1:T(8,128)}, u32[]{:S(2)}) copy-start(f32[8,4,128,128]{3,0,2,1:T(8,128)} %add_bitcast_fusion) | copy-start | bytes 6291460
  107.0 3.7 %copy-start.15 = (f32[32]{0:T(128)S(1)}, f32[32]{0:T(128)}, u32[]{:S(2)}) copy-start(f32[32]{0:T(128)} %copy-done.14) | copy-start | bytes 388
  107.0 30.9 %all-to-all-start.3 = ((bf16[8,1024,128]{2,1,0:T(8,128)(2,1)}), bf16[8,1024,128]{2,1,0:T(8,128)(2,1)S(1)}, u32[]{:S(2)}, u32[]{:S(2)}) async-start(bf16[8,1024,128]{2,1,0:T(8,128)(2,1)} %pad_maximum_fusion), calls=%async_computation.3 | async-start | bytes 4194304 | tf_op jit(solution)/shard_map/all_to_all | solution.py:242

commit v12 on v11

--- a/solution.py
+++ b/solution.py
@@ -85,10 +85,14 @@
     state_rows = split_left("di,irc->drc", w_fwd, got[:, :share])
     adjoint_rows = split_left("di,irc->drc", w_bwd, got[:, share : 2 * share])
     back = lax.all_to_all(
-        jnp.concatenate([state_rows, adjoint_rows], axis=1), axis, 0, 0, tiled=True
-    )
-    start_state = back[:, :share].reshape(heads, width, width)
-    start_adjoint = back[:, share:].reshape(heads, width, width)
+        jnp.concatenate([state_rows, adjoint_rows], axis=1).astype(jnp.bfloat16),
+        axis,
+        0,
+        0,
+        tiled=True,
+    )
+    start_state = widen(back[:, :share]).reshape(heads, width, width)
+    start_adjoint = widen(back[:, share:]).reshape(heads, width, width)
     return start_state, start_adjoint, riders
 
 

time: 150 us -> 146 us (0.973)
  waiting for transfers between devices: 66.4 us -> 61.1 us
  other arithmetic: 9.29 us -> 10.9 us
  local copies, waits for them, and re-layouts: 17.5 us -> 16 us
    all_to_all x1, waiting for transfers between devices: 16.8 us -> 11.5 us  [carried_both(): lax.all_to_all(jnp.concatenate([state_rows, adjoint_rows], axis=1).astype...]
    convert_element_type x1, other arithmetic: 0.34 us -> 1.93 us  [body(): adjoint.astype(jnp.bfloat16).reshape(peers, share, width)]
  transfers between devices with their start and end apart: 4 -> 4, of which waited for: 4 -> 4; matrix products, arithmetic and copies ran while one was open for 13% -> 14% of each run, Pallas kernels for 0% -> 0%
where the time goes in v12:
time: 146 us; the launch traced here: 144 us
  waiting for transfers between devices  61.1 us (42%)
  starting transfers between devices  24.2 us (17%)
  matrix products  21 us (14%)
  local copies, waits for them, and re-layouts  16 us (11%)
  other arithmetic  10.9 us (7%)
  Pallas kernels  9.65 us (7%)
    all_to_all x1, waiting for transfers between devices, body(): back = lax.all_to_all(returned, 'exp', 0, 0, tiled=True)  23 us
    dot_general x20, matrix products, product(): jnp.einsum(form, first_op, second_op, preferred_element_type=jnp.float32)  20.1 us
    all_to_all x1, waiting for transfers between devices, body(): got = lax.all_to_all(packed, 'exp', 0, 0, tiled=True)  16.4 us
    all_to_all x1, waiting for transfers between devices, carried_both(): lax.all_to_all(jnp.concatenate([state_rows, adjoint_rows], axis=1).astype...  11.5 us
    all_to_all x1, starting transfers between devices, carried_both(): got = lax.all_to_all(payload, axis, 0, 0, tiled=True)  11.3 us
    all_to_all x1, waiting for transfers between devices, carried_both(): got = lax.all_to_all(payload, axis, 0, 0, tiled=True)  10.2 us
    pallas_call x1, Pallas kernels, finish_call(): pl.pallas_call(finish_kernel, grid=(steps,), in_specs=[flat_spec, flat_sp...  9.65 us
    all_to_all x1, starting transfers between devices, carried_both(): lax.all_to_all(jnp.concatenate([state_rows, adjoint_rows], axis=1).astype...  4.69 us
  transfers between devices with their start and end apart: 4, of which 4 were waited for; matrix products, arithmetic and copies ran while one was open for 14% of the time, Pallas kernels for 0%

profile of v12, /device:TPU:32, one launch (start us, length us, event | category | flops | bytes accessed | tf_op | source)
XLA Modules:
  0.0 144.0 jit_solution(10242976144768154429)
XLA Ops:
  1.8 1.7 %copy.224 = bf16[128,4096]{0,1:T(8,128)(2,1)S(1)} copy(bf16[128,4096]{1,0:T(8,128)(2,1)} %param.11) | data formatting | bytes 2097152 | tf_op jit(solution)/shard_map/reshape | solution.py:131
  3.5 1.6 %copy.223 = bf16[128,4096]{0,1:T(8,128)(2,1)S(1)} copy(bf16[128,4096]{1,0:T(8,128)(2,1)} %key_ref.1) | data formatting | bytes 2097152 | tf_op jit(solution)/shard_map/reshape | solution.py:132
  8.7 1.5 %fusion.1 = bf16[8,1040,128]{2,1,0:T(8,128)(2,1)} fusion(bf16[8,4,128]{2,1,0:T(4,128)(2,1)S(1)} %bitcast.188, bf16[8,512,128]{2,1,0:T(8,128)(2,1)S(1)} %bitcast.174, bf16[8,512,128]{2,1,0:T(8,128)(2,1)S(1)} %bitcast.173), kind=kLoop, calls=%fused_computation.6 | loop fusion | flops 8519680 | bytes 4235264 | tf_op jit(solution)/shard_map/concatenate | solution.py:216
  10.2 4.5 %all-to-all-start = ((bf16[8,1040,128]{2,1,0:T(8,128)(2,1)}), bf16[8,1040,128]{2,1,0:T(8,128)(2,1)}, u32[]{:S(2)}, u32[]{:S(2)}) async-start(bf16[8,1040,128]{2,1,0:T(8,128)(2,1)} %fusion.1), calls=%async_computation | async-start | bytes 4259840 | tf_op jit(solution)/shard_map/all_to_all | solution.py:224
  15.8 2.9 %multiply_convert_fusion.1 = bf16[32,128,128]{2,1,0:T(8,128)(2,1)S(1)} fusion(f32[32,128]{1,0:T(8,128)S(1)} %bitcast.186, pred[128,128]{1,0:T(8,128)(4,1)S(1)} %iota_compare_fusion.5, bf16[128,4096]{1,0:T(8,128)(2,1)S(1)} %copy-done, bf16[128,4096]{1,0:T(8,128)(2,1)} %value_ref.1), kind=kOutput, calls=%fused_computation.15 | convolution fusion | flops 136839168 | bytes 3178496 | tf_op jit(solution)/shard_map/thd,shd->hts/dot_general | solution.py:22
  18.7 2.2 %fusion.121.qp_ref = f32[32,128,128]{2,1,0:T(8,128)} fusion(bf16[32,128,128]{2,1,0:T(8,128)(2,1)S(1)} %multiply_convert_fusion.1, bf16[128,32,128]{0,2,1:T(8,128)(2,1)S(1)} %bitcast.169), kind=kOutput, calls=%fused_computation.186 | convolution fusion | flops 134217728 | bytes 4194304 | tf_op jit(solution)/shard_map/hts,shd->htd/dot_general | solution.py:22
  20.9 2.2 %fusion.122.kp_ref = f32[32,128,128]{2,1,0:T(8,128)} fusion(bf16[32,128,128]{2,1,0:T(8,128)(2,1)S(1)} %multiply_convert_fusion.1, bf16[128,32,128]{0,2,1:T(8,128)(2,1)S(1)} %bitcast.165), kind=kOutput, calls=%fused_computation.187 | convolution fusion | flops 134217728 | bytes 4194304 | tf_op jit(solution)/shard_map/hts,thd->hsd/dot_general | solution.py:22
  23.1 2.8 %fusion.4.vp_ref = f32[32,128,128]{2,1,0:T(8,128)} fusion(bf16[128,32,128]{0,2,1:T(8,128)(2,1)S(1)} %bitcast.166, bf16[128,32,128]{0,2,1:T(8,128)(2,1)S(1)} %bitcast.170, f32[32,128]{1,0:T(8,128)S(1)} %bitcast.187, pred[128,128]{1,0:T(8,128)(4,1)S(1)} %iota_compare_fusion.5, bf16[128,4096]{1,0:T(8,128)(2,1)S(1)} %copy-done), kind=kOutput, calls=%fused_computation.21 | convolution fusion | flops 271056896 | bytes 5275648 | tf_op jit(solution)/shard_map/hts,thd->hsd/dot_general | solution.py:22
  25.9 16.4 %all-to-all-done = bf16[8,1040,128]{2,1,0:T(8,128)(2,1)} async-done(((bf16[8,1040,128]{2,1,0:T(8,128)(2,1)}), bf16[8,1040,128]{2,1,0:T(8,128)(2,1)}, u32[]{:S(2)}, u32[]{:S(2)}) %all-to-all-start) | async-done | bytes 2129952 | tf_op jit(solution)/shard_map/all_to_all | solution.py:224
  43.1 1.7 %fusion.116 = (bf16[8,512,128]{2,1,0:T(8,128)(2,1)S(1)}, bf16[8,512,128]{2,1,0:T(8,128)(2,1)S(1)}) fusion(bf16[8,1040,128]{2,1,0:T(8,128)(2,1)} %all-to-all-done), kind=kLoop, calls=%fused_computation.181 | loop fusion | bytes 4194304 | tf_op jit(solution)/shard_map/slice | solution.py:226
  50.9 11.3 %all-to-all-start.1 = ((bf16[32,48,128]{2,1,0:T(8,128)(2,1)}), bf16[32,48,128]{2,1,0:T(8,128)(2,1)S(1)}, u32[]{:S(2)}, u32[]{:S(2)}) async-start(bf16[32,48,128]{2,1,0:T(8,128)(2,1)} %pad_maximum_fusion.1), calls=%async_computation.1 | async-start | bytes 786432 | tf_op jit(solution)/shard_map/all_to_all | solution.py:66
  63.9 2.1 %add_bitcast_fusion = f32[8,4,128,128]{3,0,2,1:T(8,128)} fusion(f32[4,128,128,8]{2,3,1,0:T(8,128)S(1)} %fusion.38, bf16[8,4,128,128]{3,2,1,0:T(8,128)(2,1)S(1)} %bitcast.162, f32[8,8,4]{1,2,0:T(4,128)S(1)} %get-tuple-element.60, pred[8,8]{1,0:T(8,128)(4,1)S(1)} %copy-done.12), kind=kOutput, calls=%fused_computation.12 | convolution fusion | flops 8914176 | bytes 5243968 | tf_op jit(solution)/shard_map/ijh,jhab->ihab/dot_general | solution.py:22
  66.9 10.2 %all-to-all-done.1 = bf16[32,48,128]{2,1,0:T(8,128)(2,1)S(1)} async-done(((bf16[32,48,128]{2,1,0:T(8,128)(2,1)}), bf16[32,48,128]{2,1,0:T(8,128)(2,1)S(1)}, u32[]{:S(2)}, u32[]{:S(2)}) %all-to-all-start.1) | async-done | bytes 393248 | tf_op jit(solution)/shard_map/all_to_all | solution.py:66
  77.2 1.6 %copy.198 = bf16[32,48,128]{0,2,1:T(8,128)(2,1)} copy(bf16[32,48,128]{2,1,0:T(8,128)(2,1)S(1)} %all-to-all-done.1) | data formatting | bytes 786432 | tf_op jit(solution)/shard_map/optimization_barrier | solution.py:67
  81.5 4.7 %all-to-all-start.2 = ((bf16[32,32,128]{2,1,0:T(8,128)(2,1)}), bf16[32,32,128]{2,1,0:T(8,128)(2,1)S(1)}, u32[]{:S(2)}, u32[]{:S(2)}) async-start(bf16[32,32,128]{2,1,0:T(8,128)(2,1)} %copy.201), calls=%async_computation.2 | async-start | bytes 524288 | tf_op jit(solution)/shard_map/all_to_all | solution.py:87
  86.3 11.5 %all-to-all-done.2 = bf16[32,32,128]{2,1,0:T(8,128)(2,1)S(1)} async-done(((bf16[32,32,128]{2,1,0:T(8,128)(2,1)}), bf16[32,32,128]{2,1,0:T(8,128)(2,1)S(1)}, u32[]{:S(2)}, u32[]{:S(2)}) %all-to-all-start.2) | async-done | bytes 262176 | tf_op jit(solution)/shard_map/all_to_all | solution.py:87
  97.9 1.9 %add_convert_fusion = bf16[8,4,128,128]{3,0,2,1:T(8,128)(2,1)S(1)} fusion(f32[8,4,128,128]{3,0,2,1:T(8,128)} %add_bitcast_fusion, f32[4,128,128]{2,1,0:T(8,128)S(1)} %bitcast_convert_fusion, f32[8,4]{0,1:T(4,128)S(1)} %copy.202), kind=kLoop, calls=%fused_computation.10 | loop fusion | flops 1572864 | bytes 3408000 | tf_op jit(solution)/shard_map/convert_element_type | solution.py:242
  100.5 1.4 pad_maximum_fusion
  101.9 3.7 %all-to-all-start.3 = ((bf16[8,1024,128]{2,1,0:T(8,128)(2,1)}), bf16[8,1024,128]{2,1,0:T(8,128)(2,1)S(1)}, u32[]{:S(2)}, u32[]{:S(2)}) async-start(bf16[8,1024,128]{2,1,0:T(8,128)(2,1)} %pad_maximum_fusion), calls=%async_computation.3 | async-start | bytes 4194304 | tf_op jit(solution)/shard_map/all_to_all | solution.py:246
  105.7 2.0 %copy.206.after_ref = f32[32,128,1]{2,1,0:T(8,128)} copy(f32[32,128,1]{1,0,2:T(8,128)S(1)} %get-tuple-element.72) | data formatting | bytes 32768 | tf_op jit(solution)/shard_map/broadcast_in_dim | solution.py:251
  107.8 2.0 %copy.205.before_ref = f32[32,128,1]{2,1,0:T(8,128)} copy(f32[32,128,1]{1,0,2:T(8,128)S(1)} %get-tuple-element.73) | data formatting | bytes 32768 | tf_op jit(solution)/shard_map/broadcast_in_dim | solution.py:251
  109.8 23.0 %all-to-all-done.3 = bf16[8,1024,128]{2,1,0:T(8,128)(2,1)S(1)} async-done(((bf16[8,1024,128]{2,1,0:T(8,128)(2,1)}), bf16[8,1024,128]{2,1,0:T(8,128)(2,1)S(1)}, u32[]{:S(2)}, u32[]{:S(2)}) %all-to-all-start.3) | async-done | bytes 2097184 | tf_op jit(solution)/shard_map/all_to_all | solution.py:246
  132.8 1.4 %fusion.117 = (bf16[8,512,128]{2,1,0:T(8,128)(2,1)}, bf16[8,512,128]{2,1,0:T(8,128)(2,1)}) fusion(bf16[8,1024,128]{2,1,0:T(8,128)(2,1)S(1)} %all-to-all-done.3), kind=kLoop, calls=%fused_computation.182 | loop fusion | bytes 4194304 | tf_op jit(solution)/shard_map/slice | solution.py:248
  134.2 9.6 %shard_map.76 = (bf16[128,4096]{1,0:T(8,128)(2,1)}, bf16[128,4096]{1,0:T(8,128)(2,1)}, bf16[128,4096]{1,0:T(8,128)(2,1)}) custom-call(bf16[128,4096]{1,0:T(8,128)(2,1)} %grad_ref.1, bf16[128,4096]{1,0:T(8,128)(2,1)} %value_ref.1, bf16[128,4096]{1,0:T(8,128)(2,1)} %key_ref.1, bf16[32,128,128]{2,1,0:T(8,128)(2,1)} %bitcast.176, ...), custom_call_target="tpu_custom_call" | custom-call | tf_op jit(solution)/shard_map/pallas_call | solution.py:193
  (92 shorter events, 18.7 us)
Async XLA Ops:
  1.7 3.4 %copy-start.13 = (f32[32]{0:T(128)}, f32[32]{0:T(128)S(1)}, u32[]{:S(2)}) copy-start(f32[32]{0:T(128)S(1)} %slice_reduce_fusion) | copy-start | bytes 388
  1.7 3.4 %copy-start.1 = (bf16[128,4096]{1,0:T(8,128)(2,1)S(1)}, bf16[128,4096]{1,0:T(8,128)(2,1)}, u32[]{:S(2)}) copy-start(bf16[128,4096]{1,0:T(8,128)(2,1)} %value_ref.1) | copy-start | bytes 3145732
  5.1 1.2 copy-start.2
  6.3 1.2 copy-start
  8.0 0.7 copy-start.3
  10.2 32.1 %all-to-all-start = ((bf16[8,1040,128]{2,1,0:T(8,128)(2,1)}), bf16[8,1040,128]{2,1,0:T(8,128)(2,1)}, u32[]{:S(2)}, u32[]{:S(2)}) async-start(bf16[8,1040,128]{2,1,0:T(8,128)(2,1)} %fusion.1), calls=%async_computation | async-start | bytes 4259840 | tf_op jit(solution)/shard_map/all_to_all | solution.py:224
  15.2 29.8 %copy-start.8 = (pred[8,8]{1,0:T(8,128)(4,1)}, pred[8,8]{1,0:T(8,128)(4,1)S(1)}, u32[]{:S(2)}) copy-start(pred[8,8]{1,0:T(8,128)(4,1)S(1)} %get-tuple-element.86) | copy-start | bytes 196
  15.2 29.8 %copy-start.11 = (pred[8,8]{1,0:T(8,128)(4,1)}, pred[8,8]{1,0:T(8,128)(4,1)S(1)}, u32[]{:S(2)}) copy-start(pred[8,8]{1,0:T(8,128)(4,1)S(1)} %get-tuple-element.85) | copy-start | bytes 196
  49.0 13.2 %copy-start.4 = (pred[8,8,8]{2,1,0:T(8,128)(4,1)S(1)}, pred[8,8,8]{2,1,0:T(8,128)(4,1)}, u32[]{:S(2)}) copy-start(pred[8,8,8]{2,1,0:T(8,128)(4,1)} %get-tuple-element.87) | copy-start | bytes 1540
  49.1 13.2 %copy-start.5 = (pred[8,8,8]{2,1,0:T(8,128)(4,1)S(1)}, pred[8,8,8]{2,1,0:T(8,128)(4,1)}, u32[]{:S(2)}) copy-start(pred[8,8,8]{2,1,0:T(8,128)(4,1)} %get-tuple-element.88) | copy-start | bytes 1540
  49.1 13.4 %copy-start.12 = (pred[8,8]{1,0:T(8,128)(4,1)S(1)}, pred[8,8]{1,0:T(8,128)(4,1)}, u32[]{:S(2)}) copy-start(pred[8,8]{1,0:T(8,128)(4,1)} %copy-done.11) | copy-start | bytes 196
  50.9 12.3 %copy-start.9 = (pred[8,8]{1,0:T(8,128)(4,1)S(1)}, pred[8,8]{1,0:T(8,128)(4,1)}, u32[]{:S(2)}) copy-start(pred[8,8]{1,0:T(8,128)(4,1)} %copy-done.8) | copy-start | bytes 196
  50.9 26.1 %all-to-all-start.1 = ((bf16[32,48,128]{2,1,0:T(8,128)(2,1)}), bf16[32,48,128]{2,1,0:T(8,128)(2,1)S(1)}, u32[]{:S(2)}, u32[]{:S(2)}) async-start(bf16[32,48,128]{2,1,0:T(8,128)(2,1)} %pad_maximum_fusion.1), calls=%async_computation.1 | async-start | bytes 786432 | tf_op jit(solution)/shard_map/all_to_all | solution.py:66
  63.9 2.2 %copy-start.10 = (pred[8,8]{1,0:T(8,128)(4,1)S(1)}, pred[8,8]{1,0:T(8,128)(4,1)}, u32[]{:S(2)}) copy-start(pred[8,8]{1,0:T(8,128)(4,1)} %copy-done.8) | copy-start | bytes 196
  66.9 12.6 %copy-start.15 = (f32[4]{0:T(128)S(1)}, f32[4]{0:T(128)}, u32[]{:S(2)}) copy-start(f32[4]{0:T(128)} %compare_convert_fusion) | copy-start | bytes 52
  78.7 7.4 %copy-start.6 = (f32[8,4]{1,0:T(8,128)S(1)}, f32[8,4]{1,0:T(8,128)}, u32[]{:S(2)}) copy-start(f32[8,4]{1,0:T(8,128)} %get-tuple-element.76) | copy-start | bytes 388
  78.7 7.5 %copy-start.7 = (f32[8,4]{1,0:T(8,128)S(1)}, f32[8,4]{1,0:T(8,128)}, u32[]{:S(2)}) copy-start(f32[8,4]{1,0:T(8,128)} %get-tuple-element.79) | copy-start | bytes 388
  81.5 16.4 %all-to-all-start.2 = ((bf16[32,32,128]{2,1,0:T(8,128)(2,1)}), bf16[32,32,128]{2,1,0:T(8,128)(2,1)S(1)}, u32[]{:S(2)}, u32[]{:S(2)}) async-start(bf16[32,32,128]{2,1,0:T(8,128)(2,1)} %copy.201), calls=%async_computation.2 | async-start | bytes 524288 | tf_op jit(solution)/shard_map/all_to_all | solution.py:87
  101.9 3.7 %copy-start.14 = (f32[32]{0:T(128)S(1)}, f32[32]{0:T(128)}, u32[]{:S(2)}) copy-start(f32[32]{0:T(128)} %copy-done.13) | copy-start | bytes 388
  101.9 30.9 %all-to-all-start.3 = ((bf16[8,1024,128]{2,1,0:T(8,128)(2,1)}), bf16[8,1024,128]{2,1,0:T(8,128)(2,1)S(1)}, u32[]{:S(2)}, u32[]{:S(2)}) async-start(bf16[8,1024,128]{2,1,0:T(8,128)(2,1)} %pad_maximum_fusion), calls=%async_computation.3 | async-start | bytes 4194304 | tf_op jit(solution)/shard_map/all_to_all | solution.py:246

commit v13 on v12

--- a/solution.py
+++ b/solution.py
@@ -165,8 +165,15 @@
 ):
     group, width = state_ref.shape[0], state_ref.shape[2]
     back = (((1,), (1,)), ((), ()))
+    step = pl.program_id(0)
+    lanes = lax.broadcasted_iota(jnp.int32, before_ref.shape, 1)
+    before_all = before_ref[...]
+    after_all = after_ref[...]
     for i in range(group):
         cols = slice(i * width, (i + 1) * width)
+        head = step * group + i
+        before = jnp.sum(jnp.where(lanes == head, before_all, 0.0), axis=1, keepdims=True)
+        after = jnp.sum(jnp.where(lanes == head, after_all, 0.0), axis=1, keepdims=True)
         grad = grad_ref[:, cols]
         value = value_ref[:, cols]
         key = key_ref[:, cols]
@@ -175,12 +182,12 @@
         with_state = lax.dot_general(grad, state, back, preferred_element_type=jnp.float32)
         with_adjoint_v = lax.dot_general(value, adjoint, back, preferred_element_type=jnp.float32)
         with_adjoint_k = jnp.dot(key, adjoint, preferred_element_type=jnp.float32)
-        gq_ref[:, cols] = (qp_ref[i] + before_ref[i] * with_state).astype(gq_ref.dtype)
-        gk_ref[:, cols] = (kp_ref[i] + after_ref[i] * with_adjoint_v).astype(gk_ref.dtype)
-        gv_ref[:, cols] = (vp_ref[i] + after_ref[i] * with_adjoint_k).astype(gv_ref.dtype)
-
-
-def finish_call(out_grad, values, keys, state_in, adjoint_in, qp, kp, vp, before_t, after_t):
+        gq_ref[:, cols] = (qp_ref[i] + before * with_state).astype(gq_ref.dtype)
+        gk_ref[:, cols] = (kp_ref[i] + after * with_adjoint_v).astype(gk_ref.dtype)
+        gv_ref[:, cols] = (vp_ref[i] + after * with_adjoint_k).astype(gv_ref.dtype)
+
+
+def finish_call(out_grad, values, keys, state_in, adjoint_in, qp, kp, vp, before, after):
     length, columns = out_grad.shape
     heads, width = state_in.shape[0], state_in.shape[2]
     group = 4
@@ -188,7 +195,7 @@
     flat_spec = pl.BlockSpec((length, group * width), lambda h: (0, h))
     head_spec = pl.BlockSpec((group, width, width), lambda h: (h, 0, 0))
     part_spec = pl.BlockSpec((group, length, width), lambda h: (h, 0, 0))
-    scale_spec = pl.BlockSpec((group, length, 1), lambda h: (h, 0, 0))
+    scale_spec = pl.BlockSpec((length, heads), lambda h: (0, 0))
     out = jax.ShapeDtypeStruct((length, columns), jnp.bfloat16)
     return pl.pallas_call(
         finish_kernel,
@@ -197,7 +204,7 @@
                   part_spec, scale_spec, scale_spec],
         out_specs=[flat_spec, flat_spec, flat_spec],
         out_shape=[out, out, out],
-    )(out_grad, values, keys, state_in, adjoint_in, qp, kp, vp, before_t, after_t)
+    )(out_grad, values, keys, state_in, adjoint_in, qp, kp, vp, before, after)
 
 
 def body(queries, keys, values, out_grad, log_decay):
@@ -248,7 +255,7 @@
     adjoint_in = back[:, share:].reshape(heads, width, width)
     grad_query, grad_key, grad_value = finish_call(
         out_grad, values, keys, state_in, adjoint_in, query_part, key_part, value_part,
-        before.T[:, :, None], after.T[:, :, None],
+        before, after,
     )
     return (grad_query, grad_key, grad_value)
 

time: 146 us -> 146 us (level)
  waiting for transfers between devices: 61.1 us -> 64.5 us
  local copies, waits for them, and re-layouts: 16 us -> 13.4 us
  other arithmetic: 10.9 us -> 9.1 us
  matrix products: 21 us -> 22.7 us
    broadcast_in_dim x2 -> x0, local copies, waits for them, and re-layouts: 4.03 us -> none  [the longest x1 2.03 us: body(): after.T[:, :, None]]
    all_to_all x1, waiting for transfers between devices: 23 us -> 26.4 us  [body(): back = lax.all_to_all(returned, 'exp', 0, 0, tiled=True)]
    dot_general x20, matrix products: 20.1 us -> 22.5 us  [product(): jnp.einsum(form, first_op, second_op, preferred_element_type=jnp.float32)]
    convert_element_type x1, other arithmetic: 1.93 us -> 0.34 us  [body(): adjoint.astype(jnp.bfloat16).reshape(peers, share, width)]
  transfers between devices with their start and end apart: 4 -> 4, of which waited for: 4 -> 4; matrix products, arithmetic and copies ran while one was open for 14% -> 12% of each run, Pallas kernels for 0% -> 0%
where the time goes in v13:
time: 146 us; the launch traced here: 144 us
  waiting for transfers between devices  64.5 us (44%)
  starting transfers between devices  24.1 us (17%)
  matrix products  22.7 us (16%)
  local copies, waits for them, and re-layouts  13.4 us (9%)
  other arithmetic  9.1 us (6%)
  Pallas kernels  8.91 us (6%)
    all_to_all x1, waiting for transfers between devices, body(): back = lax.all_to_all(returned, 'exp', 0, 0, tiled=True)  26.4 us
    dot_general x20, matrix products, product(): jnp.einsum(form, first_op, second_op, preferred_element_type=jnp.float32)  22.5 us
    all_to_all x1, waiting for transfers between devices, body(): got = lax.all_to_all(packed, 'exp', 0, 0, tiled=True)  16.4 us
    all_to_all x1, waiting for transfers between devices, carried_both(): lax.all_to_all(jnp.concatenate([state_rows, adjoint_rows], axis=1).astype...  11.5 us
    all_to_all x1, starting transfers between devices, carried_both(): got = lax.all_to_all(payload, axis, 0, 0, tiled=True)  11.3 us
    all_to_all x1, waiting for transfers between devices, carried_both(): got = lax.all_to_all(payload, axis, 0, 0, tiled=True)  10.2 us
    pallas_call x1, Pallas kernels, finish_call(): pl.pallas_call(finish_kernel, grid=(steps,), in_specs=[flat_spec, flat_sp...  8.91 us
    all_to_all x1, starting transfers between devices, carried_both(): lax.all_to_all(jnp.concatenate([state_rows, adjoint_rows], axis=1).astype...  4.69 us
  transfers between devices with their start and end apart: 4, of which 4 were waited for; matrix products, arithmetic and copies ran while one was open for 12% of the time, Pallas kernels for 0%

profile of v13, /device:TPU:32, one launch (start us, length us, event | category | flops | bytes accessed | tf_op | source)
XLA Modules:
  0.0 143.8 jit_solution(17556351289997192909)
XLA Ops:
  0.7 1.7 %copy.212 = bf16[128,4096]{0,1:T(8,128)(2,1)S(1)} copy(bf16[128,4096]{1,0:T(8,128)(2,1)} %param.11) | data formatting | bytes 2097152 | tf_op jit(solution)/shard_map/reshape | solution.py:131
  3.0 1.6 %add_convert_fusion.2 = bf16[32,128,128]{2,1,0:T(8,128)(2,1)} fusion(f32[32,128,128]{2,1,0:T(8,128)S(1)} %fusion.10, bf16[128,32,128]{0,2,1:T(8,128)(2,1)S(1)} %bitcast.158, f32[128,32]{0,1:T(8,128)S(1)} %get-tuple-element.81, bf16[128,4096]{1,0:T(8,128)(2,1)S(1)} %copy-done), kind=kOutput, calls=%fused_computation.17 | convolution fusion | flops 137887744 | bytes 5259264 | tf_op jit(solution)/shard_map/tha,thb->hab/dot_general | solution.py:22
  4.6 1.6 %copy.211 = bf16[128,4096]{0,1:T(8,128)(2,1)S(1)} copy(bf16[128,4096]{1,0:T(8,128)(2,1)} %key_ref.1) | data formatting | bytes 2097152 | tf_op jit(solution)/shard_map/reshape | solution.py:132
  6.6 1.8 %fusion.9 = f32[32,128,128]{2,1,0:T(8,128)S(1)} fusion(bf16[128,32,128]{0,2,1:T(8,128)(2,1)S(1)} %bitcast.161, f32[128,32]{0,1:T(8,128)S(1)} %copy.160, bf16[128,4096]{1,0:T(8,128)(2,1)} %value_ref.1), kind=kOutput, calls=%fused_computation.26 | convolution fusion | flops 136314880 | bytes 4210688 | tf_op jit(solution)/shard_map/sha,shb->hab/dot_general | solution.py:22
  9.6 1.5 %fusion.1 = bf16[8,1040,128]{2,1,0:T(8,128)(2,1)} fusion(bf16[8,4,128]{2,1,0:T(4,128)(2,1)S(1)} %bitcast.182, bf16[8,512,128]{2,1,0:T(8,128)(2,1)S(1)} %bitcast.167, bf16[8,512,128]{2,1,0:T(8,128)(2,1)S(1)} %bitcast.170), kind=kLoop, calls=%fused_computation.6 | loop fusion | flops 8519680 | bytes 4235264 | tf_op jit(solution)/shard_map/concatenate | solution.py:223
  11.0 4.5 %all-to-all-start = ((bf16[8,1040,128]{2,1,0:T(8,128)(2,1)}), bf16[8,1040,128]{2,1,0:T(8,128)(2,1)}, u32[]{:S(2)}, u32[]{:S(2)}) async-start(bf16[8,1040,128]{2,1,0:T(8,128)(2,1)} %fusion.1), calls=%async_computation | async-start | bytes 4259840 | tf_op jit(solution)/shard_map/all_to_all | solution.py:231
  16.6 2.9 %multiply_convert_fusion.1 = bf16[32,128,128]{2,1,0:T(8,128)(2,1)S(1)} fusion(f32[32,128]{1,0:T(8,128)S(1)} %bitcast.180, pred[128,128]{1,0:T(8,128)(4,1)S(1)} %iota_compare_fusion.5, bf16[128,4096]{1,0:T(8,128)(2,1)S(1)} %copy-done, bf16[128,4096]{1,0:T(8,128)(2,1)} %value_ref.1), kind=kOutput, calls=%fused_computation.15 | convolution fusion | flops 136839168 | bytes 3178496 | tf_op jit(solution)/shard_map/thd,shd->hts/dot_general | solution.py:22
  19.5 2.2 %fusion.122.qp_ref = f32[32,128,128]{2,1,0:T(8,128)} fusion(bf16[32,128,128]{2,1,0:T(8,128)(2,1)S(1)} %multiply_convert_fusion.1, bf16[128,32,128]{0,2,1:T(8,128)(2,1)S(1)} %bitcast.163), kind=kOutput, calls=%fused_computation.185 | convolution fusion | flops 134217728 | bytes 4194304 | tf_op jit(solution)/shard_map/hts,shd->htd/dot_general | solution.py:22
  21.7 2.2 %fusion.123.kp_ref = f32[32,128,128]{2,1,0:T(8,128)} fusion(bf16[32,128,128]{2,1,0:T(8,128)(2,1)S(1)} %multiply_convert_fusion.1, bf16[128,32,128]{0,2,1:T(8,128)(2,1)S(1)} %bitcast.159), kind=kOutput, calls=%fused_computation.186 | convolution fusion | flops 134217728 | bytes 4194304 | tf_op jit(solution)/shard_map/hts,thd->hsd/dot_general | solution.py:22
  23.9 2.8 %fusion.4.vp_ref = f32[32,128,128]{2,1,0:T(8,128)} fusion(bf16[128,32,128]{0,2,1:T(8,128)(2,1)S(1)} %bitcast.160, bf16[128,32,128]{0,2,1:T(8,128)(2,1)S(1)} %bitcast.164, f32[32,128]{1,0:T(8,128)S(1)} %bitcast.181, pred[128,128]{1,0:T(8,128)(4,1)S(1)} %iota_compare_fusion.5, bf16[128,4096]{1,0:T(8,128)(2,1)S(1)} %copy-done), kind=kOutput, calls=%fused_computation.21 | convolution fusion | flops 271056896 | bytes 5275648 | tf_op jit(solution)/shard_map/hts,thd->hsd/dot_general | solution.py:22
  26.8 16.4 %all-to-all-done = bf16[8,1040,128]{2,1,0:T(8,128)(2,1)} async-done(((bf16[8,1040,128]{2,1,0:T(8,128)(2,1)}), bf16[8,1040,128]{2,1,0:T(8,128)(2,1)}, u32[]{:S(2)}, u32[]{:S(2)}) %all-to-all-start) | async-done | bytes 2129952 | tf_op jit(solution)/shard_map/all_to_all | solution.py:231
  44.0 1.7 %fusion.116 = (bf16[8,512,128]{2,1,0:T(8,128)(2,1)S(1)}, bf16[8,512,128]{2,1,0:T(8,128)(2,1)S(1)}) fusion(bf16[8,1040,128]{2,1,0:T(8,128)(2,1)} %all-to-all-done), kind=kLoop, calls=%fused_computation.179 | loop fusion | bytes 4194304 | tf_op jit(solution)/shard_map/slice | solution.py:233
  51.8 11.3 %all-to-all-start.1 = ((bf16[32,48,128]{2,1,0:T(8,128)(2,1)}), bf16[32,48,128]{2,1,0:T(8,128)(2,1)S(1)}, u32[]{:S(2)}, u32[]{:S(2)}) async-start(bf16[32,48,128]{2,1,0:T(8,128)(2,1)} %pad_maximum_fusion.1), calls=%async_computation.1 | async-start | bytes 786432 | tf_op jit(solution)/shard_map/all_to_all | solution.py:66
  64.8 2.1 %add_bitcast_fusion.1 = f32[8,4,128,128]{3,0,2,1:T(8,128)} fusion(f32[4,128,128,8]{2,3,1,0:T(8,128)S(1)} %fusion.45, bf16[8,4,128,128]{3,2,1,0:T(8,128)(2,1)S(1)} %bitcast.156, f32[8,8,4]{1,2,0:T(4,128)S(1)} %get-tuple-element.61, pred[8,8]{1,0:T(8,128)(4,1)S(1)} %copy-done.14), kind=kOutput, calls=%fused_computation.13 | convolution fusion | flops 8914176 | bytes 5243968 | tf_op jit(solution)/shard_map/ijh,jhab->ihab/dot_general | solution.py:22
  67.7 10.2 %all-to-all-done.1 = bf16[32,48,128]{2,1,0:T(8,128)(2,1)S(1)} async-done(((bf16[32,48,128]{2,1,0:T(8,128)(2,1)}), bf16[32,48,128]{2,1,0:T(8,128)(2,1)S(1)}, u32[]{:S(2)}, u32[]{:S(2)}) %all-to-all-start.1) | async-done | bytes 393248 | tf_op jit(solution)/shard_map/all_to_all | solution.py:66
  78.0 1.5 %copy.187 = bf16[32,48,128]{0,2,1:T(8,128)(2,1)} copy(bf16[32,48,128]{2,1,0:T(8,128)(2,1)S(1)} %all-to-all-done.1) | data formatting | bytes 786432 | tf_op jit(solution)/shard_map/optimization_barrier | solution.py:67
  82.3 4.7 %all-to-all-start.2 = ((bf16[32,32,128]{2,1,0:T(8,128)(2,1)}), bf16[32,32,128]{2,1,0:T(8,128)(2,1)S(1)}, u32[]{:S(2)}, u32[]{:S(2)}) async-start(bf16[32,32,128]{2,1,0:T(8,128)(2,1)} %copy.190), calls=%async_computation.2 | async-start | bytes 524288 | tf_op jit(solution)/shard_map/all_to_all | solution.py:87
  87.1 11.5 %all-to-all-done.2 = bf16[32,32,128]{2,1,0:T(8,128)(2,1)S(1)} async-done(((bf16[32,32,128]{2,1,0:T(8,128)(2,1)}), bf16[32,32,128]{2,1,0:T(8,128)(2,1)S(1)}, u32[]{:S(2)}, u32[]{:S(2)}) %all-to-all-start.2) | async-done | bytes 262176 | tf_op jit(solution)/shard_map/all_to_all | solution.py:87
  99.2 1.4 copy-done.2
  101.1 1.5 %pad_maximum_fusion = bf16[8,1024,128]{2,1,0:T(8,128)(2,1)} fusion(bf16[8,512,128]{2,1,0:T(8,128)(2,1)S(1)} %copy.193, bf16[8,512,128]{2,1,0:T(8,128)(2,1)S(1)} %copy.192), kind=kLoop, calls=%fused_computation.9 | loop fusion | flops 4194304 | bytes 4194304 | tf_op jit(solution)/shard_map/concatenate | solution.py:246
  102.5 3.6 %all-to-all-start.3 = ((bf16[8,1024,128]{2,1,0:T(8,128)(2,1)}), bf16[8,1024,128]{2,1,0:T(8,128)(2,1)S(1)}, u32[]{:S(2)}, u32[]{:S(2)}) async-start(bf16[8,1024,128]{2,1,0:T(8,128)(2,1)} %pad_maximum_fusion), calls=%async_computation.3 | async-start | bytes 4194304 | tf_op jit(solution)/shard_map/all_to_all | solution.py:253
  106.9 26.4 %all-to-all-done.3 = bf16[8,1024,128]{2,1,0:T(8,128)(2,1)S(1)} async-done(((bf16[8,1024,128]{2,1,0:T(8,128)(2,1)}), bf16[8,1024,128]{2,1,0:T(8,128)(2,1)S(1)}, u32[]{:S(2)}, u32[]{:S(2)}) %all-to-all-start.3) | async-done | bytes 2097184 | tf_op jit(solution)/shard_map/all_to_all | solution.py:253
  133.3 1.5 %fusion.117 = (bf16[8,512,128]{2,1,0:T(8,128)(2,1)}, bf16[8,512,128]{2,1,0:T(8,128)(2,1)}) fusion(bf16[8,1024,128]{2,1,0:T(8,128)(2,1)S(1)} %all-to-all-done.3), kind=kLoop, calls=%fused_computation.180 | loop fusion | bytes 4194304 | tf_op jit(solution)/shard_map/slice | solution.py:255
  134.8 8.9 %shard_map.76 = (bf16[128,4096]{1,0:T(8,128)(2,1)}, bf16[128,4096]{1,0:T(8,128)(2,1)}, bf16[128,4096]{1,0:T(8,128)(2,1)}) custom-call(bf16[128,4096]{1,0:T(8,128)(2,1)} %grad_ref.1, bf16[128,4096]{1,0:T(8,128)(2,1)} %value_ref.1, bf16[128,4096]{1,0:T(8,128)(2,1)} %key_ref.1, bf16[32,128,128]{2,1,0:T(8,128)(2,1)} %bitcast.169, ...), custom_call_target="tpu_custom_call" | custom-call | tf_op jit(solution)/shard_map/pallas_call | solution.py:200
  (92 shorter events, 17.2 us)
Async XLA Ops:
  0.6 1.7 %copy-start.5 = (bf16[128,32]{0,1:T(8,128)(2,1)S(1)}, bf16[128,32]{0,1:T(8,128)(2,1)}, u32[]{:S(2)}) copy-start(bf16[128,32]{0,1:T(8,128)(2,1)} %param.15) | copy-start | bytes 24580
  0.6 1.9 %copy-start = (bf16[128,4096]{1,0:T(8,128)(2,1)S(1)}, bf16[128,4096]{1,0:T(8,128)(2,1)}, u32[]{:S(2)}) copy-start(bf16[128,4096]{1,0:T(8,128)(2,1)} %grad_ref.1) | copy-start | bytes 3145732
  6.5 1.8 %copy-start.4 = (f32[128,32]{1,0:T(8,128)}, f32[128,32]{1,0:T(8,128)S(1)}, u32[]{:S(2)}) copy-start(f32[128,32]{1,0:T(8,128)S(1)} %subtract_exponential_fusion.after_ref) | copy-start | bytes 49156
  6.6 1.8 %copy-start.1 = (bf16[128,4096]{1,0:T(8,128)(2,1)S(1)}, bf16[128,4096]{1,0:T(8,128)(2,1)}, u32[]{:S(2)}) copy-start(bf16[128,4096]{1,0:T(8,128)(2,1)} %value_ref.1) | copy-start | bytes 3145732
  8.4 1.2 copy-start.3
  11.0 32.1 %all-to-all-start = ((bf16[8,1040,128]{2,1,0:T(8,128)(2,1)}), bf16[8,1040,128]{2,1,0:T(8,128)(2,1)}, u32[]{:S(2)}, u32[]{:S(2)}) async-start(bf16[8,1040,128]{2,1,0:T(8,128)(2,1)} %fusion.1), calls=%async_computation | async-start | bytes 4259840 | tf_op jit(solution)/shard_map/all_to_all | solution.py:231
  16.0 29.8 %copy-start.10 = (pred[8,8]{1,0:T(8,128)(4,1)}, pred[8,8]{1,0:T(8,128)(4,1)S(1)}, u32[]{:S(2)}) copy-start(pred[8,8]{1,0:T(8,128)(4,1)S(1)} %get-tuple-element.83) | copy-start | bytes 196
  16.0 29.8 %copy-start.13 = (pred[8,8]{1,0:T(8,128)(4,1)}, pred[8,8]{1,0:T(8,128)(4,1)S(1)}, u32[]{:S(2)}) copy-start(pred[8,8]{1,0:T(8,128)(4,1)S(1)} %get-tuple-element.84) | copy-start | bytes 196
  49.9 13.2 %copy-start.6 = (pred[8,8,8]{2,1,0:T(8,128)(4,1)S(1)}, pred[8,8,8]{2,1,0:T(8,128)(4,1)}, u32[]{:S(2)}) copy-start(pred[8,8,8]{2,1,0:T(8,128)(4,1)} %get-tuple-element.85) | copy-start | bytes 1540
  49.9 13.2 %copy-start.7 = (pred[8,8,8]{2,1,0:T(8,128)(4,1)S(1)}, pred[8,8,8]{2,1,0:T(8,128)(4,1)}, u32[]{:S(2)}) copy-start(pred[8,8,8]{2,1,0:T(8,128)(4,1)} %get-tuple-element.86) | copy-start | bytes 1540
  49.9 13.4 %copy-start.14 = (pred[8,8]{1,0:T(8,128)(4,1)S(1)}, pred[8,8]{1,0:T(8,128)(4,1)}, u32[]{:S(2)}) copy-start(pred[8,8]{1,0:T(8,128)(4,1)} %copy-done.13) | copy-start | bytes 196
  51.8 12.3 %copy-start.11 = (pred[8,8]{1,0:T(8,128)(4,1)S(1)}, pred[8,8]{1,0:T(8,128)(4,1)}, u32[]{:S(2)}) copy-start(pred[8,8]{1,0:T(8,128)(4,1)} %copy-done.10) | copy-start | bytes 196
  51.8 26.1 %all-to-all-start.1 = ((bf16[32,48,128]{2,1,0:T(8,128)(2,1)}), bf16[32,48,128]{2,1,0:T(8,128)(2,1)S(1)}, u32[]{:S(2)}, u32[]{:S(2)}) async-start(bf16[32,48,128]{2,1,0:T(8,128)(2,1)} %pad_maximum_fusion.1), calls=%async_computation.1 | async-start | bytes 786432 | tf_op jit(solution)/shard_map/all_to_all | solution.py:66
  64.8 2.1 %copy-start.12 = (pred[8,8]{1,0:T(8,128)(4,1)S(1)}, pred[8,8]{1,0:T(8,128)(4,1)}, u32[]{:S(2)}) copy-start(pred[8,8]{1,0:T(8,128)(4,1)} %copy-done.10) | copy-start | bytes 196
  67.7 12.6 %copy-start.15 = (f32[4]{0:T(128)S(1)}, f32[4]{0:T(128)}, u32[]{:S(2)}) copy-start(f32[4]{0:T(128)} %compare_convert_fusion) | copy-start | bytes 52
  79.5 7.4 %copy-start.9 = (f32[8,4]{1,0:T(8,128)S(1)}, f32[8,4]{1,0:T(8,128)}, u32[]{:S(2)}) copy-start(f32[8,4]{1,0:T(8,128)} %get-tuple-element.75) | copy-start | bytes 388
  79.5 7.5 %copy-start.8 = (f32[8,4]{1,0:T(8,128)S(1)}, f32[8,4]{1,0:T(8,128)}, u32[]{:S(2)}) copy-start(f32[8,4]{1,0:T(8,128)} %get-tuple-element.72) | copy-start | bytes 388
  82.3 16.4 %all-to-all-start.2 = ((bf16[32,32,128]{2,1,0:T(8,128)(2,1)}), bf16[32,32,128]{2,1,0:T(8,128)(2,1)S(1)}, u32[]{:S(2)}, u32[]{:S(2)}) async-start(bf16[32,32,128]{2,1,0:T(8,128)(2,1)} %copy.190), calls=%async_computation.2 | async-start | bytes 524288 | tf_op jit(solution)/shard_map/all_to_all | solution.py:87
  99.0 1.6 %copy-start.2 = (f32[8,4,128,128]{3,0,2,1:T(8,128)S(1)}, f32[8,4,128,128]{3,0,2,1:T(8,128)}, u32[]{:S(2)}) copy-start(f32[8,4,128,128]{3,0,2,1:T(8,128)} %add_bitcast_fusion.1) | copy-start | bytes 6291460
  102.5 30.7 %all-to-all-start.3 = ((bf16[8,1024,128]{2,1,0:T(8,128)(2,1)}), bf16[8,1024,128]{2,1,0:T(8,128)(2,1)S(1)}, u32[]{:S(2)}, u32[]{:S(2)}) async-start(bf16[8,1024,128]{2,1,0:T(8,128)(2,1)} %pad_maximum_fusion), calls=%async_computation.3 | async-start | bytes 4194304 | tf_op jit(solution)/shard_map/all_to_all | solution.py:253

commit v14 on v13

--- a/solution.py
+++ b/solution.py
@@ -67,7 +67,8 @@
     got, riders = lax.optimization_barrier((got, riders))
     head = (here * share) // width
     pick = (lax.broadcasted_iota(jnp.int32, (heads,), 0) == head).astype(jnp.float32)
-    log_rows = widen(got[:, 2 * share : 2 * share + 3 * heads, 0]).reshape(peers, 3, heads)
+    log_rows = jnp.max(widen(got[:, 2 * share : 2 * share + 3 * heads, :]), axis=2)
+    log_rows = log_rows.reshape(peers, 3, heads)
     totals = jnp.sum(log_rows[:, 0] * pick[None, :], axis=1)
     totals = totals + jnp.sum(log_rows[:, 1] * pick[None, :], axis=1)
     totals = totals + jnp.sum(log_rows[:, 2] * pick[None, :], axis=1)

time: 146 us -> 144 us (0.986)
    optimization_barrier x2 -> x1, local copies, waits for them, and re-layouts: 1.64 us -> 0.1 us  [carried_both(): got, riders = lax.optimization_barrier((got, riders))]
where the time goes in v14:
time: 144 us; the launch traced here: 142 us
  waiting for transfers between devices  64.5 us (45%)
  starting transfers between devices  24.1 us (17%)
  matrix products  22.7 us (16%)
  local copies, waits for them, and re-layouts  12 us (8%)
  other arithmetic  9.12 us (6%)
  Pallas kernels  8.91 us (6%)
    all_to_all x1, waiting for transfers between devices, body(): back = lax.all_to_all(returned, 'exp', 0, 0, tiled=True)  26.4 us
    dot_general x20, matrix products, product(): jnp.einsum(form, first_op, second_op, preferred_element_type=jnp.float32)  22.5 us
    all_to_all x1, waiting for transfers between devices, body(): got = lax.all_to_all(packed, 'exp', 0, 0, tiled=True)  16.4 us
    all_to_all x1, waiting for transfers between devices, carried_both(): lax.all_to_all(jnp.concatenate([state_rows, adjoint_rows], axis=1).astype...  11.5 us
    all_to_all x1, starting transfers between devices, carried_both(): got = lax.all_to_all(payload, axis, 0, 0, tiled=True)  11.3 us
    all_to_all x1, waiting for transfers between devices, carried_both(): got = lax.all_to_all(payload, axis, 0, 0, tiled=True)  10.2 us
    pallas_call x1, Pallas kernels, finish_call(): pl.pallas_call(finish_kernel, grid=(steps,), in_specs=[flat_spec, flat_sp...  8.91 us
    all_to_all x1, starting transfers between devices, carried_both(): lax.all_to_all(jnp.concatenate([state_rows, adjoint_rows], axis=1).astype...  4.69 us
  transfers between devices with their start and end apart: 4, of which 4 were waited for; matrix products, arithmetic and copies ran while one was open for 12% of the time, Pallas kernels for 0%

profile of v14, /device:TPU:32, one launch (start us, length us, event | category | flops | bytes accessed | tf_op | source)
XLA Modules:
  0.0 142.4 jit_solution(10137496298214605510)
XLA Ops:
  0.7 1.7 %copy.273 = bf16[128,4096]{0,1:T(8,128)(2,1)S(1)} copy(bf16[128,4096]{1,0:T(8,128)(2,1)} %param.11) | data formatting | bytes 2097152 | tf_op jit(solution)/shard_map/reshape | solution.py:132
  3.0 1.6 %add_convert_fusion.2 = bf16[32,128,128]{2,1,0:T(8,128)(2,1)} fusion(f32[32,128,128]{2,1,0:T(8,128)S(1)} %fusion.10, bf16[128,32,128]{0,2,1:T(8,128)(2,1)S(1)} %bitcast.159, f32[128,32]{0,1:T(8,128)S(1)} %get-tuple-element.81, bf16[128,4096]{1,0:T(8,128)(2,1)S(1)} %copy-done), kind=kOutput, calls=%fused_computation.17 | convolution fusion | flops 137887744 | bytes 5259264 | tf_op jit(solution)/shard_map/tha,thb->hab/dot_general | solution.py:22
  4.6 1.6 %copy.272 = bf16[128,4096]{0,1:T(8,128)(2,1)S(1)} copy(bf16[128,4096]{1,0:T(8,128)(2,1)} %key_ref.1) | data formatting | bytes 2097152 | tf_op jit(solution)/shard_map/reshape | solution.py:133
  6.6 1.8 %fusion.9 = f32[32,128,128]{2,1,0:T(8,128)S(1)} fusion(bf16[128,32,128]{0,2,1:T(8,128)(2,1)S(1)} %bitcast.162, f32[128,32]{0,1:T(8,128)S(1)} %copy.221, bf16[128,4096]{1,0:T(8,128)(2,1)} %value_ref.1), kind=kOutput, calls=%fused_computation.26 | convolution fusion | flops 136314880 | bytes 4210688 | tf_op jit(solution)/shard_map/sha,shb->hab/dot_general | solution.py:22
  9.6 1.5 %fusion.1 = bf16[8,1040,128]{2,1,0:T(8,128)(2,1)} fusion(bf16[8,4,128]{2,1,0:T(4,128)(2,1)S(1)} %bitcast.183, bf16[8,512,128]{2,1,0:T(8,128)(2,1)S(1)} %bitcast.168, bf16[8,512,128]{2,1,0:T(8,128)(2,1)S(1)} %bitcast.171), kind=kLoop, calls=%fused_computation.6 | loop fusion | flops 8519680 | bytes 4235264 | tf_op jit(solution)/shard_map/concatenate | solution.py:224
  11.1 4.5 %all-to-all-start = ((bf16[8,1040,128]{2,1,0:T(8,128)(2,1)}), bf16[8,1040,128]{2,1,0:T(8,128)(2,1)}, u32[]{:S(2)}, u32[]{:S(2)}) async-start(bf16[8,1040,128]{2,1,0:T(8,128)(2,1)} %fusion.1), calls=%async_computation | async-start | bytes 4259840 | tf_op jit(solution)/shard_map/all_to_all | solution.py:232
  16.7 2.9 %multiply_convert_fusion.1 = bf16[32,128,128]{2,1,0:T(8,128)(2,1)S(1)} fusion(f32[32,128]{1,0:T(8,128)S(1)} %bitcast.181, pred[128,128]{1,0:T(8,128)(4,1)S(1)} %iota_compare_fusion.5, bf16[128,4096]{1,0:T(8,128)(2,1)S(1)} %copy-done, bf16[128,4096]{1,0:T(8,128)(2,1)} %value_ref.1), kind=kOutput, calls=%fused_computation.15 | convolution fusion | flops 136839168 | bytes 3178496 | tf_op jit(solution)/shard_map/thd,shd->hts/dot_general | solution.py:22
  19.6 2.2 %fusion.122.qp_ref = f32[32,128,128]{2,1,0:T(8,128)} fusion(bf16[32,128,128]{2,1,0:T(8,128)(2,1)S(1)} %multiply_convert_fusion.1, bf16[128,32,128]{0,2,1:T(8,128)(2,1)S(1)} %bitcast.164), kind=kOutput, calls=%fused_computation.185 | convolution fusion | flops 134217728 | bytes 4194304 | tf_op jit(solution)/shard_map/hts,shd->htd/dot_general | solution.py:22
  21.7 2.2 %fusion.123.kp_ref = f32[32,128,128]{2,1,0:T(8,128)} fusion(bf16[32,128,128]{2,1,0:T(8,128)(2,1)S(1)} %multiply_convert_fusion.1, bf16[128,32,128]{0,2,1:T(8,128)(2,1)S(1)} %bitcast.160), kind=kOutput, calls=%fused_computation.186 | convolution fusion | flops 134217728 | bytes 4194304 | tf_op jit(solution)/shard_map/hts,thd->hsd/dot_general | solution.py:22
  23.9 2.8 %fusion.4.vp_ref = f32[32,128,128]{2,1,0:T(8,128)} fusion(bf16[128,32,128]{0,2,1:T(8,128)(2,1)S(1)} %bitcast.161, bf16[128,32,128]{0,2,1:T(8,128)(2,1)S(1)} %bitcast.165, f32[32,128]{1,0:T(8,128)S(1)} %bitcast.182, pred[128,128]{1,0:T(8,128)(4,1)S(1)} %iota_compare_fusion.5, bf16[128,4096]{1,0:T(8,128)(2,1)S(1)} %copy-done), kind=kOutput, calls=%fused_computation.21 | convolution fusion | flops 271056896 | bytes 5275648 | tf_op jit(solution)/shard_map/hts,thd->hsd/dot_general | solution.py:22
  26.8 16.4 %all-to-all-done = bf16[8,1040,128]{2,1,0:T(8,128)(2,1)} async-done(((bf16[8,1040,128]{2,1,0:T(8,128)(2,1)}), bf16[8,1040,128]{2,1,0:T(8,128)(2,1)}, u32[]{:S(2)}, u32[]{:S(2)}) %all-to-all-start) | async-done | bytes 2129952 | tf_op jit(solution)/shard_map/all_to_all | solution.py:232
  44.0 1.7 %fusion.116 = (bf16[8,512,128]{2,1,0:T(8,128)(2,1)S(1)}, bf16[8,512,128]{2,1,0:T(8,128)(2,1)S(1)}) fusion(bf16[8,1040,128]{2,1,0:T(8,128)(2,1)} %all-to-all-done), kind=kLoop, calls=%fused_computation.179 | loop fusion | bytes 4194304 | tf_op jit(solution)/shard_map/slice | solution.py:234
  51.8 11.3 %all-to-all-start.1 = ((bf16[32,48,128]{2,1,0:T(8,128)(2,1)}), bf16[32,48,128]{2,1,0:T(8,128)(2,1)S(1)}, u32[]{:S(2)}, u32[]{:S(2)}) async-start(bf16[32,48,128]{2,1,0:T(8,128)(2,1)} %pad_maximum_fusion.1), calls=%async_computation.1 | async-start | bytes 786432 | tf_op jit(solution)/shard_map/all_to_all | solution.py:66
  64.8 2.1 %add_bitcast_fusion.1 = f32[8,4,128,128]{3,0,2,1:T(8,128)} fusion(f32[4,128,128,8]{2,3,1,0:T(8,128)S(1)} %fusion.45, bf16[8,4,128,128]{3,2,1,0:T(8,128)(2,1)S(1)} %bitcast.157, f32[8,8,4]{1,2,0:T(4,128)S(1)} %get-tuple-element.61, pred[8,8]{1,0:T(8,128)(4,1)S(1)} %copy-done.14), kind=kOutput, calls=%fused_computation.13 | convolution fusion | flops 8914176 | bytes 5243968 | tf_op jit(solution)/shard_map/ijh,jhab->ihab/dot_general | solution.py:22
  67.7 10.2 %all-to-all-done.1 = bf16[32,48,128]{2,1,0:T(8,128)(2,1)S(1)} async-done(((bf16[32,48,128]{2,1,0:T(8,128)(2,1)}), bf16[32,48,128]{2,1,0:T(8,128)(2,1)S(1)}, u32[]{:S(2)}, u32[]{:S(2)}) %all-to-all-start.1) | async-done | bytes 393248 | tf_op jit(solution)/shard_map/all_to_all | solution.py:66
  80.0 0.8 copy.251
  80.8 4.7 %all-to-all-start.2 = ((bf16[32,32,128]{2,1,0:T(8,128)(2,1)}), bf16[32,32,128]{2,1,0:T(8,128)(2,1)S(1)}, u32[]{:S(2)}, u32[]{:S(2)}) async-start(bf16[32,32,128]{2,1,0:T(8,128)(2,1)} %copy.251), calls=%async_computation.2 | async-start | bytes 524288 | tf_op jit(solution)/shard_map/all_to_all | solution.py:88
  85.7 11.5 %all-to-all-done.2 = bf16[32,32,128]{2,1,0:T(8,128)(2,1)S(1)} async-done(((bf16[32,32,128]{2,1,0:T(8,128)(2,1)}), bf16[32,32,128]{2,1,0:T(8,128)(2,1)S(1)}, u32[]{:S(2)}, u32[]{:S(2)}) %all-to-all-start.2) | async-done | bytes 262176 | tf_op jit(solution)/shard_map/all_to_all | solution.py:88
  97.8 1.4 copy-done.2
  99.6 1.5 %pad_maximum_fusion = bf16[8,1024,128]{2,1,0:T(8,128)(2,1)} fusion(bf16[8,512,128]{2,1,0:T(8,128)(2,1)S(1)} %copy.254, bf16[8,512,128]{2,1,0:T(8,128)(2,1)S(1)} %copy.253), kind=kLoop, calls=%fused_computation.9 | loop fusion | flops 4194304 | bytes 4194304 | tf_op jit(solution)/shard_map/concatenate | solution.py:247
  101.1 3.6 %all-to-all-start.3 = ((bf16[8,1024,128]{2,1,0:T(8,128)(2,1)}), bf16[8,1024,128]{2,1,0:T(8,128)(2,1)S(1)}, u32[]{:S(2)}, u32[]{:S(2)}) async-start(bf16[8,1024,128]{2,1,0:T(8,128)(2,1)} %pad_maximum_fusion), calls=%async_computation.3 | async-start | bytes 4194304 | tf_op jit(solution)/shard_map/all_to_all | solution.py:254
  105.5 26.4 %all-to-all-done.3 = bf16[8,1024,128]{2,1,0:T(8,128)(2,1)S(1)} async-done(((bf16[8,1024,128]{2,1,0:T(8,128)(2,1)}), bf16[8,1024,128]{2,1,0:T(8,128)(2,1)S(1)}, u32[]{:S(2)}, u32[]{:S(2)}) %all-to-all-start.3) | async-done | bytes 2097184 | tf_op jit(solution)/shard_map/all_to_all | solution.py:254
  131.9 1.5 %fusion.117 = (bf16[8,512,128]{2,1,0:T(8,128)(2,1)}, bf16[8,512,128]{2,1,0:T(8,128)(2,1)}) fusion(bf16[8,1024,128]{2,1,0:T(8,128)(2,1)S(1)} %all-to-all-done.3), kind=kLoop, calls=%fused_computation.180 | loop fusion | bytes 4194304 | tf_op jit(solution)/shard_map/slice | solution.py:256
  133.4 8.9 %shard_map.76 = (bf16[128,4096]{1,0:T(8,128)(2,1)}, bf16[128,4096]{1,0:T(8,128)(2,1)}, bf16[128,4096]{1,0:T(8,128)(2,1)}) custom-call(bf16[128,4096]{1,0:T(8,128)(2,1)} %grad_ref.1, bf16[128,4096]{1,0:T(8,128)(2,1)} %value_ref.1, bf16[128,4096]{1,0:T(8,128)(2,1)} %key_ref.1, bf16[32,128,128]{2,1,0:T(8,128)(2,1)} %bitcast.170, ...), custom_call_target="tpu_custom_call" | custom-call | tf_op jit(solution)/shard_map/pallas_call | solution.py:201
  (91 shorter events, 16.5 us)
Async XLA Ops:
  0.6 1.7 %copy-start.5 = (bf16[128,32]{0,1:T(8,128)(2,1)S(1)}, bf16[128,32]{0,1:T(8,128)(2,1)}, u32[]{:S(2)}) copy-start(bf16[128,32]{0,1:T(8,128)(2,1)} %param.15) | copy-start | bytes 24580
  0.6 1.9 %copy-start = (bf16[128,4096]{1,0:T(8,128)(2,1)S(1)}, bf16[128,4096]{1,0:T(8,128)(2,1)}, u32[]{:S(2)}) copy-start(bf16[128,4096]{1,0:T(8,128)(2,1)} %grad_ref.1) | copy-start | bytes 3145732
  6.5 1.8 %copy-start.4 = (f32[128,32]{1,0:T(8,128)}, f32[128,32]{1,0:T(8,128)S(1)}, u32[]{:S(2)}) copy-start(f32[128,32]{1,0:T(8,128)S(1)} %subtract_exponential_fusion.after_ref) | copy-start | bytes 49156
  6.6 1.8 %copy-start.1 = (bf16[128,4096]{1,0:T(8,128)(2,1)S(1)}, bf16[128,4096]{1,0:T(8,128)(2,1)}, u32[]{:S(2)}) copy-start(bf16[128,4096]{1,0:T(8,128)(2,1)} %value_ref.1) | copy-start | bytes 3145732
  8.4 1.2 copy-start.3
  11.1 32.1 %all-to-all-start = ((bf16[8,1040,128]{2,1,0:T(8,128)(2,1)}), bf16[8,1040,128]{2,1,0:T(8,128)(2,1)}, u32[]{:S(2)}, u32[]{:S(2)}) async-start(bf16[8,1040,128]{2,1,0:T(8,128)(2,1)} %fusion.1), calls=%async_computation | async-start | bytes 4259840 | tf_op jit(solution)/shard_map/all_to_all | solution.py:232
  16.0 29.8 %copy-start.10 = (pred[8,8]{1,0:T(8,128)(4,1)}, pred[8,8]{1,0:T(8,128)(4,1)S(1)}, u32[]{:S(2)}) copy-start(pred[8,8]{1,0:T(8,128)(4,1)S(1)} %get-tuple-element.83) | copy-start | bytes 196
  16.0 29.8 %copy-start.13 = (pred[8,8]{1,0:T(8,128)(4,1)}, pred[8,8]{1,0:T(8,128)(4,1)S(1)}, u32[]{:S(2)}) copy-start(pred[8,8]{1,0:T(8,128)(4,1)S(1)} %get-tuple-element.84) | copy-start | bytes 196
  49.9 13.2 %copy-start.6 = (pred[8,8,8]{2,1,0:T(8,128)(4,1)S(1)}, pred[8,8,8]{2,1,0:T(8,128)(4,1)}, u32[]{:S(2)}) copy-start(pred[8,8,8]{2,1,0:T(8,128)(4,1)} %get-tuple-element.85) | copy-start | bytes 1540
  49.9 13.2 %copy-start.7 = (pred[8,8,8]{2,1,0:T(8,128)(4,1)S(1)}, pred[8,8,8]{2,1,0:T(8,128)(4,1)}, u32[]{:S(2)}) copy-start(pred[8,8,8]{2,1,0:T(8,128)(4,1)} %get-tuple-element.86) | copy-start | bytes 1540
  49.9 13.4 %copy-start.14 = (pred[8,8]{1,0:T(8,128)(4,1)S(1)}, pred[8,8]{1,0:T(8,128)(4,1)}, u32[]{:S(2)}) copy-start(pred[8,8]{1,0:T(8,128)(4,1)} %copy-done.13) | copy-start | bytes 196
  51.8 12.3 %copy-start.11 = (pred[8,8]{1,0:T(8,128)(4,1)S(1)}, pred[8,8]{1,0:T(8,128)(4,1)}, u32[]{:S(2)}) copy-start(pred[8,8]{1,0:T(8,128)(4,1)} %copy-done.10) | copy-start | bytes 196
  51.8 26.1 %all-to-all-start.1 = ((bf16[32,48,128]{2,1,0:T(8,128)(2,1)}), bf16[32,48,128]{2,1,0:T(8,128)(2,1)S(1)}, u32[]{:S(2)}, u32[]{:S(2)}) async-start(bf16[32,48,128]{2,1,0:T(8,128)(2,1)} %pad_maximum_fusion.1), calls=%async_computation.1 | async-start | bytes 786432 | tf_op jit(solution)/shard_map/all_to_all | solution.py:66
  64.8 2.2 %copy-start.12 = (pred[8,8]{1,0:T(8,128)(4,1)S(1)}, pred[8,8]{1,0:T(8,128)(4,1)}, u32[]{:S(2)}) copy-start(pred[8,8]{1,0:T(8,128)(4,1)} %copy-done.10) | copy-start | bytes 196
  67.7 17.8 %copy-start.9 = (f32[8,4]{1,0:T(8,128)S(1)}, f32[8,4]{1,0:T(8,128)}, u32[]{:S(2)}) copy-start(f32[8,4]{1,0:T(8,128)} %get-tuple-element.75) | copy-start | bytes 388
  67.7 17.9 %copy-start.8 = (f32[8,4]{1,0:T(8,128)S(1)}, f32[8,4]{1,0:T(8,128)}, u32[]{:S(2)}) copy-start(f32[8,4]{1,0:T(8,128)} %get-tuple-element.72) | copy-start | bytes 388
  80.8 16.4 %all-to-all-start.2 = ((bf16[32,32,128]{2,1,0:T(8,128)(2,1)}), bf16[32,32,128]{2,1,0:T(8,128)(2,1)S(1)}, u32[]{:S(2)}, u32[]{:S(2)}) async-start(bf16[32,32,128]{2,1,0:T(8,128)(2,1)} %copy.251), calls=%async_computation.2 | async-start | bytes 524288 | tf_op jit(solution)/shard_map/all_to_all | solution.py:88
  97.6 1.6 %copy-start.2 = (f32[8,4,128,128]{3,0,2,1:T(8,128)S(1)}, f32[8,4,128,128]{3,0,2,1:T(8,128)}, u32[]{:S(2)}) copy-start(f32[8,4,128,128]{3,0,2,1:T(8,128)} %add_bitcast_fusion.1) | copy-start | bytes 6291460
  101.1 30.7 %all-to-all-start.3 = ((bf16[8,1024,128]{2,1,0:T(8,128)(2,1)}), bf16[8,1024,128]{2,1,0:T(8,128)(2,1)S(1)}, u32[]{:S(2)}, u32[]{:S(2)}) async-start(bf16[8,1024,128]{2,1,0:T(8,128)(2,1)} %pad_maximum_fusion), calls=%async_computation.3 | async-start | bytes 4194304 | tf_op jit(solution)/shard_map/all_to_all | solution.py:254

commit v15 on v14

--- a/solution.py
+++ b/solution.py
@@ -37,11 +37,11 @@
 
 
 def pieces_of(array):
-    high = array.astype(jnp.bfloat16)
-    rest = array - widen(high)
-    mid = rest.astype(jnp.bfloat16)
-    low = (rest - widen(mid)).astype(jnp.bfloat16)
-    return high, mid, low
+    high = lax.reduce_precision(array, exponent_bits=8, mantissa_bits=7)
+    rest = array - high
+    mid = lax.reduce_precision(rest, exponent_bits=8, mantissa_bits=7)
+    low = (rest - mid).astype(jnp.bfloat16)
+    return high.astype(jnp.bfloat16), mid.astype(jnp.bfloat16), low
 
 
 def carried_both(dev_log, dev_state, dev_adjoint, axis, riders):

time: 144 us -> 144 us (level)
  no operation moved by 1% of the time
where the time goes in v15:
time: 144 us; the launch traced here: 142 us
  waiting for transfers between devices  64.5 us (45%)
  starting transfers between devices  24.1 us (17%)
  matrix products  22.7 us (16%)
  local copies, waits for them, and re-layouts  12 us (8%)
  other arithmetic  9.12 us (6%)
  Pallas kernels  8.91 us (6%)
    all_to_all x1, waiting for transfers between devices, body(): back = lax.all_to_all(returned, 'exp', 0, 0, tiled=True)  26.4 us
    dot_general x20, matrix products, product(): jnp.einsum(form, first_op, second_op, preferred_element_type=jnp.float32)  22.5 us
    all_to_all x1, waiting for transfers between devices, body(): got = lax.all_to_all(packed, 'exp', 0, 0, tiled=True)  16.4 us
    all_to_all x1, waiting for transfers between devices, carried_both(): lax.all_to_all(jnp.concatenate([state_rows, adjoint_rows], axis=1).astype...  11.5 us
    all_to_all x1, starting transfers between devices, carried_both(): got = lax.all_to_all(payload, axis, 0, 0, tiled=True)  11.3 us
    all_to_all x1, waiting for transfers between devices, carried_both(): got = lax.all_to_all(payload, axis, 0, 0, tiled=True)  10.2 us
    pallas_call x1, Pallas kernels, finish_call(): pl.pallas_call(finish_kernel, grid=(steps,), in_specs=[flat_spec, flat_sp...  8.91 us
    all_to_all x1, starting transfers between devices, carried_both(): lax.all_to_all(jnp.concatenate([state_rows, adjoint_rows], axis=1).astype...  4.69 us
  transfers between devices with their start and end apart: 4, of which 4 were waited for; matrix products, arithmetic and copies ran while one was open for 12% of the time, Pallas kernels for 0%

profile of v15, /device:TPU:32, one launch (start us, length us, event | category | flops | bytes accessed | tf_op | source)
XLA Modules:
  0.0 142.4 jit_solution(15850117173021408279)
XLA Ops:
  0.7 1.7 %copy.273 = bf16[128,4096]{0,1:T(8,128)(2,1)S(1)} copy(bf16[128,4096]{1,0:T(8,128)(2,1)} %param.11) | data formatting | bytes 2097152 | tf_op jit(solution)/shard_map/reshape | solution.py:132
  3.0 1.6 %add_convert_fusion.2 = bf16[32,128,128]{2,1,0:T(8,128)(2,1)} fusion(f32[32,128,128]{2,1,0:T(8,128)S(1)} %fusion.10, bf16[128,32,128]{0,2,1:T(8,128)(2,1)S(1)} %bitcast.159, f32[128,32]{0,1:T(8,128)S(1)} %get-tuple-element.81, bf16[128,4096]{1,0:T(8,128)(2,1)S(1)} %copy-done), kind=kOutput, calls=%fused_computation.17 | convolution fusion | flops 137887744 | bytes 5259264 | tf_op jit(solution)/shard_map/tha,thb->hab/dot_general | solution.py:22
  4.6 1.6 %copy.272 = bf16[128,4096]{0,1:T(8,128)(2,1)S(1)} copy(bf16[128,4096]{1,0:T(8,128)(2,1)} %key_ref.1) | data formatting | bytes 2097152 | tf_op jit(solution)/shard_map/reshape | solution.py:133
  6.6 1.8 %fusion.9 = f32[32,128,128]{2,1,0:T(8,128)S(1)} fusion(bf16[128,32,128]{0,2,1:T(8,128)(2,1)S(1)} %bitcast.162, f32[128,32]{0,1:T(8,128)S(1)} %copy.221, bf16[128,4096]{1,0:T(8,128)(2,1)} %value_ref.1), kind=kOutput, calls=%fused_computation.26 | convolution fusion | flops 136314880 | bytes 4210688 | tf_op jit(solution)/shard_map/sha,shb->hab/dot_general | solution.py:22
  9.6 1.5 %fusion.1 = bf16[8,1040,128]{2,1,0:T(8,128)(2,1)} fusion(bf16[8,4,128]{2,1,0:T(4,128)(2,1)S(1)} %bitcast.183, bf16[8,512,128]{2,1,0:T(8,128)(2,1)S(1)} %bitcast.168, bf16[8,512,128]{2,1,0:T(8,128)(2,1)S(1)} %bitcast.171), kind=kLoop, calls=%fused_computation.6 | loop fusion | flops 8519680 | bytes 4235264 | tf_op jit(solution)/shard_map/concatenate | solution.py:224
  11.1 4.5 %all-to-all-start = ((bf16[8,1040,128]{2,1,0:T(8,128)(2,1)}), bf16[8,1040,128]{2,1,0:T(8,128)(2,1)}, u32[]{:S(2)}, u32[]{:S(2)}) async-start(bf16[8,1040,128]{2,1,0:T(8,128)(2,1)} %fusion.1), calls=%async_computation | async-start | bytes 4259840 | tf_op jit(solution)/shard_map/all_to_all | solution.py:232
  16.7 2.9 %multiply_convert_fusion.1 = bf16[32,128,128]{2,1,0:T(8,128)(2,1)S(1)} fusion(f32[32,128]{1,0:T(8,128)S(1)} %bitcast.181, pred[128,128]{1,0:T(8,128)(4,1)S(1)} %iota_compare_fusion.5, bf16[128,4096]{1,0:T(8,128)(2,1)S(1)} %copy-done, bf16[128,4096]{1,0:T(8,128)(2,1)} %value_ref.1), kind=kOutput, calls=%fused_computation.15 | convolution fusion | flops 136839168 | bytes 3178496 | tf_op jit(solution)/shard_map/thd,shd->hts/dot_general | solution.py:22
  19.6 2.2 %fusion.122.qp_ref = f32[32,128,128]{2,1,0:T(8,128)} fusion(bf16[32,128,128]{2,1,0:T(8,128)(2,1)S(1)} %multiply_convert_fusion.1, bf16[128,32,128]{0,2,1:T(8,128)(2,1)S(1)} %bitcast.164), kind=kOutput, calls=%fused_computation.187 | convolution fusion | flops 134217728 | bytes 4194304 | tf_op jit(solution)/shard_map/hts,shd->htd/dot_general | solution.py:22
  21.7 2.2 %fusion.123.kp_ref = f32[32,128,128]{2,1,0:T(8,128)} fusion(bf16[32,128,128]{2,1,0:T(8,128)(2,1)S(1)} %multiply_convert_fusion.1, bf16[128,32,128]{0,2,1:T(8,128)(2,1)S(1)} %bitcast.160), kind=kOutput, calls=%fused_computation.188 | convolution fusion | flops 134217728 | bytes 4194304 | tf_op jit(solution)/shard_map/hts,thd->hsd/dot_general | solution.py:22
  23.9 2.8 %fusion.4.vp_ref = f32[32,128,128]{2,1,0:T(8,128)} fusion(bf16[128,32,128]{0,2,1:T(8,128)(2,1)S(1)} %bitcast.161, bf16[128,32,128]{0,2,1:T(8,128)(2,1)S(1)} %bitcast.165, f32[32,128]{1,0:T(8,128)S(1)} %bitcast.182, pred[128,128]{1,0:T(8,128)(4,1)S(1)} %iota_compare_fusion.5, bf16[128,4096]{1,0:T(8,128)(2,1)S(1)} %copy-done), kind=kOutput, calls=%fused_computation.21 | convolution fusion | flops 271056896 | bytes 5275648 | tf_op jit(solution)/shard_map/hts,thd->hsd/dot_general | solution.py:22
  26.8 16.4 %all-to-all-done = bf16[8,1040,128]{2,1,0:T(8,128)(2,1)} async-done(((bf16[8,1040,128]{2,1,0:T(8,128)(2,1)}), bf16[8,1040,128]{2,1,0:T(8,128)(2,1)}, u32[]{:S(2)}, u32[]{:S(2)}) %all-to-all-start) | async-done | bytes 2129952 | tf_op jit(solution)/shard_map/all_to_all | solution.py:232
  44.0 1.7 %fusion.116 = (bf16[8,512,128]{2,1,0:T(8,128)(2,1)S(1)}, bf16[8,512,128]{2,1,0:T(8,128)(2,1)S(1)}) fusion(bf16[8,1040,128]{2,1,0:T(8,128)(2,1)} %all-to-all-done), kind=kLoop, calls=%fused_computation.181 | loop fusion | bytes 4194304 | tf_op jit(solution)/shard_map/slice | solution.py:234
  51.8 11.3 %all-to-all-start.1 = ((bf16[32,48,128]{2,1,0:T(8,128)(2,1)}), bf16[32,48,128]{2,1,0:T(8,128)(2,1)S(1)}, u32[]{:S(2)}, u32[]{:S(2)}) async-start(bf16[32,48,128]{2,1,0:T(8,128)(2,1)} %pad_maximum_fusion.1), calls=%async_computation.1 | async-start | bytes 786432 | tf_op jit(solution)/shard_map/all_to_all | solution.py:66
  64.8 2.1 %add_bitcast_fusion.1 = f32[8,4,128,128]{3,0,2,1:T(8,128)} fusion(f32[4,128,128,8]{2,3,1,0:T(8,128)S(1)} %fusion.45, bf16[8,4,128,128]{3,2,1,0:T(8,128)(2,1)S(1)} %bitcast.157, f32[8,8,4]{1,2,0:T(4,128)S(1)} %get-tuple-element.61, pred[8,8]{1,0:T(8,128)(4,1)S(1)} %copy-done.14), kind=kOutput, calls=%fused_computation.13 | convolution fusion | flops 8914176 | bytes 5243968 | tf_op jit(solution)/shard_map/ijh,jhab->ihab/dot_general | solution.py:22
  67.7 10.2 %all-to-all-done.1 = bf16[32,48,128]{2,1,0:T(8,128)(2,1)S(1)} async-done(((bf16[32,48,128]{2,1,0:T(8,128)(2,1)}), bf16[32,48,128]{2,1,0:T(8,128)(2,1)S(1)}, u32[]{:S(2)}, u32[]{:S(2)}) %all-to-all-start.1) | async-done | bytes 393248 | tf_op jit(solution)/shard_map/all_to_all | solution.py:66
  80.0 0.8 copy.251
  80.8 4.7 %all-to-all-start.2 = ((bf16[32,32,128]{2,1,0:T(8,128)(2,1)}), bf16[32,32,128]{2,1,0:T(8,128)(2,1)S(1)}, u32[]{:S(2)}, u32[]{:S(2)}) async-start(bf16[32,32,128]{2,1,0:T(8,128)(2,1)} %copy.251), calls=%async_computation.2 | async-start | bytes 524288 | tf_op jit(solution)/shard_map/all_to_all | solution.py:88
  85.7 11.5 %all-to-all-done.2 = bf16[32,32,128]{2,1,0:T(8,128)(2,1)S(1)} async-done(((bf16[32,32,128]{2,1,0:T(8,128)(2,1)}), bf16[32,32,128]{2,1,0:T(8,128)(2,1)S(1)}, u32[]{:S(2)}, u32[]{:S(2)}) %all-to-all-start.2) | async-done | bytes 262176 | tf_op jit(solution)/shard_map/all_to_all | solution.py:88
  97.8 1.4 copy-done.2
  99.6 1.5 %pad_maximum_fusion = bf16[8,1024,128]{2,1,0:T(8,128)(2,1)} fusion(bf16[8,512,128]{2,1,0:T(8,128)(2,1)S(1)} %copy.254, bf16[8,512,128]{2,1,0:T(8,128)(2,1)S(1)} %copy.253), kind=kLoop, calls=%fused_computation.9 | loop fusion | flops 4194304 | bytes 4194304 | tf_op jit(solution)/shard_map/concatenate | solution.py:247
  101.1 3.6 %all-to-all-start.3 = ((bf16[8,1024,128]{2,1,0:T(8,128)(2,1)}), bf16[8,1024,128]{2,1,0:T(8,128)(2,1)S(1)}, u32[]{:S(2)}, u32[]{:S(2)}) async-start(bf16[8,1024,128]{2,1,0:T(8,128)(2,1)} %pad_maximum_fusion), calls=%async_computation.3 | async-start | bytes 4194304 | tf_op jit(solution)/shard_map/all_to_all | solution.py:254
  105.5 26.4 %all-to-all-done.3 = bf16[8,1024,128]{2,1,0:T(8,128)(2,1)S(1)} async-done(((bf16[8,1024,128]{2,1,0:T(8,128)(2,1)}), bf16[8,1024,128]{2,1,0:T(8,128)(2,1)S(1)}, u32[]{:S(2)}, u32[]{:S(2)}) %all-to-all-start.3) | async-done | bytes 2097184 | tf_op jit(solution)/shard_map/all_to_all | solution.py:254
  131.9 1.5 %fusion.117 = (bf16[8,512,128]{2,1,0:T(8,128)(2,1)}, bf16[8,512,128]{2,1,0:T(8,128)(2,1)}) fusion(bf16[8,1024,128]{2,1,0:T(8,128)(2,1)S(1)} %all-to-all-done.3), kind=kLoop, calls=%fused_computation.182 | loop fusion | bytes 4194304 | tf_op jit(solution)/shard_map/slice | solution.py:256
  133.4 8.9 %shard_map.76 = (bf16[128,4096]{1,0:T(8,128)(2,1)}, bf16[128,4096]{1,0:T(8,128)(2,1)}, bf16[128,4096]{1,0:T(8,128)(2,1)}) custom-call(bf16[128,4096]{1,0:T(8,128)(2,1)} %grad_ref.1, bf16[128,4096]{1,0:T(8,128)(2,1)} %value_ref.1, bf16[128,4096]{1,0:T(8,128)(2,1)} %key_ref.1, bf16[32,128,128]{2,1,0:T(8,128)(2,1)} %bitcast.170, ...), custom_call_target="tpu_custom_call" | custom-call | tf_op jit(solution)/shard_map/pallas_call | solution.py:201
  (91 shorter events, 16.5 us)
Async XLA Ops:
  0.6 1.7 %copy-start.5 = (bf16[128,32]{0,1:T(8,128)(2,1)S(1)}, bf16[128,32]{0,1:T(8,128)(2,1)}, u32[]{:S(2)}) copy-start(bf16[128,32]{0,1:T(8,128)(2,1)} %param.15) | copy-start | bytes 24580
  0.6 1.9 %copy-start = (bf16[128,4096]{1,0:T(8,128)(2,1)S(1)}, bf16[128,4096]{1,0:T(8,128)(2,1)}, u32[]{:S(2)}) copy-start(bf16[128,4096]{1,0:T(8,128)(2,1)} %grad_ref.1) | copy-start | bytes 3145732
  6.5 1.8 %copy-start.4 = (f32[128,32]{1,0:T(8,128)}, f32[128,32]{1,0:T(8,128)S(1)}, u32[]{:S(2)}) copy-start(f32[128,32]{1,0:T(8,128)S(1)} %subtract_exponential_fusion.after_ref) | copy-start | bytes 49156
  6.6 1.8 %copy-start.1 = (bf16[128,4096]{1,0:T(8,128)(2,1)S(1)}, bf16[128,4096]{1,0:T(8,128)(2,1)}, u32[]{:S(2)}) copy-start(bf16[128,4096]{1,0:T(8,128)(2,1)} %value_ref.1) | copy-start | bytes 3145732
  8.4 1.2 copy-start.3
  11.1 32.1 %all-to-all-start = ((bf16[8,1040,128]{2,1,0:T(8,128)(2,1)}), bf16[8,1040,128]{2,1,0:T(8,128)(2,1)}, u32[]{:S(2)}, u32[]{:S(2)}) async-start(bf16[8,1040,128]{2,1,0:T(8,128)(2,1)} %fusion.1), calls=%async_computation | async-start | bytes 4259840 | tf_op jit(solution)/shard_map/all_to_all | solution.py:232
  16.0 29.8 %copy-start.10 = (pred[8,8]{1,0:T(8,128)(4,1)}, pred[8,8]{1,0:T(8,128)(4,1)S(1)}, u32[]{:S(2)}) copy-start(pred[8,8]{1,0:T(8,128)(4,1)S(1)} %get-tuple-element.83) | copy-start | bytes 196
  16.0 29.8 %copy-start.13 = (pred[8,8]{1,0:T(8,128)(4,1)}, pred[8,8]{1,0:T(8,128)(4,1)S(1)}, u32[]{:S(2)}) copy-start(pred[8,8]{1,0:T(8,128)(4,1)S(1)} %get-tuple-element.84) | copy-start | bytes 196
  49.9 13.2 %copy-start.6 = (pred[8,8,8]{2,1,0:T(8,128)(4,1)S(1)}, pred[8,8,8]{2,1,0:T(8,128)(4,1)}, u32[]{:S(2)}) copy-start(pred[8,8,8]{2,1,0:T(8,128)(4,1)} %get-tuple-element.85) | copy-start | bytes 1540
  49.9 13.2 %copy-start.7 = (pred[8,8,8]{2,1,0:T(8,128)(4,1)S(1)}, pred[8,8,8]{2,1,0:T(8,128)(4,1)}, u32[]{:S(2)}) copy-start(pred[8,8,8]{2,1,0:T(8,128)(4,1)} %get-tuple-element.86) | copy-start | bytes 1540
  49.9 13.4 %copy-start.14 = (pred[8,8]{1,0:T(8,128)(4,1)S(1)}, pred[8,8]{1,0:T(8,128)(4,1)}, u32[]{:S(2)}) copy-start(pred[8,8]{1,0:T(8,128)(4,1)} %copy-done.13) | copy-start | bytes 196
  51.8 12.3 %copy-start.11 = (pred[8,8]{1,0:T(8,128)(4,1)S(1)}, pred[8,8]{1,0:T(8,128)(4,1)}, u32[]{:S(2)}) copy-start(pred[8,8]{1,0:T(8,128)(4,1)} %copy-done.10) | copy-start | bytes 196
  51.8 26.1 %all-to-all-start.1 = ((bf16[32,48,128]{2,1,0:T(8,128)(2,1)}), bf16[32,48,128]{2,1,0:T(8,128)(2,1)S(1)}, u32[]{:S(2)}, u32[]{:S(2)}) async-start(bf16[32,48,128]{2,1,0:T(8,128)(2,1)} %pad_maximum_fusion.1), calls=%async_computation.1 | async-start | bytes 786432 | tf_op jit(solution)/shard_map/all_to_all | solution.py:66
  64.8 2.2 %copy-start.12 = (pred[8,8]{1,0:T(8,128)(4,1)S(1)}, pred[8,8]{1,0:T(8,128)(4,1)}, u32[]{:S(2)}) copy-start(pred[8,8]{1,0:T(8,128)(4,1)} %copy-done.10) | copy-start | bytes 196
  67.7 17.8 %copy-start.9 = (f32[8,4]{1,0:T(8,128)S(1)}, f32[8,4]{1,0:T(8,128)}, u32[]{:S(2)}) copy-start(f32[8,4]{1,0:T(8,128)} %get-tuple-element.75) | copy-start | bytes 388
  67.7 17.9 %copy-start.8 = (f32[8,4]{1,0:T(8,128)S(1)}, f32[8,4]{1,0:T(8,128)}, u32[]{:S(2)}) copy-start(f32[8,4]{1,0:T(8,128)} %get-tuple-element.72) | copy-start | bytes 388
  80.8 16.4 %all-to-all-start.2 = ((bf16[32,32,128]{2,1,0:T(8,128)(2,1)}), bf16[32,32,128]{2,1,0:T(8,128)(2,1)S(1)}, u32[]{:S(2)}, u32[]{:S(2)}) async-start(bf16[32,32,128]{2,1,0:T(8,128)(2,1)} %copy.251), calls=%async_computation.2 | async-start | bytes 524288 | tf_op jit(solution)/shard_map/all_to_all | solution.py:88
  97.6 1.6 %copy-start.2 = (f32[8,4,128,128]{3,0,2,1:T(8,128)S(1)}, f32[8,4,128,128]{3,0,2,1:T(8,128)}, u32[]{:S(2)}) copy-start(f32[8,4,128,128]{3,0,2,1:T(8,128)} %add_bitcast_fusion.1) | copy-start | bytes 6291460
  101.1 30.7 %all-to-all-start.3 = ((bf16[8,1024,128]{2,1,0:T(8,128)(2,1)}), bf16[8,1024,128]{2,1,0:T(8,128)(2,1)S(1)}, u32[]{:S(2)}, u32[]{:S(2)}) async-start(bf16[8,1024,128]{2,1,0:T(8,128)(2,1)} %pad_maximum_fusion), calls=%async_computation.3 | async-start | bytes 4194304 | tf_op jit(solution)/shard_map/all_to_all | solution.py:254

commit v16 on v15

--- a/solution.py
+++ b/solution.py
@@ -191,7 +191,7 @@
 def finish_call(out_grad, values, keys, state_in, adjoint_in, qp, kp, vp, before, after):
     length, columns = out_grad.shape
     heads, width = state_in.shape[0], state_in.shape[2]
-    group = 4
+    group = 8
     steps = heads // group
     flat_spec = pl.BlockSpec((length, group * width), lambda h: (0, h))
     head_spec = pl.BlockSpec((group, width, width), lambda h: (h, 0, 0))

time: 144 us -> 142 us (0.986)
  Pallas kernels: 8.91 us -> 7.33 us
    pallas_call x1, Pallas kernels: 8.91 us -> 7.33 us  [finish_call(): pl.pallas_call(finish_kernel, grid=(steps,), in_specs=[flat_spec, flat_sp...]
where the time goes in v16:
time: 142 us; the launch traced here: 141 us
  waiting for transfers between devices  64.5 us (45%)
  starting transfers between devices  24.1 us (17%)
  matrix products  22.7 us (16%)
  local copies, waits for them, and re-layouts  12 us (8%)
  other arithmetic  9.12 us (6%)
  Pallas kernels  7.33 us (5%)
    all_to_all x1, waiting for transfers between devices, body(): back = lax.all_to_all(returned, 'exp', 0, 0, tiled=True)  26.4 us
    dot_general x20, matrix products, product(): jnp.einsum(form, first_op, second_op, preferred_element_type=jnp.float32)  22.5 us
    all_to_all x1, waiting for transfers between devices, body(): got = lax.all_to_all(packed, 'exp', 0, 0, tiled=True)  16.4 us
    all_to_all x1, waiting for transfers between devices, carried_both(): lax.all_to_all(jnp.concatenate([state_rows, adjoint_rows], axis=1).astype...  11.5 us
    all_to_all x1, starting transfers between devices, carried_both(): got = lax.all_to_all(payload, axis, 0, 0, tiled=True)  11.3 us
    all_to_all x1, waiting for transfers between devices, carried_both(): got = lax.all_to_all(payload, axis, 0, 0, tiled=True)  10.2 us
    pallas_call x1, Pallas kernels, finish_call(): pl.pallas_call(finish_kernel, grid=(steps,), in_specs=[flat_spec, flat_sp...  7.33 us
    all_to_all x1, starting transfers between devices, carried_both(): lax.all_to_all(jnp.concatenate([state_rows, adjoint_rows], axis=1).astype...  4.69 us
  transfers between devices with their start and end apart: 4, of which 4 were waited for; matrix products, arithmetic and copies ran while one was open for 12% of the time, Pallas kernels for 0%

profile of v16, /device:TPU:32, one launch (start us, length us, event | category | flops | bytes accessed | tf_op | source)
XLA Modules:
  0.0 140.8 jit_solution(8295967091493622262)
XLA Ops:
  0.7 1.7 %copy.273 = bf16[128,4096]{0,1:T(8,128)(2,1)S(1)} copy(bf16[128,4096]{1,0:T(8,128)(2,1)} %param.11) | data formatting | bytes 2097152 | tf_op jit(solution)/shard_map/reshape | solution.py:132
  3.0 1.6 %add_convert_fusion.2 = bf16[32,128,128]{2,1,0:T(8,128)(2,1)} fusion(f32[32,128,128]{2,1,0:T(8,128)S(1)} %fusion.10, bf16[128,32,128]{0,2,1:T(8,128)(2,1)S(1)} %bitcast.159, f32[128,32]{0,1:T(8,128)S(1)} %get-tuple-element.81, bf16[128,4096]{1,0:T(8,128)(2,1)S(1)} %copy-done), kind=kOutput, calls=%fused_computation.17 | convolution fusion | flops 137887744 | bytes 5259264 | tf_op jit(solution)/shard_map/tha,thb->hab/dot_general | solution.py:22
  4.6 1.6 %copy.272 = bf16[128,4096]{0,1:T(8,128)(2,1)S(1)} copy(bf16[128,4096]{1,0:T(8,128)(2,1)} %key_ref.1) | data formatting | bytes 2097152 | tf_op jit(solution)/shard_map/reshape | solution.py:133
  6.6 1.8 %fusion.9 = f32[32,128,128]{2,1,0:T(8,128)S(1)} fusion(bf16[128,32,128]{0,2,1:T(8,128)(2,1)S(1)} %bitcast.162, f32[128,32]{0,1:T(8,128)S(1)} %copy.221, bf16[128,4096]{1,0:T(8,128)(2,1)} %value_ref.1), kind=kOutput, calls=%fused_computation.26 | convolution fusion | flops 136314880 | bytes 4210688 | tf_op jit(solution)/shard_map/sha,shb->hab/dot_general | solution.py:22
  9.6 1.5 %fusion.1 = bf16[8,1040,128]{2,1,0:T(8,128)(2,1)} fusion(bf16[8,4,128]{2,1,0:T(4,128)(2,1)S(1)} %bitcast.183, bf16[8,512,128]{2,1,0:T(8,128)(2,1)S(1)} %bitcast.168, bf16[8,512,128]{2,1,0:T(8,128)(2,1)S(1)} %bitcast.171), kind=kLoop, calls=%fused_computation.6 | loop fusion | flops 8519680 | bytes 4235264 | tf_op jit(solution)/shard_map/concatenate | solution.py:224
  11.1 4.5 %all-to-all-start = ((bf16[8,1040,128]{2,1,0:T(8,128)(2,1)}), bf16[8,1040,128]{2,1,0:T(8,128)(2,1)}, u32[]{:S(2)}, u32[]{:S(2)}) async-start(bf16[8,1040,128]{2,1,0:T(8,128)(2,1)} %fusion.1), calls=%async_computation | async-start | bytes 4259840 | tf_op jit(solution)/shard_map/all_to_all | solution.py:232
  16.7 2.9 %multiply_convert_fusion.1 = bf16[32,128,128]{2,1,0:T(8,128)(2,1)S(1)} fusion(f32[32,128]{1,0:T(8,128)S(1)} %bitcast.181, pred[128,128]{1,0:T(8,128)(4,1)S(1)} %iota_compare_fusion.5, bf16[128,4096]{1,0:T(8,128)(2,1)S(1)} %copy-done, bf16[128,4096]{1,0:T(8,128)(2,1)} %value_ref.1), kind=kOutput, calls=%fused_computation.15 | convolution fusion | flops 136839168 | bytes 3178496 | tf_op jit(solution)/shard_map/thd,shd->hts/dot_general | solution.py:22
  19.6 2.2 %fusion.122.qp_ref = f32[32,128,128]{2,1,0:T(8,128)} fusion(bf16[32,128,128]{2,1,0:T(8,128)(2,1)S(1)} %multiply_convert_fusion.1, bf16[128,32,128]{0,2,1:T(8,128)(2,1)S(1)} %bitcast.164), kind=kOutput, calls=%fused_computation.187 | convolution fusion | flops 134217728 | bytes 4194304 | tf_op jit(solution)/shard_map/hts,shd->htd/dot_general | solution.py:22
  21.7 2.2 %fusion.123.kp_ref = f32[32,128,128]{2,1,0:T(8,128)} fusion(bf16[32,128,128]{2,1,0:T(8,128)(2,1)S(1)} %multiply_convert_fusion.1, bf16[128,32,128]{0,2,1:T(8,128)(2,1)S(1)} %bitcast.160), kind=kOutput, calls=%fused_computation.188 | convolution fusion | flops 134217728 | bytes 4194304 | tf_op jit(solution)/shard_map/hts,thd->hsd/dot_general | solution.py:22
  23.9 2.8 %fusion.4.vp_ref = f32[32,128,128]{2,1,0:T(8,128)} fusion(bf16[128,32,128]{0,2,1:T(8,128)(2,1)S(1)} %bitcast.161, bf16[128,32,128]{0,2,1:T(8,128)(2,1)S(1)} %bitcast.165, f32[32,128]{1,0:T(8,128)S(1)} %bitcast.182, pred[128,128]{1,0:T(8,128)(4,1)S(1)} %iota_compare_fusion.5, bf16[128,4096]{1,0:T(8,128)(2,1)S(1)} %copy-done), kind=kOutput, calls=%fused_computation.21 | convolution fusion | flops 271056896 | bytes 5275648 | tf_op jit(solution)/shard_map/hts,thd->hsd/dot_general | solution.py:22
  26.8 16.4 %all-to-all-done = bf16[8,1040,128]{2,1,0:T(8,128)(2,1)} async-done(((bf16[8,1040,128]{2,1,0:T(8,128)(2,1)}), bf16[8,1040,128]{2,1,0:T(8,128)(2,1)}, u32[]{:S(2)}, u32[]{:S(2)}) %all-to-all-start) | async-done | bytes 2129952 | tf_op jit(solution)/shard_map/all_to_all | solution.py:232
  44.0 1.7 %fusion.116 = (bf16[8,512,128]{2,1,0:T(8,128)(2,1)S(1)}, bf16[8,512,128]{2,1,0:T(8,128)(2,1)S(1)}) fusion(bf16[8,1040,128]{2,1,0:T(8,128)(2,1)} %all-to-all-done), kind=kLoop, calls=%fused_computation.181 | loop fusion | bytes 4194304 | tf_op jit(solution)/shard_map/slice | solution.py:234
  51.8 11.3 %all-to-all-start.1 = ((bf16[32,48,128]{2,1,0:T(8,128)(2,1)}), bf16[32,48,128]{2,1,0:T(8,128)(2,1)S(1)}, u32[]{:S(2)}, u32[]{:S(2)}) async-start(bf16[32,48,128]{2,1,0:T(8,128)(2,1)} %pad_maximum_fusion.1), calls=%async_computation.1 | async-start | bytes 786432 | tf_op jit(solution)/shard_map/all_to_all | solution.py:66
  64.8 2.1 %add_bitcast_fusion.1 = f32[8,4,128,128]{3,0,2,1:T(8,128)} fusion(f32[4,128,128,8]{2,3,1,0:T(8,128)S(1)} %fusion.45, bf16[8,4,128,128]{3,2,1,0:T(8,128)(2,1)S(1)} %bitcast.157, f32[8,8,4]{1,2,0:T(4,128)S(1)} %get-tuple-element.61, pred[8,8]{1,0:T(8,128)(4,1)S(1)} %copy-done.14), kind=kOutput, calls=%fused_computation.13 | convolution fusion | flops 8914176 | bytes 5243968 | tf_op jit(solution)/shard_map/ijh,jhab->ihab/dot_general | solution.py:22
  67.7 10.2 %all-to-all-done.1 = bf16[32,48,128]{2,1,0:T(8,128)(2,1)S(1)} async-done(((bf16[32,48,128]{2,1,0:T(8,128)(2,1)}), bf16[32,48,128]{2,1,0:T(8,128)(2,1)S(1)}, u32[]{:S(2)}, u32[]{:S(2)}) %all-to-all-start.1) | async-done | bytes 393248 | tf_op jit(solution)/shard_map/all_to_all | solution.py:66
  80.0 0.8 copy.251
  80.8 4.7 %all-to-all-start.2 = ((bf16[32,32,128]{2,1,0:T(8,128)(2,1)}), bf16[32,32,128]{2,1,0:T(8,128)(2,1)S(1)}, u32[]{:S(2)}, u32[]{:S(2)}) async-start(bf16[32,32,128]{2,1,0:T(8,128)(2,1)} %copy.251), calls=%async_computation.2 | async-start | bytes 524288 | tf_op jit(solution)/shard_map/all_to_all | solution.py:88
  85.7 11.5 %all-to-all-done.2 = bf16[32,32,128]{2,1,0:T(8,128)(2,1)S(1)} async-done(((bf16[32,32,128]{2,1,0:T(8,128)(2,1)}), bf16[32,32,128]{2,1,0:T(8,128)(2,1)S(1)}, u32[]{:S(2)}, u32[]{:S(2)}) %all-to-all-start.2) | async-done | bytes 262176 | tf_op jit(solution)/shard_map/all_to_all | solution.py:88
  97.8 1.4 %copy-done.2 = f32[8,4,128,128]{3,0,2,1:T(8,128)S(1)} copy-done((f32[8,4,128,128]{3,0,2,1:T(8,128)S(1)}, f32[8,4,128,128]{3,0,2,1:T(8,128)}, u32[]{:S(2)}) %copy-start.2) | copy-done | bytes 2097176
  99.6 1.5 %pad_maximum_fusion = bf16[8,1024,128]{2,1,0:T(8,128)(2,1)} fusion(bf16[8,512,128]{2,1,0:T(8,128)(2,1)S(1)} %copy.254, bf16[8,512,128]{2,1,0:T(8,128)(2,1)S(1)} %copy.253), kind=kLoop, calls=%fused_computation.9 | loop fusion | flops 4194304 | bytes 4194304 | tf_op jit(solution)/shard_map/concatenate | solution.py:247
  101.1 3.6 %all-to-all-start.3 = ((bf16[8,1024,128]{2,1,0:T(8,128)(2,1)}), bf16[8,1024,128]{2,1,0:T(8,128)(2,1)S(1)}, u32[]{:S(2)}, u32[]{:S(2)}) async-start(bf16[8,1024,128]{2,1,0:T(8,128)(2,1)} %pad_maximum_fusion), calls=%async_computation.3 | async-start | bytes 4194304 | tf_op jit(solution)/shard_map/all_to_all | solution.py:254
  105.5 26.4 %all-to-all-done.3 = bf16[8,1024,128]{2,1,0:T(8,128)(2,1)S(1)} async-done(((bf16[8,1024,128]{2,1,0:T(8,128)(2,1)}), bf16[8,1024,128]{2,1,0:T(8,128)(2,1)S(1)}, u32[]{:S(2)}, u32[]{:S(2)}) %all-to-all-start.3) | async-done | bytes 2097184 | tf_op jit(solution)/shard_map/all_to_all | solution.py:254
  131.9 1.5 %fusion.117 = (bf16[8,512,128]{2,1,0:T(8,128)(2,1)}, bf16[8,512,128]{2,1,0:T(8,128)(2,1)}) fusion(bf16[8,1024,128]{2,1,0:T(8,128)(2,1)S(1)} %all-to-all-done.3), kind=kLoop, calls=%fused_computation.182 | loop fusion | bytes 4194304 | tf_op jit(solution)/shard_map/slice | solution.py:256
  133.4 7.3 %shard_map.76 = (bf16[128,4096]{1,0:T(8,128)(2,1)}, bf16[128,4096]{1,0:T(8,128)(2,1)}, bf16[128,4096]{1,0:T(8,128)(2,1)}) custom-call(bf16[128,4096]{1,0:T(8,128)(2,1)} %grad_ref.1, bf16[128,4096]{1,0:T(8,128)(2,1)} %value_ref.1, bf16[128,4096]{1,0:T(8,128)(2,1)} %key_ref.1, bf16[32,128,128]{2,1,0:T(8,128)(2,1)} %bitcast.170, ...), custom_call_target="tpu_custom_call" | custom-call | tf_op jit(solution)/shard_map/pallas_call | solution.py:201
  (91 shorter events, 16.5 us)
Async XLA Ops:
  0.6 1.7 %copy-start.5 = (bf16[128,32]{0,1:T(8,128)(2,1)S(1)}, bf16[128,32]{0,1:T(8,128)(2,1)}, u32[]{:S(2)}) copy-start(bf16[128,32]{0,1:T(8,128)(2,1)} %param.15) | copy-start | bytes 24580
  0.6 1.9 %copy-start = (bf16[128,4096]{1,0:T(8,128)(2,1)S(1)}, bf16[128,4096]{1,0:T(8,128)(2,1)}, u32[]{:S(2)}) copy-start(bf16[128,4096]{1,0:T(8,128)(2,1)} %grad_ref.1) | copy-start | bytes 3145732
  6.5 1.8 %copy-start.4 = (f32[128,32]{1,0:T(8,128)}, f32[128,32]{1,0:T(8,128)S(1)}, u32[]{:S(2)}) copy-start(f32[128,32]{1,0:T(8,128)S(1)} %subtract_exponential_fusion.after_ref) | copy-start | bytes 49156
  6.6 1.8 %copy-start.1 = (bf16[128,4096]{1,0:T(8,128)(2,1)S(1)}, bf16[128,4096]{1,0:T(8,128)(2,1)}, u32[]{:S(2)}) copy-start(bf16[128,4096]{1,0:T(8,128)(2,1)} %value_ref.1) | copy-start | bytes 3145732
  8.4 1.2 copy-start.3
  11.1 32.1 %all-to-all-start = ((bf16[8,1040,128]{2,1,0:T(8,128)(2,1)}), bf16[8,1040,128]{2,1,0:T(8,128)(2,1)}, u32[]{:S(2)}, u32[]{:S(2)}) async-start(bf16[8,1040,128]{2,1,0:T(8,128)(2,1)} %fusion.1), calls=%async_computation | async-start | bytes 4259840 | tf_op jit(solution)/shard_map/all_to_all | solution.py:232
  16.0 29.8 %copy-start.10 = (pred[8,8]{1,0:T(8,128)(4,1)}, pred[8,8]{1,0:T(8,128)(4,1)S(1)}, u32[]{:S(2)}) copy-start(pred[8,8]{1,0:T(8,128)(4,1)S(1)} %get-tuple-element.83) | copy-start | bytes 196
  16.0 29.8 %copy-start.13 = (pred[8,8]{1,0:T(8,128)(4,1)}, pred[8,8]{1,0:T(8,128)(4,1)S(1)}, u32[]{:S(2)}) copy-start(pred[8,8]{1,0:T(8,128)(4,1)S(1)} %get-tuple-element.84) | copy-start | bytes 196
  49.9 13.2 %copy-start.6 = (pred[8,8,8]{2,1,0:T(8,128)(4,1)S(1)}, pred[8,8,8]{2,1,0:T(8,128)(4,1)}, u32[]{:S(2)}) copy-start(pred[8,8,8]{2,1,0:T(8,128)(4,1)} %get-tuple-element.85) | copy-start | bytes 1540
  49.9 13.2 %copy-start.7 = (pred[8,8,8]{2,1,0:T(8,128)(4,1)S(1)}, pred[8,8,8]{2,1,0:T(8,128)(4,1)}, u32[]{:S(2)}) copy-start(pred[8,8,8]{2,1,0:T(8,128)(4,1)} %get-tuple-element.86) | copy-start | bytes 1540
  49.9 13.4 %copy-start.14 = (pred[8,8]{1,0:T(8,128)(4,1)S(1)}, pred[8,8]{1,0:T(8,128)(4,1)}, u32[]{:S(2)}) copy-start(pred[8,8]{1,0:T(8,128)(4,1)} %copy-done.13) | copy-start | bytes 196
  51.8 12.3 %copy-start.11 = (pred[8,8]{1,0:T(8,128)(4,1)S(1)}, pred[8,8]{1,0:T(8,128)(4,1)}, u32[]{:S(2)}) copy-start(pred[8,8]{1,0:T(8,128)(4,1)} %copy-done.10) | copy-start | bytes 196
  51.8 26.1 %all-to-all-start.1 = ((bf16[32,48,128]{2,1,0:T(8,128)(2,1)}), bf16[32,48,128]{2,1,0:T(8,128)(2,1)S(1)}, u32[]{:S(2)}, u32[]{:S(2)}) async-start(bf16[32,48,128]{2,1,0:T(8,128)(2,1)} %pad_maximum_fusion.1), calls=%async_computation.1 | async-start | bytes 786432 | tf_op jit(solution)/shard_map/all_to_all | solution.py:66
  64.8 2.2 %copy-start.12 = (pred[8,8]{1,0:T(8,128)(4,1)S(1)}, pred[8,8]{1,0:T(8,128)(4,1)}, u32[]{:S(2)}) copy-start(pred[8,8]{1,0:T(8,128)(4,1)} %copy-done.10) | copy-start | bytes 196
  67.7 17.8 %copy-start.9 = (f32[8,4]{1,0:T(8,128)S(1)}, f32[8,4]{1,0:T(8,128)}, u32[]{:S(2)}) copy-start(f32[8,4]{1,0:T(8,128)} %get-tuple-element.75) | copy-start | bytes 388
  67.7 17.9 %copy-start.8 = (f32[8,4]{1,0:T(8,128)S(1)}, f32[8,4]{1,0:T(8,128)}, u32[]{:S(2)}) copy-start(f32[8,4]{1,0:T(8,128)} %get-tuple-element.72) | copy-start | bytes 388
  80.8 16.4 %all-to-all-start.2 = ((bf16[32,32,128]{2,1,0:T(8,128)(2,1)}), bf16[32,32,128]{2,1,0:T(8,128)(2,1)S(1)}, u32[]{:S(2)}, u32[]{:S(2)}) async-start(bf16[32,32,128]{2,1,0:T(8,128)(2,1)} %copy.251), calls=%async_computation.2 | async-start | bytes 524288 | tf_op jit(solution)/shard_map/all_to_all | solution.py:88
  97.6 1.6 %copy-start.2 = (f32[8,4,128,128]{3,0,2,1:T(8,128)S(1)}, f32[8,4,128,128]{3,0,2,1:T(8,128)}, u32[]{:S(2)}) copy-start(f32[8,4,128,128]{3,0,2,1:T(8,128)} %add_bitcast_fusion.1) | copy-start | bytes 6291460
  101.1 30.7 %all-to-all-start.3 = ((bf16[8,1024,128]{2,1,0:T(8,128)(2,1)}), bf16[8,1024,128]{2,1,0:T(8,128)(2,1)S(1)}, u32[]{:S(2)}, u32[]{:S(2)}) async-start(bf16[8,1024,128]{2,1,0:T(8,128)(2,1)} %pad_maximum_fusion), calls=%async_computation.3 | async-start | bytes 4194304 | tf_op jit(solution)/shard_map/all_to_all | solution.py:254

commit v17 on v16

--- a/solution.py
+++ b/solution.py
@@ -191,7 +191,7 @@
 def finish_call(out_grad, values, keys, state_in, adjoint_in, qp, kp, vp, before, after):
     length, columns = out_grad.shape
     heads, width = state_in.shape[0], state_in.shape[2]
-    group = 8
+    group = 16
     steps = heads // group
     flat_spec = pl.BlockSpec((length, group * width), lambda h: (0, h))
     head_spec = pl.BlockSpec((group, width, width), lambda h: (h, 0, 0))

time: 142 us -> 141 us (level)
  no operation moved by 1% of the time
where the time goes in v17:
time: 141 us; the launch traced here: 140 us
  waiting for transfers between devices  64.5 us (46%)
  starting transfers between devices  24.1 us (17%)
  matrix products  22.7 us (16%)
  local copies, waits for them, and re-layouts  12 us (9%)
  other arithmetic  9.12 us (6%)
  Pallas kernels  6.49 us (5%)
    all_to_all x1, waiting for transfers between devices, body(): back = lax.all_to_all(returned, 'exp', 0, 0, tiled=True)  26.4 us
    dot_general x20, matrix products, product(): jnp.einsum(form, first_op, second_op, preferred_element_type=jnp.float32)  22.5 us
    all_to_all x1, waiting for transfers between devices, body(): got = lax.all_to_all(packed, 'exp', 0, 0, tiled=True)  16.4 us
    all_to_all x1, waiting for transfers between devices, carried_both(): lax.all_to_all(jnp.concatenate([state_rows, adjoint_rows], axis=1).astype...  11.5 us
    all_to_all x1, starting transfers between devices, carried_both(): got = lax.all_to_all(payload, axis, 0, 0, tiled=True)  11.3 us
    all_to_all x1, waiting for transfers between devices, carried_both(): got = lax.all_to_all(payload, axis, 0, 0, tiled=True)  10.2 us
    pallas_call x1, Pallas kernels, finish_call(): pl.pallas_call(finish_kernel, grid=(steps,), in_specs=[flat_spec, flat_sp...  6.49 us
    all_to_all x1, starting transfers between devices, carried_both(): lax.all_to_all(jnp.concatenate([state_rows, adjoint_rows], axis=1).astype...  4.69 us
  transfers between devices with their start and end apart: 4, of which 4 were waited for; matrix products, arithmetic and copies ran while one was open for 12% of the time, Pallas kernels for 0%

profile of v17, /device:TPU:32, one launch (start us, length us, event | category | flops | bytes accessed | tf_op | source)
XLA Modules:
  0.0 139.9 jit_solution(1101999453510190397)
XLA Ops:
  0.7 1.7 %copy.273 = bf16[128,4096]{0,1:T(8,128)(2,1)S(1)} copy(bf16[128,4096]{1,0:T(8,128)(2,1)} %param.11) | data formatting | bytes 2097152 | tf_op jit(solution)/shard_map/reshape | solution.py:132
  3.0 1.6 %add_convert_fusion.2 = bf16[32,128,128]{2,1,0:T(8,128)(2,1)} fusion(f32[32,128,128]{2,1,0:T(8,128)S(1)} %fusion.10, bf16[128,32,128]{0,2,1:T(8,128)(2,1)S(1)} %bitcast.159, f32[128,32]{0,1:T(8,128)S(1)} %get-tuple-element.81, bf16[128,4096]{1,0:T(8,128)(2,1)S(1)} %copy-done), kind=kOutput, calls=%fused_computation.17 | convolution fusion | flops 137887744 | bytes 5259264 | tf_op jit(solution)/shard_map/tha,thb->hab/dot_general | solution.py:22
  4.6 1.6 %copy.272 = bf16[128,4096]{0,1:T(8,128)(2,1)S(1)} copy(bf16[128,4096]{1,0:T(8,128)(2,1)} %key_ref.1) | data formatting | bytes 2097152 | tf_op jit(solution)/shard_map/reshape | solution.py:133
  6.6 1.8 %fusion.9 = f32[32,128,128]{2,1,0:T(8,128)S(1)} fusion(bf16[128,32,128]{0,2,1:T(8,128)(2,1)S(1)} %bitcast.162, f32[128,32]{0,1:T(8,128)S(1)} %copy.221, bf16[128,4096]{1,0:T(8,128)(2,1)} %value_ref.1), kind=kOutput, calls=%fused_computation.26 | convolution fusion | flops 136314880 | bytes 4210688 | tf_op jit(solution)/shard_map/sha,shb->hab/dot_general | solution.py:22
  9.6 1.5 %fusion.1 = bf16[8,1040,128]{2,1,0:T(8,128)(2,1)} fusion(bf16[8,4,128]{2,1,0:T(4,128)(2,1)S(1)} %bitcast.183, bf16[8,512,128]{2,1,0:T(8,128)(2,1)S(1)} %bitcast.168, bf16[8,512,128]{2,1,0:T(8,128)(2,1)S(1)} %bitcast.171), kind=kLoop, calls=%fused_computation.6 | loop fusion | flops 8519680 | bytes 4235264 | tf_op jit(solution)/shard_map/concatenate | solution.py:224
  11.1 4.5 %all-to-all-start = ((bf16[8,1040,128]{2,1,0:T(8,128)(2,1)}), bf16[8,1040,128]{2,1,0:T(8,128)(2,1)}, u32[]{:S(2)}, u32[]{:S(2)}) async-start(bf16[8,1040,128]{2,1,0:T(8,128)(2,1)} %fusion.1), calls=%async_computation | async-start | bytes 4259840 | tf_op jit(solution)/shard_map/all_to_all | solution.py:232
  16.7 2.9 %multiply_convert_fusion.1 = bf16[32,128,128]{2,1,0:T(8,128)(2,1)S(1)} fusion(f32[32,128]{1,0:T(8,128)S(1)} %bitcast.181, pred[128,128]{1,0:T(8,128)(4,1)S(1)} %iota_compare_fusion.5, bf16[128,4096]{1,0:T(8,128)(2,1)S(1)} %copy-done, bf16[128,4096]{1,0:T(8,128)(2,1)} %value_ref.1), kind=kOutput, calls=%fused_computation.15 | convolution fusion | flops 136839168 | bytes 3178496 | tf_op jit(solution)/shard_map/thd,shd->hts/dot_general | solution.py:22
  19.6 2.2 %fusion.122.qp_ref = f32[32,128,128]{2,1,0:T(8,128)} fusion(bf16[32,128,128]{2,1,0:T(8,128)(2,1)S(1)} %multiply_convert_fusion.1, bf16[128,32,128]{0,2,1:T(8,128)(2,1)S(1)} %bitcast.164), kind=kOutput, calls=%fused_computation.187 | convolution fusion | flops 134217728 | bytes 4194304 | tf_op jit(solution)/shard_map/hts,shd->htd/dot_general | solution.py:22
  21.7 2.2 %fusion.123.kp_ref = f32[32,128,128]{2,1,0:T(8,128)} fusion(bf16[32,128,128]{2,1,0:T(8,128)(2,1)S(1)} %multiply_convert_fusion.1, bf16[128,32,128]{0,2,1:T(8,128)(2,1)S(1)} %bitcast.160), kind=kOutput, calls=%fused_computation.188 | convolution fusion | flops 134217728 | bytes 4194304 | tf_op jit(solution)/shard_map/hts,thd->hsd/dot_general | solution.py:22
  23.9 2.8 %fusion.4.vp_ref = f32[32,128,128]{2,1,0:T(8,128)} fusion(bf16[128,32,128]{0,2,1:T(8,128)(2,1)S(1)} %bitcast.161, bf16[128,32,128]{0,2,1:T(8,128)(2,1)S(1)} %bitcast.165, f32[32,128]{1,0:T(8,128)S(1)} %bitcast.182, pred[128,128]{1,0:T(8,128)(4,1)S(1)} %iota_compare_fusion.5, bf16[128,4096]{1,0:T(8,128)(2,1)S(1)} %copy-done), kind=kOutput, calls=%fused_computation.21 | convolution fusion | flops 271056896 | bytes 5275648 | tf_op jit(solution)/shard_map/hts,thd->hsd/dot_general | solution.py:22
  26.8 16.4 %all-to-all-done = bf16[8,1040,128]{2,1,0:T(8,128)(2,1)} async-done(((bf16[8,1040,128]{2,1,0:T(8,128)(2,1)}), bf16[8,1040,128]{2,1,0:T(8,128)(2,1)}, u32[]{:S(2)}, u32[]{:S(2)}) %all-to-all-start) | async-done | bytes 2129952 | tf_op jit(solution)/shard_map/all_to_all | solution.py:232
  44.0 1.7 %fusion.116 = (bf16[8,512,128]{2,1,0:T(8,128)(2,1)S(1)}, bf16[8,512,128]{2,1,0:T(8,128)(2,1)S(1)}) fusion(bf16[8,1040,128]{2,1,0:T(8,128)(2,1)} %all-to-all-done), kind=kLoop, calls=%fused_computation.181 | loop fusion | bytes 4194304 | tf_op jit(solution)/shard_map/slice | solution.py:234
  51.8 11.3 %all-to-all-start.1 = ((bf16[32,48,128]{2,1,0:T(8,128)(2,1)}), bf16[32,48,128]{2,1,0:T(8,128)(2,1)S(1)}, u32[]{:S(2)}, u32[]{:S(2)}) async-start(bf16[32,48,128]{2,1,0:T(8,128)(2,1)} %pad_maximum_fusion.1), calls=%async_computation.1 | async-start | bytes 786432 | tf_op jit(solution)/shard_map/all_to_all | solution.py:66
  64.8 2.1 %add_bitcast_fusion.1 = f32[8,4,128,128]{3,0,2,1:T(8,128)} fusion(f32[4,128,128,8]{2,3,1,0:T(8,128)S(1)} %fusion.45, bf16[8,4,128,128]{3,2,1,0:T(8,128)(2,1)S(1)} %bitcast.157, f32[8,8,4]{1,2,0:T(4,128)S(1)} %get-tuple-element.61, pred[8,8]{1,0:T(8,128)(4,1)S(1)} %copy-done.14), kind=kOutput, calls=%fused_computation.13 | convolution fusion | flops 8914176 | bytes 5243968 | tf_op jit(solution)/shard_map/ijh,jhab->ihab/dot_general | solution.py:22
  67.7 10.2 %all-to-all-done.1 = bf16[32,48,128]{2,1,0:T(8,128)(2,1)S(1)} async-done(((bf16[32,48,128]{2,1,0:T(8,128)(2,1)}), bf16[32,48,128]{2,1,0:T(8,128)(2,1)S(1)}, u32[]{:S(2)}, u32[]{:S(2)}) %all-to-all-start.1) | async-done | bytes 393248 | tf_op jit(solution)/shard_map/all_to_all | solution.py:66
  80.0 0.8 copy.251
  80.8 4.7 %all-to-all-start.2 = ((bf16[32,32,128]{2,1,0:T(8,128)(2,1)}), bf16[32,32,128]{2,1,0:T(8,128)(2,1)S(1)}, u32[]{:S(2)}, u32[]{:S(2)}) async-start(bf16[32,32,128]{2,1,0:T(8,128)(2,1)} %copy.251), calls=%async_computation.2 | async-start | bytes 524288 | tf_op jit(solution)/shard_map/all_to_all | solution.py:88
  85.7 11.5 %all-to-all-done.2 = bf16[32,32,128]{2,1,0:T(8,128)(2,1)S(1)} async-done(((bf16[32,32,128]{2,1,0:T(8,128)(2,1)}), bf16[32,32,128]{2,1,0:T(8,128)(2,1)S(1)}, u32[]{:S(2)}, u32[]{:S(2)}) %all-to-all-start.2) | async-done | bytes 262176 | tf_op jit(solution)/shard_map/all_to_all | solution.py:88
  97.8 1.4 %copy-done.2 = f32[8,4,128,128]{3,0,2,1:T(8,128)S(1)} copy-done((f32[8,4,128,128]{3,0,2,1:T(8,128)S(1)}, f32[8,4,128,128]{3,0,2,1:T(8,128)}, u32[]{:S(2)}) %copy-start.2) | copy-done | bytes 2097176
  99.6 1.5 %pad_maximum_fusion = bf16[8,1024,128]{2,1,0:T(8,128)(2,1)} fusion(bf16[8,512,128]{2,1,0:T(8,128)(2,1)S(1)} %copy.254, bf16[8,512,128]{2,1,0:T(8,128)(2,1)S(1)} %copy.253), kind=kLoop, calls=%fused_computation.9 | loop fusion | flops 4194304 | bytes 4194304 | tf_op jit(solution)/shard_map/concatenate | solution.py:247
  101.1 3.6 %all-to-all-start.3 = ((bf16[8,1024,128]{2,1,0:T(8,128)(2,1)}), bf16[8,1024,128]{2,1,0:T(8,128)(2,1)S(1)}, u32[]{:S(2)}, u32[]{:S(2)}) async-start(bf16[8,1024,128]{2,1,0:T(8,128)(2,1)} %pad_maximum_fusion), calls=%async_computation.3 | async-start | bytes 4194304 | tf_op jit(solution)/shard_map/all_to_all | solution.py:254
  105.5 26.4 %all-to-all-done.3 = bf16[8,1024,128]{2,1,0:T(8,128)(2,1)S(1)} async-done(((bf16[8,1024,128]{2,1,0:T(8,128)(2,1)}), bf16[8,1024,128]{2,1,0:T(8,128)(2,1)S(1)}, u32[]{:S(2)}, u32[]{:S(2)}) %all-to-all-start.3) | async-done | bytes 2097184 | tf_op jit(solution)/shard_map/all_to_all | solution.py:254
  131.9 1.5 %fusion.117 = (bf16[8,512,128]{2,1,0:T(8,128)(2,1)}, bf16[8,512,128]{2,1,0:T(8,128)(2,1)}) fusion(bf16[8,1024,128]{2,1,0:T(8,128)(2,1)S(1)} %all-to-all-done.3), kind=kLoop, calls=%fused_computation.182 | loop fusion | bytes 4194304 | tf_op jit(solution)/shard_map/slice | solution.py:256
  133.4 6.5 %shard_map.76 = (bf16[128,4096]{1,0:T(8,128)(2,1)}, bf16[128,4096]{1,0:T(8,128)(2,1)}, bf16[128,4096]{1,0:T(8,128)(2,1)}) custom-call(bf16[128,4096]{1,0:T(8,128)(2,1)} %grad_ref.1, bf16[128,4096]{1,0:T(8,128)(2,1)} %value_ref.1, bf16[128,4096]{1,0:T(8,128)(2,1)} %key_ref.1, bf16[32,128,128]{2,1,0:T(8,128)(2,1)} %bitcast.170, ...), custom_call_target="tpu_custom_call" | custom-call | tf_op jit(solution)/shard_map/pallas_call | solution.py:201
  (91 shorter events, 16.5 us)
Async XLA Ops:
  0.6 1.7 %copy-start.5 = (bf16[128,32]{0,1:T(8,128)(2,1)S(1)}, bf16[128,32]{0,1:T(8,128)(2,1)}, u32[]{:S(2)}) copy-start(bf16[128,32]{0,1:T(8,128)(2,1)} %param.15) | copy-start | bytes 24580
  0.6 1.9 %copy-start = (bf16[128,4096]{1,0:T(8,128)(2,1)S(1)}, bf16[128,4096]{1,0:T(8,128)(2,1)}, u32[]{:S(2)}) copy-start(bf16[128,4096]{1,0:T(8,128)(2,1)} %grad_ref.1) | copy-start | bytes 3145732
  6.5 1.8 %copy-start.4 = (f32[128,32]{1,0:T(8,128)}, f32[128,32]{1,0:T(8,128)S(1)}, u32[]{:S(2)}) copy-start(f32[128,32]{1,0:T(8,128)S(1)} %subtract_exponential_fusion.after_ref) | copy-start | bytes 49156
  6.6 1.8 %copy-start.1 = (bf16[128,4096]{1,0:T(8,128)(2,1)S(1)}, bf16[128,4096]{1,0:T(8,128)(2,1)}, u32[]{:S(2)}) copy-start(bf16[128,4096]{1,0:T(8,128)(2,1)} %value_ref.1) | copy-start | bytes 3145732
  8.4 1.2 copy-start.3
  11.1 32.1 %all-to-all-start = ((bf16[8,1040,128]{2,1,0:T(8,128)(2,1)}), bf16[8,1040,128]{2,1,0:T(8,128)(2,1)}, u32[]{:S(2)}, u32[]{:S(2)}) async-start(bf16[8,1040,128]{2,1,0:T(8,128)(2,1)} %fusion.1), calls=%async_computation | async-start | bytes 4259840 | tf_op jit(solution)/shard_map/all_to_all | solution.py:232
  16.0 29.8 %copy-start.10 = (pred[8,8]{1,0:T(8,128)(4,1)}, pred[8,8]{1,0:T(8,128)(4,1)S(1)}, u32[]{:S(2)}) copy-start(pred[8,8]{1,0:T(8,128)(4,1)S(1)} %get-tuple-element.83) | copy-start | bytes 196
  16.0 29.8 %copy-start.13 = (pred[8,8]{1,0:T(8,128)(4,1)}, pred[8,8]{1,0:T(8,128)(4,1)S(1)}, u32[]{:S(2)}) copy-start(pred[8,8]{1,0:T(8,128)(4,1)S(1)} %get-tuple-element.84) | copy-start | bytes 196
  49.9 13.2 %copy-start.6 = (pred[8,8,8]{2,1,0:T(8,128)(4,1)S(1)}, pred[8,8,8]{2,1,0:T(8,128)(4,1)}, u32[]{:S(2)}) copy-start(pred[8,8,8]{2,1,0:T(8,128)(4,1)} %get-tuple-element.85) | copy-start | bytes 1540
  49.9 13.2 %copy-start.7 = (pred[8,8,8]{2,1,0:T(8,128)(4,1)S(1)}, pred[8,8,8]{2,1,0:T(8,128)(4,1)}, u32[]{:S(2)}) copy-start(pred[8,8,8]{2,1,0:T(8,128)(4,1)} %get-tuple-element.86) | copy-start | bytes 1540
  49.9 13.4 %copy-start.14 = (pred[8,8]{1,0:T(8,128)(4,1)S(1)}, pred[8,8]{1,0:T(8,128)(4,1)}, u32[]{:S(2)}) copy-start(pred[8,8]{1,0:T(8,128)(4,1)} %copy-done.13) | copy-start | bytes 196
  51.8 12.3 %copy-start.11 = (pred[8,8]{1,0:T(8,128)(4,1)S(1)}, pred[8,8]{1,0:T(8,128)(4,1)}, u32[]{:S(2)}) copy-start(pred[8,8]{1,0:T(8,128)(4,1)} %copy-done.10) | copy-start | bytes 196
  51.8 26.1 %all-to-all-start.1 = ((bf16[32,48,128]{2,1,0:T(8,128)(2,1)}), bf16[32,48,128]{2,1,0:T(8,128)(2,1)S(1)}, u32[]{:S(2)}, u32[]{:S(2)}) async-start(bf16[32,48,128]{2,1,0:T(8,128)(2,1)} %pad_maximum_fusion.1), calls=%async_computation.1 | async-start | bytes 786432 | tf_op jit(solution)/shard_map/all_to_all | solution.py:66
  64.8 2.2 %copy-start.12 = (pred[8,8]{1,0:T(8,128)(4,1)S(1)}, pred[8,8]{1,0:T(8,128)(4,1)}, u32[]{:S(2)}) copy-start(pred[8,8]{1,0:T(8,128)(4,1)} %copy-done.10) | copy-start | bytes 196
  67.7 17.8 %copy-start.9 = (f32[8,4]{1,0:T(8,128)S(1)}, f32[8,4]{1,0:T(8,128)}, u32[]{:S(2)}) copy-start(f32[8,4]{1,0:T(8,128)} %get-tuple-element.75) | copy-start | bytes 388
  67.7 17.9 %copy-start.8 = (f32[8,4]{1,0:T(8,128)S(1)}, f32[8,4]{1,0:T(8,128)}, u32[]{:S(2)}) copy-start(f32[8,4]{1,0:T(8,128)} %get-tuple-element.72) | copy-start | bytes 388
  80.8 16.4 %all-to-all-start.2 = ((bf16[32,32,128]{2,1,0:T(8,128)(2,1)}), bf16[32,32,128]{2,1,0:T(8,128)(2,1)S(1)}, u32[]{:S(2)}, u32[]{:S(2)}) async-start(bf16[32,32,128]{2,1,0:T(8,128)(2,1)} %copy.251), calls=%async_computation.2 | async-start | bytes 524288 | tf_op jit(solution)/shard_map/all_to_all | solution.py:88
  97.6 1.6 %copy-start.2 = (f32[8,4,128,128]{3,0,2,1:T(8,128)S(1)}, f32[8,4,128,128]{3,0,2,1:T(8,128)}, u32[]{:S(2)}) copy-start(f32[8,4,128,128]{3,0,2,1:T(8,128)} %add_bitcast_fusion.1) | copy-start | bytes 6291460
  101.1 30.7 %all-to-all-start.3 = ((bf16[8,1024,128]{2,1,0:T(8,128)(2,1)}), bf16[8,1024,128]{2,1,0:T(8,128)(2,1)S(1)}, u32[]{:S(2)}, u32[]{:S(2)}) async-start(bf16[8,1024,128]{2,1,0:T(8,128)(2,1)} %pad_maximum_fusion), calls=%async_computation.3 | async-start | bytes 4194304 | tf_op jit(solution)/shard_map/all_to_all | solution.py:254
